TPU v7x, 32 devices: a whole 2x2x4 slice. The times are simulated.
32 devices in a mesh: grp: 2 (over y), seq: 4 (over z), head: 2 (over x), sub: 2 (over core).
Axes of the slice: x: 2, y: 2, z: 4, core: 2. Of those that a mesh axis runs over, the one named last changes fastest.
Arguments:
- queries: bfloat16 [4096, 64, 128], P(('grp', 'seq'), ('head', 'sub')), parts along dimension 0, may hold values from -6 to 6
- key_rows: bfloat16 [4096, 64, 128], P(('grp', 'seq'), ('head', 'sub')), parts along dimension 0, may hold values from -6 to 6
- value_rows: bfloat16 [4096, 64, 128], P(('grp', 'seq'), ('head', 'sub')), parts along dimension 0, may hold values from -6 to 6
- out_adjoint: bfloat16 [4096, 64, 128], P(('grp', 'seq'), ('head', 'sub')), parts along dimension 0, may hold values from -6 to 6
Outputs:
- attended: bfloat16 [4096, 64, 128], P(('grp', 'seq'), ('head', 'sub')), parts along dimension 0
- query_grad: bfloat16 [4096, 64, 128], P(('grp', 'seq', 'head', 'sub')), parts along dimension 0
- key_grad: bfloat16 [4096, 64, 128], P(('grp', 'seq', 'head', 'sub')), parts along dimension 0
- value_grad: bfloat16 [4096, 64, 128], P(('grp', 'seq', 'head', 'sub')), parts along dimension 0
There are 2 independent parts, one for each index of `grp`. A program takes and returns all parts, laid end to end along the dimension named above; each array names one. Nothing has to cross between parts.
All inputs are finite; a program needn't handle non-finite values.
Results may differ from a plain program's by a relative error of at most 0.0058.
Values may be sent and summed in bfloat16 or wider, within the bound.
No kernel may reach another device: no remote copies, remote signals or barrier semaphores. Data moves between devices by JAX's collectives and lax.ppermute only.
A program may use at most 128 MiB of HBM per device.

v0:
```python
import functools

import jax
import jax.numpy as jnp
from jax import lax
from jax.experimental import pallas as pl
from jax.experimental.pallas import tpu as pltpu
from jax.sharding import PartitionSpec as P

SPAN = 64
F32 = jnp.float32
BF16 = jnp.bfloat16


def dot_nn(a, b):
    return jnp.dot(a, b, preferred_element_type=F32)


def dot_nt(a, b):
    return lax.dot_general(a, b, (((1,), (1,)), ((), ())), preferred_element_type=F32)


def dot_tn(a, b):
    return lax.dot_general(a, b, (((0,), (0,)), ((), ())), preferred_element_type=F32)


def totals_kernel(heads, q_ref, k_ref, v_ref, d_ref, f_ref, kv_ref, adj_ref):
    @pl.when(pl.program_id(0) == 0)
    def _():
        kv_ref[...] = jnp.zeros_like(kv_ref)
        adj_ref[...] = jnp.zeros_like(adj_ref)

    factor = f_ref[...]
    for h in range(heads):
        qsc = (q_ref[:, h, :].astype(F32) * factor).astype(BF16)
        kv_ref[h] += dot_tn(k_ref[:, h, :], v_ref[:, h, :])
        adj_ref[h] += dot_tn(d_ref[:, h, :], qsc)


def main_kernel(heads, q_ref, k_ref, v_ref, d_ref, f_ref, before_ref, rest_ref,
                a_ref, qg_ref, kg_ref, vg_ref, state, suffix):
    @pl.when(pl.program_id(0) == 0)
    def _():
        state[...] = before_ref[...]
        suffix[...] = rest_ref[...]

    factor = f_ref[...]
    span = factor.shape[0]
    row = lax.broadcasted_iota(jnp.int32, (span, span), 0)
    col = lax.broadcasted_iota(jnp.int32, (span, span), 1)
    causal = row >= col
    for h in range(heads):
        q = q_ref[:, h, :]
        k = k_ref[:, h, :]
        v = v_ref[:, h, :]
        d = d_ref[:, h, :]
        qsc = (q.astype(F32) * factor).astype(BF16)
        prev = state[h]
        state_low = prev.astype(BF16)
        state[h] = prev + dot_tn(k, v)
        rest = suffix[h] - dot_tn(d, qsc)
        suffix[h] = rest
        suffix_low = rest.astype(BF16)
        scores = jnp.where(causal, dot_nt(qsc, k), 0.0).astype(BF16)
        adj_scores = jnp.where(causal, dot_nt(d, v), 0.0).astype(BF16)
        a_ref[:, h, :] = (dot_nn(qsc, state_low) + dot_nn(scores, v)).astype(a_ref.dtype)
        qg_ref[:, h, :] = ((dot_nt(d, state_low) + dot_nn(adj_scores, k)) * factor).astype(qg_ref.dtype)
        kg_ref[:, h, :] = (dot_nn(v, suffix_low) + dot_tn(adj_scores, qsc)).astype(kg_ref.dtype)
        vg_ref[:, h, :] = (dot_nt(k, suffix_low) + dot_tn(scores, d)).astype(vg_ref.dtype)


def exclusive_scan(total, axis, count, reverse):
    carried = jnp.zeros_like(total)
    acc = jnp.zeros_like(total)
    for hop in range(count - 1):
        pair = (count - 1 - hop, count - 2 - hop) if reverse else (hop, hop + 1)
        got = lax.ppermute(carried + total, axis, perm=[pair])
        acc = acc + got
        carried = got
    return acc


def per_device(queries, key_rows, value_rows, out_adjoint, seq_count):
    tok_dev, heads, head_dim = queries.shape
    span = SPAN
    blocks = tok_dev // span
    offset = lax.axis_index("seq") * tok_dev
    position = offset + jnp.arange(tok_dev, dtype=jnp.int32)
    factor = lax.rsqrt(jnp.float32(head_dim) * (position + 1).astype(jnp.float32))[:, None]

    tile = pl.BlockSpec((span, heads, head_dim), lambda c: (c, 0, 0))
    fac = pl.BlockSpec((span, 1), lambda c: (c, 0))
    whole = pl.BlockSpec((heads, head_dim, head_dim), lambda c: (0, 0, 0))
    state_shape = jax.ShapeDtypeStruct((heads, head_dim, head_dim), F32)
    kv_total, adj_total = pl.pallas_call(
        functools.partial(totals_kernel, heads),
        grid=(blocks,),
        in_specs=[tile, tile, tile, tile, fac],
        out_specs=[whole, whole],
        out_shape=[state_shape, state_shape],
        compiler_params=pltpu.CompilerParams(dimension_semantics=("arbitrary",)),
    )(queries, key_rows, value_rows, out_adjoint, factor)

    before = exclusive_scan(kv_total, "seq", seq_count, False)
    after = exclusive_scan(adj_total, "seq", seq_count, True)
    rest = after + adj_total

    out_tile = jax.ShapeDtypeStruct((tok_dev, heads, head_dim), BF16)
    attended, query_grad, key_grad, value_grad = pl.pallas_call(
        functools.partial(main_kernel, heads),
        grid=(blocks,),
        in_specs=[tile, tile, tile, tile, fac, whole, whole],
        out_specs=[tile, tile, tile, tile],
        out_shape=[out_tile] * 4,
        scratch_shapes=[pltpu.VMEM((heads, head_dim, head_dim), F32)] * 2,
        compiler_params=pltpu.CompilerParams(dimension_semantics=("arbitrary",)),
    )(queries, key_rows, value_rows, out_adjoint, factor, before, rest)

    outs = tuple(
        lax.all_to_all(g, ("head", "sub"), split_axis=0, concat_axis=1, tiled=True)
        for g in (query_grad, key_grad, value_grad)
    )
    return (attended,) + outs


def solution(mesh):
    seq_count = mesh.shape["seq"]
    spec_in = P(("grp", "seq"), ("head", "sub"), None)
    spec_grad = P(("grp", "seq", "head", "sub"), None, None)
    return jax.shard_map(
        lambda *a: per_device(*a, seq_count),
        mesh=mesh,
        in_specs=(spec_in,) * 4,
        out_specs=(spec_in, spec_grad, spec_grad, spec_grad),
        check_vma=False,
    )
```

profile of v0, /device:TPU:0, one launch (start us, length us, event | category | flops | bytes accessed | tf_op | source)
XLA Modules:
  0.0 236.7 jit_solution(106961696673277441)
XLA Ops:
  0.6 0.8 multiply_rsqrt_fusion.f_ref
  1.4 17.0 %shard_map.75 = (f32[16,128,128]{2,1,0:T(8,128)}, f32[16,128,128]{2,1,0:T(8,128)}) custom-call(bf16[512,16,128]{2,1,0:T(8,128)(2,1)} %q_ref.3, bf16[512,16,128]{2,1,0:T(8,128)(2,1)} %k_ref.3, bf16[512,16,128]{2,1,0:T(8,128)(2,1)} %v_ref.3, bf16[512,16,128]{2,1,0:T(8,128)(2,1)} %d_ref.3, f32[512,1]{1,0:T(8,128)} %multiply_rsqrt_fusion.f_ref), custom_call_target="tpu_custom_call" | custom-call | tf_op jit(solution)/shard_map/pallas_call | solution.py:95
  18.4 5.1 %collective-permute-start = (f32[16,128,128]{2,1,0:T(8,128)}, f32[16,128,128]{2,1,0:T(8,128)S(1)}, u32[]{:S(2)}, u32[]{:S(2)}) collective-permute-start(f32[16,128,128]{2,1,0:T(8,128)} %get-tuple-element.10), channel_id=1, source_target_pairs={{0,4},{1,5},{2,6},{3,7},{16,20},{17,21},{18,22},{19,23}} | collective-permute-start | bytes 3145736 | tf_op jit(solution)/shard_map/ppermute | solution.py:77
  23.5 0.7 collective-permute-start.3
  24.3 21.9 %collective-permute-done = f32[16,128,128]{2,1,0:T(8,128)S(1)} collective-permute-done((f32[16,128,128]{2,1,0:T(8,128)}, f32[16,128,128]{2,1,0:T(8,128)S(1)}, u32[]{:S(2)}, u32[]{:S(2)}) %collective-permute-start) | collective-permute-done | bytes 1048608 | tf_op jit(solution)/shard_map/ppermute | solution.py:77
  46.2 1.4 add.57
  47.6 0.9 collective-permute-start.1
  48.5 0.1 add.61
  48.6 0.7 collective-permute-start.4
  49.3 0.1 add.59
  49.5 0.7 collective-permute-start.2
  50.2 0.1 add.63
  50.4 1.3 collective-permute-start.5
  51.7 1.2 add_add_fusion.1.before_ref
  52.9 47.4 %collective-permute-done.5 = f32[16,128,128]{2,1,0:T(8,128)S(1)} collective-permute-done((f32[16,128,128]{2,1,0:T(8,128)S(1)}, f32[16,128,128]{2,1,0:T(8,128)S(1)}, u32[]{:S(2)}, u32[]{:S(2)}) %collective-permute-start.5) | collective-permute-done | bytes 1048608 | tf_op jit(solution)/shard_map/ppermute | solution.py:77
  100.3 1.2 add_add_fusion.rest_ref
  101.5 44.7 %shard_map.76 = (bf16[512,16,128]{2,1,0:T(8,128)(2,1)}, bf16[512,16,128]{2,1,0:T(8,128)(2,1)}, bf16[512,16,128]{2,1,0:T(8,128)(2,1)}, bf16[512,16,128]{2,1,0:T(8,128)(2,1)}) custom-call(bf16[512,16,128]{2,1,0:T(8,128)(2,1)} %q_ref.3, bf16[512,16,128]{2,1,0:T(8,128)(2,1)} %k_ref.3, bf16[512,16,128]{2,1,0:T(8,128)(2,1)} %v_ref.3, bf16[512,16,128]{2,1,0:T(8,128)(2,1)} %d_ref.3, ...), custom_call_target="tpu_custom_call" | custom-call | tf_op jit(solution)/shard_map/pallas_call | solution.py:109
  146.3 30.3 %all_to_all.54 = bf16[512,16,128]{2,1,0:T(8,128)(2,1)} all-to-all(bf16[512,16,128]{2,1,0:T(8,128)(2,1)} %get-tuple-element.13), channel_id=1, replica_groups=mesh['grp'=2,'seq'=4,'head'=2,'sub'=2] {'head','sub'}, dimensions={0} | all-to-all | bytes 4194304 | tf_op jit(solution)/shard_map/all_to_all | solution.py:120
  176.6 28.9 %all_to_all.55 = bf16[512,16,128]{2,1,0:T(8,128)(2,1)} all-to-all(bf16[512,16,128]{2,1,0:T(8,128)(2,1)S(1)} %copy-done.3), channel_id=1, replica_groups=mesh['grp'=2,'seq'=4,'head'=2,'sub'=2] {'head','sub'}, dimensions={0} | all-to-all | bytes 4194304 | tf_op jit(solution)/shard_map/all_to_all | solution.py:120
  205.5 3.6 %all-to-all-start.2 = ((bf16[512,16,128]{2,1,0:T(8,128)(2,1)}), bf16[512,16,128]{2,1,0:T(8,128)(2,1)S(1)}, u32[]{:S(2)}, u32[]{:S(2)}) async-start(bf16[512,16,128]{2,1,0:T(8,128)(2,1)} %get-tuple-element.15), calls=%async_computation.2 | async-start | bytes 4194304 | tf_op jit(solution)/shard_map/all_to_all | solution.py:120
  209.1 3.7 %copy.12 = bf16[128,4,16,128]{3,2,1,0:T(8,128)(2,1)} copy(bf16[128,4,16,128]{3,2,0,1:T(8,128)(2,1)} %bitcast.13) | data formatting | bytes 4194304 | tf_op jit(solution)/shard_map/all_to_all | solution.py:120
  212.8 2.0 copy.13
  214.8 20.0 %all-to-all-done.2 = bf16[512,16,128]{2,1,0:T(8,128)(2,1)S(1)} async-done(((bf16[512,16,128]{2,1,0:T(8,128)(2,1)}), bf16[512,16,128]{2,1,0:T(8,128)(2,1)S(1)}, u32[]{:S(2)}, u32[]{:S(2)}) %all-to-all-start.2) | async-done | bytes 2097184 | tf_op jit(solution)/shard_map/all_to_all | solution.py:120
  234.8 2.0 copy.14
  (12 shorter events, 0.0 us)
Async XLA Ops:
  18.4 30.0 %copy-start = (f32[16,128,128]{2,1,0:T(8,128)S(1)}, f32[16,128,128]{2,1,0:T(8,128)}, u32[]{:S(2)}) copy-start(f32[16,128,128]{2,1,0:T(8,128)} %get-tuple-element.11) | copy-start | bytes 3145732
  18.4 27.8 %collective-permute-start = (f32[16,128,128]{2,1,0:T(8,128)}, f32[16,128,128]{2,1,0:T(8,128)S(1)}, u32[]{:S(2)}, u32[]{:S(2)}) collective-permute-start(f32[16,128,128]{2,1,0:T(8,128)} %get-tuple-element.10), channel_id=1, source_target_pairs={{0,4},{1,5},{2,6},{3,7},{16,20},{17,21},{18,22},{19,23}} | collective-permute-start | bytes 3145736 | tf_op jit(solution)/shard_map/ppermute | solution.py:77
  23.5 24.9 %collective-permute-start.3 = (f32[16,128,128]{2,1,0:T(8,128)}, f32[16,128,128]{2,1,0:T(8,128)S(1)}, u32[]{:S(2)}, u32[]{:S(2)}) collective-permute-start(f32[16,128,128]{2,1,0:T(8,128)} %get-tuple-element.11), channel_id=1, source_target_pairs={{12,8},{13,9},{14,10},{15,11},{28,24},{29,25},{30,26},{31,27}} | collective-permute-start | bytes 3145736 | tf_op jit(solution)/shard_map/ppermute | solution.py:77
  47.6 1.8 copy-start.2
  47.6 1.7 collective-permute-start.1
  48.6 1.6 collective-permute-start.4
  49.5 2.2 collective-permute-start.2
  50.4 49.9 %collective-permute-start.5 = (f32[16,128,128]{2,1,0:T(8,128)S(1)}, f32[16,128,128]{2,1,0:T(8,128)S(1)}, u32[]{:S(2)}, u32[]{:S(2)}) collective-permute-start(f32[16,128,128]{2,1,0:T(8,128)S(1)} %add.63), channel_id=1, source_target_pairs={{4,0},{5,1},{6,2},{7,3},{20,16},{21,17},{22,18},{23,19}} | collective-permute-start | bytes 3145736 | tf_op jit(solution)/shard_map/ppermute | solution.py:77
  146.3 30.3 %copy-start.3 = (bf16[512,16,128]{2,1,0:T(8,128)(2,1)S(1)}, bf16[512,16,128]{2,1,0:T(8,128)(2,1)}, u32[]{:S(2)}) copy-start(bf16[512,16,128]{2,1,0:T(8,128)(2,1)} %get-tuple-element.14) | copy-start | bytes 6291460
  205.5 29.3 %all-to-all-start.2 = ((bf16[512,16,128]{2,1,0:T(8,128)(2,1)}), bf16[512,16,128]{2,1,0:T(8,128)(2,1)S(1)}, u32[]{:S(2)}, u32[]{:S(2)}) async-start(bf16[512,16,128]{2,1,0:T(8,128)(2,1)} %get-tuple-element.15), calls=%async_computation.2 | async-start | bytes 4194304 | tf_op jit(solution)/shard_map/all_to_all | solution.py:120
  209.1 3.7 %copy-start.1 = (bf16[512,16,128]{2,1,0:T(8,128)(2,1)S(1)}, bf16[512,16,128]{2,1,0:T(8,128)(2,1)}, u32[]{:S(2)}) copy-start(bf16[512,16,128]{2,1,0:T(8,128)(2,1)} %all_to_all.55) | copy-start | bytes 6291460
where the time goes:
time: 237 us
  waiting for transfers between devices  89.3 us (38%)
  Pallas kernels  61.8 us (26%)
  blocking collectives  59.2 us (25%)
  starting transfers between devices  13.1 us (6%)
  local copies, waits for them, and re-layouts  7.7 us (3%)
  other arithmetic  4.94 us (2%)
    ppermute x6, waiting for transfers between devices, exclusive_scan(): got = lax.ppermute(carried + total, axis, perm=[pair])  69.3 us
    all_to_all x2, blocking collectives, per_device(): lax.all_to_all(g, ('head', 'sub'), split_axis=0, concat_axis=1, tiled=True)  59.2 us
    pallas_call x1, Pallas kernels, per_device(): pl.pallas_call(functools.partial(main_kernel, heads), grid=(blocks,), in_...  44.7 us
    all_to_all x1, waiting for transfers between devices, per_device(): lax.all_to_all(g, ('head', 'sub'), split_axis=0, concat_axis=1, tiled=True)  20 us
    pallas_call x1, Pallas kernels, per_device(): pl.pallas_call(functools.partial(totals_kernel, heads), grid=(blocks,), i...  17 us
    ppermute x6, starting transfers between devices, exclusive_scan(): got = lax.ppermute(carried + total, axis, perm=[pair])  9.45 us
    all_to_all x3, local copies, waits for them, and re-layouts, per_device(): lax.all_to_all(g, ('head', 'sub'), split_axis=0, concat_axis=1, tiled=True)  7.68 us
  transfers between devices with their start and end apart: 7, of which 3 were waited for; matrix products, arithmetic and copies ran while one was open for 4% of the time, Pallas kernels for 0%

commit v1 on v0

--- a/solution.py
+++ b/solution.py
@@ -37,8 +37,10 @@
         adj_ref[h] += dot_tn(d_ref[:, h, :], qsc)
 
 
-def main_kernel(heads, q_ref, k_ref, v_ref, d_ref, f_ref, before_ref, rest_ref,
-                a_ref, qg_ref, kg_ref, vg_ref, state, suffix):
+def main_kernel(first, heads, aliased, q_ref, k_ref, v_ref, d_ref, f_ref, before_ref, rest_ref, *refs):
+    if aliased:
+        refs = refs[1:]
+    a_ref, qg_ref, kg_ref, vg_ref, state, suffix = refs
     @pl.when(pl.program_id(0) == 0)
     def _():
         state[...] = before_ref[...]
@@ -105,21 +107,47 @@
     after = exclusive_scan(adj_total, "seq", seq_count, True)
     rest = after + adj_total
 
-    out_tile = jax.ShapeDtypeStruct((tok_dev, heads, head_dim), BF16)
-    attended, query_grad, key_grad, value_grad = pl.pallas_call(
-        functools.partial(main_kernel, heads),
-        grid=(blocks,),
-        in_specs=[tile, tile, tile, tile, fac, whole, whole],
-        out_specs=[tile, tile, tile, tile],
-        out_shape=[out_tile] * 4,
-        scratch_shapes=[pltpu.VMEM((heads, head_dim, head_dim), F32)] * 2,
-        compiler_params=pltpu.CompilerParams(dimension_semantics=("arbitrary",)),
-    )(queries, key_rows, value_rows, out_adjoint, factor, before, rest)
-
-    outs = tuple(
-        lax.all_to_all(g, ("head", "sub"), split_axis=0, concat_axis=1, tiled=True)
-        for g in (query_grad, key_grad, value_grad)
-    )
+    width = 8 if heads % 8 == 0 and heads > 8 else heads
+    groups = heads // width
+    attended = None
+    grads = []
+    for g in range(groups):
+        sel = slice(g * width, (g + 1) * width)
+        before = exclusive_scan(kv_total[sel], "seq", seq_count, False)
+        rest = exclusive_scan(adj_total[sel], "seq", seq_count, True) + adj_total[sel]
+        gtile = pl.BlockSpec((span, width, head_dim), lambda c, g=g: (c, g, 0))
+        gwhole = pl.BlockSpec((width, head_dim, head_dim), lambda c: (0, 0, 0))
+        grad_shape = jax.ShapeDtypeStruct((tok_dev, width, head_dim), BF16)
+        args = [queries, key_rows, value_rows, out_adjoint, factor, before, rest]
+        specs = [gtile] * 4 + [fac, gwhole, gwhole]
+        aliases = {}
+        if attended is not None:
+            args.append(attended)
+            specs.append(pl.BlockSpec(memory_space=pl.ANY))
+            aliases = {7: 0}
+        outs = pl.pallas_call(
+            functools.partial(main_kernel, g * width, width, attended is not None),
+            grid=(blocks,),
+            in_specs=specs,
+            out_specs=[gtile] + [pl.BlockSpec((span, width, head_dim), lambda c: (c, 0, 0))] * 3,
+            out_shape=[jax.ShapeDtypeStruct((tok_dev, heads, head_dim), BF16)] + [grad_shape] * 3,
+            scratch_shapes=[pltpu.VMEM((width, head_dim, head_dim), F32)] * 2,
+            input_output_aliases=aliases,
+            compiler_params=pltpu.CompilerParams(dimension_semantics=("arbitrary",)),
+        )(*args)
+        attended = outs[0]
+        grads.append([
+            lax.all_to_all(x, ("head", "sub"), split_axis=0, concat_axis=1, tiled=True)
+            for x in outs[1:]
+        ])
+    if groups == 1:
+        outs = tuple(grads[0])
+    else:
+        outs = tuple(
+            jnp.stack([grads[g][i].reshape(grads[g][i].shape[0], -1, width, head_dim)
+                       for g in range(groups)], 2).reshape(grads[0][i].shape[0], -1, head_dim)
+            for i in range(3)
+        )
     return (attended,) + outs
 
 

time: 237 us -> 221 us (0.932)
  waiting for transfers between devices: 89.3 us -> 58.4 us
  blocking collectives: 59.2 us -> 36.5 us
  starting transfers between devices: 13.1 us -> 35.4 us
  other arithmetic: 4.94 us -> 15.4 us
  Pallas kernels: 61.8 us -> 64.9 us
    ppermute x6 -> x12, waiting for transfers between devices: 69.3 us -> 31.2 us  [exclusive_scan(): got = lax.ppermute(carried + total, axis, perm=[pair])]
    all_to_all x2, blocking collectives: 59.2 us -> 36.5 us  [per_device(): lax.all_to_all(x, ('head', 'sub'), split_axis=0, concat_axis=1, tiled=True)]
    all_to_all x1 -> x4, starting transfers between devices: 3.61 us -> 14.8 us  [per_device(): lax.all_to_all(x, ('head', 'sub'), split_axis=0, concat_axis=1, tiled=True)]
    ppermute x6 -> x12, starting transfers between devices: 9.45 us -> 20.6 us  [exclusive_scan(): got = lax.ppermute(carried + total, axis, perm=[pair])]
    all_to_all x3 -> x0, local copies, waits for them, and re-layouts: 7.68 us -> none  [per_device(): lax.all_to_all(g, ('head', 'sub'), split_axis=0, concat_axis=1, tiled=True)]
    all_to_all x1 -> x4, waiting for transfers between devices: 20 us -> 27.2 us  [per_device(): lax.all_to_all(x, ('head', 'sub'), split_axis=0, concat_axis=1, tiled=True)]
    another operation x0 -> x3, local copies, waits for them, and re-layouts: none -> 5.76 us  [per_device(): jnp.stack([grads[g][i].reshape(grads[g][i].shape[0], -1, width, head_dim)...]
    add x4 -> x6, other arithmetic: 1.76 us -> 5.06 us  [exclusive_scan(): got = lax.ppermute(carried + total, axis, perm=[pair])]
  transfers between devices with their start and end apart: 7 -> 16, of which waited for: 3 -> 7; matrix products, arithmetic and copies ran while one was open for 4% -> 8% of each run, Pallas kernels for 0% -> 11%
where the time goes in v1:
time: 221 us; the launch traced here: 220 us
  Pallas kernels  64.9 us (29%)
  waiting for transfers between devices  58.4 us (26%)
  blocking collectives  36.5 us (17%)
  starting transfers between devices  35.4 us (16%)
  other arithmetic  15.4 us (7%)
  local copies, waits for them, and re-layouts  8.83 us (4%)
    pallas_call x2, Pallas kernels, per_device(): pl.pallas_call(functools.partial(main_kernel, g * width, width, attended...  47.9 us
    all_to_all x2, blocking collectives, per_device(): lax.all_to_all(x, ('head', 'sub'), split_axis=0, concat_axis=1, tiled=True)  36.5 us
    ppermute x12, waiting for transfers between devices, exclusive_scan(): got = lax.ppermute(carried + total, axis, perm=[pair])  31.2 us
    all_to_all x4, waiting for transfers between devices, per_device(): lax.all_to_all(x, ('head', 'sub'), split_axis=0, concat_axis=1, tiled=True)  27.2 us
    ppermute x12, starting transfers between devices, exclusive_scan(): got = lax.ppermute(carried + total, axis, perm=[pair])  20.6 us
    pallas_call x1, Pallas kernels, per_device(): pl.pallas_call(functools.partial(totals_kernel, heads), grid=(blocks,), i...  17 us
    all_to_all x4, starting transfers between devices, per_device(): lax.all_to_all(x, ('head', 'sub'), split_axis=0, concat_axis=1, tiled=True)  14.8 us
    another operation x3, local copies, waits for them, and re-layouts, per_device(): jnp.stack([grads[g][i].reshape(grads[g][i].shape[0], -1, width, head_dim)...  5.76 us
  transfers between devices with their start and end apart: 16, of which 7 were waited for; matrix products, arithmetic and copies ran while one was open for 8% of the time, Pallas kernels for 11%

profile of v1, /device:TPU:0, one launch (start us, length us, event | category | flops | bytes accessed | tf_op | source)
XLA Modules:
  0.0 220.2 jit_solution(18406482191029272944)
XLA Ops:
  1.4 17.0 %shard_map.75 = (f32[16,128,128]{2,1,0:T(8,128)}, f32[16,128,128]{2,1,0:T(8,128)}) custom-call(bf16[512,16,128]{2,1,0:T(8,128)(2,1)} %q_ref.5, bf16[512,16,128]{2,1,0:T(8,128)(2,1)} %k_ref.5, bf16[512,16,128]{2,1,0:T(8,128)(2,1)} %v_ref.5, bf16[512,16,128]{2,1,0:T(8,128)(2,1)} %d_ref.5, f32[512,1]{1,0:T(8,128)} %multiply_rsqrt_fusion.f_ref), custom_call_target="tpu_custom_call" | custom-call | tf_op jit(solution)/shard_map/pallas_call | solution.py:97
  19.6 5.1 %collective-permute-start.6 = (f32[8,128,128]{2,1,0:T(8,128)S(1)}, f32[8,128,128]{2,1,0:T(8,128)S(1)}, u32[]{:S(2)}, u32[]{:S(2)}) collective-permute-start(f32[8,128,128]{2,1,0:T(8,128)S(1)} %slice.16), channel_id=1, source_target_pairs={{0,4},{1,5},{2,6},{3,7},{16,20},{17,21},{18,22},{19,23}} | collective-permute-start | bytes 1572872 | tf_op jit(solution)/shard_map/ppermute | solution.py:79
  26.5 9.3 %collective-permute-done.6 = f32[8,128,128]{2,1,0:T(8,128)S(1)} collective-permute-done((f32[8,128,128]{2,1,0:T(8,128)S(1)}, f32[8,128,128]{2,1,0:T(8,128)S(1)}, u32[]{:S(2)}, u32[]{:S(2)}) %collective-permute-start.6) | collective-permute-done | bytes 524320 | tf_op jit(solution)/shard_map/ppermute | solution.py:79
  36.6 5.0 %collective-permute-start = (f32[8,128,128]{2,1,0:T(8,128)S(1)}, f32[8,128,128]{2,1,0:T(8,128)S(1)}, u32[]{:S(2)}, u32[]{:S(2)}) collective-permute-start(f32[8,128,128]{2,1,0:T(8,128)S(1)} %get-tuple-element.31), channel_id=1, source_target_pairs={{0,4},{1,5},{2,6},{3,7},{16,20},{17,21},{18,22},{19,23}} | collective-permute-start | bytes 1572872 | tf_op jit(solution)/shard_map/ppermute | solution.py:79
  42.5 9.4 %collective-permute-done = f32[8,128,128]{2,1,0:T(8,128)S(1)} collective-permute-done((f32[8,128,128]{2,1,0:T(8,128)S(1)}, f32[8,128,128]{2,1,0:T(8,128)S(1)}, u32[]{:S(2)}, u32[]{:S(2)}) %collective-permute-start) | collective-permute-done | bytes 524320 | tf_op jit(solution)/shard_map/ppermute | solution.py:79
  56.7 11.0 %collective-permute-done.11 = f32[8,128,128]{2,1,0:T(8,128)S(1)} collective-permute-done((f32[8,128,128]{2,1,0:T(8,128)S(1)}, f32[8,128,128]{2,1,0:T(8,128)S(1)}, u32[]{:S(2)}, u32[]{:S(2)}) %collective-permute-start.11) | collective-permute-done | bytes 524320 | tf_op jit(solution)/shard_map/ppermute | solution.py:79
  69.7 23.9 %shard_map.76 = (bf16[512,16,128]{2,1,0:T(8,128)(2,1)}, bf16[512,8,128]{2,1,0:T(8,128)(2,1)}, bf16[512,8,128]{2,1,0:T(8,128)(2,1)}, bf16[512,8,128]{2,1,0:T(8,128)(2,1)}) custom-call(bf16[512,16,128]{2,1,0:T(8,128)(2,1)} %q_ref.5, bf16[512,16,128]{2,1,0:T(8,128)(2,1)} %k_ref.5, bf16[512,16,128]{2,1,0:T(8,128)(2,1)} %v_ref.5, bf16[512,16,128]{2,1,0:T(8,128)(2,1)} %d_ref.5, ...), custom_call_target="tpu_custom_call" | custom-call | tf_op jit(solution)/shard_map/pallas_call | solution.py:128
  93.6 3.5 %all-to-all-start = ((bf16[512,8,128]{2,1,0:T(8,128)(2,1)}), bf16[512,8,128]{2,1,0:T(8,128)(2,1)S(1)}, u32[]{:S(2)}, u32[]{:S(2)}) async-start(bf16[512,8,128]{2,1,0:T(8,128)(2,1)} %get-tuple-element.18), calls=%async_computation | async-start | bytes 2097152 | tf_op jit(solution)/shard_map/all_to_all | solution.py:140
  100.1 11.5 %all-to-all-done = bf16[512,8,128]{2,1,0:T(8,128)(2,1)S(1)} async-done(((bf16[512,8,128]{2,1,0:T(8,128)(2,1)}), bf16[512,8,128]{2,1,0:T(8,128)(2,1)S(1)}, u32[]{:S(2)}, u32[]{:S(2)}) %all-to-all-start) | async-done | bytes 1048608 | tf_op jit(solution)/shard_map/all_to_all | solution.py:140
  111.6 4.2 %all-to-all-start.2 = ((bf16[512,8,128]{2,1,0:T(8,128)(2,1)}), bf16[512,8,128]{2,1,0:T(8,128)(2,1)}, u32[]{:S(2)}, u32[]{:S(2)}) async-start(bf16[512,8,128]{2,1,0:T(8,128)(2,1)} %get-tuple-element.20), calls=%async_computation.2 | async-start | bytes 2097152 | tf_op jit(solution)/shard_map/all_to_all | solution.py:140
  115.8 1.9 slice_add_fusion.2
  119.2 1.9 slice_add_fusion.6
  122.4 8.0 %all-to-all-done.2 = bf16[512,8,128]{2,1,0:T(8,128)(2,1)} async-done(((bf16[512,8,128]{2,1,0:T(8,128)(2,1)}), bf16[512,8,128]{2,1,0:T(8,128)(2,1)}, u32[]{:S(2)}, u32[]{:S(2)}) %all-to-all-start.2) | async-done | bytes 1048608 | tf_op jit(solution)/shard_map/all_to_all | solution.py:140
  130.3 3.5 %all-to-all-start.4 = ((bf16[512,8,128]{2,1,0:T(8,128)(2,1)}), bf16[512,8,128]{2,1,0:T(8,128)(2,1)S(1)}, u32[]{:S(2)}, u32[]{:S(2)}) async-start(bf16[512,8,128]{2,1,0:T(8,128)(2,1)} %get-tuple-element.22), calls=%async_computation.4 | async-start | bytes 2097152 | tf_op jit(solution)/shard_map/all_to_all | solution.py:140
  133.9 2.3 %add_add_fusion.3.before_ref = f32[8,128,128]{2,1,0:T(8,128)} fusion(f32[8,128,128]{2,1,0:T(8,128)} %collective-permute-done.2, f32[8,128,128]{2,1,0:T(8,128)} %copy-done.3, f32[8,128,128]{2,1,0:T(8,128)} %collective-permute-done.1), kind=kLoop, calls=%fused_computation.6 | loop fusion | flops 262144 | bytes 2097152 | tf_op jit(solution)/shard_map/add | solution.py:80
  137.6 2.1 add_add_fusion.2.rest_ref
  139.7 23.9 %shard_map.77 = (bf16[512,16,128]{2,1,0:T(8,128)(2,1)}, bf16[512,8,128]{2,1,0:T(8,128)(2,1)}, bf16[512,8,128]{2,1,0:T(8,128)(2,1)}, bf16[512,8,128]{2,1,0:T(8,128)(2,1)}) custom-call(bf16[512,16,128]{2,1,0:T(8,128)(2,1)} %q_ref.5, bf16[512,16,128]{2,1,0:T(8,128)(2,1)} %k_ref.5, bf16[512,16,128]{2,1,0:T(8,128)(2,1)} %v_ref.5, ...), custom_call_target="tpu_custom_call", output_to_operand_aliasing={{0}: (7, {})} | custom-call | tf_op jit(solution)/shard_map/pallas_call | solution.py:128
  163.6 18.9 %all_to_all.90 = bf16[512,8,128]{2,1,0:T(8,128)(2,1)} all-to-all(bf16[512,8,128]{2,1,0:T(8,128)(2,1)} %get-tuple-element.19), channel_id=1, replica_groups=mesh['grp'=2,'seq'=4,'head'=2,'sub'=2] {'head','sub'}, dimensions={0} | all-to-all | bytes 2097152 | tf_op jit(solution)/shard_map/all_to_all | solution.py:140
  182.5 17.6 %all_to_all.91 = bf16[512,8,128]{2,1,0:T(8,128)(2,1)} all-to-all(bf16[512,8,128]{2,1,0:T(8,128)(2,1)S(1)} %copy-done.6), channel_id=1, replica_groups=mesh['grp'=2,'seq'=4,'head'=2,'sub'=2] {'head','sub'}, dimensions={0} | all-to-all | bytes 2097152 | tf_op jit(solution)/shard_map/all_to_all | solution.py:140
  200.1 3.5 %all-to-all-start.5 = ((bf16[512,8,128]{2,1,0:T(8,128)(2,1)}), bf16[512,8,128]{2,1,0:T(8,128)(2,1)S(1)}, u32[]{:S(2)}, u32[]{:S(2)}) async-start(bf16[512,8,128]{2,1,0:T(8,128)(2,1)} %get-tuple-element.23), calls=%async_computation.5 | async-start | bytes 2097152 | tf_op jit(solution)/shard_map/all_to_all | solution.py:140
  205.1 1.9 copy.13
  208.4 1.9 copy.14
  210.3 7.7 %all-to-all-done.5 = bf16[512,8,128]{2,1,0:T(8,128)(2,1)S(1)} async-done(((bf16[512,8,128]{2,1,0:T(8,128)(2,1)}), bf16[512,8,128]{2,1,0:T(8,128)(2,1)S(1)}, u32[]{:S(2)}, u32[]{:S(2)}) %all-to-all-start.5) | async-done | bytes 1048608 | tf_op jit(solution)/shard_map/all_to_all | solution.py:140
  218.3 1.9 copy.15
  (46 shorter events, 22.1 us)
Async XLA Ops:
  18.4 17.4 %copy-start.1 = (f32[16,128,128]{2,1,0:T(8,128)S(1)}, f32[16,128,128]{2,1,0:T(8,128)}, u32[]{:S(2)}) copy-start(f32[16,128,128]{2,1,0:T(8,128)} %get-tuple-element.14) | copy-start | bytes 3145732
  19.6 22.1 %copy-start = (f32[16,128,128]{2,1,0:T(8,128)S(1)}, f32[16,128,128]{2,1,0:T(8,128)}, u32[]{:S(2)}) copy-start(f32[16,128,128]{2,1,0:T(8,128)} %get-tuple-element.15) | copy-start | bytes 3145732
  19.6 16.2 %collective-permute-start.6 = (f32[8,128,128]{2,1,0:T(8,128)S(1)}, f32[8,128,128]{2,1,0:T(8,128)S(1)}, u32[]{:S(2)}, u32[]{:S(2)}) collective-permute-start(f32[8,128,128]{2,1,0:T(8,128)S(1)} %slice.16), channel_id=1, source_target_pairs={{0,4},{1,5},{2,6},{3,7},{16,20},{17,21},{18,22},{19,23}} | collective-permute-start | bytes 1572872 | tf_op jit(solution)/shard_map/ppermute | solution.py:79
  25.8 15.9 %collective-permute-start.9 = (f32[8,128,128]{2,1,0:T(8,128)S(1)}, f32[8,128,128]{2,1,0:T(8,128)S(1)}, u32[]{:S(2)}, u32[]{:S(2)}) collective-permute-start(f32[8,128,128]{2,1,0:T(8,128)S(1)} %slice.17), channel_id=1, source_target_pairs={{12,8},{13,9},{14,10},{15,11},{28,24},{29,25},{30,26},{31,27}} | collective-permute-start | bytes 1572872 | tf_op jit(solution)/shard_map/ppermute | solution.py:79
  35.9 6.6 %collective-permute-start.7 = (f32[8,128,128]{2,1,0:T(8,128)S(1)}, f32[8,128,128]{2,1,0:T(8,128)S(1)}, u32[]{:S(2)}, u32[]{:S(2)}) collective-permute-start(f32[8,128,128]{2,1,0:T(8,128)S(1)} %get-tuple-element.30), channel_id=1, source_target_pairs={{4,8},{5,9},{6,10},{7,11},{20,24},{21,25},{22,26},{23,27}} | collective-permute-start | bytes 1572872 | tf_op jit(solution)/shard_map/ppermute | solution.py:79
  36.6 15.3 %collective-permute-start = (f32[8,128,128]{2,1,0:T(8,128)S(1)}, f32[8,128,128]{2,1,0:T(8,128)S(1)}, u32[]{:S(2)}, u32[]{:S(2)}) collective-permute-start(f32[8,128,128]{2,1,0:T(8,128)S(1)} %get-tuple-element.31), channel_id=1, source_target_pairs={{0,4},{1,5},{2,6},{3,7},{16,20},{17,21},{18,22},{19,23}} | collective-permute-start | bytes 1572872 | tf_op jit(solution)/shard_map/ppermute | solution.py:79
  41.8 11.8 %collective-permute-start.10 = (f32[8,128,128]{2,1,0:T(8,128)S(1)}, f32[8,128,128]{2,1,0:T(8,128)S(1)}, u32[]{:S(2)}, u32[]{:S(2)}) collective-permute-start(f32[8,128,128]{2,1,0:T(8,128)S(1)} %slice_add_fusion.5), channel_id=1, source_target_pairs={{8,4},{9,5},{10,6},{11,7},{24,20},{25,21},{26,22},{27,23}} | collective-permute-start | bytes 1572872 | tf_op jit(solution)/shard_map/ppermute | solution.py:79
  52.0 1.8 copy-start.3
  52.9 2.8 %collective-permute-start.8 = (f32[8,128,128]{2,1,0:T(8,128)S(1)}, f32[8,128,128]{2,1,0:T(8,128)S(1)}, u32[]{:S(2)}, u32[]{:S(2)}) collective-permute-start(f32[8,128,128]{2,1,0:T(8,128)S(1)} %get-tuple-element.28), channel_id=1, source_target_pairs={{8,12},{9,13},{10,14},{11,15},{24,28},{25,29},{26,30},{27,31}} | collective-permute-start | bytes 1572872 | tf_op jit(solution)/shard_map/ppermute | solution.py:79
  53.8 13.9 %collective-permute-start.11 = (f32[8,128,128]{2,1,0:T(8,128)S(1)}, f32[8,128,128]{2,1,0:T(8,128)S(1)}, u32[]{:S(2)}, u32[]{:S(2)}) collective-permute-start(f32[8,128,128]{2,1,0:T(8,128)S(1)} %get-tuple-element.26), channel_id=1, source_target_pairs={{4,0},{5,1},{6,2},{7,3},{20,16},{21,17},{22,18},{23,19}} | collective-permute-start | bytes 1572872 | tf_op jit(solution)/shard_map/ppermute | solution.py:79
  55.1 12.6 %collective-permute-start.3 = (f32[8,128,128]{2,1,0:T(8,128)S(1)}, f32[8,128,128]{2,1,0:T(8,128)S(1)}, u32[]{:S(2)}, u32[]{:S(2)}) collective-permute-start(f32[8,128,128]{2,1,0:T(8,128)S(1)} %get-tuple-element.27), channel_id=1, source_target_pairs={{12,8},{13,9},{14,10},{15,11},{28,24},{29,25},{30,26},{31,27}} | collective-permute-start | bytes 1572872 | tf_op jit(solution)/shard_map/ppermute | solution.py:79
  67.7 0.8 copy-start.4
  93.6 18.0 %all-to-all-start = ((bf16[512,8,128]{2,1,0:T(8,128)(2,1)}), bf16[512,8,128]{2,1,0:T(8,128)(2,1)S(1)}, u32[]{:S(2)}, u32[]{:S(2)}) async-start(bf16[512,8,128]{2,1,0:T(8,128)(2,1)} %get-tuple-element.18), calls=%async_computation | async-start | bytes 2097152 | tf_op jit(solution)/shard_map/all_to_all | solution.py:140
  97.1 18.7 %collective-permute-start.1 = (f32[8,128,128]{2,1,0:T(8,128)}, f32[8,128,128]{2,1,0:T(8,128)}, u32[]{:S(2)}, u32[]{:S(2)}) collective-permute-start(f32[8,128,128]{2,1,0:T(8,128)} %get-tuple-element.29), channel_id=1, source_target_pairs={{4,8},{5,9},{6,10},{7,11},{20,24},{21,25},{22,26},{23,27}} | collective-permute-start | bytes 1572872 | tf_op jit(solution)/shard_map/ppermute | solution.py:79
  98.6 20.6 %collective-permute-start.4 = (f32[8,128,128]{2,1,0:T(8,128)}, f32[8,128,128]{2,1,0:T(8,128)}, u32[]{:S(2)}, u32[]{:S(2)}) collective-permute-start(f32[8,128,128]{2,1,0:T(8,128)} %get-tuple-element.25), channel_id=1, source_target_pairs={{8,4},{9,5},{10,6},{11,7},{24,20},{25,21},{26,22},{27,23}} | collective-permute-start | bytes 1572872 | tf_op jit(solution)/shard_map/ppermute | solution.py:79
  111.6 18.8 %all-to-all-start.2 = ((bf16[512,8,128]{2,1,0:T(8,128)(2,1)}), bf16[512,8,128]{2,1,0:T(8,128)(2,1)}, u32[]{:S(2)}, u32[]{:S(2)}) async-start(bf16[512,8,128]{2,1,0:T(8,128)(2,1)} %get-tuple-element.20), calls=%async_computation.2 | async-start | bytes 2097152 | tf_op jit(solution)/shard_map/all_to_all | solution.py:140
  117.7 16.2 %collective-permute-start.2 = (f32[8,128,128]{2,1,0:T(8,128)}, f32[8,128,128]{2,1,0:T(8,128)}, u32[]{:S(2)}, u32[]{:S(2)}) collective-permute-start(f32[8,128,128]{2,1,0:T(8,128)} %slice_add_fusion.2), channel_id=1, source_target_pairs={{8,12},{9,13},{10,14},{11,15},{24,28},{25,29},{26,30},{27,31}} | collective-permute-start | bytes 1572872 | tf_op jit(solution)/shard_map/ppermute | solution.py:79
  121.1 16.5 %collective-permute-start.5 = (f32[8,128,128]{2,1,0:T(8,128)}, f32[8,128,128]{2,1,0:T(8,128)}, u32[]{:S(2)}, u32[]{:S(2)}) collective-permute-start(f32[8,128,128]{2,1,0:T(8,128)} %slice_add_fusion.6), channel_id=1, source_target_pairs={{4,0},{5,1},{6,2},{7,3},{20,16},{21,17},{22,18},{23,19}} | collective-permute-start | bytes 1572872 | tf_op jit(solution)/shard_map/ppermute | solution.py:79
  130.3 33.3 %all-to-all-start.4 = ((bf16[512,8,128]{2,1,0:T(8,128)(2,1)}), bf16[512,8,128]{2,1,0:T(8,128)(2,1)S(1)}, u32[]{:S(2)}, u32[]{:S(2)}) async-start(bf16[512,8,128]{2,1,0:T(8,128)(2,1)} %get-tuple-element.22), calls=%async_computation.4 | async-start | bytes 2097152 | tf_op jit(solution)/shard_map/all_to_all | solution.py:140
  133.8 3.7 %copy-start.5 = (f32[8,128,128]{2,1,0:T(8,128)S(1)}, f32[8,128,128]{2,1,0:T(8,128)}, u32[]{:S(2)}) copy-start(f32[8,128,128]{2,1,0:T(8,128)} %copy-done.4) | copy-start | bytes 1572868
  163.6 18.9 %copy-start.6 = (bf16[512,8,128]{2,1,0:T(8,128)(2,1)S(1)}, bf16[512,8,128]{2,1,0:T(8,128)(2,1)}, u32[]{:S(2)}) copy-start(bf16[512,8,128]{2,1,0:T(8,128)(2,1)} %get-tuple-element.21) | copy-start | bytes 3145732
  200.1 18.0 %all-to-all-start.5 = ((bf16[512,8,128]{2,1,0:T(8,128)(2,1)}), bf16[512,8,128]{2,1,0:T(8,128)(2,1)S(1)}, u32[]{:S(2)}, u32[]{:S(2)}) async-start(bf16[512,8,128]{2,1,0:T(8,128)(2,1)} %get-tuple-element.23), calls=%async_computation.5 | async-start | bytes 2097152 | tf_op jit(solution)/shard_map/all_to_all | solution.py:140
  205.1 1.9 copy-start.2

commit v2 on v1

--- a/solution.py
+++ b/solution.py
@@ -71,6 +71,29 @@
         vg_ref[:, h, :] = (dot_nt(k, suffix_low) + dot_tn(scores, d)).astype(vg_ref.dtype)
 
 
+def interleave_kernel(groups, *refs):
+    o_ref = refs[groups]
+    g = pl.program_id(1)
+    for i in range(groups):
+        @pl.when(g == i)
+        def _():
+            o_ref[...] = refs[i][...]
+
+
+def interleave(parts):
+    peers, tok, width, head_dim = parts[0].shape
+    groups = len(parts)
+    nbytes = 2 * groups * peers * tok * width * head_dim * parts[0].dtype.itemsize
+    return pl.pallas_call(
+        functools.partial(interleave_kernel, groups),
+        grid=(peers, groups),
+        in_specs=[pl.BlockSpec((None, tok, width, head_dim), lambda j, g: (j, 0, 0, 0))] * groups,
+        out_specs=pl.BlockSpec((tok, width, head_dim), lambda j, g: (0, j * groups + g, 0)),
+        out_shape=jax.ShapeDtypeStruct((tok, peers * groups * width, head_dim), parts[0].dtype),
+        cost_estimate=pl.CostEstimate(flops=0, transcendentals=0, bytes_accessed=nbytes),
+    )(*parts)
+
+
 def exclusive_scan(total, axis, count, reverse):
     carried = jnp.zeros_like(total)
     acc = jnp.zeros_like(total)
@@ -90,33 +113,26 @@
     position = offset + jnp.arange(tok_dev, dtype=jnp.int32)
     factor = lax.rsqrt(jnp.float32(head_dim) * (position + 1).astype(jnp.float32))[:, None]
 
-    tile = pl.BlockSpec((span, heads, head_dim), lambda c: (c, 0, 0))
     fac = pl.BlockSpec((span, 1), lambda c: (c, 0))
-    whole = pl.BlockSpec((heads, head_dim, head_dim), lambda c: (0, 0, 0))
-    state_shape = jax.ShapeDtypeStruct((heads, head_dim, head_dim), F32)
-    kv_total, adj_total = pl.pallas_call(
-        functools.partial(totals_kernel, heads),
-        grid=(blocks,),
-        in_specs=[tile, tile, tile, tile, fac],
-        out_specs=[whole, whole],
-        out_shape=[state_shape, state_shape],
-        compiler_params=pltpu.CompilerParams(dimension_semantics=("arbitrary",)),
-    )(queries, key_rows, value_rows, out_adjoint, factor)
-
-    before = exclusive_scan(kv_total, "seq", seq_count, False)
-    after = exclusive_scan(adj_total, "seq", seq_count, True)
-    rest = after + adj_total
-
     width = 8 if heads % 8 == 0 and heads > 8 else heads
     groups = heads // width
+    peers = lax.psum(1, ("head", "sub"))
     attended = None
     grads = []
     for g in range(groups):
-        sel = slice(g * width, (g + 1) * width)
-        before = exclusive_scan(kv_total[sel], "seq", seq_count, False)
-        rest = exclusive_scan(adj_total[sel], "seq", seq_count, True) + adj_total[sel]
         gtile = pl.BlockSpec((span, width, head_dim), lambda c, g=g: (c, g, 0))
         gwhole = pl.BlockSpec((width, head_dim, head_dim), lambda c: (0, 0, 0))
+        state_shape = jax.ShapeDtypeStruct((width, head_dim, head_dim), F32)
+        kv_total, adj_total = pl.pallas_call(
+            functools.partial(totals_kernel, width),
+            grid=(blocks,),
+            in_specs=[gtile] * 4 + [fac],
+            out_specs=[gwhole, gwhole],
+            out_shape=[state_shape, state_shape],
+            compiler_params=pltpu.CompilerParams(dimension_semantics=("arbitrary",)),
+        )(queries, key_rows, value_rows, out_adjoint, factor)
+        before = exclusive_scan(kv_total, "seq", seq_count, False)
+        rest = exclusive_scan(adj_total, "seq", seq_count, True) + adj_total
         grad_shape = jax.ShapeDtypeStruct((tok_dev, width, head_dim), BF16)
         args = [queries, key_rows, value_rows, out_adjoint, factor, before, rest]
         specs = [gtile] * 4 + [fac, gwhole, gwhole]
@@ -136,18 +152,23 @@
             compiler_params=pltpu.CompilerParams(dimension_semantics=("arbitrary",)),
         )(*args)
         attended = outs[0]
-        grads.append([
-            lax.all_to_all(x, ("head", "sub"), split_axis=0, concat_axis=1, tiled=True)
-            for x in outs[1:]
-        ])
-    if groups == 1:
+        if width % 8:
+            grads.append([
+                lax.all_to_all(x, ("head", "sub"), split_axis=0, concat_axis=1, tiled=True)
+                for x in outs[1:]
+            ])
+        else:
+            grads.append([
+                lax.all_to_all(
+                    x.reshape(peers, tok_dev // peers, width, head_dim), ("head", "sub"),
+                    split_axis=0, concat_axis=0, tiled=True,
+                )
+                for x in outs[1:]
+            ])
+    if width % 8:
         outs = tuple(grads[0])
     else:
-        outs = tuple(
-            jnp.stack([grads[g][i].reshape(grads[g][i].shape[0], -1, width, head_dim)
-                       for g in range(groups)], 2).reshape(grads[0][i].shape[0], -1, head_dim)
-            for i in range(3)
-        )
+        outs = tuple(interleave([grads[g][i] for g in range(groups)]) for i in range(3))
     return (attended,) + outs
 
 

time: 221 us -> 242 us (1.095)
  Pallas kernels: 64.9 us -> 85.3 us
  waiting for transfers between devices: 58.4 us -> 71.8 us
  local copies, waits for them, and re-layouts: 8.83 us -> 1.04 us
  starting transfers between devices: 35.4 us -> 30.6 us
    ppermute x12, waiting for transfers between devices: 31.2 us -> 60.8 us  [exclusive_scan(): got = lax.ppermute(carried + total, axis, perm=[pair])]
    pallas_call x1 -> x5, Pallas kernels: 17 us -> 37.4 us  [the longest x2 20.5 us: per_device(): pl.pallas_call(functools.partial(totals_kernel, width), grid=(blocks,), i...]
    all_to_all x4, waiting for transfers between devices: 27.2 us -> 11 us  [per_device(): lax.all_to_all(x.reshape(peers, tok_dev // peers, width, head_dim), ('hea...]
    another operation x3 -> x0, local copies, waits for them, and re-layouts: 5.76 us -> none  [per_device(): jnp.stack([grads[g][i].reshape(grads[g][i].shape[0], -1, width, head_dim)...]
    ppermute x12, starting transfers between devices: 20.6 us -> 16.5 us  [exclusive_scan(): got = lax.ppermute(carried + total, axis, perm=[pair])]
    another operation x3 -> x0, other arithmetic: 3.03 us -> none  [per_device(): jnp.stack([grads[g][i].reshape(grads[g][i].shape[0], -1, width, head_dim)...]
    add x6 -> x8, other arithmetic: 5.06 us -> 7.47 us  [exclusive_scan(): got = lax.ppermute(carried + total, axis, perm=[pair])]
  transfers between devices with their start and end apart: 16 -> 16, of which waited for: 7 -> 6; matrix products, arithmetic and copies ran while one was open for 8% -> 5% of each run, Pallas kernels for 11% -> 19%
where the time goes in v2:
time: 242 us; the launch traced here: 240 us
  Pallas kernels  85.3 us (35%)
  waiting for transfers between devices  71.8 us (30%)
  blocking collectives  36.5 us (15%)
  starting transfers between devices  30.6 us (13%)
  other arithmetic  14.3 us (6%)
    ppermute x12, waiting for transfers between devices, exclusive_scan(): got = lax.ppermute(carried + total, axis, perm=[pair])  60.8 us
    pallas_call x2, Pallas kernels, per_device(): pl.pallas_call(functools.partial(main_kernel, g * width, width, attended...  47.9 us
    all_to_all x2, blocking collectives, per_device(): lax.all_to_all(x.reshape(peers, tok_dev // peers, width, head_dim), ('hea...  36.5 us
    pallas_call x2, Pallas kernels, per_device(): pl.pallas_call(functools.partial(totals_kernel, width), grid=(blocks,), i...  20.5 us
    pallas_call x3, Pallas kernels, interleave(): pl.pallas_call(functools.partial(interleave_kernel, groups), grid=(peers,...  16.9 us
    ppermute x12, starting transfers between devices, exclusive_scan(): got = lax.ppermute(carried + total, axis, perm=[pair])  16.5 us
    all_to_all x4, starting transfers between devices, per_device(): lax.all_to_all(x.reshape(peers, tok_dev // peers, width, head_dim), ('hea...  14.1 us
    all_to_all x4, waiting for transfers between devices, per_device(): lax.all_to_all(x.reshape(peers, tok_dev // peers, width, head_dim), ('hea...  11 us
  transfers between devices with their start and end apart: 16, of which 6 were waited for; matrix products, arithmetic and copies ran while one was open for 5% of the time, Pallas kernels for 19%

profile of v2, /device:TPU:0, one launch (start us, length us, event | category | flops | bytes accessed | tf_op | source)
XLA Modules:
  0.0 240.4 jit_solution(15543624829204506170)
XLA Ops:
  1.4 10.2 %shard_map.76 = (f32[8,128,128]{2,1,0:T(8,128)}, f32[8,128,128]{2,1,0:T(8,128)}) custom-call(bf16[512,16,128]{2,1,0:T(8,128)(2,1)} %q_ref.7, bf16[512,16,128]{2,1,0:T(8,128)(2,1)} %k_ref.7, bf16[512,16,128]{2,1,0:T(8,128)(2,1)} %v_ref.7, bf16[512,16,128]{2,1,0:T(8,128)(2,1)} %d_ref.7, f32[512,1]{1,0:T(8,128)} %multiply_rsqrt_fusion.f_ref), custom_call_target="tpu_custom_call" | custom-call | tf_op jit(solution)/shard_map/pallas_call | solution.py:126
  11.7 5.1 %collective-permute-start.6 = (f32[8,128,128]{2,1,0:T(8,128)}, f32[8,128,128]{2,1,0:T(8,128)S(1)}, u32[]{:S(2)}, u32[]{:S(2)}) collective-permute-start(f32[8,128,128]{2,1,0:T(8,128)} %get-tuple-element.18), channel_id=1, source_target_pairs={{0,4},{1,5},{2,6},{3,7},{16,20},{17,21},{18,22},{19,23}} | collective-permute-start | bytes 1572872 | tf_op jit(solution)/shard_map/ppermute | solution.py:102
  17.6 10.6 %collective-permute-done.6 = f32[8,128,128]{2,1,0:T(8,128)S(1)} collective-permute-done((f32[8,128,128]{2,1,0:T(8,128)}, f32[8,128,128]{2,1,0:T(8,128)S(1)}, u32[]{:S(2)}, u32[]{:S(2)}) %collective-permute-start.6) | collective-permute-done | bytes 524320 | tf_op jit(solution)/shard_map/ppermute | solution.py:102
  34.9 25.4 %collective-permute-done.11 = f32[8,128,128]{2,1,0:T(8,128)S(1)} collective-permute-done((f32[8,128,128]{2,1,0:T(8,128)S(1)}, f32[8,128,128]{2,1,0:T(8,128)S(1)}, u32[]{:S(2)}, u32[]{:S(2)}) %collective-permute-start.11) | collective-permute-done | bytes 524320 | tf_op jit(solution)/shard_map/ppermute | solution.py:102
  61.2 23.9 %shard_map.77 = (bf16[512,16,128]{2,1,0:T(8,128)(2,1)}, bf16[512,8,128]{2,1,0:T(8,128)(2,1)}, bf16[512,8,128]{2,1,0:T(8,128)(2,1)}, bf16[512,8,128]{2,1,0:T(8,128)(2,1)}) custom-call(bf16[512,16,128]{2,1,0:T(8,128)(2,1)} %q_ref.7, bf16[512,16,128]{2,1,0:T(8,128)(2,1)} %k_ref.7, bf16[512,16,128]{2,1,0:T(8,128)(2,1)} %v_ref.7, bf16[512,16,128]{2,1,0:T(8,128)(2,1)} %d_ref.7, ...), custom_call_target="tpu_custom_call" | custom-call | tf_op jit(solution)/shard_map/pallas_call | solution.py:144
  85.1 3.5 %all-to-all-start = ((bf16[4,128,8,128]{3,2,1,0:T(8,128)(2,1)}), bf16[4,128,8,128]{3,2,1,0:T(8,128)(2,1)S(1)}, u32[]{:S(2)}, u32[]{:S(2)}) async-start(bf16[4,128,8,128]{3,2,1,0:T(8,128)(2,1)} %bitcast.8), calls=%async_computation | async-start | bytes 2097152 | tf_op jit(solution)/shard_map/all_to_all | solution.py:162
  88.6 10.3 %shard_map.75 = (f32[8,128,128]{2,1,0:T(8,128)}, f32[8,128,128]{2,1,0:T(8,128)}) custom-call(bf16[512,16,128]{2,1,0:T(8,128)(2,1)} %q_ref.7, bf16[512,16,128]{2,1,0:T(8,128)(2,1)} %k_ref.7, bf16[512,16,128]{2,1,0:T(8,128)(2,1)} %v_ref.7, bf16[512,16,128]{2,1,0:T(8,128)(2,1)} %d_ref.7, f32[512,1]{1,0:T(8,128)} %multiply_rsqrt_fusion.f_ref), custom_call_target="tpu_custom_call" | custom-call | tf_op jit(solution)/shard_map/pallas_call | solution.py:126
  101.2 11.5 %collective-permute-done = f32[8,128,128]{2,1,0:T(8,128)S(1)} collective-permute-done((f32[8,128,128]{2,1,0:T(8,128)}, f32[8,128,128]{2,1,0:T(8,128)S(1)}, u32[]{:S(2)}, u32[]{:S(2)}) %collective-permute-start) | collective-permute-done | bytes 524320 | tf_op jit(solution)/shard_map/ppermute | solution.py:102
  112.7 2.1 add.84
  116.3 3.5 %all-to-all-start.2 = ((bf16[4,128,8,128]{3,2,1,0:T(8,128)(2,1)}), bf16[4,128,8,128]{3,2,1,0:T(8,128)(2,1)S(1)}, u32[]{:S(2)}, u32[]{:S(2)}) async-start(bf16[4,128,8,128]{3,2,1,0:T(8,128)(2,1)} %bitcast.7), calls=%async_computation.2 | async-start | bytes 2097152 | tf_op jit(solution)/shard_map/all_to_all | solution.py:162
  120.6 2.0 add.86
  126.4 7.8 %all-to-all-done.2.refs_0_ = bf16[4,128,8,128]{3,2,1,0:T(8,128)(2,1)S(1)} async-done(((bf16[4,128,8,128]{3,2,1,0:T(8,128)(2,1)}), bf16[4,128,8,128]{3,2,1,0:T(8,128)(2,1)S(1)}, u32[]{:S(2)}, u32[]{:S(2)}) %all-to-all-start.2) | async-done | bytes 1048608 | tf_op jit(solution)/shard_map/all_to_all | solution.py:162
  134.2 3.5 %all-to-all-start.4 = ((bf16[4,128,8,128]{3,2,1,0:T(8,128)(2,1)}), bf16[4,128,8,128]{3,2,1,0:T(8,128)(2,1)S(1)}, u32[]{:S(2)}, u32[]{:S(2)}) async-start(bf16[4,128,8,128]{3,2,1,0:T(8,128)(2,1)} %bitcast.6), calls=%async_computation.4 | async-start | bytes 2097152 | tf_op jit(solution)/shard_map/all_to_all | solution.py:162
  137.8 2.3 add_add_fusion.3.before_ref
  140.1 13.3 %collective-permute-done.5 = f32[8,128,128]{2,1,0:T(8,128)} collective-permute-done((f32[8,128,128]{2,1,0:T(8,128)}, f32[8,128,128]{2,1,0:T(8,128)}, u32[]{:S(2)}, u32[]{:S(2)}) %collective-permute-start.5) | collective-permute-done | bytes 524320 | tf_op jit(solution)/shard_map/ppermute | solution.py:102
  153.4 2.0 add_add_fusion.2.rest_ref
  155.3 23.9 %shard_map.78 = (bf16[512,16,128]{2,1,0:T(8,128)(2,1)}, bf16[512,8,128]{2,1,0:T(8,128)(2,1)}, bf16[512,8,128]{2,1,0:T(8,128)(2,1)}, bf16[512,8,128]{2,1,0:T(8,128)(2,1)}) custom-call(bf16[512,16,128]{2,1,0:T(8,128)(2,1)} %q_ref.7, bf16[512,16,128]{2,1,0:T(8,128)(2,1)} %k_ref.7, bf16[512,16,128]{2,1,0:T(8,128)(2,1)} %v_ref.7, ...), custom_call_target="tpu_custom_call", output_to_operand_aliasing={{0}: (7, {})} | custom-call | tf_op jit(solution)/shard_map/pallas_call | solution.py:144
  179.3 18.9 %all_to_all.30.refs_1_ = bf16[4,128,8,128]{3,2,1,0:T(8,128)(2,1)} all-to-all(bf16[4,128,8,128]{3,2,1,0:T(8,128)(2,1)} %bitcast.10), channel_id=1, replica_groups=mesh['grp'=2,'seq'=4,'head'=2,'sub'=2] {'head','sub'}, dimensions={0} | all-to-all | bytes 2097152 | tf_op jit(solution)/shard_map/all_to_all | solution.py:162
  198.2 17.6 %all_to_all.31.refs_1_ = bf16[4,128,8,128]{3,2,1,0:T(8,128)(2,1)} all-to-all(bf16[4,128,8,128]{3,2,1,0:T(8,128)(2,1)S(1)} %bitcast.9), channel_id=1, replica_groups=mesh['grp'=2,'seq'=4,'head'=2,'sub'=2] {'head','sub'}, dimensions={0} | all-to-all | bytes 2097152 | tf_op jit(solution)/shard_map/all_to_all | solution.py:162
  215.8 3.5 %all-to-all-start.5 = ((bf16[4,128,8,128]{3,2,1,0:T(8,128)(2,1)}), bf16[4,128,8,128]{3,2,1,0:T(8,128)(2,1)S(1)}, u32[]{:S(2)}, u32[]{:S(2)}) async-start(bf16[4,128,8,128]{3,2,1,0:T(8,128)(2,1)} %bitcast.5), calls=%async_computation.5 | async-start | bytes 2097152 | tf_op jit(solution)/shard_map/all_to_all | solution.py:162
  219.3 5.6 %shard_map.79 = bf16[128,64,128]{2,1,0:T(8,128)(2,1)} custom-call(bf16[4,128,8,128]{3,2,1,0:T(8,128)(2,1)} %copy-done.2, bf16[4,128,8,128]{3,2,1,0:T(8,128)(2,1)} %all_to_all.30.refs_1_), custom_call_target="tpu_custom_call" | custom-call | bytes 4194304 | tf_op jit(solution)/shard_map/pallas_call | solution.py:87
  225.0 5.6 %shard_map.80 = bf16[128,64,128]{2,1,0:T(8,128)(2,1)} custom-call(bf16[4,128,8,128]{3,2,1,0:T(8,128)(2,1)} %copy-done.3, bf16[4,128,8,128]{3,2,1,0:T(8,128)(2,1)} %all_to_all.31.refs_1_), custom_call_target="tpu_custom_call" | custom-call | bytes 4194304 | tf_op jit(solution)/shard_map/pallas_call | solution.py:87
  230.6 3.2 %all-to-all-done.5.refs_1_ = bf16[4,128,8,128]{3,2,1,0:T(8,128)(2,1)S(1)} async-done(((bf16[4,128,8,128]{3,2,1,0:T(8,128)(2,1)}), bf16[4,128,8,128]{3,2,1,0:T(8,128)(2,1)S(1)}, u32[]{:S(2)}, u32[]{:S(2)}) %all-to-all-start.5) | async-done | bytes 1048608 | tf_op jit(solution)/shard_map/all_to_all | solution.py:162
  234.7 5.6 %shard_map.81 = bf16[128,64,128]{2,1,0:T(8,128)(2,1)} custom-call(bf16[4,128,8,128]{3,2,1,0:T(8,128)(2,1)} %copy-done.4, bf16[4,128,8,128]{3,2,1,0:T(8,128)(2,1)} %copy-done.5), custom_call_target="tpu_custom_call" | custom-call | bytes 4194304 | tf_op jit(solution)/shard_map/pallas_call | solution.py:87
  (52 shorter events, 18.3 us)
Async XLA Ops:
  11.7 20.2 %copy-start.8 = (f32[8,128,128]{2,1,0:T(8,128)S(1)}, f32[8,128,128]{2,1,0:T(8,128)}, u32[]{:S(2)}) copy-start(f32[8,128,128]{2,1,0:T(8,128)} %get-tuple-element.18) | copy-start | bytes 1572868
  11.7 16.5 %collective-permute-start.6 = (f32[8,128,128]{2,1,0:T(8,128)}, f32[8,128,128]{2,1,0:T(8,128)S(1)}, u32[]{:S(2)}, u32[]{:S(2)}) collective-permute-start(f32[8,128,128]{2,1,0:T(8,128)} %get-tuple-element.18), channel_id=1, source_target_pairs={{0,4},{1,5},{2,6},{3,7},{16,20},{17,21},{18,22},{19,23}} | collective-permute-start | bytes 1572872 | tf_op jit(solution)/shard_map/ppermute | solution.py:102
  16.7 15.9 %copy-start.1 = (f32[8,128,128]{2,1,0:T(8,128)S(1)}, f32[8,128,128]{2,1,0:T(8,128)}, u32[]{:S(2)}) copy-start(f32[8,128,128]{2,1,0:T(8,128)} %get-tuple-element.19) | copy-start | bytes 1572868
  16.8 13.2 %collective-permute-start.9 = (f32[8,128,128]{2,1,0:T(8,128)}, f32[8,128,128]{2,1,0:T(8,128)S(1)}, u32[]{:S(2)}, u32[]{:S(2)}) collective-permute-start(f32[8,128,128]{2,1,0:T(8,128)} %get-tuple-element.19), channel_id=1, source_target_pairs={{12,8},{13,9},{14,10},{15,11},{28,24},{29,25},{30,26},{31,27}} | collective-permute-start | bytes 1572872 | tf_op jit(solution)/shard_map/ppermute | solution.py:102
  29.3 2.5 %collective-permute-start.7 = (f32[8,128,128]{2,1,0:T(8,128)S(1)}, f32[8,128,128]{2,1,0:T(8,128)S(1)}, u32[]{:S(2)}, u32[]{:S(2)}) collective-permute-start(f32[8,128,128]{2,1,0:T(8,128)S(1)} %add.93), channel_id=1, source_target_pairs={{4,8},{5,9},{6,10},{7,11},{20,24},{21,25},{22,26},{23,27}} | collective-permute-start | bytes 1572872 | tf_op jit(solution)/shard_map/ppermute | solution.py:102
  31.1 1.5 collective-permute-start.10
  31.9 2.1 collective-permute-start.8
  32.7 27.6 %collective-permute-start.11 = (f32[8,128,128]{2,1,0:T(8,128)S(1)}, f32[8,128,128]{2,1,0:T(8,128)S(1)}, u32[]{:S(2)}, u32[]{:S(2)}) collective-permute-start(f32[8,128,128]{2,1,0:T(8,128)S(1)} %add.99), channel_id=1, source_target_pairs={{4,0},{5,1},{6,2},{7,3},{20,16},{21,17},{22,18},{23,19}} | collective-permute-start | bytes 1572872 | tf_op jit(solution)/shard_map/ppermute | solution.py:102
  85.1 31.2 %all-to-all-start = ((bf16[4,128,8,128]{3,2,1,0:T(8,128)(2,1)}), bf16[4,128,8,128]{3,2,1,0:T(8,128)(2,1)S(1)}, u32[]{:S(2)}, u32[]{:S(2)}) async-start(bf16[4,128,8,128]{3,2,1,0:T(8,128)(2,1)} %bitcast.8), calls=%async_computation | async-start | bytes 2097152 | tf_op jit(solution)/shard_map/all_to_all | solution.py:162
  98.9 20.9 %copy-start = (f32[8,128,128]{2,1,0:T(8,128)S(1)}, f32[8,128,128]{2,1,0:T(8,128)}, u32[]{:S(2)}) copy-start(f32[8,128,128]{2,1,0:T(8,128)} %get-tuple-element.17) | copy-start | bytes 1572868
  98.9 13.8 %collective-permute-start = (f32[8,128,128]{2,1,0:T(8,128)}, f32[8,128,128]{2,1,0:T(8,128)S(1)}, u32[]{:S(2)}, u32[]{:S(2)}) collective-permute-start(f32[8,128,128]{2,1,0:T(8,128)} %get-tuple-element.16), channel_id=1, source_target_pairs={{0,4},{1,5},{2,6},{3,7},{16,20},{17,21},{18,22},{19,23}} | collective-permute-start | bytes 1572872 | tf_op jit(solution)/shard_map/ppermute | solution.py:102
  100.5 19.3 %collective-permute-start.3 = (f32[8,128,128]{2,1,0:T(8,128)}, f32[8,128,128]{2,1,0:T(8,128)S(1)}, u32[]{:S(2)}, u32[]{:S(2)}) collective-permute-start(f32[8,128,128]{2,1,0:T(8,128)} %get-tuple-element.17), channel_id=1, source_target_pairs={{12,8},{13,9},{14,10},{15,11},{28,24},{29,25},{30,26},{31,27}} | collective-permute-start | bytes 1572872 | tf_op jit(solution)/shard_map/ppermute | solution.py:102
  114.8 5.8 %collective-permute-start.1 = (f32[8,128,128]{2,1,0:T(8,128)}, f32[8,128,128]{2,1,0:T(8,128)}, u32[]{:S(2)}, u32[]{:S(2)}) collective-permute-start(f32[8,128,128]{2,1,0:T(8,128)} %add.84), channel_id=1, source_target_pairs={{4,8},{5,9},{6,10},{7,11},{20,24},{21,25},{22,26},{23,27}} | collective-permute-start | bytes 1572872 | tf_op jit(solution)/shard_map/ppermute | solution.py:102
  116.3 6.4 %copy-start.2 = (bf16[4,128,8,128]{3,2,1,0:T(8,128)(2,1)}, bf16[4,128,8,128]{3,2,1,0:T(8,128)(2,1)S(1)}, u32[]{:S(2)}) copy-start(bf16[4,128,8,128]{3,2,1,0:T(8,128)(2,1)S(1)} %all-to-all-done.refs_0_) | copy-start | bytes 3145732
  116.3 18.0 %all-to-all-start.2 = ((bf16[4,128,8,128]{3,2,1,0:T(8,128)(2,1)}), bf16[4,128,8,128]{3,2,1,0:T(8,128)(2,1)S(1)}, u32[]{:S(2)}, u32[]{:S(2)}) async-start(bf16[4,128,8,128]{3,2,1,0:T(8,128)(2,1)} %bitcast.7), calls=%async_computation.2 | async-start | bytes 2097152 | tf_op jit(solution)/shard_map/all_to_all | solution.py:162
  119.9 4.2 %collective-permute-start.4 = (f32[8,128,128]{2,1,0:T(8,128)S(1)}, f32[8,128,128]{2,1,0:T(8,128)S(1)}, u32[]{:S(2)}, u32[]{:S(2)}) collective-permute-start(f32[8,128,128]{2,1,0:T(8,128)S(1)} %add.88), channel_id=1, source_target_pairs={{8,4},{9,5},{10,6},{11,7},{24,20},{25,21},{26,22},{27,23}} | collective-permute-start | bytes 1572872 | tf_op jit(solution)/shard_map/ppermute | solution.py:102
  122.6 15.1 %collective-permute-start.2 = (f32[8,128,128]{2,1,0:T(8,128)}, f32[8,128,128]{2,1,0:T(8,128)}, u32[]{:S(2)}, u32[]{:S(2)}) collective-permute-start(f32[8,128,128]{2,1,0:T(8,128)} %add.86), channel_id=1, source_target_pairs={{8,12},{9,13},{10,14},{11,15},{24,28},{25,29},{26,30},{27,31}} | collective-permute-start | bytes 1572872 | tf_op jit(solution)/shard_map/ppermute | solution.py:102
  125.1 28.3 %collective-permute-start.5 = (f32[8,128,128]{2,1,0:T(8,128)}, f32[8,128,128]{2,1,0:T(8,128)}, u32[]{:S(2)}, u32[]{:S(2)}) collective-permute-start(f32[8,128,128]{2,1,0:T(8,128)} %add.90), channel_id=1, source_target_pairs={{4,0},{5,1},{6,2},{7,3},{20,16},{21,17},{22,18},{23,19}} | collective-permute-start | bytes 1572872 | tf_op jit(solution)/shard_map/ppermute | solution.py:102
  134.2 5.8 %copy-start.3 = (bf16[4,128,8,128]{3,2,1,0:T(8,128)(2,1)}, bf16[4,128,8,128]{3,2,1,0:T(8,128)(2,1)S(1)}, u32[]{:S(2)}) copy-start(bf16[4,128,8,128]{3,2,1,0:T(8,128)(2,1)S(1)} %all-to-all-done.2.refs_0_) | copy-start | bytes 3145732
  134.2 45.0 %all-to-all-start.4 = ((bf16[4,128,8,128]{3,2,1,0:T(8,128)(2,1)}), bf16[4,128,8,128]{3,2,1,0:T(8,128)(2,1)S(1)}, u32[]{:S(2)}, u32[]{:S(2)}) async-start(bf16[4,128,8,128]{3,2,1,0:T(8,128)(2,1)} %bitcast.6), calls=%async_computation.4 | async-start | bytes 2097152 | tf_op jit(solution)/shard_map/all_to_all | solution.py:162
  137.8 15.6 %copy-start.7 = (f32[8,128,128]{2,1,0:T(8,128)S(1)}, f32[8,128,128]{2,1,0:T(8,128)}, u32[]{:S(2)}) copy-start(f32[8,128,128]{2,1,0:T(8,128)} %copy-done.6) | copy-start | bytes 1572868
  179.3 19.0 %copy-start.10 = (bf16[512,8,128]{2,1,0:T(8,128)(2,1)S(1)}, bf16[512,8,128]{2,1,0:T(8,128)(2,1)}, u32[]{:S(2)}) copy-start(bf16[512,8,128]{2,1,0:T(8,128)(2,1)} %get-tuple-element.25) | copy-start | bytes 3145732
  179.3 36.5 %copy-start.4 = (bf16[4,128,8,128]{3,2,1,0:T(8,128)(2,1)}, bf16[4,128,8,128]{3,2,1,0:T(8,128)(2,1)S(1)}, u32[]{:S(2)}) copy-start(bf16[4,128,8,128]{3,2,1,0:T(8,128)(2,1)S(1)} %all-to-all-done.4.refs_0_) | copy-start | bytes 3145732
  215.8 18.0 %all-to-all-start.5 = ((bf16[4,128,8,128]{3,2,1,0:T(8,128)(2,1)}), bf16[4,128,8,128]{3,2,1,0:T(8,128)(2,1)S(1)}, u32[]{:S(2)}, u32[]{:S(2)}) async-start(bf16[4,128,8,128]{3,2,1,0:T(8,128)(2,1)} %bitcast.5), calls=%async_computation.5 | async-start | bytes 2097152 | tf_op jit(solution)/shard_map/all_to_all | solution.py:162
  (3 other events, 4.1 us)

commit v3 on v1

--- a/solution.py
+++ b/solution.py
@@ -71,6 +71,27 @@
         vg_ref[:, h, :] = (dot_nt(k, suffix_low) + dot_tn(scores, d)).astype(vg_ref.dtype)
 
 
+def skewed_scan(first, second, axis, count, reverse):
+    place = lax.axis_index(axis)
+    pos = count - 1 - place if reverse else place
+    dev = (lambda i: count - 1 - i) if reverse else (lambda i: i)
+    got_first = jnp.zeros_like(first)
+    got_second = jnp.zeros_like(second)
+    for step in range(count):
+        pairs = []
+        if step + 1 < count:
+            pairs.append((dev(step), dev(step + 1)))
+        if step >= 1:
+            pairs.append((dev(step - 1), dev(step)))
+        send = jnp.where(pos == step, got_first + first, got_second + second)
+        got = lax.ppermute(send, axis, perm=pairs)
+        if step + 1 < count:
+            got_first = got_first + jnp.where(pos == step + 1, got, 0.0)
+        if step >= 1:
+            got_second = got_second + jnp.where(pos == step, got, 0.0)
+    return got_first, got_second
+
+
 def exclusive_scan(total, axis, count, reverse):
     carried = jnp.zeros_like(total)
     acc = jnp.zeros_like(total)
@@ -111,10 +132,17 @@
     groups = heads // width
     attended = None
     grads = []
+    if groups == 2:
+        befores = skewed_scan(kv_total[:width], kv_total[width:], "seq", seq_count, False)
+        afters = skewed_scan(adj_total[:width], adj_total[width:], "seq", seq_count, True)
     for g in range(groups):
         sel = slice(g * width, (g + 1) * width)
-        before = exclusive_scan(kv_total[sel], "seq", seq_count, False)
-        rest = exclusive_scan(adj_total[sel], "seq", seq_count, True) + adj_total[sel]
+        if groups == 2:
+            before = befores[g]
+            rest = afters[g] + adj_total[sel]
+        else:
+            before = exclusive_scan(kv_total[sel], "seq", seq_count, False)
+            rest = exclusive_scan(adj_total[sel], "seq", seq_count, True) + adj_total[sel]
         gtile = pl.BlockSpec((span, width, head_dim), lambda c, g=g: (c, g, 0))
         gwhole = pl.BlockSpec((width, head_dim, head_dim), lambda c: (0, 0, 0))
         grad_shape = jax.ShapeDtypeStruct((tok_dev, width, head_dim), BF16)

time: 221 us -> 227 us (1.027); the launches traced: 220 us -> 223 us
  blocking collectives: 36.5 us -> 54.5 us
  waiting for transfers between devices: 58.4 us -> 47 us
  starting transfers between devices: 35.4 us -> 29 us
  other arithmetic: 15.4 us -> 21.3 us
  local copies, waits for them, and re-layouts: 8.83 us -> 5.77 us
    all_to_all x2 -> x3, blocking collectives: 36.5 us -> 54.5 us  [per_device(): lax.all_to_all(x, ('head', 'sub'), split_axis=0, concat_axis=1, tiled=True)]
    select_n x0 -> x7, other arithmetic: none -> 12.3 us  [skewed_scan(): send = jnp.where(pos == step, got_first + first, got_second + second)]
    all_to_all x4 -> x3, waiting for transfers between devices: 27.2 us -> 20.6 us  [per_device(): lax.all_to_all(x, ('head', 'sub'), split_axis=0, concat_axis=1, tiled=True)]
    add x10 -> x3, other arithmetic: 11.5 us -> 5.26 us  [the longest x1 2.4 us: skewed_scan(): got_first = got_first + jnp.where(pos == step + 1, got, 0.0)]
    ppermute x12 -> x8, waiting for transfers between devices: 31.2 us -> 26.4 us  [skewed_scan(): got = lax.ppermute(send, axis, perm=pairs)]
    all_to_all x4 -> x3, starting transfers between devices: 14.8 us -> 11.3 us  [per_device(): lax.all_to_all(x, ('head', 'sub'), split_axis=0, concat_axis=1, tiled=True)]
    ppermute x12 -> x8, starting transfers between devices: 20.6 us -> 17.8 us  [skewed_scan(): got = lax.ppermute(send, axis, perm=pairs)]
  transfers between devices with their start and end apart: 16 -> 11, of which waited for: 7 -> 5; matrix products, arithmetic and copies ran while one was open for 8% -> 8% of each run, Pallas kernels for 11% -> 11%
where the time goes in v3:
time: 227 us; the launch traced here: 223 us
  Pallas kernels  64.9 us (29%)
  blocking collectives  54.5 us (24%)
  waiting for transfers between devices  47 us (21%)
  starting transfers between devices  29 us (13%)
  other arithmetic  21.3 us (9%)
  local copies, waits for them, and re-layouts  5.77 us (3%)
    all_to_all x3, blocking collectives, per_device(): lax.all_to_all(x, ('head', 'sub'), split_axis=0, concat_axis=1, tiled=True)  54.5 us
    pallas_call x2, Pallas kernels, per_device(): pl.pallas_call(functools.partial(main_kernel, g * width, width, attended...  47.9 us
    ppermute x8, waiting for transfers between devices, skewed_scan(): got = lax.ppermute(send, axis, perm=pairs)  26.4 us
    all_to_all x3, waiting for transfers between devices, per_device(): lax.all_to_all(x, ('head', 'sub'), split_axis=0, concat_axis=1, tiled=True)  20.6 us
    ppermute x8, starting transfers between devices, skewed_scan(): got = lax.ppermute(send, axis, perm=pairs)  17.8 us
    pallas_call x1, Pallas kernels, per_device(): pl.pallas_call(functools.partial(totals_kernel, heads), grid=(blocks,), i...  17 us
    select_n x7, other arithmetic, skewed_scan(): send = jnp.where(pos == step, got_first + first, got_second + second)  12.3 us
    all_to_all x3, starting transfers between devices, per_device(): lax.all_to_all(x, ('head', 'sub'), split_axis=0, concat_axis=1, tiled=True)  11.3 us
  transfers between devices with their start and end apart: 11, of which 5 were waited for; matrix products, arithmetic and copies ran while one was open for 8% of the time, Pallas kernels for 11%

profile of v3, /device:TPU:0, one launch (start us, length us, event | category | flops | bytes accessed | tf_op | source)
XLA Modules:
  0.0 223.3 jit_solution(2968975170403723230)
XLA Ops:
  1.4 17.0 %shard_map.75 = (f32[16,128,128]{2,1,0:T(8,128)}, f32[16,128,128]{2,1,0:T(8,128)}) custom-call(bf16[512,16,128]{2,1,0:T(8,128)(2,1)} %q_ref.5, bf16[512,16,128]{2,1,0:T(8,128)(2,1)} %k_ref.5, bf16[512,16,128]{2,1,0:T(8,128)(2,1)} %v_ref.5, bf16[512,16,128]{2,1,0:T(8,128)(2,1)} %d_ref.5, f32[512,1]{1,0:T(8,128)} %multiply_rsqrt_fusion.f_ref), custom_call_target="tpu_custom_call" | custom-call | tf_op jit(solution)/shard_map/pallas_call | solution.py:118
  18.4 2.1 slice_select_fusion
  21.4 2.1 slice_select_fusion.1
  23.4 5.0 %collective-permute-start = (f32[8,128,128]{2,1,0:T(8,128)}, f32[8,128,128]{2,1,0:T(8,128)S(1)}, u32[]{:S(2)}, u32[]{:S(2)}) collective-permute-start(f32[8,128,128]{2,1,0:T(8,128)} %slice_select_fusion.1), channel_id=1, source_target_pairs={{0,4},{1,5},{2,6},{3,7},{16,20},{17,21},{18,22},{19,23}} | collective-permute-start | bytes 1572872 | tf_op jit(solution)/shard_map/ppermute | solution.py:87
  30.7 9.1 %collective-permute-done = f32[8,128,128]{2,1,0:T(8,128)S(1)} collective-permute-done((f32[8,128,128]{2,1,0:T(8,128)}, f32[8,128,128]{2,1,0:T(8,128)S(1)}, u32[]{:S(2)}, u32[]{:S(2)}) %collective-permute-start) | collective-permute-done | bytes 524320 | tf_op jit(solution)/shard_map/ppermute | solution.py:87
  40.7 5.1 %collective-permute-start.1 = (f32[8,128,128]{2,1,0:T(8,128)}, f32[8,128,128]{2,1,0:T(8,128)}, u32[]{:S(2)}, u32[]{:S(2)}) collective-permute-start(f32[8,128,128]{2,1,0:T(8,128)} %add_select_fusion.5), channel_id=1, source_target_pairs={{4,8},{0,4},{5,9},{1,5},{6,10},{2,6},{7,11},{3,7},{20,24},{16,20},... | collective-permute-start | bytes 1572872 | tf_op jit(solution)/shard_map/ppermute | solution.py:87
  45.8 2.0 add_select_fusion.1
  49.0 6.6 %collective-permute-done.1 = f32[8,128,128]{2,1,0:T(8,128)} collective-permute-done((f32[8,128,128]{2,1,0:T(8,128)}, f32[8,128,128]{2,1,0:T(8,128)}, u32[]{:S(2)}, u32[]{:S(2)}) %collective-permute-start.1) | collective-permute-done | bytes 524320 | tf_op jit(solution)/shard_map/ppermute | solution.py:87
  55.6 2.0 add_select_fusion.4
  59.0 10.7 %collective-permute-done.6 = f32[8,128,128]{2,1,0:T(8,128)} collective-permute-done((f32[8,128,128]{2,1,0:T(8,128)}, f32[8,128,128]{2,1,0:T(8,128)}, u32[]{:S(2)}, u32[]{:S(2)}) %collective-permute-start.6) | collective-permute-done | bytes 524320 | tf_op jit(solution)/shard_map/ppermute | solution.py:87
  69.8 2.4 %add_select_fusion = (f32[8,128,128]{2,1,0:T(8,128)}, f32[8,128,128]{2,1,0:T(8,128)}) fusion(f32[16,128,128]{2,1,0:T(8,128)S(1)} %copy-done, pred[]{:T(512)S(6)} %eq.43, f32[8,128,128]{2,1,0:T(8,128)} %collective-permute-done.6, pred[]{:T(512)S(6)} %eq.42, f32[8,128,128]{2,1,0:T(8,128)} %collective-permute-done.5, pred[]{:T(512)S(6)} %eq.40, ...), kind=kLoop, calls=%fused_computation.4 | loop fusion | flops 1441792 | bytes 3670019 | tf_op jit(solution)/shard_map/jit(_where)/select_n | solution.py:86
  72.2 2.4 %select_add_fusion.3 = (f32[8,128,128]{2,1,0:T(8,128)}, f32[8,128,128]{2,1,0:T(8,128)}) fusion(f32[8,128,128]{2,1,0:T(8,128)} %collective-permute-done.2, f32[8,128,128]{2,1,0:T(8,128)} %collective-permute-done.1, f32[8,128,128]{2,1,0:T(8,128)S(1)} %collective-permute-done, pred[]{:T(512)S(6)} %eq.19, pred[]{:T(512)S(6)} %eq.18, pred[]{:T(512)S(6)} %eq.16, ...), kind=kLoop, calls=%fused_computation.12 | loop fusion | flops 1441792 | bytes 3670019 | tf_op jit(solution)/shard_map/add | solution.py:89
  74.6 24.0 %shard_map.76 = (bf16[512,16,128]{2,1,0:T(8,128)(2,1)}, bf16[512,8,128]{2,1,0:T(8,128)(2,1)}, bf16[512,8,128]{2,1,0:T(8,128)(2,1)}, bf16[512,8,128]{2,1,0:T(8,128)(2,1)}) custom-call(bf16[512,16,128]{2,1,0:T(8,128)(2,1)} %q_ref.5, bf16[512,16,128]{2,1,0:T(8,128)(2,1)} %k_ref.5, bf16[512,16,128]{2,1,0:T(8,128)(2,1)} %v_ref.5, bf16[512,16,128]{2,1,0:T(8,128)(2,1)} %d_ref.5, ...), custom_call_target="tpu_custom_call" | custom-call | tf_op jit(solution)/shard_map/pallas_call | solution.py:156
  98.5 17.9 %all_to_all.90 = bf16[512,8,128]{2,1,0:T(8,128)(2,1)S(1)} all-to-all(bf16[512,8,128]{2,1,0:T(8,128)(2,1)} %get-tuple-element.18), channel_id=1, replica_groups=mesh['grp'=2,'seq'=4,'head'=2,'sub'=2] {'head','sub'}, dimensions={0} | all-to-all | bytes 2097152 | tf_op jit(solution)/shard_map/all_to_all | solution.py:168
  116.5 3.5 %all-to-all-start.2 = ((bf16[512,8,128]{2,1,0:T(8,128)(2,1)}), bf16[512,8,128]{2,1,0:T(8,128)(2,1)S(1)}, u32[]{:S(2)}, u32[]{:S(2)}) async-start(bf16[512,8,128]{2,1,0:T(8,128)(2,1)} %get-tuple-element.20), calls=%async_computation.2 | async-start | bytes 2097152 | tf_op jit(solution)/shard_map/all_to_all | solution.py:168
  122.7 11.7 %all-to-all-done.2 = bf16[512,8,128]{2,1,0:T(8,128)(2,1)S(1)} async-done(((bf16[512,8,128]{2,1,0:T(8,128)(2,1)}), bf16[512,8,128]{2,1,0:T(8,128)(2,1)S(1)}, u32[]{:S(2)}, u32[]{:S(2)}) %all-to-all-start.2) | async-done | bytes 1048608 | tf_op jit(solution)/shard_map/all_to_all | solution.py:168
  134.4 4.2 %all-to-all-start.4 = ((bf16[512,8,128]{2,1,0:T(8,128)(2,1)}), bf16[512,8,128]{2,1,0:T(8,128)(2,1)}, u32[]{:S(2)}, u32[]{:S(2)}) async-start(bf16[512,8,128]{2,1,0:T(8,128)(2,1)} %get-tuple-element.22), calls=%async_computation.4 | async-start | bytes 2097152 | tf_op jit(solution)/shard_map/all_to_all | solution.py:168
  139.6 1.9 add_add_fusion.rest_ref
  141.5 23.9 %shard_map.77 = (bf16[512,16,128]{2,1,0:T(8,128)(2,1)}, bf16[512,8,128]{2,1,0:T(8,128)(2,1)}, bf16[512,8,128]{2,1,0:T(8,128)(2,1)}, bf16[512,8,128]{2,1,0:T(8,128)(2,1)}) custom-call(bf16[512,16,128]{2,1,0:T(8,128)(2,1)} %q_ref.5, bf16[512,16,128]{2,1,0:T(8,128)(2,1)} %k_ref.5, bf16[512,16,128]{2,1,0:T(8,128)(2,1)} %v_ref.5, ...), custom_call_target="tpu_custom_call", output_to_operand_aliasing={{0}: (7, {})} | custom-call | tf_op jit(solution)/shard_map/pallas_call | solution.py:156
  165.5 18.9 %all_to_all.91 = bf16[512,8,128]{2,1,0:T(8,128)(2,1)} all-to-all(bf16[512,8,128]{2,1,0:T(8,128)(2,1)} %get-tuple-element.19), channel_id=1, replica_groups=mesh['grp'=2,'seq'=4,'head'=2,'sub'=2] {'head','sub'}, dimensions={0} | all-to-all | bytes 2097152 | tf_op jit(solution)/shard_map/all_to_all | solution.py:168
  184.4 17.6 %all_to_all.92 = bf16[512,8,128]{2,1,0:T(8,128)(2,1)} all-to-all(bf16[512,8,128]{2,1,0:T(8,128)(2,1)S(1)} %copy-done.3), channel_id=1, replica_groups=mesh['grp'=2,'seq'=4,'head'=2,'sub'=2] {'head','sub'}, dimensions={0} | all-to-all | bytes 2097152 | tf_op jit(solution)/shard_map/all_to_all | solution.py:168
  202.0 3.5 %all-to-all-start.5 = ((bf16[512,8,128]{2,1,0:T(8,128)(2,1)}), bf16[512,8,128]{2,1,0:T(8,128)(2,1)S(1)}, u32[]{:S(2)}, u32[]{:S(2)}) async-start(bf16[512,8,128]{2,1,0:T(8,128)(2,1)} %get-tuple-element.23), calls=%async_computation.5 | async-start | bytes 2097152 | tf_op jit(solution)/shard_map/all_to_all | solution.py:168
  206.9 1.9 copy.13
  211.0 9.0 %all-to-all-done.5 = bf16[512,8,128]{2,1,0:T(8,128)(2,1)S(1)} async-done(((bf16[512,8,128]{2,1,0:T(8,128)(2,1)}), bf16[512,8,128]{2,1,0:T(8,128)(2,1)S(1)}, u32[]{:S(2)}, u32[]{:S(2)}) %all-to-all-start.5) | async-done | bytes 1048608 | tf_op jit(solution)/shard_map/all_to_all | solution.py:168
  (29 shorter events, 18.1 us)
Async XLA Ops:
  18.4 10.0 %copy-start = (f32[16,128,128]{2,1,0:T(8,128)S(1)}, f32[16,128,128]{2,1,0:T(8,128)}, u32[]{:S(2)}) copy-start(f32[16,128,128]{2,1,0:T(8,128)} %get-tuple-element.15) | copy-start | bytes 3145732
  20.6 19.3 %copy-start.1 = (f32[16,128,128]{2,1,0:T(8,128)S(1)}, f32[16,128,128]{2,1,0:T(8,128)}, u32[]{:S(2)}) copy-start(f32[16,128,128]{2,1,0:T(8,128)} %get-tuple-element.14) | copy-start | bytes 3145732
  20.6 7.8 %collective-permute-start.4 = (f32[8,128,128]{2,1,0:T(8,128)}, f32[8,128,128]{2,1,0:T(8,128)S(1)}, u32[]{:S(2)}, u32[]{:S(2)}) collective-permute-start(f32[8,128,128]{2,1,0:T(8,128)} %slice_select_fusion), channel_id=1, source_target_pairs={{12,8},{13,9},{14,10},{15,11},{28,24},{29,25},{30,26},{31,27}} | collective-permute-start | bytes 1572872 | tf_op jit(solution)/shard_map/ppermute | solution.py:87
  23.4 16.4 %collective-permute-start = (f32[8,128,128]{2,1,0:T(8,128)}, f32[8,128,128]{2,1,0:T(8,128)S(1)}, u32[]{:S(2)}, u32[]{:S(2)}) collective-permute-start(f32[8,128,128]{2,1,0:T(8,128)} %slice_select_fusion.1), channel_id=1, source_target_pairs={{0,4},{1,5},{2,6},{3,7},{16,20},{17,21},{18,22},{19,23}} | collective-permute-start | bytes 1572872 | tf_op jit(solution)/shard_map/ppermute | solution.py:87
  29.3 16.5 %collective-permute-start.5 = (f32[8,128,128]{2,1,0:T(8,128)}, f32[8,128,128]{2,1,0:T(8,128)}, u32[]{:S(2)}, u32[]{:S(2)}) collective-permute-start(f32[8,128,128]{2,1,0:T(8,128)} %add_select_fusion.2), channel_id=1, source_target_pairs={{8,4},{12,8},{9,5},{13,9},{10,6},{14,10},{11,7},{15,11},{24,20},{2... | collective-permute-start | bytes 1572872 | tf_op jit(solution)/shard_map/ppermute | solution.py:87
  40.7 14.9 %collective-permute-start.1 = (f32[8,128,128]{2,1,0:T(8,128)}, f32[8,128,128]{2,1,0:T(8,128)}, u32[]{:S(2)}, u32[]{:S(2)}) collective-permute-start(f32[8,128,128]{2,1,0:T(8,128)} %add_select_fusion.5), channel_id=1, source_target_pairs={{4,8},{0,4},{5,9},{1,5},{6,10},{2,6},{7,11},{3,7},{20,24},{16,20},... | collective-permute-start | bytes 1572872 | tf_op jit(solution)/shard_map/ppermute | solution.py:87
  47.8 22.0 %collective-permute-start.6 = (f32[8,128,128]{2,1,0:T(8,128)}, f32[8,128,128]{2,1,0:T(8,128)}, u32[]{:S(2)}, u32[]{:S(2)}) collective-permute-start(f32[8,128,128]{2,1,0:T(8,128)} %add_select_fusion.1), channel_id=1, source_target_pairs={{4,0},{8,4},{5,1},{9,5},{6,2},{10,6},{7,3},{11,7},{20,16},{24,20},... | collective-permute-start | bytes 1572872 | tf_op jit(solution)/shard_map/ppermute | solution.py:87
  57.6 14.6 %collective-permute-start.2 = (f32[8,128,128]{2,1,0:T(8,128)}, f32[8,128,128]{2,1,0:T(8,128)}, u32[]{:S(2)}, u32[]{:S(2)}) collective-permute-start(f32[8,128,128]{2,1,0:T(8,128)} %add_select_fusion.4), channel_id=1, source_target_pairs={{8,12},{4,8},{9,13},{5,9},{10,14},{6,10},{11,15},{7,11},{24,28},{2... | collective-permute-start | bytes 1572872 | tf_op jit(solution)/shard_map/ppermute | solution.py:87
  116.5 18.0 %all-to-all-start.2 = ((bf16[512,8,128]{2,1,0:T(8,128)(2,1)}), bf16[512,8,128]{2,1,0:T(8,128)(2,1)S(1)}, u32[]{:S(2)}, u32[]{:S(2)}) async-start(bf16[512,8,128]{2,1,0:T(8,128)(2,1)} %get-tuple-element.20), calls=%async_computation.2 | async-start | bytes 2097152 | tf_op jit(solution)/shard_map/all_to_all | solution.py:168
  120.0 18.7 %collective-permute-start.3 = (f32[8,128,128]{2,1,0:T(8,128)}, f32[8,128,128]{2,1,0:T(8,128)}, u32[]{:S(2)}, u32[]{:S(2)}) collective-permute-start(f32[8,128,128]{2,1,0:T(8,128)} %get-tuple-element.27), channel_id=1, source_target_pairs={{8,12},{9,13},{10,14},{11,15},{24,28},{25,29},{26,30},{27,31}} | collective-permute-start | bytes 1572872 | tf_op jit(solution)/shard_map/ppermute | solution.py:87
  121.4 18.1 %collective-permute-start.7 = (f32[8,128,128]{2,1,0:T(8,128)}, f32[8,128,128]{2,1,0:T(8,128)}, u32[]{:S(2)}, u32[]{:S(2)}) collective-permute-start(f32[8,128,128]{2,1,0:T(8,128)} %get-tuple-element.24), channel_id=1, source_target_pairs={{4,0},{5,1},{6,2},{7,3},{20,16},{21,17},{22,18},{23,19}} | collective-permute-start | bytes 1572872 | tf_op jit(solution)/shard_map/ppermute | solution.py:87
  134.4 31.1 %all-to-all-start.4 = ((bf16[512,8,128]{2,1,0:T(8,128)(2,1)}), bf16[512,8,128]{2,1,0:T(8,128)(2,1)}, u32[]{:S(2)}, u32[]{:S(2)}) async-start(bf16[512,8,128]{2,1,0:T(8,128)(2,1)} %get-tuple-element.22), calls=%async_computation.4 | async-start | bytes 2097152 | tf_op jit(solution)/shard_map/all_to_all | solution.py:168
  165.5 18.9 %copy-start.3 = (bf16[512,8,128]{2,1,0:T(8,128)(2,1)S(1)}, bf16[512,8,128]{2,1,0:T(8,128)(2,1)}, u32[]{:S(2)}) copy-start(bf16[512,8,128]{2,1,0:T(8,128)(2,1)} %get-tuple-element.21) | copy-start | bytes 3145732
  202.0 18.0 %all-to-all-start.5 = ((bf16[512,8,128]{2,1,0:T(8,128)(2,1)}), bf16[512,8,128]{2,1,0:T(8,128)(2,1)S(1)}, u32[]{:S(2)}, u32[]{:S(2)}) async-start(bf16[512,8,128]{2,1,0:T(8,128)(2,1)} %get-tuple-element.23), calls=%async_computation.5 | async-start | bytes 2097152 | tf_op jit(solution)/shard_map/all_to_all | solution.py:168
  206.9 1.9 copy-start.2

commit v4 on v1

--- a/solution.py
+++ b/solution.py
@@ -51,6 +51,7 @@
     row = lax.broadcasted_iota(jnp.int32, (span, span), 0)
     col = lax.broadcasted_iota(jnp.int32, (span, span), 1)
     causal = row >= col
+    upper = row <= col
     for h in range(heads):
         q = q_ref[:, h, :]
         k = k_ref[:, h, :]
@@ -67,8 +68,10 @@
         adj_scores = jnp.where(causal, dot_nt(d, v), 0.0).astype(BF16)
         a_ref[:, h, :] = (dot_nn(qsc, state_low) + dot_nn(scores, v)).astype(a_ref.dtype)
         qg_ref[:, h, :] = ((dot_nt(d, state_low) + dot_nn(adj_scores, k)) * factor).astype(qg_ref.dtype)
-        kg_ref[:, h, :] = (dot_nn(v, suffix_low) + dot_tn(adj_scores, qsc)).astype(kg_ref.dtype)
-        vg_ref[:, h, :] = (dot_nt(k, suffix_low) + dot_tn(scores, d)).astype(vg_ref.dtype)
+        adj_scores_t = jnp.where(upper, dot_nt(v, d), 0.0).astype(BF16)
+        scores_t = jnp.where(upper, dot_nt(k, qsc), 0.0).astype(BF16)
+        kg_ref[:, h, :] = (dot_nn(v, suffix_low) + dot_nn(adj_scores_t, qsc)).astype(kg_ref.dtype)
+        vg_ref[:, h, :] = (dot_nt(k, suffix_low) + dot_nn(scores_t, d)).astype(vg_ref.dtype)
 
 
 def exclusive_scan(total, axis, count, reverse):

time: 221 us -> 236 us (1.068)
  Pallas kernels: 64.9 us -> 79.6 us
    pallas_call x2, Pallas kernels: 47.9 us -> 62.6 us  [per_device(): pl.pallas_call(functools.partial(main_kernel, g * width, width, attended...]
  transfers between devices with their start and end apart: 16 -> 16, of which waited for: 7 -> 7; matrix products, arithmetic and copies ran while one was open for 8% -> 8% of each run, Pallas kernels for 11% -> 13%
where the time goes in v4:
time: 236 us; the launch traced here: 235 us
  Pallas kernels  79.6 us (34%)
  waiting for transfers between devices  58.4 us (25%)
  blocking collectives  36.5 us (15%)
  starting transfers between devices  35.4 us (15%)
  other arithmetic  15.4 us (7%)
  local copies, waits for them, and re-layouts  8.83 us (4%)
    pallas_call x2, Pallas kernels, per_device(): pl.pallas_call(functools.partial(main_kernel, g * width, width, attended...  62.6 us
    all_to_all x2, blocking collectives, per_device(): lax.all_to_all(x, ('head', 'sub'), split_axis=0, concat_axis=1, tiled=True)  36.5 us
    ppermute x12, waiting for transfers between devices, exclusive_scan(): got = lax.ppermute(carried + total, axis, perm=[pair])  31.2 us
    all_to_all x4, waiting for transfers between devices, per_device(): lax.all_to_all(x, ('head', 'sub'), split_axis=0, concat_axis=1, tiled=True)  27.2 us
    ppermute x12, starting transfers between devices, exclusive_scan(): got = lax.ppermute(carried + total, axis, perm=[pair])  20.6 us
    pallas_call x1, Pallas kernels, per_device(): pl.pallas_call(functools.partial(totals_kernel, heads), grid=(blocks,), i...  17 us
    all_to_all x4, starting transfers between devices, per_device(): lax.all_to_all(x, ('head', 'sub'), split_axis=0, concat_axis=1, tiled=True)  14.8 us
    another operation x3, local copies, waits for them, and re-layouts, per_device(): jnp.stack([grads[g][i].reshape(grads[g][i].shape[0], -1, width, head_dim)...  5.76 us
  transfers between devices with their start and end apart: 16, of which 7 were waited for; matrix products, arithmetic and copies ran while one was open for 8% of the time, Pallas kernels for 13%

profile of v4, /device:TPU:0, one launch (start us, length us, event | category | flops | bytes accessed | tf_op | source)
XLA Modules:
  0.0 234.9 jit_solution(10025340806888945609)
XLA Ops:
  1.4 17.0 %shard_map.75 = (f32[16,128,128]{2,1,0:T(8,128)}, f32[16,128,128]{2,1,0:T(8,128)}) custom-call(bf16[512,16,128]{2,1,0:T(8,128)(2,1)} %q_ref.5, bf16[512,16,128]{2,1,0:T(8,128)(2,1)} %k_ref.5, bf16[512,16,128]{2,1,0:T(8,128)(2,1)} %v_ref.5, bf16[512,16,128]{2,1,0:T(8,128)(2,1)} %d_ref.5, f32[512,1]{1,0:T(8,128)} %multiply_rsqrt_fusion.f_ref), custom_call_target="tpu_custom_call" | custom-call | tf_op jit(solution)/shard_map/pallas_call | solution.py:100
  19.6 5.1 %collective-permute-start.6 = (f32[8,128,128]{2,1,0:T(8,128)S(1)}, f32[8,128,128]{2,1,0:T(8,128)S(1)}, u32[]{:S(2)}, u32[]{:S(2)}) collective-permute-start(f32[8,128,128]{2,1,0:T(8,128)S(1)} %slice.16), channel_id=1, source_target_pairs={{0,4},{1,5},{2,6},{3,7},{16,20},{17,21},{18,22},{19,23}} | collective-permute-start | bytes 1572872 | tf_op jit(solution)/shard_map/ppermute | solution.py:82
  26.5 9.3 %collective-permute-done.6 = f32[8,128,128]{2,1,0:T(8,128)S(1)} collective-permute-done((f32[8,128,128]{2,1,0:T(8,128)S(1)}, f32[8,128,128]{2,1,0:T(8,128)S(1)}, u32[]{:S(2)}, u32[]{:S(2)}) %collective-permute-start.6) | collective-permute-done | bytes 524320 | tf_op jit(solution)/shard_map/ppermute | solution.py:82
  36.6 5.0 %collective-permute-start = (f32[8,128,128]{2,1,0:T(8,128)S(1)}, f32[8,128,128]{2,1,0:T(8,128)S(1)}, u32[]{:S(2)}, u32[]{:S(2)}) collective-permute-start(f32[8,128,128]{2,1,0:T(8,128)S(1)} %get-tuple-element.31), channel_id=1, source_target_pairs={{0,4},{1,5},{2,6},{3,7},{16,20},{17,21},{18,22},{19,23}} | collective-permute-start | bytes 1572872 | tf_op jit(solution)/shard_map/ppermute | solution.py:82
  42.5 9.4 %collective-permute-done = f32[8,128,128]{2,1,0:T(8,128)S(1)} collective-permute-done((f32[8,128,128]{2,1,0:T(8,128)S(1)}, f32[8,128,128]{2,1,0:T(8,128)S(1)}, u32[]{:S(2)}, u32[]{:S(2)}) %collective-permute-start) | collective-permute-done | bytes 524320 | tf_op jit(solution)/shard_map/ppermute | solution.py:82
  56.7 11.0 %collective-permute-done.11 = f32[8,128,128]{2,1,0:T(8,128)S(1)} collective-permute-done((f32[8,128,128]{2,1,0:T(8,128)S(1)}, f32[8,128,128]{2,1,0:T(8,128)S(1)}, u32[]{:S(2)}, u32[]{:S(2)}) %collective-permute-start.11) | collective-permute-done | bytes 524320 | tf_op jit(solution)/shard_map/ppermute | solution.py:82
  69.7 31.3 %shard_map.76 = (bf16[512,16,128]{2,1,0:T(8,128)(2,1)}, bf16[512,8,128]{2,1,0:T(8,128)(2,1)}, bf16[512,8,128]{2,1,0:T(8,128)(2,1)}, bf16[512,8,128]{2,1,0:T(8,128)(2,1)}) custom-call(bf16[512,16,128]{2,1,0:T(8,128)(2,1)} %q_ref.5, bf16[512,16,128]{2,1,0:T(8,128)(2,1)} %k_ref.5, bf16[512,16,128]{2,1,0:T(8,128)(2,1)} %v_ref.5, bf16[512,16,128]{2,1,0:T(8,128)(2,1)} %d_ref.5, ...), custom_call_target="tpu_custom_call" | custom-call | tf_op jit(solution)/shard_map/pallas_call | solution.py:131
  100.9 3.5 %all-to-all-start = ((bf16[512,8,128]{2,1,0:T(8,128)(2,1)}), bf16[512,8,128]{2,1,0:T(8,128)(2,1)S(1)}, u32[]{:S(2)}, u32[]{:S(2)}) async-start(bf16[512,8,128]{2,1,0:T(8,128)(2,1)} %get-tuple-element.18), calls=%async_computation | async-start | bytes 2097152 | tf_op jit(solution)/shard_map/all_to_all | solution.py:143
  107.4 11.5 %all-to-all-done = bf16[512,8,128]{2,1,0:T(8,128)(2,1)S(1)} async-done(((bf16[512,8,128]{2,1,0:T(8,128)(2,1)}), bf16[512,8,128]{2,1,0:T(8,128)(2,1)S(1)}, u32[]{:S(2)}, u32[]{:S(2)}) %all-to-all-start) | async-done | bytes 1048608 | tf_op jit(solution)/shard_map/all_to_all | solution.py:143
  118.9 4.2 %all-to-all-start.2 = ((bf16[512,8,128]{2,1,0:T(8,128)(2,1)}), bf16[512,8,128]{2,1,0:T(8,128)(2,1)}, u32[]{:S(2)}, u32[]{:S(2)}) async-start(bf16[512,8,128]{2,1,0:T(8,128)(2,1)} %get-tuple-element.20), calls=%async_computation.2 | async-start | bytes 2097152 | tf_op jit(solution)/shard_map/all_to_all | solution.py:143
  123.1 1.9 slice_add_fusion.2
  126.5 1.9 slice_add_fusion.6
  129.7 8.0 %all-to-all-done.2 = bf16[512,8,128]{2,1,0:T(8,128)(2,1)} async-done(((bf16[512,8,128]{2,1,0:T(8,128)(2,1)}), bf16[512,8,128]{2,1,0:T(8,128)(2,1)}, u32[]{:S(2)}, u32[]{:S(2)}) %all-to-all-start.2) | async-done | bytes 1048608 | tf_op jit(solution)/shard_map/all_to_all | solution.py:143
  137.6 3.5 %all-to-all-start.4 = ((bf16[512,8,128]{2,1,0:T(8,128)(2,1)}), bf16[512,8,128]{2,1,0:T(8,128)(2,1)S(1)}, u32[]{:S(2)}, u32[]{:S(2)}) async-start(bf16[512,8,128]{2,1,0:T(8,128)(2,1)} %get-tuple-element.22), calls=%async_computation.4 | async-start | bytes 2097152 | tf_op jit(solution)/shard_map/all_to_all | solution.py:143
  141.2 2.3 add_add_fusion.3.before_ref
  144.9 2.1 add_add_fusion.2.rest_ref
  147.0 31.3 %shard_map.77 = (bf16[512,16,128]{2,1,0:T(8,128)(2,1)}, bf16[512,8,128]{2,1,0:T(8,128)(2,1)}, bf16[512,8,128]{2,1,0:T(8,128)(2,1)}, bf16[512,8,128]{2,1,0:T(8,128)(2,1)}) custom-call(bf16[512,16,128]{2,1,0:T(8,128)(2,1)} %q_ref.5, bf16[512,16,128]{2,1,0:T(8,128)(2,1)} %k_ref.5, bf16[512,16,128]{2,1,0:T(8,128)(2,1)} %v_ref.5, ...), custom_call_target="tpu_custom_call", output_to_operand_aliasing={{0}: (7, {})} | custom-call | tf_op jit(solution)/shard_map/pallas_call | solution.py:131
  178.3 18.9 %all_to_all.90 = bf16[512,8,128]{2,1,0:T(8,128)(2,1)} all-to-all(bf16[512,8,128]{2,1,0:T(8,128)(2,1)} %get-tuple-element.19), channel_id=1, replica_groups=mesh['grp'=2,'seq'=4,'head'=2,'sub'=2] {'head','sub'}, dimensions={0} | all-to-all | bytes 2097152 | tf_op jit(solution)/shard_map/all_to_all | solution.py:143
  197.3 17.6 %all_to_all.91 = bf16[512,8,128]{2,1,0:T(8,128)(2,1)} all-to-all(bf16[512,8,128]{2,1,0:T(8,128)(2,1)S(1)} %copy-done.6), channel_id=1, replica_groups=mesh['grp'=2,'seq'=4,'head'=2,'sub'=2] {'head','sub'}, dimensions={0} | all-to-all | bytes 2097152 | tf_op jit(solution)/shard_map/all_to_all | solution.py:143
  214.8 3.5 %all-to-all-start.5 = ((bf16[512,8,128]{2,1,0:T(8,128)(2,1)}), bf16[512,8,128]{2,1,0:T(8,128)(2,1)S(1)}, u32[]{:S(2)}, u32[]{:S(2)}) async-start(bf16[512,8,128]{2,1,0:T(8,128)(2,1)} %get-tuple-element.23), calls=%async_computation.5 | async-start | bytes 2097152 | tf_op jit(solution)/shard_map/all_to_all | solution.py:143
  219.8 1.9 copy.13
  223.1 1.9 copy.14
  225.1 7.7 %all-to-all-done.5 = bf16[512,8,128]{2,1,0:T(8,128)(2,1)S(1)} async-done(((bf16[512,8,128]{2,1,0:T(8,128)(2,1)}), bf16[512,8,128]{2,1,0:T(8,128)(2,1)S(1)}, u32[]{:S(2)}, u32[]{:S(2)}) %all-to-all-start.5) | async-done | bytes 1048608 | tf_op jit(solution)/shard_map/all_to_all | solution.py:143
  233.0 1.9 copy.15
  (46 shorter events, 22.1 us)
Async XLA Ops:
  18.4 17.4 %copy-start.1 = (f32[16,128,128]{2,1,0:T(8,128)S(1)}, f32[16,128,128]{2,1,0:T(8,128)}, u32[]{:S(2)}) copy-start(f32[16,128,128]{2,1,0:T(8,128)} %get-tuple-element.14) | copy-start | bytes 3145732
  19.6 22.1 %copy-start = (f32[16,128,128]{2,1,0:T(8,128)S(1)}, f32[16,128,128]{2,1,0:T(8,128)}, u32[]{:S(2)}) copy-start(f32[16,128,128]{2,1,0:T(8,128)} %get-tuple-element.15) | copy-start | bytes 3145732
  19.6 16.2 %collective-permute-start.6 = (f32[8,128,128]{2,1,0:T(8,128)S(1)}, f32[8,128,128]{2,1,0:T(8,128)S(1)}, u32[]{:S(2)}, u32[]{:S(2)}) collective-permute-start(f32[8,128,128]{2,1,0:T(8,128)S(1)} %slice.16), channel_id=1, source_target_pairs={{0,4},{1,5},{2,6},{3,7},{16,20},{17,21},{18,22},{19,23}} | collective-permute-start | bytes 1572872 | tf_op jit(solution)/shard_map/ppermute | solution.py:82
  25.8 15.9 %collective-permute-start.9 = (f32[8,128,128]{2,1,0:T(8,128)S(1)}, f32[8,128,128]{2,1,0:T(8,128)S(1)}, u32[]{:S(2)}, u32[]{:S(2)}) collective-permute-start(f32[8,128,128]{2,1,0:T(8,128)S(1)} %slice.17), channel_id=1, source_target_pairs={{12,8},{13,9},{14,10},{15,11},{28,24},{29,25},{30,26},{31,27}} | collective-permute-start | bytes 1572872 | tf_op jit(solution)/shard_map/ppermute | solution.py:82
  35.9 6.6 %collective-permute-start.7 = (f32[8,128,128]{2,1,0:T(8,128)S(1)}, f32[8,128,128]{2,1,0:T(8,128)S(1)}, u32[]{:S(2)}, u32[]{:S(2)}) collective-permute-start(f32[8,128,128]{2,1,0:T(8,128)S(1)} %get-tuple-element.30), channel_id=1, source_target_pairs={{4,8},{5,9},{6,10},{7,11},{20,24},{21,25},{22,26},{23,27}} | collective-permute-start | bytes 1572872 | tf_op jit(solution)/shard_map/ppermute | solution.py:82
  36.6 15.3 %collective-permute-start = (f32[8,128,128]{2,1,0:T(8,128)S(1)}, f32[8,128,128]{2,1,0:T(8,128)S(1)}, u32[]{:S(2)}, u32[]{:S(2)}) collective-permute-start(f32[8,128,128]{2,1,0:T(8,128)S(1)} %get-tuple-element.31), channel_id=1, source_target_pairs={{0,4},{1,5},{2,6},{3,7},{16,20},{17,21},{18,22},{19,23}} | collective-permute-start | bytes 1572872 | tf_op jit(solution)/shard_map/ppermute | solution.py:82
  41.8 11.8 %collective-permute-start.10 = (f32[8,128,128]{2,1,0:T(8,128)S(1)}, f32[8,128,128]{2,1,0:T(8,128)S(1)}, u32[]{:S(2)}, u32[]{:S(2)}) collective-permute-start(f32[8,128,128]{2,1,0:T(8,128)S(1)} %slice_add_fusion.5), channel_id=1, source_target_pairs={{8,4},{9,5},{10,6},{11,7},{24,20},{25,21},{26,22},{27,23}} | collective-permute-start | bytes 1572872 | tf_op jit(solution)/shard_map/ppermute | solution.py:82
  52.0 1.8 copy-start.3
  52.9 2.8 %collective-permute-start.8 = (f32[8,128,128]{2,1,0:T(8,128)S(1)}, f32[8,128,128]{2,1,0:T(8,128)S(1)}, u32[]{:S(2)}, u32[]{:S(2)}) collective-permute-start(f32[8,128,128]{2,1,0:T(8,128)S(1)} %get-tuple-element.28), channel_id=1, source_target_pairs={{8,12},{9,13},{10,14},{11,15},{24,28},{25,29},{26,30},{27,31}} | collective-permute-start | bytes 1572872 | tf_op jit(solution)/shard_map/ppermute | solution.py:82
  53.8 13.9 %collective-permute-start.11 = (f32[8,128,128]{2,1,0:T(8,128)S(1)}, f32[8,128,128]{2,1,0:T(8,128)S(1)}, u32[]{:S(2)}, u32[]{:S(2)}) collective-permute-start(f32[8,128,128]{2,1,0:T(8,128)S(1)} %get-tuple-element.26), channel_id=1, source_target_pairs={{4,0},{5,1},{6,2},{7,3},{20,16},{21,17},{22,18},{23,19}} | collective-permute-start | bytes 1572872 | tf_op jit(solution)/shard_map/ppermute | solution.py:82
  55.1 12.6 %collective-permute-start.3 = (f32[8,128,128]{2,1,0:T(8,128)S(1)}, f32[8,128,128]{2,1,0:T(8,128)S(1)}, u32[]{:S(2)}, u32[]{:S(2)}) collective-permute-start(f32[8,128,128]{2,1,0:T(8,128)S(1)} %get-tuple-element.27), channel_id=1, source_target_pairs={{12,8},{13,9},{14,10},{15,11},{28,24},{29,25},{30,26},{31,27}} | collective-permute-start | bytes 1572872 | tf_op jit(solution)/shard_map/ppermute | solution.py:82
  67.7 0.8 copy-start.4
  100.9 18.0 %all-to-all-start = ((bf16[512,8,128]{2,1,0:T(8,128)(2,1)}), bf16[512,8,128]{2,1,0:T(8,128)(2,1)S(1)}, u32[]{:S(2)}, u32[]{:S(2)}) async-start(bf16[512,8,128]{2,1,0:T(8,128)(2,1)} %get-tuple-element.18), calls=%async_computation | async-start | bytes 2097152 | tf_op jit(solution)/shard_map/all_to_all | solution.py:143
  104.5 18.7 %collective-permute-start.1 = (f32[8,128,128]{2,1,0:T(8,128)}, f32[8,128,128]{2,1,0:T(8,128)}, u32[]{:S(2)}, u32[]{:S(2)}) collective-permute-start(f32[8,128,128]{2,1,0:T(8,128)} %get-tuple-element.29), channel_id=1, source_target_pairs={{4,8},{5,9},{6,10},{7,11},{20,24},{21,25},{22,26},{23,27}} | collective-permute-start | bytes 1572872 | tf_op jit(solution)/shard_map/ppermute | solution.py:82
  105.9 20.6 %collective-permute-start.4 = (f32[8,128,128]{2,1,0:T(8,128)}, f32[8,128,128]{2,1,0:T(8,128)}, u32[]{:S(2)}, u32[]{:S(2)}) collective-permute-start(f32[8,128,128]{2,1,0:T(8,128)} %get-tuple-element.25), channel_id=1, source_target_pairs={{8,4},{9,5},{10,6},{11,7},{24,20},{25,21},{26,22},{27,23}} | collective-permute-start | bytes 1572872 | tf_op jit(solution)/shard_map/ppermute | solution.py:82
  118.9 18.8 %all-to-all-start.2 = ((bf16[512,8,128]{2,1,0:T(8,128)(2,1)}), bf16[512,8,128]{2,1,0:T(8,128)(2,1)}, u32[]{:S(2)}, u32[]{:S(2)}) async-start(bf16[512,8,128]{2,1,0:T(8,128)(2,1)} %get-tuple-element.20), calls=%async_computation.2 | async-start | bytes 2097152 | tf_op jit(solution)/shard_map/all_to_all | solution.py:143
  125.0 16.2 %collective-permute-start.2 = (f32[8,128,128]{2,1,0:T(8,128)}, f32[8,128,128]{2,1,0:T(8,128)}, u32[]{:S(2)}, u32[]{:S(2)}) collective-permute-start(f32[8,128,128]{2,1,0:T(8,128)} %slice_add_fusion.2), channel_id=1, source_target_pairs={{8,12},{9,13},{10,14},{11,15},{24,28},{25,29},{26,30},{27,31}} | collective-permute-start | bytes 1572872 | tf_op jit(solution)/shard_map/ppermute | solution.py:82
  128.4 16.5 %collective-permute-start.5 = (f32[8,128,128]{2,1,0:T(8,128)}, f32[8,128,128]{2,1,0:T(8,128)}, u32[]{:S(2)}, u32[]{:S(2)}) collective-permute-start(f32[8,128,128]{2,1,0:T(8,128)} %slice_add_fusion.6), channel_id=1, source_target_pairs={{4,0},{5,1},{6,2},{7,3},{20,16},{21,17},{22,18},{23,19}} | collective-permute-start | bytes 1572872 | tf_op jit(solution)/shard_map/ppermute | solution.py:82
  137.6 40.7 %all-to-all-start.4 = ((bf16[512,8,128]{2,1,0:T(8,128)(2,1)}), bf16[512,8,128]{2,1,0:T(8,128)(2,1)S(1)}, u32[]{:S(2)}, u32[]{:S(2)}) async-start(bf16[512,8,128]{2,1,0:T(8,128)(2,1)} %get-tuple-element.22), calls=%async_computation.4 | async-start | bytes 2097152 | tf_op jit(solution)/shard_map/all_to_all | solution.py:143
  141.2 3.7 %copy-start.5 = (f32[8,128,128]{2,1,0:T(8,128)S(1)}, f32[8,128,128]{2,1,0:T(8,128)}, u32[]{:S(2)}) copy-start(f32[8,128,128]{2,1,0:T(8,128)} %copy-done.4) | copy-start | bytes 1572868
  178.3 18.9 %copy-start.6 = (bf16[512,8,128]{2,1,0:T(8,128)(2,1)S(1)}, bf16[512,8,128]{2,1,0:T(8,128)(2,1)}, u32[]{:S(2)}) copy-start(bf16[512,8,128]{2,1,0:T(8,128)(2,1)} %get-tuple-element.21) | copy-start | bytes 3145732
  214.8 18.0 %all-to-all-start.5 = ((bf16[512,8,128]{2,1,0:T(8,128)(2,1)}), bf16[512,8,128]{2,1,0:T(8,128)(2,1)S(1)}, u32[]{:S(2)}, u32[]{:S(2)}) async-start(bf16[512,8,128]{2,1,0:T(8,128)(2,1)} %get-tuple-element.23), calls=%async_computation.5 | async-start | bytes 2097152 | tf_op jit(solution)/shard_map/all_to_all | solution.py:143
  219.8 1.9 copy-start.2

commit v5 on v1

--- a/solution.py
+++ b/solution.py
@@ -25,16 +25,11 @@
 
 
 def totals_kernel(heads, q_ref, k_ref, v_ref, d_ref, f_ref, kv_ref, adj_ref):
-    @pl.when(pl.program_id(0) == 0)
-    def _():
-        kv_ref[...] = jnp.zeros_like(kv_ref)
-        adj_ref[...] = jnp.zeros_like(adj_ref)
-
     factor = f_ref[...]
     for h in range(heads):
         qsc = (q_ref[:, h, :].astype(F32) * factor).astype(BF16)
-        kv_ref[h] += dot_tn(k_ref[:, h, :], v_ref[:, h, :])
-        adj_ref[h] += dot_tn(d_ref[:, h, :], qsc)
+        kv_ref[h] = dot_tn(k_ref[:, h, :], v_ref[:, h, :])
+        adj_ref[h] = dot_tn(d_ref[:, h, :], qsc)
 
 
 def main_kernel(first, heads, aliased, q_ref, k_ref, v_ref, d_ref, f_ref, before_ref, rest_ref, *refs):
@@ -90,24 +85,19 @@
     position = offset + jnp.arange(tok_dev, dtype=jnp.int32)
     factor = lax.rsqrt(jnp.float32(head_dim) * (position + 1).astype(jnp.float32))[:, None]
 
-    tile = pl.BlockSpec((span, heads, head_dim), lambda c: (c, 0, 0))
     fac = pl.BlockSpec((span, 1), lambda c: (c, 0))
-    whole = pl.BlockSpec((heads, head_dim, head_dim), lambda c: (0, 0, 0))
+    width = 8 if heads % 8 == 0 and heads > 8 else heads
     state_shape = jax.ShapeDtypeStruct((heads, head_dim, head_dim), F32)
+    rows = pl.BlockSpec((tok_dev, width, head_dim), lambda g: (0, g, 0))
+    group_state = pl.BlockSpec((width, head_dim, head_dim), lambda g: (g, 0, 0))
     kv_total, adj_total = pl.pallas_call(
-        functools.partial(totals_kernel, heads),
-        grid=(blocks,),
-        in_specs=[tile, tile, tile, tile, fac],
-        out_specs=[whole, whole],
+        functools.partial(totals_kernel, width),
+        grid=(heads // width,),
+        in_specs=[rows] * 4 + [pl.BlockSpec((tok_dev, 1), lambda g: (0, 0))],
+        out_specs=[group_state, group_state],
         out_shape=[state_shape, state_shape],
-        compiler_params=pltpu.CompilerParams(dimension_semantics=("arbitrary",)),
     )(queries, key_rows, value_rows, out_adjoint, factor)
 
-    before = exclusive_scan(kv_total, "seq", seq_count, False)
-    after = exclusive_scan(adj_total, "seq", seq_count, True)
-    rest = after + adj_total
-
-    width = 8 if heads % 8 == 0 and heads > 8 else heads
     groups = heads // width
     attended = None
     grads = []

time: 221 us -> 221 us (level)
  no operation moved by 1% of the time
where the time goes in v5:
time: 221 us; the launch traced here: 220 us
  Pallas kernels  64.3 us (29%)
  waiting for transfers between devices  58.4 us (26%)
  blocking collectives  36.5 us (17%)
  starting transfers between devices  35.5 us (16%)
  other arithmetic  15.4 us (7%)
  local copies, waits for them, and re-layouts  8.83 us (4%)
    pallas_call x2, Pallas kernels, per_device(): pl.pallas_call(functools.partial(main_kernel, g * width, width, attended...  47.9 us
    all_to_all x2, blocking collectives, per_device(): lax.all_to_all(x, ('head', 'sub'), split_axis=0, concat_axis=1, tiled=True)  36.5 us
    ppermute x12, waiting for transfers between devices, exclusive_scan(): got = lax.ppermute(carried + total, axis, perm=[pair])  31.4 us
    all_to_all x4, waiting for transfers between devices, per_device(): lax.all_to_all(x, ('head', 'sub'), split_axis=0, concat_axis=1, tiled=True)  27 us
    ppermute x12, starting transfers between devices, exclusive_scan(): got = lax.ppermute(carried + total, axis, perm=[pair])  20.7 us
    pallas_call x1, Pallas kernels, per_device(): pl.pallas_call(functools.partial(totals_kernel, width), grid=(heads // wi...  16.4 us
    all_to_all x4, starting transfers between devices, per_device(): lax.all_to_all(x, ('head', 'sub'), split_axis=0, concat_axis=1, tiled=True)  14.8 us
    another operation x3, local copies, waits for them, and re-layouts, per_device(): jnp.stack([grads[g][i].reshape(grads[g][i].shape[0], -1, width, head_dim)...  5.76 us
  transfers between devices with their start and end apart: 16, of which 7 were waited for; matrix products, arithmetic and copies ran while one was open for 8% of the time, Pallas kernels for 11%

profile of v5, /device:TPU:0, one launch (start us, length us, event | category | flops | bytes accessed | tf_op | source)
XLA Modules:
  0.0 219.8 jit_solution(14802764416966574050)
XLA Ops:
  1.4 16.4 %shard_map.75 = (f32[16,128,128]{2,1,0:T(8,128)}, f32[16,128,128]{2,1,0:T(8,128)}) custom-call(bf16[512,16,128]{2,1,0:T(8,128)(2,1)} %q_ref.5, bf16[512,16,128]{2,1,0:T(8,128)(2,1)} %k_ref.5, bf16[512,16,128]{2,1,0:T(8,128)(2,1)} %v_ref.5, bf16[512,16,128]{2,1,0:T(8,128)(2,1)} %d_ref.5, f32[512,1]{1,0:T(8,128)} %multiply_rsqrt_fusion.f_ref), custom_call_target="tpu_custom_call" | custom-call | tf_op jit(solution)/shard_map/pallas_call | solution.py:93
  19.0 5.1 %collective-permute-start.6 = (f32[8,128,128]{2,1,0:T(8,128)S(1)}, f32[8,128,128]{2,1,0:T(8,128)S(1)}, u32[]{:S(2)}, u32[]{:S(2)}) collective-permute-start(f32[8,128,128]{2,1,0:T(8,128)S(1)} %slice.16), channel_id=1, source_target_pairs={{0,4},{1,5},{2,6},{3,7},{16,20},{17,21},{18,22},{19,23}} | collective-permute-start | bytes 1572872 | tf_op jit(solution)/shard_map/ppermute | solution.py:74
  25.9 9.3 %collective-permute-done.6 = f32[8,128,128]{2,1,0:T(8,128)S(1)} collective-permute-done((f32[8,128,128]{2,1,0:T(8,128)S(1)}, f32[8,128,128]{2,1,0:T(8,128)S(1)}, u32[]{:S(2)}, u32[]{:S(2)}) %collective-permute-start.6) | collective-permute-done | bytes 524320 | tf_op jit(solution)/shard_map/ppermute | solution.py:74
  36.1 5.0 %collective-permute-start = (f32[8,128,128]{2,1,0:T(8,128)S(1)}, f32[8,128,128]{2,1,0:T(8,128)S(1)}, u32[]{:S(2)}, u32[]{:S(2)}) collective-permute-start(f32[8,128,128]{2,1,0:T(8,128)S(1)} %get-tuple-element.31), channel_id=1, source_target_pairs={{0,4},{1,5},{2,6},{3,7},{16,20},{17,21},{18,22},{19,23}} | collective-permute-start | bytes 1572872 | tf_op jit(solution)/shard_map/ppermute | solution.py:74
  41.9 9.4 %collective-permute-done = f32[8,128,128]{2,1,0:T(8,128)S(1)} collective-permute-done((f32[8,128,128]{2,1,0:T(8,128)S(1)}, f32[8,128,128]{2,1,0:T(8,128)S(1)}, u32[]{:S(2)}, u32[]{:S(2)}) %collective-permute-start) | collective-permute-done | bytes 524320 | tf_op jit(solution)/shard_map/ppermute | solution.py:74
  56.1 11.0 %collective-permute-done.11 = f32[8,128,128]{2,1,0:T(8,128)S(1)} collective-permute-done((f32[8,128,128]{2,1,0:T(8,128)S(1)}, f32[8,128,128]{2,1,0:T(8,128)S(1)}, u32[]{:S(2)}, u32[]{:S(2)}) %collective-permute-start.11) | collective-permute-done | bytes 524320 | tf_op jit(solution)/shard_map/ppermute | solution.py:74
  69.1 23.9 %shard_map.76 = (bf16[512,16,128]{2,1,0:T(8,128)(2,1)}, bf16[512,8,128]{2,1,0:T(8,128)(2,1)}, bf16[512,8,128]{2,1,0:T(8,128)(2,1)}, bf16[512,8,128]{2,1,0:T(8,128)(2,1)}) custom-call(bf16[512,16,128]{2,1,0:T(8,128)(2,1)} %q_ref.5, bf16[512,16,128]{2,1,0:T(8,128)(2,1)} %k_ref.5, bf16[512,16,128]{2,1,0:T(8,128)(2,1)} %v_ref.5, bf16[512,16,128]{2,1,0:T(8,128)(2,1)} %d_ref.5, ...), custom_call_target="tpu_custom_call" | custom-call | tf_op jit(solution)/shard_map/pallas_call | solution.py:118
  93.0 3.5 %all-to-all-start = ((bf16[512,8,128]{2,1,0:T(8,128)(2,1)}), bf16[512,8,128]{2,1,0:T(8,128)(2,1)S(1)}, u32[]{:S(2)}, u32[]{:S(2)}) async-start(bf16[512,8,128]{2,1,0:T(8,128)(2,1)} %get-tuple-element.18), calls=%async_computation | async-start | bytes 2097152 | tf_op jit(solution)/shard_map/all_to_all | solution.py:130
  99.5 11.5 %all-to-all-done = bf16[512,8,128]{2,1,0:T(8,128)(2,1)S(1)} async-done(((bf16[512,8,128]{2,1,0:T(8,128)(2,1)}), bf16[512,8,128]{2,1,0:T(8,128)(2,1)S(1)}, u32[]{:S(2)}, u32[]{:S(2)}) %all-to-all-start) | async-done | bytes 1048608 | tf_op jit(solution)/shard_map/all_to_all | solution.py:130
  111.0 4.2 %all-to-all-start.2 = ((bf16[512,8,128]{2,1,0:T(8,128)(2,1)}), bf16[512,8,128]{2,1,0:T(8,128)(2,1)}, u32[]{:S(2)}, u32[]{:S(2)}) async-start(bf16[512,8,128]{2,1,0:T(8,128)(2,1)} %get-tuple-element.20), calls=%async_computation.2 | async-start | bytes 2097152 | tf_op jit(solution)/shard_map/all_to_all | solution.py:130
  115.2 1.9 slice_add_fusion.2
  118.8 1.9 slice_add_fusion.6
  122.0 7.8 %all-to-all-done.2 = bf16[512,8,128]{2,1,0:T(8,128)(2,1)} async-done(((bf16[512,8,128]{2,1,0:T(8,128)(2,1)}), bf16[512,8,128]{2,1,0:T(8,128)(2,1)}, u32[]{:S(2)}, u32[]{:S(2)}) %all-to-all-start.2) | async-done | bytes 1048608 | tf_op jit(solution)/shard_map/all_to_all | solution.py:130
  129.8 3.5 %all-to-all-start.4 = ((bf16[512,8,128]{2,1,0:T(8,128)(2,1)}), bf16[512,8,128]{2,1,0:T(8,128)(2,1)S(1)}, u32[]{:S(2)}, u32[]{:S(2)}) async-start(bf16[512,8,128]{2,1,0:T(8,128)(2,1)} %get-tuple-element.22), calls=%async_computation.4 | async-start | bytes 2097152 | tf_op jit(solution)/shard_map/all_to_all | solution.py:130
  133.3 2.3 %add_add_fusion.3.before_ref = f32[8,128,128]{2,1,0:T(8,128)} fusion(f32[8,128,128]{2,1,0:T(8,128)} %collective-permute-done.2, f32[8,128,128]{2,1,0:T(8,128)} %copy-done.3, f32[8,128,128]{2,1,0:T(8,128)} %collective-permute-done.1), kind=kLoop, calls=%fused_computation.6 | loop fusion | flops 262144 | bytes 2097152 | tf_op jit(solution)/shard_map/add | solution.py:75
  137.2 2.1 add_add_fusion.2.rest_ref
  139.3 23.9 %shard_map.77 = (bf16[512,16,128]{2,1,0:T(8,128)(2,1)}, bf16[512,8,128]{2,1,0:T(8,128)(2,1)}, bf16[512,8,128]{2,1,0:T(8,128)(2,1)}, bf16[512,8,128]{2,1,0:T(8,128)(2,1)}) custom-call(bf16[512,16,128]{2,1,0:T(8,128)(2,1)} %q_ref.5, bf16[512,16,128]{2,1,0:T(8,128)(2,1)} %k_ref.5, bf16[512,16,128]{2,1,0:T(8,128)(2,1)} %v_ref.5, ...), custom_call_target="tpu_custom_call", output_to_operand_aliasing={{0}: (7, {})} | custom-call | tf_op jit(solution)/shard_map/pallas_call | solution.py:118
  163.2 18.9 %all_to_all.90 = bf16[512,8,128]{2,1,0:T(8,128)(2,1)} all-to-all(bf16[512,8,128]{2,1,0:T(8,128)(2,1)} %get-tuple-element.19), channel_id=1, replica_groups=mesh['grp'=2,'seq'=4,'head'=2,'sub'=2] {'head','sub'}, dimensions={0} | all-to-all | bytes 2097152 | tf_op jit(solution)/shard_map/all_to_all | solution.py:130
  182.2 17.6 %all_to_all.91 = bf16[512,8,128]{2,1,0:T(8,128)(2,1)} all-to-all(bf16[512,8,128]{2,1,0:T(8,128)(2,1)S(1)} %copy-done.6), channel_id=1, replica_groups=mesh['grp'=2,'seq'=4,'head'=2,'sub'=2] {'head','sub'}, dimensions={0} | all-to-all | bytes 2097152 | tf_op jit(solution)/shard_map/all_to_all | solution.py:130
  199.7 3.5 %all-to-all-start.5 = ((bf16[512,8,128]{2,1,0:T(8,128)(2,1)}), bf16[512,8,128]{2,1,0:T(8,128)(2,1)S(1)}, u32[]{:S(2)}, u32[]{:S(2)}) async-start(bf16[512,8,128]{2,1,0:T(8,128)(2,1)} %get-tuple-element.23), calls=%async_computation.5 | async-start | bytes 2097152 | tf_op jit(solution)/shard_map/all_to_all | solution.py:130
  204.7 1.9 copy.13
  208.0 1.9 copy.14
  210.0 7.7 %all-to-all-done.5 = bf16[512,8,128]{2,1,0:T(8,128)(2,1)S(1)} async-done(((bf16[512,8,128]{2,1,0:T(8,128)(2,1)}), bf16[512,8,128]{2,1,0:T(8,128)(2,1)S(1)}, u32[]{:S(2)}, u32[]{:S(2)}) %all-to-all-start.5) | async-done | bytes 1048608 | tf_op jit(solution)/shard_map/all_to_all | solution.py:130
  217.9 1.9 copy.15
  (46 shorter events, 22.5 us)
Async XLA Ops:
  17.9 17.4 %copy-start.1 = (f32[16,128,128]{2,1,0:T(8,128)S(1)}, f32[16,128,128]{2,1,0:T(8,128)}, u32[]{:S(2)}) copy-start(f32[16,128,128]{2,1,0:T(8,128)} %get-tuple-element.14) | copy-start | bytes 3145732
  19.0 22.1 %copy-start = (f32[16,128,128]{2,1,0:T(8,128)S(1)}, f32[16,128,128]{2,1,0:T(8,128)}, u32[]{:S(2)}) copy-start(f32[16,128,128]{2,1,0:T(8,128)} %get-tuple-element.15) | copy-start | bytes 3145732
  19.0 16.2 %collective-permute-start.6 = (f32[8,128,128]{2,1,0:T(8,128)S(1)}, f32[8,128,128]{2,1,0:T(8,128)S(1)}, u32[]{:S(2)}, u32[]{:S(2)}) collective-permute-start(f32[8,128,128]{2,1,0:T(8,128)S(1)} %slice.16), channel_id=1, source_target_pairs={{0,4},{1,5},{2,6},{3,7},{16,20},{17,21},{18,22},{19,23}} | collective-permute-start | bytes 1572872 | tf_op jit(solution)/shard_map/ppermute | solution.py:74
  25.2 15.9 %collective-permute-start.9 = (f32[8,128,128]{2,1,0:T(8,128)S(1)}, f32[8,128,128]{2,1,0:T(8,128)S(1)}, u32[]{:S(2)}, u32[]{:S(2)}) collective-permute-start(f32[8,128,128]{2,1,0:T(8,128)S(1)} %slice.17), channel_id=1, source_target_pairs={{12,8},{13,9},{14,10},{15,11},{28,24},{29,25},{30,26},{31,27}} | collective-permute-start | bytes 1572872 | tf_op jit(solution)/shard_map/ppermute | solution.py:74
  35.4 6.6 %collective-permute-start.7 = (f32[8,128,128]{2,1,0:T(8,128)S(1)}, f32[8,128,128]{2,1,0:T(8,128)S(1)}, u32[]{:S(2)}, u32[]{:S(2)}) collective-permute-start(f32[8,128,128]{2,1,0:T(8,128)S(1)} %get-tuple-element.30), channel_id=1, source_target_pairs={{4,8},{5,9},{6,10},{7,11},{20,24},{21,25},{22,26},{23,27}} | collective-permute-start | bytes 1572872 | tf_op jit(solution)/shard_map/ppermute | solution.py:74
  36.1 15.3 %collective-permute-start = (f32[8,128,128]{2,1,0:T(8,128)S(1)}, f32[8,128,128]{2,1,0:T(8,128)S(1)}, u32[]{:S(2)}, u32[]{:S(2)}) collective-permute-start(f32[8,128,128]{2,1,0:T(8,128)S(1)} %get-tuple-element.31), channel_id=1, source_target_pairs={{0,4},{1,5},{2,6},{3,7},{16,20},{17,21},{18,22},{19,23}} | collective-permute-start | bytes 1572872 | tf_op jit(solution)/shard_map/ppermute | solution.py:74
  41.2 11.8 %collective-permute-start.10 = (f32[8,128,128]{2,1,0:T(8,128)S(1)}, f32[8,128,128]{2,1,0:T(8,128)S(1)}, u32[]{:S(2)}, u32[]{:S(2)}) collective-permute-start(f32[8,128,128]{2,1,0:T(8,128)S(1)} %slice_add_fusion.5), channel_id=1, source_target_pairs={{8,4},{9,5},{10,6},{11,7},{24,20},{25,21},{26,22},{27,23}} | collective-permute-start | bytes 1572872 | tf_op jit(solution)/shard_map/ppermute | solution.py:74
  51.4 1.8 copy-start.3
  52.4 2.8 %collective-permute-start.8 = (f32[8,128,128]{2,1,0:T(8,128)S(1)}, f32[8,128,128]{2,1,0:T(8,128)S(1)}, u32[]{:S(2)}, u32[]{:S(2)}) collective-permute-start(f32[8,128,128]{2,1,0:T(8,128)S(1)} %get-tuple-element.28), channel_id=1, source_target_pairs={{8,12},{9,13},{10,14},{11,15},{24,28},{25,29},{26,30},{27,31}} | collective-permute-start | bytes 1572872 | tf_op jit(solution)/shard_map/ppermute | solution.py:74
  53.2 13.9 %collective-permute-start.11 = (f32[8,128,128]{2,1,0:T(8,128)S(1)}, f32[8,128,128]{2,1,0:T(8,128)S(1)}, u32[]{:S(2)}, u32[]{:S(2)}) collective-permute-start(f32[8,128,128]{2,1,0:T(8,128)S(1)} %get-tuple-element.26), channel_id=1, source_target_pairs={{4,0},{5,1},{6,2},{7,3},{20,16},{21,17},{22,18},{23,19}} | collective-permute-start | bytes 1572872 | tf_op jit(solution)/shard_map/ppermute | solution.py:74
  54.5 12.6 %collective-permute-start.3 = (f32[8,128,128]{2,1,0:T(8,128)S(1)}, f32[8,128,128]{2,1,0:T(8,128)S(1)}, u32[]{:S(2)}, u32[]{:S(2)}) collective-permute-start(f32[8,128,128]{2,1,0:T(8,128)S(1)} %get-tuple-element.27), channel_id=1, source_target_pairs={{12,8},{13,9},{14,10},{15,11},{28,24},{29,25},{30,26},{31,27}} | collective-permute-start | bytes 1572872 | tf_op jit(solution)/shard_map/ppermute | solution.py:74
  67.1 0.8 copy-start.4
  93.0 18.0 %all-to-all-start = ((bf16[512,8,128]{2,1,0:T(8,128)(2,1)}), bf16[512,8,128]{2,1,0:T(8,128)(2,1)S(1)}, u32[]{:S(2)}, u32[]{:S(2)}) async-start(bf16[512,8,128]{2,1,0:T(8,128)(2,1)} %get-tuple-element.18), calls=%async_computation | async-start | bytes 2097152 | tf_op jit(solution)/shard_map/all_to_all | solution.py:130
  96.6 18.7 %collective-permute-start.1 = (f32[8,128,128]{2,1,0:T(8,128)}, f32[8,128,128]{2,1,0:T(8,128)}, u32[]{:S(2)}, u32[]{:S(2)}) collective-permute-start(f32[8,128,128]{2,1,0:T(8,128)} %get-tuple-element.29), channel_id=1, source_target_pairs={{4,8},{5,9},{6,10},{7,11},{20,24},{21,25},{22,26},{23,27}} | collective-permute-start | bytes 1572872 | tf_op jit(solution)/shard_map/ppermute | solution.py:74
  98.0 20.8 %collective-permute-start.4 = (f32[8,128,128]{2,1,0:T(8,128)}, f32[8,128,128]{2,1,0:T(8,128)}, u32[]{:S(2)}, u32[]{:S(2)}) collective-permute-start(f32[8,128,128]{2,1,0:T(8,128)} %get-tuple-element.25), channel_id=1, source_target_pairs={{8,4},{9,5},{10,6},{11,7},{24,20},{25,21},{26,22},{27,23}} | collective-permute-start | bytes 1572872 | tf_op jit(solution)/shard_map/ppermute | solution.py:74
  111.0 18.8 %all-to-all-start.2 = ((bf16[512,8,128]{2,1,0:T(8,128)(2,1)}), bf16[512,8,128]{2,1,0:T(8,128)(2,1)}, u32[]{:S(2)}, u32[]{:S(2)}) async-start(bf16[512,8,128]{2,1,0:T(8,128)(2,1)} %get-tuple-element.20), calls=%async_computation.2 | async-start | bytes 2097152 | tf_op jit(solution)/shard_map/all_to_all | solution.py:130
  117.1 16.2 %collective-permute-start.2 = (f32[8,128,128]{2,1,0:T(8,128)}, f32[8,128,128]{2,1,0:T(8,128)}, u32[]{:S(2)}, u32[]{:S(2)}) collective-permute-start(f32[8,128,128]{2,1,0:T(8,128)} %slice_add_fusion.2), channel_id=1, source_target_pairs={{8,12},{9,13},{10,14},{11,15},{24,28},{25,29},{26,30},{27,31}} | collective-permute-start | bytes 1572872 | tf_op jit(solution)/shard_map/ppermute | solution.py:74
  120.7 16.5 %collective-permute-start.5 = (f32[8,128,128]{2,1,0:T(8,128)}, f32[8,128,128]{2,1,0:T(8,128)}, u32[]{:S(2)}, u32[]{:S(2)}) collective-permute-start(f32[8,128,128]{2,1,0:T(8,128)} %slice_add_fusion.6), channel_id=1, source_target_pairs={{4,0},{5,1},{6,2},{7,3},{20,16},{21,17},{22,18},{23,19}} | collective-permute-start | bytes 1572872 | tf_op jit(solution)/shard_map/ppermute | solution.py:74
  129.8 33.5 %all-to-all-start.4 = ((bf16[512,8,128]{2,1,0:T(8,128)(2,1)}), bf16[512,8,128]{2,1,0:T(8,128)(2,1)S(1)}, u32[]{:S(2)}, u32[]{:S(2)}) async-start(bf16[512,8,128]{2,1,0:T(8,128)(2,1)} %get-tuple-element.22), calls=%async_computation.4 | async-start | bytes 2097152 | tf_op jit(solution)/shard_map/all_to_all | solution.py:130
  133.3 3.9 %copy-start.5 = (f32[8,128,128]{2,1,0:T(8,128)S(1)}, f32[8,128,128]{2,1,0:T(8,128)}, u32[]{:S(2)}) copy-start(f32[8,128,128]{2,1,0:T(8,128)} %copy-done.4) | copy-start | bytes 1572868
  163.2 18.9 %copy-start.6 = (bf16[512,8,128]{2,1,0:T(8,128)(2,1)S(1)}, bf16[512,8,128]{2,1,0:T(8,128)(2,1)}, u32[]{:S(2)}) copy-start(bf16[512,8,128]{2,1,0:T(8,128)(2,1)} %get-tuple-element.21) | copy-start | bytes 3145732
  199.7 18.0 %all-to-all-start.5 = ((bf16[512,8,128]{2,1,0:T(8,128)(2,1)}), bf16[512,8,128]{2,1,0:T(8,128)(2,1)S(1)}, u32[]{:S(2)}, u32[]{:S(2)}) async-start(bf16[512,8,128]{2,1,0:T(8,128)(2,1)} %get-tuple-element.23), calls=%async_computation.5 | async-start | bytes 2097152 | tf_op jit(solution)/shard_map/all_to_all | solution.py:130
  204.7 1.9 copy-start.2

commit v6 on v5

v6 whole, which is shorter than its diff:
```python
import functools

import jax
import jax.numpy as jnp
from jax import lax
from jax.experimental import pallas as pl
from jax.experimental.pallas import tpu as pltpu
from jax.sharding import PartitionSpec as P

SPAN = 64
F32 = jnp.float32
BF16 = jnp.bfloat16


def dot_nn(a, b):
    return jnp.dot(a, b, preferred_element_type=F32)


def dot_nt(a, b):
    return lax.dot_general(a, b, (((1,), (1,)), ((), ())), preferred_element_type=F32)


def dot_tn(a, b):
    return lax.dot_general(a, b, (((0,), (0,)), ((), ())), preferred_element_type=F32)


def totals_kernel(heads, q_ref, k_ref, v_ref, d_ref, kv_ref, adj_ref):
    for h in range(heads):
        kv_ref[h] = dot_tn(k_ref[h], v_ref[h])
        adj_ref[h] = dot_tn(d_ref[h], q_ref[h])


def main_kernel(heads, aliased, q_ref, k_ref, v_ref, d_ref, f_ref, before_ref, rest_ref, *refs):
    if aliased:
        refs = refs[1:]
    a_ref, qg_ref, kg_ref, vg_ref, state, suffix = refs

    @pl.when(pl.program_id(0) == 0)
    def _():
        state[...] = before_ref[...]
        suffix[...] = rest_ref[...]

    factor = f_ref[...]
    span = factor.shape[0]
    row = lax.broadcasted_iota(jnp.int32, (span, span), 0)
    col = lax.broadcasted_iota(jnp.int32, (span, span), 1)
    causal = row >= col
    for h in range(heads):
        qsc = q_ref[h]
        k = k_ref[h]
        v = v_ref[h]
        d = d_ref[h]
        prev = state[h]
        state_low = prev.astype(BF16)
        state[h] = prev + dot_tn(k, v)
        rest = suffix[h] - dot_tn(d, qsc)
        suffix[h] = rest
        suffix_low = rest.astype(BF16)
        scores = jnp.where(causal, dot_nt(qsc, k), 0.0).astype(BF16)
        adj_scores = jnp.where(causal, dot_nt(d, v), 0.0).astype(BF16)
        a_ref[h] = (dot_nn(qsc, state_low) + dot_nn(scores, v)).astype(a_ref.dtype)
        qg_ref[h] = ((dot_nt(d, state_low) + dot_nn(adj_scores, k)) * factor).astype(qg_ref.dtype)
        kg_ref[h] = (dot_nn(v, suffix_low) + dot_tn(adj_scores, qsc)).astype(kg_ref.dtype)
        vg_ref[h] = (dot_nt(k, suffix_low) + dot_tn(scores, d)).astype(vg_ref.dtype)


def exclusive_scan(total, axis, count, reverse):
    carried = jnp.zeros_like(total)
    acc = jnp.zeros_like(total)
    for hop in range(count - 1):
        pair = (count - 1 - hop, count - 2 - hop) if reverse else (hop, hop + 1)
        got = lax.ppermute(carried + total, axis, perm=[pair])
        acc = acc + got
        carried = got
    return acc


def per_device(queries, key_rows, value_rows, out_adjoint, seq_count):
    tok_dev, heads, head_dim = queries.shape
    span = SPAN
    blocks = tok_dev // span
    offset = lax.axis_index("seq") * tok_dev
    position = offset + jnp.arange(tok_dev, dtype=jnp.int32)
    factor = lax.rsqrt(jnp.float32(head_dim) * (position + 1).astype(jnp.float32))[:, None]
    scaled = (queries.astype(F32) * factor[:, :, None]).astype(BF16)
    qh, kh, vh, dh = (jnp.transpose(x, (1, 0, 2)) for x in (scaled, key_rows, value_rows, out_adjoint))

    width = 8 if heads % 8 == 0 and heads > 8 else heads
    groups = heads // width
    state_shape = jax.ShapeDtypeStruct((heads, head_dim, head_dim), F32)
    rows = pl.BlockSpec((width, tok_dev, head_dim), lambda g: (g, 0, 0))
    group_state = pl.BlockSpec((width, head_dim, head_dim), lambda g: (g, 0, 0))
    kv_total, adj_total = pl.pallas_call(
        functools.partial(totals_kernel, width),
        grid=(groups,),
        in_specs=[rows] * 4,
        out_specs=[group_state, group_state],
        out_shape=[state_shape, state_shape],
    )(qh, kh, vh, dh)

    fac = pl.BlockSpec((span, 1), lambda c: (c, 0))
    peers = lax.psum(1, ("head", "sub"))
    attended = None
    grads = []
    for g in range(groups):
        sel = slice(g * width, (g + 1) * width)
        before = exclusive_scan(kv_total[sel], "seq", seq_count, False)
        rest = exclusive_scan(adj_total[sel], "seq", seq_count, True) + adj_total[sel]
        gtile = pl.BlockSpec((width, span, head_dim), lambda c, g=g: (g, c, 0))
        otile = pl.BlockSpec((width, span, head_dim), lambda c: (0, c, 0))
        gwhole = pl.BlockSpec((width, head_dim, head_dim), lambda c: (0, 0, 0))
        grad_shape = jax.ShapeDtypeStruct((width, tok_dev, head_dim), BF16)
        args = [qh, kh, vh, dh, factor, before, rest]
        specs = [gtile] * 4 + [fac, gwhole, gwhole]
        aliases = {}
        if attended is not None:
            args.append(attended)
            specs.append(pl.BlockSpec(memory_space=pl.ANY))
            aliases = {7: 0}
        outs = pl.pallas_call(
            functools.partial(main_kernel, width, attended is not None),
            grid=(blocks,),
            in_specs=specs,
            out_specs=[gtile] + [otile] * 3,
            out_shape=[jax.ShapeDtypeStruct((heads, tok_dev, head_dim), BF16)] + [grad_shape] * 3,
            scratch_shapes=[pltpu.VMEM((width, head_dim, head_dim), F32)] * 2,
            input_output_aliases=aliases,
            compiler_params=pltpu.CompilerParams(dimension_semantics=("arbitrary",)),
        )(*args)
        attended = outs[0]
        grads.append([
            lax.all_to_all(x, ("head", "sub"), split_axis=1, concat_axis=0, tiled=True)
            for x in outs[1:]
        ])
    tok_out = tok_dev // peers
    outs = tuple(
        jnp.transpose(
            jnp.stack([grads[g][i].reshape(peers, width, tok_out, head_dim) for g in range(groups)], 1)
            .reshape(heads * peers, tok_out, head_dim),
            (1, 0, 2),
        )
        for i in range(3)
    )
    return (jnp.transpose(attended, (1, 0, 2)),) + outs


def solution(mesh):
    seq_count = mesh.shape["seq"]
    spec_in = P(("grp", "seq"), ("head", "sub"), None)
    spec_grad = P(("grp", "seq", "head", "sub"), None, None)
    return jax.shard_map(
        lambda *a: per_device(*a, seq_count),
        mesh=mesh,
        in_specs=(spec_in,) * 4,
        out_specs=(spec_in, spec_grad, spec_grad, spec_grad),
        check_vma=False,
    )
```

time: 221 us -> 219 us (level)
  blocking collectives: 36.5 us -> 0 us
  local copies, waits for them, and re-layouts: 8.83 us -> 34.8 us
  Pallas kernels: 64.3 us -> 46.4 us
  waiting for transfers between devices: 58.4 us -> 74.1 us
  starting transfers between devices: 35.5 us -> 44.1 us
  other arithmetic: 15.4 us -> 18 us
    all_to_all x2 -> x0, blocking collectives: 36.5 us -> none  [per_device(): lax.all_to_all(x, ('head', 'sub'), split_axis=0, concat_axis=1, tiled=True)]
    pallas_call x3, Pallas kernels: 64.3 us -> 46.4 us  [the longest x2 41.2 us: per_device(): pl.pallas_call(functools.partial(main_kernel, width, attended is not None...]
    all_to_all x4 -> x6, waiting for transfers between devices: 27 us -> 43.8 us  [per_device(): lax.all_to_all(x, ('head', 'sub'), split_axis=1, concat_axis=0, tiled=True)]
    pallas_call x0 -> x6, local copies, waits for them, and re-layouts: none -> 16.2 us  [per_device(): pl.pallas_call(functools.partial(main_kernel, width, attended is not None...]
    all_to_all x4 -> x6, starting transfers between devices: 14.8 us -> 23.5 us  [per_device(): lax.all_to_all(x, ('head', 'sub'), split_axis=1, concat_axis=0, tiled=True)]
    unnamed x14 -> x30, local copies, waits for them, and re-layouts: 0.83 us -> 7.29 us
    transpose x0 -> x1, local copies, waits for them, and re-layouts: none -> 3.26 us  [per_device(): jnp.transpose(x, (1, 0, 2))]
  transfers between devices with their start and end apart: 16 -> 18, of which waited for: 7 -> 9; matrix products, arithmetic and copies ran while one was open for 8% -> 16% of each run, Pallas kernels for 11% -> 9%
where the time goes in v6:
time: 219 us; the launch traced here: 218 us
  waiting for transfers between devices  74.1 us (34%)
  Pallas kernels  46.4 us (21%)
  starting transfers between devices  44.1 us (20%)
  local copies, waits for them, and re-layouts  34.8 us (16%)
  other arithmetic  18 us (8%)
    all_to_all x6, waiting for transfers between devices, per_device(): lax.all_to_all(x, ('head', 'sub'), split_axis=1, concat_axis=0, tiled=True)  43.8 us
    pallas_call x2, Pallas kernels, per_device(): pl.pallas_call(functools.partial(main_kernel, width, attended is not None...  41.2 us
    ppermute x12, waiting for transfers between devices, exclusive_scan(): got = lax.ppermute(carried + total, axis, perm=[pair])  30.3 us
    all_to_all x6, starting transfers between devices, per_device(): lax.all_to_all(x, ('head', 'sub'), split_axis=1, concat_axis=0, tiled=True)  23.5 us
    ppermute x12, starting transfers between devices, exclusive_scan(): got = lax.ppermute(carried + total, axis, perm=[pair])  20.6 us
    pallas_call x6, local copies, waits for them, and re-layouts, per_device(): pl.pallas_call(functools.partial(main_kernel, width, attended is not None...  16.2 us
    unnamed x30, local copies, waits for them, and re-layouts  7.29 us
    another operation x3, local copies, waits for them, and re-layouts, per_device(): jnp.stack([grads[g][i].reshape(peers, width, tok_out, head_dim) for g in...  5.76 us
  transfers between devices with their start and end apart: 18, of which 9 were waited for; matrix products, arithmetic and copies ran while one was open for 16% of the time, Pallas kernels for 9%

profile of v6, /device:TPU:0, one launch (start us, length us, event | category | flops | bytes accessed | tf_op | source)
XLA Modules:
  0.0 218.2 jit_solution(4020298750856133667)
XLA Ops:
  0.7 3.6 %copy.50 = bf16[512,16,128]{2,0,1:T(8,128)(2,1)} copy(bf16[512,16,128]{2,1,0:T(8,128)(2,1)} %param.5) | data formatting | bytes 4194304 | tf_op args[1]
  7.2 3.3 %copy_bitcast_fusion = (bf16[16,512,128]{2,1,0:T(8,128)(2,1)}, bf16[16,512,128]{2,1,0:T(8,128)(2,1)}) fusion(bf16[512,16,128]{2,1,0:T(8,128)(2,1)S(1)} %copy-done.8, bf16[512,16,128]{2,1,0:T(8,128)(2,1)S(1)} %copy-done.9), kind=kLoop, calls=%fused_computation.5 | loop fusion | bytes 8388608 | tf_op jit(solution)/shard_map/transpose | solution.py:86
  10.5 5.1 %shard_map.75 = (f32[16,128,128]{2,1,0:T(8,128)}, f32[16,128,128]{2,1,0:T(8,128)}) custom-call(bf16[16,512,128]{2,1,0:T(8,128)(2,1)} %fusion.q_ref, bf16[16,512,128]{2,1,0:T(8,128)(2,1)} %bitcast.49, bf16[16,512,128]{2,1,0:T(8,128)(2,1)} %get-tuple-element.45.v_ref, bf16[16,512,128]{2,1,0:T(8,128)(2,1)} %get-tuple-element.44.d_ref), custom_call_target="tpu_custom_call" | custom-call | tf_op jit(solution)/shard_map/pallas_call | solution.py:93
  16.8 5.1 %collective-permute-start.6 = (f32[8,128,128]{2,1,0:T(8,128)S(1)}, f32[8,128,128]{2,1,0:T(8,128)S(1)}, u32[]{:S(2)}, u32[]{:S(2)}) collective-permute-start(f32[8,128,128]{2,1,0:T(8,128)S(1)} %slice.16), channel_id=1, source_target_pairs={{0,4},{1,5},{2,6},{3,7},{16,20},{17,21},{18,22},{19,23}} | collective-permute-start | bytes 1572872 | tf_op jit(solution)/shard_map/ppermute | solution.py:72
  23.7 9.3 %collective-permute-done.6 = f32[8,128,128]{2,1,0:T(8,128)S(1)} collective-permute-done((f32[8,128,128]{2,1,0:T(8,128)S(1)}, f32[8,128,128]{2,1,0:T(8,128)S(1)}, u32[]{:S(2)}, u32[]{:S(2)}) %collective-permute-start.6) | collective-permute-done | bytes 524320 | tf_op jit(solution)/shard_map/ppermute | solution.py:72
  33.9 5.0 %collective-permute-start = (f32[8,128,128]{2,1,0:T(8,128)S(1)}, f32[8,128,128]{2,1,0:T(8,128)S(1)}, u32[]{:S(2)}, u32[]{:S(2)}) collective-permute-start(f32[8,128,128]{2,1,0:T(8,128)S(1)} %get-tuple-element.43), channel_id=1, source_target_pairs={{0,4},{1,5},{2,6},{3,7},{16,20},{17,21},{18,22},{19,23}} | collective-permute-start | bytes 1572872 | tf_op jit(solution)/shard_map/ppermute | solution.py:72
  39.7 9.4 %collective-permute-done = f32[8,128,128]{2,1,0:T(8,128)S(1)} collective-permute-done((f32[8,128,128]{2,1,0:T(8,128)S(1)}, f32[8,128,128]{2,1,0:T(8,128)S(1)}, u32[]{:S(2)}, u32[]{:S(2)}) %collective-permute-start) | collective-permute-done | bytes 524320 | tf_op jit(solution)/shard_map/ppermute | solution.py:72
  54.7 10.2 %collective-permute-done.11 = f32[8,128,128]{2,1,0:T(8,128)S(1)} collective-permute-done((f32[8,128,128]{2,1,0:T(8,128)S(1)}, f32[8,128,128]{2,1,0:T(8,128)S(1)}, u32[]{:S(2)}, u32[]{:S(2)}) %collective-permute-start.11) | collective-permute-done | bytes 524320 | tf_op jit(solution)/shard_map/ppermute | solution.py:72
  66.1 20.6 %shard_map.76 = (bf16[16,512,128]{2,1,0:T(8,128)(2,1)}, bf16[8,512,128]{2,1,0:T(8,128)(2,1)}, bf16[8,512,128]{2,1,0:T(8,128)(2,1)}, bf16[8,512,128]{2,1,0:T(8,128)(2,1)}) custom-call(bf16[16,512,128]{2,1,0:T(8,128)(2,1)} %fusion.q_ref, bf16[16,512,128]{2,1,0:T(8,128)(2,1)} %bitcast.50, bf16[16,512,128]{2,1,0:T(8,128)(2,1)} %get-tuple-element.45.v_ref, ...), custom_call_target="tpu_custom_call" | custom-call | tf_op jit(solution)/shard_map/pallas_call | solution.py:120
  86.8 2.9 %copy.36 = bf16[8,512,128]{2,0,1:T(8,128)(2,1)} copy(bf16[8,512,128]{2,1,0:T(8,128)(2,1)} %get-tuple-element.18) | data formatting | bytes 2097152 | tf_op jit(solution)/shard_map/pallas_call | solution.py:120
  89.7 3.5 %all-to-all-start = ((bf16[8,512,128]{2,0,1:T(8,128)(2,1)}), bf16[8,512,128]{2,0,1:T(8,128)(2,1)S(1)}, u32[]{:S(2)}, u32[]{:S(2)}) async-start(bf16[8,512,128]{2,0,1:T(8,128)(2,1)} %copy.36), calls=%async_computation | async-start | bytes 2097152 | tf_op jit(solution)/shard_map/all_to_all | solution.py:132
  96.2 2.9 %copy.39 = bf16[8,512,128]{2,0,1:T(8,128)(2,1)} copy(bf16[8,512,128]{2,1,0:T(8,128)(2,1)} %get-tuple-element.20) | data formatting | bytes 2097152 | tf_op jit(solution)/shard_map/pallas_call | solution.py:120
  99.1 8.5 %all-to-all-done = bf16[8,512,128]{2,0,1:T(8,128)(2,1)S(1)} async-done(((bf16[8,512,128]{2,0,1:T(8,128)(2,1)}), bf16[8,512,128]{2,0,1:T(8,128)(2,1)S(1)}, u32[]{:S(2)}, u32[]{:S(2)}) %all-to-all-start) | async-done | bytes 1048608 | tf_op jit(solution)/shard_map/all_to_all | solution.py:132
  107.6 4.3 %all-to-all-start.2 = ((bf16[8,512,128]{2,0,1:T(8,128)(2,1)}), bf16[8,512,128]{2,0,1:T(8,128)(2,1)}, u32[]{:S(2)}, u32[]{:S(2)}) async-start(bf16[8,512,128]{2,0,1:T(8,128)(2,1)} %copy.39), calls=%async_computation.2 | async-start | bytes 2097152 | tf_op jit(solution)/shard_map/all_to_all | solution.py:132
  120.2 6.2 %all-to-all-done.2 = bf16[8,512,128]{2,0,1:T(8,128)(2,1)} async-done(((bf16[8,512,128]{2,0,1:T(8,128)(2,1)}), bf16[8,512,128]{2,0,1:T(8,128)(2,1)}, u32[]{:S(2)}, u32[]{:S(2)}) %all-to-all-start.2) | async-done | bytes 1048608 | tf_op jit(solution)/shard_map/all_to_all | solution.py:132
  126.4 3.7 %all-to-all-start.4 = ((bf16[8,512,128]{2,0,1:T(8,128)(2,1)}), bf16[8,512,128]{2,0,1:T(8,128)(2,1)S(1)}, u32[]{:S(2)}, u32[]{:S(2)}) async-start(bf16[8,512,128]{2,0,1:T(8,128)(2,1)} %copy.42), calls=%async_computation.4 | async-start | bytes 2097152 | tf_op jit(solution)/shard_map/all_to_all | solution.py:132
  135.9 20.6 %shard_map.77 = (bf16[16,512,128]{2,1,0:T(8,128)(2,1)}, bf16[8,512,128]{2,1,0:T(8,128)(2,1)}, bf16[8,512,128]{2,1,0:T(8,128)(2,1)}, bf16[8,512,128]{2,1,0:T(8,128)(2,1)}) custom-call(bf16[16,512,128]{2,1,0:T(8,128)(2,1)} %fusion.q_ref, bf16[16,512,128]{2,1,0:T(8,128)(2,1)} %bitcast.51, ...), custom_call_target="tpu_custom_call", output_to_operand_aliasing={{0}: (7, {})} | custom-call | tf_op jit(solution)/shard_map/pallas_call | solution.py:120
  159.4 3.5 %all-to-all-start.1 = ((bf16[8,512,128]{2,0,1:T(8,128)(2,1)}), bf16[8,512,128]{2,0,1:T(8,128)(2,1)S(1)}, u32[]{:S(2)}, u32[]{:S(2)}) async-start(bf16[8,512,128]{2,0,1:T(8,128)(2,1)} %copy.37), calls=%async_computation.1 | async-start | bytes 2097152 | tf_op jit(solution)/shard_map/all_to_all | solution.py:132
  165.8 11.6 %all-to-all-done.1 = bf16[8,512,128]{2,0,1:T(8,128)(2,1)S(1)} async-done(((bf16[8,512,128]{2,0,1:T(8,128)(2,1)}), bf16[8,512,128]{2,0,1:T(8,128)(2,1)S(1)}, u32[]{:S(2)}, u32[]{:S(2)}) %all-to-all-start.1) | async-done | bytes 1048608 | tf_op jit(solution)/shard_map/all_to_all | solution.py:132
  177.3 4.3 %all-to-all-start.3 = ((bf16[8,512,128]{2,0,1:T(8,128)(2,1)}), bf16[8,512,128]{2,0,1:T(8,128)(2,1)}, u32[]{:S(2)}, u32[]{:S(2)}) async-start(bf16[8,512,128]{2,0,1:T(8,128)(2,1)} %copy.40), calls=%async_computation.3 | async-start | bytes 2097152 | tf_op jit(solution)/shard_map/all_to_all | solution.py:132
  181.6 3.0 %copy.43 = bf16[8,512,128]{2,0,1:T(8,128)(2,1)} copy(bf16[8,512,128]{2,1,0:T(8,128)(2,1)} %get-tuple-element.23) | data formatting | bytes 2097152 | tf_op jit(solution)/shard_map/pallas_call | solution.py:120
  184.6 11.5 %all-to-all-done.3 = bf16[8,512,128]{2,0,1:T(8,128)(2,1)} async-done(((bf16[8,512,128]{2,0,1:T(8,128)(2,1)}), bf16[8,512,128]{2,0,1:T(8,128)(2,1)}, u32[]{:S(2)}, u32[]{:S(2)}) %all-to-all-start.3) | async-done | bytes 1048608 | tf_op jit(solution)/shard_map/all_to_all | solution.py:132
  196.1 4.3 %all-to-all-start.5 = ((bf16[8,512,128]{2,0,1:T(8,128)(2,1)}), bf16[8,512,128]{2,0,1:T(8,128)(2,1)}, u32[]{:S(2)}, u32[]{:S(2)}) async-start(bf16[8,512,128]{2,0,1:T(8,128)(2,1)} %copy.43), calls=%async_computation.5 | async-start | bytes 2097152 | tf_op jit(solution)/shard_map/all_to_all | solution.py:132
  208.8 6.0 %all-to-all-done.5 = bf16[8,512,128]{2,0,1:T(8,128)(2,1)} async-done(((bf16[8,512,128]{2,0,1:T(8,128)(2,1)}), bf16[8,512,128]{2,0,1:T(8,128)(2,1)}, u32[]{:S(2)}, u32[]{:S(2)}) %all-to-all-start.5) | async-done | bytes 1048608 | tf_op jit(solution)/shard_map/all_to_all | solution.py:132
  (73 shorter events, 48.8 us)
Async XLA Ops:
  15.6 17.4 %copy-start.1 = (f32[16,128,128]{2,1,0:T(8,128)S(1)}, f32[16,128,128]{2,1,0:T(8,128)}, u32[]{:S(2)}) copy-start(f32[16,128,128]{2,1,0:T(8,128)} %get-tuple-element.14) | copy-start | bytes 3145732
  16.8 22.1 %copy-start = (f32[16,128,128]{2,1,0:T(8,128)S(1)}, f32[16,128,128]{2,1,0:T(8,128)}, u32[]{:S(2)}) copy-start(f32[16,128,128]{2,1,0:T(8,128)} %get-tuple-element.15) | copy-start | bytes 3145732
  16.8 16.2 %collective-permute-start.6 = (f32[8,128,128]{2,1,0:T(8,128)S(1)}, f32[8,128,128]{2,1,0:T(8,128)S(1)}, u32[]{:S(2)}, u32[]{:S(2)}) collective-permute-start(f32[8,128,128]{2,1,0:T(8,128)S(1)} %slice.16), channel_id=1, source_target_pairs={{0,4},{1,5},{2,6},{3,7},{16,20},{17,21},{18,22},{19,23}} | collective-permute-start | bytes 1572872 | tf_op jit(solution)/shard_map/ppermute | solution.py:72
  23.0 15.9 %collective-permute-start.9 = (f32[8,128,128]{2,1,0:T(8,128)S(1)}, f32[8,128,128]{2,1,0:T(8,128)S(1)}, u32[]{:S(2)}, u32[]{:S(2)}) collective-permute-start(f32[8,128,128]{2,1,0:T(8,128)S(1)} %slice.17), channel_id=1, source_target_pairs={{12,8},{13,9},{14,10},{15,11},{28,24},{29,25},{30,26},{31,27}} | collective-permute-start | bytes 1572872 | tf_op jit(solution)/shard_map/ppermute | solution.py:72
  33.2 6.6 %collective-permute-start.7 = (f32[8,128,128]{2,1,0:T(8,128)S(1)}, f32[8,128,128]{2,1,0:T(8,128)S(1)}, u32[]{:S(2)}, u32[]{:S(2)}) collective-permute-start(f32[8,128,128]{2,1,0:T(8,128)S(1)} %get-tuple-element.42), channel_id=1, source_target_pairs={{4,8},{5,9},{6,10},{7,11},{20,24},{21,25},{22,26},{23,27}} | collective-permute-start | bytes 1572872 | tf_op jit(solution)/shard_map/ppermute | solution.py:72
  33.9 15.3 %collective-permute-start = (f32[8,128,128]{2,1,0:T(8,128)S(1)}, f32[8,128,128]{2,1,0:T(8,128)S(1)}, u32[]{:S(2)}, u32[]{:S(2)}) collective-permute-start(f32[8,128,128]{2,1,0:T(8,128)S(1)} %get-tuple-element.43), channel_id=1, source_target_pairs={{0,4},{1,5},{2,6},{3,7},{16,20},{17,21},{18,22},{19,23}} | collective-permute-start | bytes 1572872 | tf_op jit(solution)/shard_map/ppermute | solution.py:72
  39.0 11.8 %collective-permute-start.10 = (f32[8,128,128]{2,1,0:T(8,128)S(1)}, f32[8,128,128]{2,1,0:T(8,128)S(1)}, u32[]{:S(2)}, u32[]{:S(2)}) collective-permute-start(f32[8,128,128]{2,1,0:T(8,128)S(1)} %slice_add_fusion.5), channel_id=1, source_target_pairs={{8,4},{9,5},{10,6},{11,7},{24,20},{25,21},{26,22},{27,23}} | collective-permute-start | bytes 1572872 | tf_op jit(solution)/shard_map/ppermute | solution.py:72
  50.2 3.6 %collective-permute-start.8 = (f32[8,128,128]{2,1,0:T(8,128)S(1)}, f32[8,128,128]{2,1,0:T(8,128)S(1)}, u32[]{:S(2)}, u32[]{:S(2)}) collective-permute-start(f32[8,128,128]{2,1,0:T(8,128)S(1)} %get-tuple-element.40), channel_id=1, source_target_pairs={{8,12},{9,13},{10,14},{11,15},{24,28},{25,29},{26,30},{27,31}} | collective-permute-start | bytes 1572872 | tf_op jit(solution)/shard_map/ppermute | solution.py:72
  51.0 13.9 %collective-permute-start.11 = (f32[8,128,128]{2,1,0:T(8,128)S(1)}, f32[8,128,128]{2,1,0:T(8,128)S(1)}, u32[]{:S(2)}, u32[]{:S(2)}) collective-permute-start(f32[8,128,128]{2,1,0:T(8,128)S(1)} %get-tuple-element.38), channel_id=1, source_target_pairs={{4,0},{5,1},{6,2},{7,3},{20,16},{21,17},{22,18},{23,19}} | collective-permute-start | bytes 1572872 | tf_op jit(solution)/shard_map/ppermute | solution.py:72
  52.3 12.6 %collective-permute-start.3 = (f32[8,128,128]{2,1,0:T(8,128)S(1)}, f32[8,128,128]{2,1,0:T(8,128)S(1)}, u32[]{:S(2)}, u32[]{:S(2)}) collective-permute-start(f32[8,128,128]{2,1,0:T(8,128)S(1)} %get-tuple-element.39), channel_id=1, source_target_pairs={{12,8},{13,9},{14,10},{15,11},{28,24},{29,25},{30,26},{31,27}} | collective-permute-start | bytes 1572872 | tf_op jit(solution)/shard_map/ppermute | solution.py:72
  89.7 18.0 %all-to-all-start = ((bf16[8,512,128]{2,0,1:T(8,128)(2,1)}), bf16[8,512,128]{2,0,1:T(8,128)(2,1)S(1)}, u32[]{:S(2)}, u32[]{:S(2)}) async-start(bf16[8,512,128]{2,0,1:T(8,128)(2,1)} %copy.36), calls=%async_computation | async-start | bytes 2097152 | tf_op jit(solution)/shard_map/all_to_all | solution.py:132
  93.2 18.7 %collective-permute-start.1 = (f32[8,128,128]{2,1,0:T(8,128)}, f32[8,128,128]{2,1,0:T(8,128)}, u32[]{:S(2)}, u32[]{:S(2)}) collective-permute-start(f32[8,128,128]{2,1,0:T(8,128)} %get-tuple-element.41), channel_id=1, source_target_pairs={{4,8},{5,9},{6,10},{7,11},{20,24},{21,25},{22,26},{23,27}} | collective-permute-start | bytes 1572872 | tf_op jit(solution)/shard_map/ppermute | solution.py:72
  94.7 20.7 %collective-permute-start.4 = (f32[8,128,128]{2,1,0:T(8,128)}, f32[8,128,128]{2,1,0:T(8,128)}, u32[]{:S(2)}, u32[]{:S(2)}) collective-permute-start(f32[8,128,128]{2,1,0:T(8,128)} %get-tuple-element.37), channel_id=1, source_target_pairs={{8,4},{9,5},{10,6},{11,7},{24,20},{25,21},{26,22},{27,23}} | collective-permute-start | bytes 1572872 | tf_op jit(solution)/shard_map/ppermute | solution.py:72
  107.6 18.8 %all-to-all-start.2 = ((bf16[8,512,128]{2,0,1:T(8,128)(2,1)}), bf16[8,512,128]{2,0,1:T(8,128)(2,1)}, u32[]{:S(2)}, u32[]{:S(2)}) async-start(bf16[8,512,128]{2,0,1:T(8,128)(2,1)} %copy.39), calls=%async_computation.2 | async-start | bytes 2097152 | tf_op jit(solution)/shard_map/all_to_all | solution.py:132
  111.9 6.7 %copy-start.13 = (bf16[8,512,128]{2,1,0:T(8,128)(2,1)S(1)}, bf16[8,512,128]{2,1,0:T(8,128)(2,1)}, u32[]{:S(2)}) copy-start(bf16[8,512,128]{2,1,0:T(8,128)(2,1)} %get-tuple-element.22) | copy-start | bytes 3145732
  113.9 16.2 %collective-permute-start.2 = (f32[8,128,128]{2,1,0:T(8,128)}, f32[8,128,128]{2,1,0:T(8,128)}, u32[]{:S(2)}, u32[]{:S(2)}) collective-permute-start(f32[8,128,128]{2,1,0:T(8,128)} %slice_add_fusion.2), channel_id=1, source_target_pairs={{8,12},{9,13},{10,14},{11,15},{24,28},{25,29},{26,30},{27,31}} | collective-permute-start | bytes 1572872 | tf_op jit(solution)/shard_map/ppermute | solution.py:72
  117.3 16.5 %collective-permute-start.5 = (f32[8,128,128]{2,1,0:T(8,128)}, f32[8,128,128]{2,1,0:T(8,128)}, u32[]{:S(2)}, u32[]{:S(2)}) collective-permute-start(f32[8,128,128]{2,1,0:T(8,128)} %slice_add_fusion.6), channel_id=1, source_target_pairs={{4,0},{5,1},{6,2},{7,3},{20,16},{21,17},{22,18},{23,19}} | collective-permute-start | bytes 1572872 | tf_op jit(solution)/shard_map/ppermute | solution.py:72
  126.4 33.0 %all-to-all-start.4 = ((bf16[8,512,128]{2,0,1:T(8,128)(2,1)}), bf16[8,512,128]{2,0,1:T(8,128)(2,1)S(1)}, u32[]{:S(2)}, u32[]{:S(2)}) async-start(bf16[8,512,128]{2,0,1:T(8,128)(2,1)} %copy.42), calls=%async_computation.4 | async-start | bytes 2097152 | tf_op jit(solution)/shard_map/all_to_all | solution.py:132
  159.4 6.4 %copy-start.3 = (bf16[8,512,128]{2,0,1:T(8,128)(2,1)}, bf16[8,512,128]{2,0,1:T(8,128)(2,1)S(1)}, u32[]{:S(2)}) copy-start(bf16[8,512,128]{2,0,1:T(8,128)(2,1)S(1)} %all-to-all-done.4) | copy-start | bytes 3145732
  159.4 18.0 %all-to-all-start.1 = ((bf16[8,512,128]{2,0,1:T(8,128)(2,1)}), bf16[8,512,128]{2,0,1:T(8,128)(2,1)S(1)}, u32[]{:S(2)}, u32[]{:S(2)}) async-start(bf16[8,512,128]{2,0,1:T(8,128)(2,1)} %copy.37), calls=%async_computation.1 | async-start | bytes 2097152 | tf_op jit(solution)/shard_map/all_to_all | solution.py:132
  177.3 18.8 %all-to-all-start.3 = ((bf16[8,512,128]{2,0,1:T(8,128)(2,1)}), bf16[8,512,128]{2,0,1:T(8,128)(2,1)}, u32[]{:S(2)}, u32[]{:S(2)}) async-start(bf16[8,512,128]{2,0,1:T(8,128)(2,1)} %copy.40), calls=%async_computation.3 | async-start | bytes 2097152 | tf_op jit(solution)/shard_map/all_to_all | solution.py:132
  181.6 18.8 %copy-start.2 = (bf16[16,512,128]{2,1,0:T(8,128)(2,1)S(1)}, bf16[16,512,128]{2,1,0:T(8,128)(2,1)}, u32[]{:S(2)}) copy-start(bf16[16,512,128]{2,1,0:T(8,128)(2,1)} %get-tuple-element.17) | copy-start | bytes 6291460
  196.1 18.8 %all-to-all-start.5 = ((bf16[8,512,128]{2,0,1:T(8,128)(2,1)}), bf16[8,512,128]{2,0,1:T(8,128)(2,1)}, u32[]{:S(2)}, u32[]{:S(2)}) async-start(bf16[8,512,128]{2,0,1:T(8,128)(2,1)} %copy.43), calls=%async_computation.5 | async-start | bytes 2097152 | tf_op jit(solution)/shard_map/all_to_all | solution.py:132
  206.9 8.0 %copy-start.4 = (bf16[8,512,128]{2,0,1:T(8,128)(2,1)S(1)}, bf16[8,512,128]{2,0,1:T(8,128)(2,1)}, u32[]{:S(2)}) copy-start(bf16[8,512,128]{2,0,1:T(8,128)(2,1)} %copy-done.3) | copy-start | bytes 3145732
  (8 other events, 26.0 us)

commit v7 on v6

--- a/solution.py
+++ b/solution.py
@@ -100,6 +100,9 @@
 
     fac = pl.BlockSpec((span, 1), lambda c: (c, 0))
     peers = lax.psum(1, ("head", "sub"))
+    tok_out = tok_dev // peers
+    split_out = tok_out % span == 0
+    per_peer = tok_out // span
     attended = None
     grads = []
     for g in range(groups):
@@ -107,9 +110,15 @@
         before = exclusive_scan(kv_total[sel], "seq", seq_count, False)
         rest = exclusive_scan(adj_total[sel], "seq", seq_count, True) + adj_total[sel]
         gtile = pl.BlockSpec((width, span, head_dim), lambda c, g=g: (g, c, 0))
-        otile = pl.BlockSpec((width, span, head_dim), lambda c: (0, c, 0))
         gwhole = pl.BlockSpec((width, head_dim, head_dim), lambda c: (0, 0, 0))
-        grad_shape = jax.ShapeDtypeStruct((width, tok_dev, head_dim), BF16)
+        if split_out:
+            otile = pl.BlockSpec(
+                (None, width, span, head_dim), lambda c: (c // per_peer, 0, c % per_peer, 0)
+            )
+            grad_shape = jax.ShapeDtypeStruct((peers, width, tok_out, head_dim), BF16)
+        else:
+            otile = pl.BlockSpec((width, span, head_dim), lambda c: (0, c, 0))
+            grad_shape = jax.ShapeDtypeStruct((width, tok_dev, head_dim), BF16)
         args = [qh, kh, vh, dh, factor, before, rest]
         specs = [gtile] * 4 + [fac, gwhole, gwhole]
         aliases = {}
@@ -128,11 +137,11 @@
             compiler_params=pltpu.CompilerParams(dimension_semantics=("arbitrary",)),
         )(*args)
         attended = outs[0]
+        axis = 0 if split_out else 1
         grads.append([
-            lax.all_to_all(x, ("head", "sub"), split_axis=1, concat_axis=0, tiled=True)
+            lax.all_to_all(x, ("head", "sub"), split_axis=axis, concat_axis=0, tiled=True)
             for x in outs[1:]
         ])
-    tok_out = tok_dev // peers
     outs = tuple(
         jnp.transpose(
             jnp.stack([grads[g][i].reshape(peers, width, tok_out, head_dim) for g in range(groups)], 1)

time: 219 us -> 215 us (0.982)
  blocking collectives: 0 us -> 36.7 us
  waiting for transfers between devices: 74.1 us -> 54 us
  local copies, waits for them, and re-layouts: 34.8 us -> 21.5 us
  starting transfers between devices: 44.1 us -> 36.3 us
    all_to_all x0 -> x2, blocking collectives: none -> 36.7 us  [per_device(): lax.all_to_all(x, ('head', 'sub'), split_axis=axis, concat_axis=0, tiled=...]
    all_to_all x6 -> x4, waiting for transfers between devices: 43.8 us -> 23.6 us  [per_device(): lax.all_to_all(x, ('head', 'sub'), split_axis=axis, concat_axis=0, tiled=...]
    pallas_call x6 -> x0, local copies, waits for them, and re-layouts: 16.2 us -> none  [per_device(): pl.pallas_call(functools.partial(main_kernel, width, attended is not None...]
    unnamed x30 -> x33, local copies, waits for them, and re-layouts: 7.29 us -> 15.3 us
    all_to_all x6 -> x4, starting transfers between devices: 23.5 us -> 15.7 us  [per_device(): lax.all_to_all(x, ('head', 'sub'), split_axis=axis, concat_axis=0, tiled=...]
    another operation x3, local copies, waits for them, and re-layouts: 5.76 us -> 0.71 us  [per_device(): jnp.stack([grads[g][i].reshape(peers, width, tok_out, head_dim) for g in...]
  transfers between devices with their start and end apart: 18 -> 16, of which waited for: 9 -> 7; matrix products, arithmetic and copies ran while one was open for 16% -> 10% of each run, Pallas kernels for 9% -> 10%
where the time goes in v7:
time: 215 us; the launch traced here: 214 us
  waiting for transfers between devices  54 us (25%)
  Pallas kernels  46.8 us (22%)
  blocking collectives  36.7 us (17%)
  starting transfers between devices  36.3 us (17%)
  local copies, waits for them, and re-layouts  21.5 us (10%)
  other arithmetic  17.5 us (8%)
    pallas_call x2, Pallas kernels, per_device(): pl.pallas_call(functools.partial(main_kernel, width, attended is not None...  41.6 us
    all_to_all x2, blocking collectives, per_device(): lax.all_to_all(x, ('head', 'sub'), split_axis=axis, concat_axis=0, tiled=...  36.7 us
    ppermute x12, waiting for transfers between devices, exclusive_scan(): got = lax.ppermute(carried + total, axis, perm=[pair])  30.4 us
    all_to_all x4, waiting for transfers between devices, per_device(): lax.all_to_all(x, ('head', 'sub'), split_axis=axis, concat_axis=0, tiled=...  23.6 us
    ppermute x12, starting transfers between devices, exclusive_scan(): got = lax.ppermute(carried + total, axis, perm=[pair])  20.6 us
    all_to_all x4, starting transfers between devices, per_device(): lax.all_to_all(x, ('head', 'sub'), split_axis=axis, concat_axis=0, tiled=...  15.7 us
    unnamed x33, local copies, waits for them, and re-layouts  15.3 us
    pallas_call x1, Pallas kernels, per_device(): pl.pallas_call(functools.partial(totals_kernel, width), grid=(groups,), i...  5.17 us
  transfers between devices with their start and end apart: 16, of which 7 were waited for; matrix products, arithmetic and copies ran while one was open for 10% of the time, Pallas kernels for 10%

profile of v7, /device:TPU:0, one launch (start us, length us, event | category | flops | bytes accessed | tf_op | source)
XLA Modules:
  0.0 213.7 jit_solution(10783790485959301443)
XLA Ops:
  0.7 3.6 %copy.41 = bf16[512,16,128]{2,0,1:T(8,128)(2,1)} copy(bf16[512,16,128]{2,1,0:T(8,128)(2,1)} %param.5) | data formatting | bytes 4194304 | tf_op args[1]
  7.2 3.3 %copy_bitcast_fusion = (bf16[16,512,128]{2,1,0:T(8,128)(2,1)}, bf16[16,512,128]{2,1,0:T(8,128)(2,1)}) fusion(bf16[512,16,128]{2,1,0:T(8,128)(2,1)S(1)} %copy-done.8, bf16[512,16,128]{2,1,0:T(8,128)(2,1)S(1)} %copy-done.9), kind=kLoop, calls=%fused_computation.5 | loop fusion | bytes 8388608 | tf_op jit(solution)/shard_map/transpose | solution.py:86
  10.5 5.2 %shard_map.75 = (f32[16,128,128]{2,1,0:T(8,128)}, f32[16,128,128]{2,1,0:T(8,128)}) custom-call(bf16[16,512,128]{2,1,0:T(8,128)(2,1)} %fusion.q_ref, bf16[16,512,128]{2,1,0:T(8,128)(2,1)} %bitcast.25, bf16[16,512,128]{2,1,0:T(8,128)(2,1)} %get-tuple-element.45.v_ref, bf16[16,512,128]{2,1,0:T(8,128)(2,1)} %get-tuple-element.44.d_ref), custom_call_target="tpu_custom_call" | custom-call | tf_op jit(solution)/shard_map/pallas_call | solution.py:93
  16.9 5.1 %collective-permute-start.6 = (f32[8,128,128]{2,1,0:T(8,128)S(1)}, f32[8,128,128]{2,1,0:T(8,128)S(1)}, u32[]{:S(2)}, u32[]{:S(2)}) collective-permute-start(f32[8,128,128]{2,1,0:T(8,128)S(1)} %slice.16), channel_id=1, source_target_pairs={{0,4},{1,5},{2,6},{3,7},{16,20},{17,21},{18,22},{19,23}} | collective-permute-start | bytes 1572872 | tf_op jit(solution)/shard_map/ppermute | solution.py:72
  23.7 9.3 %collective-permute-done.6 = f32[8,128,128]{2,1,0:T(8,128)S(1)} collective-permute-done((f32[8,128,128]{2,1,0:T(8,128)S(1)}, f32[8,128,128]{2,1,0:T(8,128)S(1)}, u32[]{:S(2)}, u32[]{:S(2)}) %collective-permute-start.6) | collective-permute-done | bytes 524320 | tf_op jit(solution)/shard_map/ppermute | solution.py:72
  33.9 5.0 %collective-permute-start = (f32[8,128,128]{2,1,0:T(8,128)S(1)}, f32[8,128,128]{2,1,0:T(8,128)S(1)}, u32[]{:S(2)}, u32[]{:S(2)}) collective-permute-start(f32[8,128,128]{2,1,0:T(8,128)S(1)} %get-tuple-element.43), channel_id=1, source_target_pairs={{0,4},{1,5},{2,6},{3,7},{16,20},{17,21},{18,22},{19,23}} | collective-permute-start | bytes 1572872 | tf_op jit(solution)/shard_map/ppermute | solution.py:72
  39.8 9.4 %collective-permute-done = f32[8,128,128]{2,1,0:T(8,128)S(1)} collective-permute-done((f32[8,128,128]{2,1,0:T(8,128)S(1)}, f32[8,128,128]{2,1,0:T(8,128)S(1)}, u32[]{:S(2)}, u32[]{:S(2)}) %collective-permute-start) | collective-permute-done | bytes 524320 | tf_op jit(solution)/shard_map/ppermute | solution.py:72
  54.7 10.2 %collective-permute-done.11 = f32[8,128,128]{2,1,0:T(8,128)S(1)} collective-permute-done((f32[8,128,128]{2,1,0:T(8,128)S(1)}, f32[8,128,128]{2,1,0:T(8,128)S(1)}, u32[]{:S(2)}, u32[]{:S(2)}) %collective-permute-start.11) | collective-permute-done | bytes 524320 | tf_op jit(solution)/shard_map/ppermute | solution.py:72
  66.2 20.8 %shard_map.76 = (bf16[16,512,128]{2,1,0:T(8,128)(2,1)}, bf16[4,8,128,128]{3,2,1,0:T(8,128)(2,1)}, bf16[4,8,128,128]{3,2,1,0:T(8,128)(2,1)}, bf16[4,8,128,128]{3,2,1,0:T(8,128)(2,1)}) custom-call(bf16[16,512,128]{2,1,0:T(8,128)(2,1)} %fusion.q_ref, bf16[16,512,128]{2,1,0:T(8,128)(2,1)} %bitcast.26, bf16[16,512,128]{2,1,0:T(8,128)(2,1)} %get-tuple-element.45.v_ref, ...), custom_call_target="tpu_custom_call" | custom-call | tf_op jit(solution)/shard_map/pallas_call | solution.py:129
  87.0 3.5 %all-to-all-start = ((bf16[4,8,128,128]{3,2,1,0:T(8,128)(2,1)}), bf16[4,8,128,128]{3,2,1,0:T(8,128)(2,1)S(1)}, u32[]{:S(2)}, u32[]{:S(2)}) async-start(bf16[4,8,128,128]{3,2,1,0:T(8,128)(2,1)} %get-tuple-element.18), calls=%async_computation | async-start | bytes 2097152 | tf_op jit(solution)/shard_map/all_to_all | solution.py:142
  93.5 11.4 %all-to-all-done = bf16[4,8,128,128]{3,2,1,0:T(8,128)(2,1)S(1)} async-done(((bf16[4,8,128,128]{3,2,1,0:T(8,128)(2,1)}), bf16[4,8,128,128]{3,2,1,0:T(8,128)(2,1)S(1)}, u32[]{:S(2)}, u32[]{:S(2)}) %all-to-all-start) | async-done | bytes 1048608 | tf_op jit(solution)/shard_map/all_to_all | solution.py:142
  104.9 4.3 %all-to-all-start.2 = ((bf16[4,8,128,128]{3,2,1,0:T(8,128)(2,1)}), bf16[4,8,128,128]{3,2,1,0:T(8,128)(2,1)}, u32[]{:S(2)}, u32[]{:S(2)}) async-start(bf16[4,8,128,128]{3,2,1,0:T(8,128)(2,1)} %get-tuple-element.20), calls=%async_computation.2 | async-start | bytes 2097152 | tf_op jit(solution)/shard_map/all_to_all | solution.py:142
  115.8 8.0 %all-to-all-done.2 = bf16[4,8,128,128]{3,2,1,0:T(8,128)(2,1)} async-done(((bf16[4,8,128,128]{3,2,1,0:T(8,128)(2,1)}), bf16[4,8,128,128]{3,2,1,0:T(8,128)(2,1)}, u32[]{:S(2)}, u32[]{:S(2)}) %all-to-all-start.2) | async-done | bytes 1048608 | tf_op jit(solution)/shard_map/all_to_all | solution.py:142
  123.7 3.5 %all-to-all-start.4 = ((bf16[4,8,128,128]{3,2,1,0:T(8,128)(2,1)}), bf16[4,8,128,128]{3,2,1,0:T(8,128)(2,1)S(1)}, u32[]{:S(2)}, u32[]{:S(2)}) async-start(bf16[4,8,128,128]{3,2,1,0:T(8,128)(2,1)} %get-tuple-element.22), calls=%async_computation.4 | async-start | bytes 2097152 | tf_op jit(solution)/shard_map/all_to_all | solution.py:142
  127.3 2.3 %add_add_fusion.3.before_ref = f32[8,128,128]{2,1,0:T(8,128)} fusion(f32[8,128,128]{2,1,0:T(8,128)} %collective-permute-done.2, f32[8,128,128]{2,1,0:T(8,128)} %copy-done.10, f32[8,128,128]{2,1,0:T(8,128)} %collective-permute-done.1), kind=kLoop, calls=%fused_computation.11 | loop fusion | flops 262144 | bytes 2097152 | tf_op jit(solution)/shard_map/add | solution.py:73
  133.1 20.8 %shard_map.77 = (bf16[16,512,128]{2,1,0:T(8,128)(2,1)}, bf16[4,8,128,128]{3,2,1,0:T(8,128)(2,1)}, bf16[4,8,128,128]{3,2,1,0:T(8,128)(2,1)}, bf16[4,8,128,128]{3,2,1,0:T(8,128)(2,1)}) custom-call(bf16[16,512,128]{2,1,0:T(8,128)(2,1)} %fusion.q_ref, bf16[16,512,128]{2,1,0:T(8,128)(2,1)} %bitcast.27, ...), custom_call_target="tpu_custom_call", output_to_operand_aliasing={{0}: (7, {})} | custom-call | tf_op jit(solution)/shard_map/pallas_call | solution.py:129
  153.9 18.9 %all_to_all.30 = bf16[4,8,128,128]{3,2,1,0:T(8,128)(2,1)} all-to-all(bf16[4,8,128,128]{3,2,1,0:T(8,128)(2,1)} %get-tuple-element.19), channel_id=1, replica_groups=mesh['grp'=2,'seq'=4,'head'=2,'sub'=2] {'head','sub'}, dimensions={0} | all-to-all | bytes 2097152 | tf_op jit(solution)/shard_map/all_to_all | solution.py:142
  172.8 17.7 %all_to_all.31 = bf16[4,8,128,128]{3,2,1,0:T(8,128)(2,1)} all-to-all(bf16[4,8,128,128]{3,2,1,0:T(8,128)(2,1)S(1)} %copy-done.13), channel_id=1, replica_groups=mesh['grp'=2,'seq'=4,'head'=2,'sub'=2] {'head','sub'}, dimensions={0} | all-to-all | bytes 2097152 | tf_op jit(solution)/shard_map/all_to_all | solution.py:142
  190.6 4.4 %all-to-all-start.5 = ((bf16[4,8,128,128]{3,2,1,0:T(8,128)(2,1)}), bf16[4,8,128,128]{3,2,1,0:T(8,128)(2,1)}, u32[]{:S(2)}, u32[]{:S(2)}) async-start(bf16[4,8,128,128]{3,2,1,0:T(8,128)(2,1)} %get-tuple-element.23), calls=%async_computation.5 | async-start | bytes 2097152 | tf_op jit(solution)/shard_map/all_to_all | solution.py:142
  195.0 2.7 %copy.33 = bf16[512,16,128]{2,1,0:T(8,128)(2,1)} copy(bf16[512,16,128]{2,0,1:T(8,128)(2,1)S(1)} %bitcast.31) | data formatting | bytes 4194304
  198.2 2.7 %copy.34 = bf16[128,64,128]{2,1,0:T(8,128)(2,1)} copy(bf16[128,64,128]{2,0,1:T(8,128)(2,1)S(1)} %bitcast.28) | data formatting | bytes 4194304
  202.5 2.7 %copy.35 = bf16[128,64,128]{2,1,0:T(8,128)(2,1)} copy(bf16[128,64,128]{2,0,1:T(8,128)(2,1)S(1)} %bitcast.29) | data formatting | bytes 4194304
  205.2 4.2 %all-to-all-done.5 = bf16[4,8,128,128]{3,2,1,0:T(8,128)(2,1)} async-done(((bf16[4,8,128,128]{3,2,1,0:T(8,128)(2,1)}), bf16[4,8,128,128]{3,2,1,0:T(8,128)(2,1)}, u32[]{:S(2)}, u32[]{:S(2)}) %all-to-all-start.5) | async-done | bytes 1048608 | tf_op jit(solution)/shard_map/all_to_all | solution.py:142
  211.0 2.7 %copy.36 = bf16[128,64,128]{2,1,0:T(8,128)(2,1)} copy(bf16[128,64,128]{2,0,1:T(8,128)(2,1)S(1)} %bitcast.30) | data formatting | bytes 4194304
  (68 shorter events, 31.0 us)
Async XLA Ops:
  0.6 3.6 %copy-start.7 = (bf16[512,16,128]{2,1,0:T(8,128)(2,1)S(1)}, bf16[512,16,128]{2,1,0:T(8,128)(2,1)}, u32[]{:S(2)}) copy-start(bf16[512,16,128]{2,1,0:T(8,128)(2,1)} %param.4) | copy-start | bytes 6291460
  15.7 17.4 %copy-start.1 = (f32[16,128,128]{2,1,0:T(8,128)S(1)}, f32[16,128,128]{2,1,0:T(8,128)}, u32[]{:S(2)}) copy-start(f32[16,128,128]{2,1,0:T(8,128)} %get-tuple-element.14) | copy-start | bytes 3145732
  16.8 22.1 %copy-start = (f32[16,128,128]{2,1,0:T(8,128)S(1)}, f32[16,128,128]{2,1,0:T(8,128)}, u32[]{:S(2)}) copy-start(f32[16,128,128]{2,1,0:T(8,128)} %get-tuple-element.15) | copy-start | bytes 3145732
  16.9 16.2 %collective-permute-start.6 = (f32[8,128,128]{2,1,0:T(8,128)S(1)}, f32[8,128,128]{2,1,0:T(8,128)S(1)}, u32[]{:S(2)}, u32[]{:S(2)}) collective-permute-start(f32[8,128,128]{2,1,0:T(8,128)S(1)} %slice.16), channel_id=1, source_target_pairs={{0,4},{1,5},{2,6},{3,7},{16,20},{17,21},{18,22},{19,23}} | collective-permute-start | bytes 1572872 | tf_op jit(solution)/shard_map/ppermute | solution.py:72
  23.0 15.9 %collective-permute-start.9 = (f32[8,128,128]{2,1,0:T(8,128)S(1)}, f32[8,128,128]{2,1,0:T(8,128)S(1)}, u32[]{:S(2)}, u32[]{:S(2)}) collective-permute-start(f32[8,128,128]{2,1,0:T(8,128)S(1)} %slice.17), channel_id=1, source_target_pairs={{12,8},{13,9},{14,10},{15,11},{28,24},{29,25},{30,26},{31,27}} | collective-permute-start | bytes 1572872 | tf_op jit(solution)/shard_map/ppermute | solution.py:72
  33.2 6.6 %collective-permute-start.7 = (f32[8,128,128]{2,1,0:T(8,128)S(1)}, f32[8,128,128]{2,1,0:T(8,128)S(1)}, u32[]{:S(2)}, u32[]{:S(2)}) collective-permute-start(f32[8,128,128]{2,1,0:T(8,128)S(1)} %get-tuple-element.42), channel_id=1, source_target_pairs={{4,8},{5,9},{6,10},{7,11},{20,24},{21,25},{22,26},{23,27}} | collective-permute-start | bytes 1572872 | tf_op jit(solution)/shard_map/ppermute | solution.py:72
  33.9 15.3 %collective-permute-start = (f32[8,128,128]{2,1,0:T(8,128)S(1)}, f32[8,128,128]{2,1,0:T(8,128)S(1)}, u32[]{:S(2)}, u32[]{:S(2)}) collective-permute-start(f32[8,128,128]{2,1,0:T(8,128)S(1)} %get-tuple-element.43), channel_id=1, source_target_pairs={{0,4},{1,5},{2,6},{3,7},{16,20},{17,21},{18,22},{19,23}} | collective-permute-start | bytes 1572872 | tf_op jit(solution)/shard_map/ppermute | solution.py:72
  39.1 11.8 %collective-permute-start.10 = (f32[8,128,128]{2,1,0:T(8,128)S(1)}, f32[8,128,128]{2,1,0:T(8,128)S(1)}, u32[]{:S(2)}, u32[]{:S(2)}) collective-permute-start(f32[8,128,128]{2,1,0:T(8,128)S(1)} %slice_add_fusion.5), channel_id=1, source_target_pairs={{8,4},{9,5},{10,6},{11,7},{24,20},{25,21},{26,22},{27,23}} | collective-permute-start | bytes 1572872 | tf_op jit(solution)/shard_map/ppermute | solution.py:72
  50.2 3.6 %collective-permute-start.8 = (f32[8,128,128]{2,1,0:T(8,128)S(1)}, f32[8,128,128]{2,1,0:T(8,128)S(1)}, u32[]{:S(2)}, u32[]{:S(2)}) collective-permute-start(f32[8,128,128]{2,1,0:T(8,128)S(1)} %get-tuple-element.40), channel_id=1, source_target_pairs={{8,12},{9,13},{10,14},{11,15},{24,28},{25,29},{26,30},{27,31}} | collective-permute-start | bytes 1572872 | tf_op jit(solution)/shard_map/ppermute | solution.py:72
  51.0 13.9 %collective-permute-start.11 = (f32[8,128,128]{2,1,0:T(8,128)S(1)}, f32[8,128,128]{2,1,0:T(8,128)S(1)}, u32[]{:S(2)}, u32[]{:S(2)}) collective-permute-start(f32[8,128,128]{2,1,0:T(8,128)S(1)} %get-tuple-element.38), channel_id=1, source_target_pairs={{4,0},{5,1},{6,2},{7,3},{20,16},{21,17},{22,18},{23,19}} | collective-permute-start | bytes 1572872 | tf_op jit(solution)/shard_map/ppermute | solution.py:72
  52.3 12.6 %collective-permute-start.3 = (f32[8,128,128]{2,1,0:T(8,128)S(1)}, f32[8,128,128]{2,1,0:T(8,128)S(1)}, u32[]{:S(2)}, u32[]{:S(2)}) collective-permute-start(f32[8,128,128]{2,1,0:T(8,128)S(1)} %get-tuple-element.39), channel_id=1, source_target_pairs={{12,8},{13,9},{14,10},{15,11},{28,24},{29,25},{30,26},{31,27}} | collective-permute-start | bytes 1572872 | tf_op jit(solution)/shard_map/ppermute | solution.py:72
  87.0 18.0 %all-to-all-start = ((bf16[4,8,128,128]{3,2,1,0:T(8,128)(2,1)}), bf16[4,8,128,128]{3,2,1,0:T(8,128)(2,1)S(1)}, u32[]{:S(2)}, u32[]{:S(2)}) async-start(bf16[4,8,128,128]{3,2,1,0:T(8,128)(2,1)} %get-tuple-element.18), calls=%async_computation | async-start | bytes 2097152 | tf_op jit(solution)/shard_map/all_to_all | solution.py:142
  90.5 18.7 %collective-permute-start.1 = (f32[8,128,128]{2,1,0:T(8,128)}, f32[8,128,128]{2,1,0:T(8,128)}, u32[]{:S(2)}, u32[]{:S(2)}) collective-permute-start(f32[8,128,128]{2,1,0:T(8,128)} %get-tuple-element.41), channel_id=1, source_target_pairs={{4,8},{5,9},{6,10},{7,11},{20,24},{21,25},{22,26},{23,27}} | collective-permute-start | bytes 1572872 | tf_op jit(solution)/shard_map/ppermute | solution.py:72
  92.0 20.6 %collective-permute-start.4 = (f32[8,128,128]{2,1,0:T(8,128)}, f32[8,128,128]{2,1,0:T(8,128)}, u32[]{:S(2)}, u32[]{:S(2)}) collective-permute-start(f32[8,128,128]{2,1,0:T(8,128)} %get-tuple-element.37), channel_id=1, source_target_pairs={{8,4},{9,5},{10,6},{11,7},{24,20},{25,21},{26,22},{27,23}} | collective-permute-start | bytes 1572872 | tf_op jit(solution)/shard_map/ppermute | solution.py:72
  104.9 18.8 %all-to-all-start.2 = ((bf16[4,8,128,128]{3,2,1,0:T(8,128)(2,1)}), bf16[4,8,128,128]{3,2,1,0:T(8,128)(2,1)}, u32[]{:S(2)}, u32[]{:S(2)}) async-start(bf16[4,8,128,128]{3,2,1,0:T(8,128)(2,1)} %get-tuple-element.20), calls=%async_computation.2 | async-start | bytes 2097152 | tf_op jit(solution)/shard_map/all_to_all | solution.py:142
  111.1 16.1 %collective-permute-start.2 = (f32[8,128,128]{2,1,0:T(8,128)}, f32[8,128,128]{2,1,0:T(8,128)}, u32[]{:S(2)}, u32[]{:S(2)}) collective-permute-start(f32[8,128,128]{2,1,0:T(8,128)} %slice_add_fusion.2), channel_id=1, source_target_pairs={{8,12},{9,13},{10,14},{11,15},{24,28},{25,29},{26,30},{27,31}} | collective-permute-start | bytes 1572872 | tf_op jit(solution)/shard_map/ppermute | solution.py:72
  114.5 16.5 %collective-permute-start.5 = (f32[8,128,128]{2,1,0:T(8,128)}, f32[8,128,128]{2,1,0:T(8,128)}, u32[]{:S(2)}, u32[]{:S(2)}) collective-permute-start(f32[8,128,128]{2,1,0:T(8,128)} %slice_add_fusion.6), channel_id=1, source_target_pairs={{4,0},{5,1},{6,2},{7,3},{20,16},{21,17},{22,18},{23,19}} | collective-permute-start | bytes 1572872 | tf_op jit(solution)/shard_map/ppermute | solution.py:72
  123.7 30.2 %all-to-all-start.4 = ((bf16[4,8,128,128]{3,2,1,0:T(8,128)(2,1)}), bf16[4,8,128,128]{3,2,1,0:T(8,128)(2,1)S(1)}, u32[]{:S(2)}, u32[]{:S(2)}) async-start(bf16[4,8,128,128]{3,2,1,0:T(8,128)(2,1)} %get-tuple-element.22), calls=%async_computation.4 | async-start | bytes 2097152 | tf_op jit(solution)/shard_map/all_to_all | solution.py:142
  127.3 3.7 %copy-start.12 = (f32[8,128,128]{2,1,0:T(8,128)S(1)}, f32[8,128,128]{2,1,0:T(8,128)}, u32[]{:S(2)}) copy-start(f32[8,128,128]{2,1,0:T(8,128)} %copy-done.11) | copy-start | bytes 1572868
  153.9 18.9 %copy-start.3 = (bf16[4,8,128,128]{3,2,1,0:T(8,128)(2,1)}, bf16[4,8,128,128]{3,2,1,0:T(8,128)(2,1)S(1)}, u32[]{:S(2)}) copy-start(bf16[4,8,128,128]{3,2,1,0:T(8,128)(2,1)S(1)} %all-to-all-done.4) | copy-start | bytes 3145732
  153.9 18.9 %copy-start.13 = (bf16[4,8,128,128]{3,2,1,0:T(8,128)(2,1)S(1)}, bf16[4,8,128,128]{3,2,1,0:T(8,128)(2,1)}, u32[]{:S(2)}) copy-start(bf16[4,8,128,128]{3,2,1,0:T(8,128)(2,1)} %get-tuple-element.21) | copy-start | bytes 3145732
  172.8 22.2 %copy-start.2 = (bf16[16,512,128]{2,1,0:T(8,128)(2,1)S(1)}, bf16[16,512,128]{2,1,0:T(8,128)(2,1)}, u32[]{:S(2)}) copy-start(bf16[16,512,128]{2,1,0:T(8,128)(2,1)} %get-tuple-element.17) | copy-start | bytes 6291460
  190.6 18.8 %all-to-all-start.5 = ((bf16[4,8,128,128]{3,2,1,0:T(8,128)(2,1)}), bf16[4,8,128,128]{3,2,1,0:T(8,128)(2,1)}, u32[]{:S(2)}, u32[]{:S(2)}) async-start(bf16[4,8,128,128]{3,2,1,0:T(8,128)(2,1)} %get-tuple-element.23), calls=%async_computation.5 | async-start | bytes 2097152 | tf_op jit(solution)/shard_map/all_to_all | solution.py:142
  202.5 6.9 %copy-start.4 = (bf16[4,8,128,128]{3,2,1,0:T(8,128)(2,1)S(1)}, bf16[4,8,128,128]{3,2,1,0:T(8,128)(2,1)}, u32[]{:S(2)}) copy-start(bf16[4,8,128,128]{3,2,1,0:T(8,128)(2,1)} %copy-done.3) | copy-start | bytes 3145732
  (6 other events, 13.4 us)

commit v8 on v7

--- a/solution.py
+++ b/solution.py
@@ -30,7 +30,26 @@
         adj_ref[h] = dot_tn(d_ref[h], q_ref[h])
 
 
-def main_kernel(heads, aliased, q_ref, k_ref, v_ref, d_ref, f_ref, before_ref, rest_ref, *refs):
+def intra_kernel(heads, q_ref, k_ref, v_ref, d_ref, a_ref, qg_ref, kg_ref, vg_ref):
+    span = q_ref.shape[1]
+    row = lax.broadcasted_iota(jnp.int32, (span, span), 0)
+    col = lax.broadcasted_iota(jnp.int32, (span, span), 1)
+    causal = row >= col
+    for h in range(heads):
+        qsc = q_ref[h]
+        k = k_ref[h]
+        v = v_ref[h]
+        d = d_ref[h]
+        scores = jnp.where(causal, dot_nt(qsc, k), 0.0).astype(BF16)
+        adj_scores = jnp.where(causal, dot_nt(d, v), 0.0).astype(BF16)
+        a_ref[h] = dot_nn(scores, v)
+        qg_ref[h] = dot_nn(adj_scores, k)
+        kg_ref[h] = dot_tn(adj_scores, qsc)
+        vg_ref[h] = dot_tn(scores, d)
+
+
+def main_kernel(heads, aliased, q_ref, k_ref, v_ref, d_ref, f_ref, before_ref, rest_ref,
+                ai_ref, qgi_ref, kgi_ref, vgi_ref, *refs):
     if aliased:
         refs = refs[1:]
     a_ref, qg_ref, kg_ref, vg_ref, state, suffix = refs
@@ -41,10 +60,6 @@
         suffix[...] = rest_ref[...]
 
     factor = f_ref[...]
-    span = factor.shape[0]
-    row = lax.broadcasted_iota(jnp.int32, (span, span), 0)
-    col = lax.broadcasted_iota(jnp.int32, (span, span), 1)
-    causal = row >= col
     for h in range(heads):
         qsc = q_ref[h]
         k = k_ref[h]
@@ -56,12 +71,10 @@
         rest = suffix[h] - dot_tn(d, qsc)
         suffix[h] = rest
         suffix_low = rest.astype(BF16)
-        scores = jnp.where(causal, dot_nt(qsc, k), 0.0).astype(BF16)
-        adj_scores = jnp.where(causal, dot_nt(d, v), 0.0).astype(BF16)
-        a_ref[h] = (dot_nn(qsc, state_low) + dot_nn(scores, v)).astype(a_ref.dtype)
-        qg_ref[h] = ((dot_nt(d, state_low) + dot_nn(adj_scores, k)) * factor).astype(qg_ref.dtype)
-        kg_ref[h] = (dot_nn(v, suffix_low) + dot_tn(adj_scores, qsc)).astype(kg_ref.dtype)
-        vg_ref[h] = (dot_nt(k, suffix_low) + dot_tn(scores, d)).astype(vg_ref.dtype)
+        a_ref[h] = (dot_nn(qsc, state_low) + ai_ref[h]).astype(a_ref.dtype)
+        qg_ref[h] = ((dot_nt(d, state_low) + qgi_ref[h]) * factor).astype(qg_ref.dtype)
+        kg_ref[h] = (dot_nn(v, suffix_low) + kgi_ref[h]).astype(kg_ref.dtype)
+        vg_ref[h] = (dot_nt(k, suffix_low) + vgi_ref[h]).astype(vg_ref.dtype)
 
 
 def exclusive_scan(total, axis, count, reverse):
@@ -98,6 +111,21 @@
         out_shape=[state_shape, state_shape],
     )(qh, kh, vh, dh)
 
+    all_tile = pl.BlockSpec((heads, span, head_dim), lambda c: (0, c, 0))
+    part_shape = jax.ShapeDtypeStruct((heads, tok_dev, head_dim), F32)
+    intra = pl.pallas_call(
+        functools.partial(intra_kernel, heads),
+        grid=(blocks,),
+        in_specs=[all_tile] * 4,
+        out_specs=[all_tile] * 4,
+        out_shape=[part_shape] * 4,
+        cost_estimate=pl.CostEstimate(
+            flops=12 * heads * tok_dev * span * head_dim,
+            transcendentals=0,
+            bytes_accessed=24 * heads * tok_dev * head_dim,
+        ),
+    )(qh, kh, vh, dh)
+
     fac = pl.BlockSpec((span, 1), lambda c: (c, 0))
     peers = lax.psum(1, ("head", "sub"))
     tok_out = tok_dev // peers
@@ -119,13 +147,13 @@
         else:
             otile = pl.BlockSpec((width, span, head_dim), lambda c: (0, c, 0))
             grad_shape = jax.ShapeDtypeStruct((width, tok_dev, head_dim), BF16)
-        args = [qh, kh, vh, dh, factor, before, rest]
-        specs = [gtile] * 4 + [fac, gwhole, gwhole]
+        args = [qh, kh, vh, dh, factor, before, rest] + list(intra)
+        specs = [gtile] * 4 + [fac, gwhole, gwhole] + [gtile] * 4
         aliases = {}
         if attended is not None:
             args.append(attended)
             specs.append(pl.BlockSpec(memory_space=pl.ANY))
-            aliases = {7: 0}
+            aliases = {11: 0}
         outs = pl.pallas_call(
             functools.partial(main_kernel, width, attended is not None),
             grid=(blocks,),

time: 215 us -> 228 us (1.060)
  Pallas kernels: 46.8 us -> 61.5 us
  waiting for transfers between devices: 54 us -> 44.9 us
  other arithmetic: 17.5 us -> 22.1 us
    pallas_call x0 -> x1, Pallas kernels: none -> 29.1 us  [per_device(): pl.pallas_call(functools.partial(intra_kernel, heads), grid=(blocks,), in...]
    pallas_call x2, Pallas kernels: 41.6 us -> 27.3 us  [per_device(): pl.pallas_call(functools.partial(main_kernel, width, attended is not None...]
    ppermute x12, waiting for transfers between devices: 30.4 us -> 21.3 us  [exclusive_scan(): got = lax.ppermute(carried + total, axis, perm=[pair])]
    unnamed x33 -> x41, local copies, waits for them, and re-layouts: 15.3 us -> 16.1 us
  transfers between devices with their start and end apart: 16 -> 16, of which waited for: 7 -> 6; matrix products, arithmetic and copies ran while one was open for 10% -> 11% of each run, Pallas kernels for 10% -> 19%
where the time goes in v8:
time: 228 us; the launch traced here: 226 us
  Pallas kernels  61.5 us (27%)
  waiting for transfers between devices  44.9 us (20%)
  starting transfers between devices  37.9 us (17%)
  blocking collectives  36.7 us (16%)
  local copies, waits for them, and re-layouts  22.3 us (10%)
  other arithmetic  22.1 us (10%)
    all_to_all x2, blocking collectives, per_device(): lax.all_to_all(x, ('head', 'sub'), split_axis=axis, concat_axis=0, tiled=...  36.7 us
    pallas_call x1, Pallas kernels, per_device(): pl.pallas_call(functools.partial(intra_kernel, heads), grid=(blocks,), in...  29.1 us
    pallas_call x2, Pallas kernels, per_device(): pl.pallas_call(functools.partial(main_kernel, width, attended is not None...  27.3 us
    all_to_all x4, waiting for transfers between devices, per_device(): lax.all_to_all(x, ('head', 'sub'), split_axis=axis, concat_axis=0, tiled=...  23.6 us
    ppermute x12, starting transfers between devices, exclusive_scan(): got = lax.ppermute(carried + total, axis, perm=[pair])  22.2 us
    ppermute x12, waiting for transfers between devices, exclusive_scan(): got = lax.ppermute(carried + total, axis, perm=[pair])  21.3 us
    unnamed x41, local copies, waits for them, and re-layouts  16.1 us
    all_to_all x4, starting transfers between devices, per_device(): lax.all_to_all(x, ('head', 'sub'), split_axis=axis, concat_axis=0, tiled=...  15.7 us
  transfers between devices with their start and end apart: 16, of which 6 were waited for; matrix products, arithmetic and copies ran while one was open for 11% of the time, Pallas kernels for 19%

profile of v8, /device:TPU:0, one launch (start us, length us, event | category | flops | bytes accessed | tf_op | source)
XLA Modules:
  0.0 226.4 jit_solution(1980934553067746354)
XLA Ops:
  0.7 3.6 %copy.41 = bf16[512,16,128]{2,0,1:T(8,128)(2,1)} copy(bf16[512,16,128]{2,1,0:T(8,128)(2,1)} %param.5) | data formatting | bytes 4194304 | tf_op args[1]
  7.2 3.3 %copy_bitcast_fusion = (bf16[16,512,128]{2,1,0:T(8,128)(2,1)}, bf16[16,512,128]{2,1,0:T(8,128)(2,1)}) fusion(bf16[512,16,128]{2,1,0:T(8,128)(2,1)S(1)} %copy-done.8, bf16[512,16,128]{2,1,0:T(8,128)(2,1)S(1)} %copy-done.9), kind=kLoop, calls=%fused_computation.5 | loop fusion | bytes 8388608 | tf_op jit(solution)/shard_map/transpose | solution.py:99
  10.5 5.1 %shard_map.75 = (f32[16,128,128]{2,1,0:T(8,128)}, f32[16,128,128]{2,1,0:T(8,128)}) custom-call(bf16[16,512,128]{2,1,0:T(8,128)(2,1)} %fusion.q_ref, bf16[16,512,128]{2,1,0:T(8,128)(2,1)} %bitcast.25, bf16[16,512,128]{2,1,0:T(8,128)(2,1)} %get-tuple-element.53.v_ref, bf16[16,512,128]{2,1,0:T(8,128)(2,1)} %get-tuple-element.52.d_ref), custom_call_target="tpu_custom_call" | custom-call | tf_op jit(solution)/shard_map/pallas_call | solution.py:106
  16.8 5.1 %collective-permute-start.6 = (f32[8,128,128]{2,1,0:T(8,128)S(1)}, f32[8,128,128]{2,1,0:T(8,128)S(1)}, u32[]{:S(2)}, u32[]{:S(2)}) collective-permute-start(f32[8,128,128]{2,1,0:T(8,128)S(1)} %slice.16), channel_id=1, source_target_pairs={{0,4},{1,5},{2,6},{3,7},{16,20},{17,21},{18,22},{19,23}} | collective-permute-start | bytes 1572872 | tf_op jit(solution)/shard_map/ppermute | solution.py:85
  23.7 9.3 %collective-permute-done.6 = f32[8,128,128]{2,1,0:T(8,128)S(1)} collective-permute-done((f32[8,128,128]{2,1,0:T(8,128)S(1)}, f32[8,128,128]{2,1,0:T(8,128)S(1)}, u32[]{:S(2)}, u32[]{:S(2)}) %collective-permute-start.6) | collective-permute-done | bytes 524320 | tf_op jit(solution)/shard_map/ppermute | solution.py:85
  34.7 5.0 %collective-permute-start = (f32[8,128,128]{2,1,0:T(8,128)S(1)}, f32[8,128,128]{2,1,0:T(8,128)S(1)}, u32[]{:S(2)}, u32[]{:S(2)}) collective-permute-start(f32[8,128,128]{2,1,0:T(8,128)S(1)} %get-tuple-element.51), channel_id=1, source_target_pairs={{0,4},{1,5},{2,6},{3,7},{16,20},{17,21},{18,22},{19,23}} | collective-permute-start | bytes 1572872 | tf_op jit(solution)/shard_map/ppermute | solution.py:85
  40.5 9.5 %collective-permute-done = f32[8,128,128]{2,1,0:T(8,128)S(1)} collective-permute-done((f32[8,128,128]{2,1,0:T(8,128)S(1)}, f32[8,128,128]{2,1,0:T(8,128)S(1)}, u32[]{:S(2)}, u32[]{:S(2)}) %collective-permute-start) | collective-permute-done | bytes 524320 | tf_op jit(solution)/shard_map/ppermute | solution.py:85
  57.6 29.1 %shard_map.76 = (f32[16,512,128]{2,1,0:T(8,128)}, f32[16,512,128]{2,1,0:T(8,128)}, f32[16,512,128]{2,1,0:T(8,128)}, f32[16,512,128]{2,1,0:T(8,128)}) custom-call(bf16[16,512,128]{2,1,0:T(8,128)(2,1)} %fusion.q_ref, bf16[16,512,128]{2,1,0:T(8,128)(2,1)} %bitcast.26, bf16[16,512,128]{2,1,0:T(8,128)(2,1)} %get-tuple-element.53.v_ref, ...), custom_call_target="tpu_custom_call" | custom-call | flops 805306368 | bytes 25165824 | tf_op jit(solution)/shard_map/pallas_call | solution.py:116
  89.5 2.5 %add_add_fusion = (f32[8,128,128]{2,1,0:T(8,128)}, f32[8,128,128]{2,1,0:T(8,128)}) fusion(f32[8,128,128]{2,1,0:T(8,128)} %collective-permute-done.11, f32[8,128,128]{2,1,0:T(8,128)S(1)} %copy-done.14, f32[8,128,128]{2,1,0:T(8,128)S(1)} %copy-done.16, f32[16,128,128]{2,1,0:T(8,128)S(1)} %copy-done, f32[8,128,128]{2,1,0:T(8,128)S(1)} %collective-permute-done.3), kind=kLoop, calls=%fused_computation.8 | loop fusion | flops 524288 | bytes 4194304 | tf_op jit(solution)/shard_map/add | solution.py:139
  92.0 13.6 %shard_map.77 = (bf16[16,512,128]{2,1,0:T(8,128)(2,1)}, bf16[4,8,128,128]{3,2,1,0:T(8,128)(2,1)}, bf16[4,8,128,128]{3,2,1,0:T(8,128)(2,1)}, bf16[4,8,128,128]{3,2,1,0:T(8,128)(2,1)}) custom-call(bf16[16,512,128]{2,1,0:T(8,128)(2,1)} %fusion.q_ref, bf16[16,512,128]{2,1,0:T(8,128)(2,1)} %bitcast.27, bf16[16,512,128]{2,1,0:T(8,128)(2,1)} %get-tuple-element.53.v_ref, ...), custom_call_target="tpu_custom_call" | custom-call | tf_op jit(solution)/shard_map/pallas_call | solution.py:157
  105.7 3.5 %all-to-all-start = ((bf16[4,8,128,128]{3,2,1,0:T(8,128)(2,1)}), bf16[4,8,128,128]{3,2,1,0:T(8,128)(2,1)S(1)}, u32[]{:S(2)}, u32[]{:S(2)}) async-start(bf16[4,8,128,128]{3,2,1,0:T(8,128)(2,1)} %get-tuple-element.26), calls=%async_computation | async-start | bytes 2097152 | tf_op jit(solution)/shard_map/all_to_all | solution.py:170
  112.1 11.5 %all-to-all-done = bf16[4,8,128,128]{3,2,1,0:T(8,128)(2,1)S(1)} async-done(((bf16[4,8,128,128]{3,2,1,0:T(8,128)(2,1)}), bf16[4,8,128,128]{3,2,1,0:T(8,128)(2,1)S(1)}, u32[]{:S(2)}, u32[]{:S(2)}) %all-to-all-start) | async-done | bytes 1048608 | tf_op jit(solution)/shard_map/all_to_all | solution.py:170
  123.6 4.3 %all-to-all-start.2 = ((bf16[4,8,128,128]{3,2,1,0:T(8,128)(2,1)}), bf16[4,8,128,128]{3,2,1,0:T(8,128)(2,1)}, u32[]{:S(2)}, u32[]{:S(2)}) async-start(bf16[4,8,128,128]{3,2,1,0:T(8,128)(2,1)} %get-tuple-element.28), calls=%async_computation.2 | async-start | bytes 2097152 | tf_op jit(solution)/shard_map/all_to_all | solution.py:170
  134.5 7.9 %all-to-all-done.2 = bf16[4,8,128,128]{3,2,1,0:T(8,128)(2,1)} async-done(((bf16[4,8,128,128]{3,2,1,0:T(8,128)(2,1)}), bf16[4,8,128,128]{3,2,1,0:T(8,128)(2,1)}, u32[]{:S(2)}, u32[]{:S(2)}) %all-to-all-start.2) | async-done | bytes 1048608 | tf_op jit(solution)/shard_map/all_to_all | solution.py:170
  142.4 3.5 %all-to-all-start.4 = ((bf16[4,8,128,128]{3,2,1,0:T(8,128)(2,1)}), bf16[4,8,128,128]{3,2,1,0:T(8,128)(2,1)S(1)}, u32[]{:S(2)}, u32[]{:S(2)}) async-start(bf16[4,8,128,128]{3,2,1,0:T(8,128)(2,1)} %get-tuple-element.30), calls=%async_computation.4 | async-start | bytes 2097152 | tf_op jit(solution)/shard_map/all_to_all | solution.py:170
  152.8 13.7 %shard_map.78 = (bf16[16,512,128]{2,1,0:T(8,128)(2,1)}, bf16[4,8,128,128]{3,2,1,0:T(8,128)(2,1)}, bf16[4,8,128,128]{3,2,1,0:T(8,128)(2,1)}, bf16[4,8,128,128]{3,2,1,0:T(8,128)(2,1)}) custom-call(bf16[16,512,128]{2,1,0:T(8,128)(2,1)} %fusion.q_ref, bf16[16,512,128]{2,1,0:T(8,128)(2,1)} %bitcast.28, ...), custom_call_target="tpu_custom_call", output_to_operand_aliasing={{0}: (11, {})} | custom-call | tf_op jit(solution)/shard_map/pallas_call | solution.py:157
  166.6 18.9 %all_to_all.30 = bf16[4,8,128,128]{3,2,1,0:T(8,128)(2,1)} all-to-all(bf16[4,8,128,128]{3,2,1,0:T(8,128)(2,1)} %get-tuple-element.27), channel_id=1, replica_groups=mesh['grp'=2,'seq'=4,'head'=2,'sub'=2] {'head','sub'}, dimensions={0} | all-to-all | bytes 2097152 | tf_op jit(solution)/shard_map/all_to_all | solution.py:170
  185.5 17.7 %all_to_all.31 = bf16[4,8,128,128]{3,2,1,0:T(8,128)(2,1)} all-to-all(bf16[4,8,128,128]{3,2,1,0:T(8,128)(2,1)S(1)} %copy-done.17), channel_id=1, replica_groups=mesh['grp'=2,'seq'=4,'head'=2,'sub'=2] {'head','sub'}, dimensions={0} | all-to-all | bytes 2097152 | tf_op jit(solution)/shard_map/all_to_all | solution.py:170
  203.2 4.4 %all-to-all-start.5 = ((bf16[4,8,128,128]{3,2,1,0:T(8,128)(2,1)}), bf16[4,8,128,128]{3,2,1,0:T(8,128)(2,1)}, u32[]{:S(2)}, u32[]{:S(2)}) async-start(bf16[4,8,128,128]{3,2,1,0:T(8,128)(2,1)} %get-tuple-element.31), calls=%async_computation.5 | async-start | bytes 2097152 | tf_op jit(solution)/shard_map/all_to_all | solution.py:170
  207.7 2.7 %copy.33 = bf16[512,16,128]{2,1,0:T(8,128)(2,1)} copy(bf16[512,16,128]{2,0,1:T(8,128)(2,1)S(1)} %bitcast.29) | data formatting | bytes 4194304
  210.8 2.7 %copy.34 = bf16[128,64,128]{2,1,0:T(8,128)(2,1)} copy(bf16[128,64,128]{2,0,1:T(8,128)(2,1)S(1)} %bitcast.30) | data formatting | bytes 4194304
  215.2 2.7 %copy.35 = bf16[128,64,128]{2,1,0:T(8,128)(2,1)} copy(bf16[128,64,128]{2,0,1:T(8,128)(2,1)S(1)} %bitcast.31) | data formatting | bytes 4194304
  217.9 4.2 %all-to-all-done.5 = bf16[4,8,128,128]{3,2,1,0:T(8,128)(2,1)} async-done(((bf16[4,8,128,128]{3,2,1,0:T(8,128)(2,1)}), bf16[4,8,128,128]{3,2,1,0:T(8,128)(2,1)}, u32[]{:S(2)}, u32[]{:S(2)}) %all-to-all-start.5) | async-done | bytes 1048608 | tf_op jit(solution)/shard_map/all_to_all | solution.py:170
  223.7 2.7 %copy.36 = bf16[128,64,128]{2,1,0:T(8,128)(2,1)} copy(bf16[128,64,128]{2,0,1:T(8,128)(2,1)S(1)} %bitcast.32) | data formatting | bytes 4194304
  (77 shorter events, 38.9 us)
Async XLA Ops:
  15.6 17.4 %copy-start.1 = (f32[16,128,128]{2,1,0:T(8,128)S(1)}, f32[16,128,128]{2,1,0:T(8,128)}, u32[]{:S(2)}) copy-start(f32[16,128,128]{2,1,0:T(8,128)} %get-tuple-element.18) | copy-start | bytes 3145732
  16.8 22.9 %copy-start = (f32[16,128,128]{2,1,0:T(8,128)S(1)}, f32[16,128,128]{2,1,0:T(8,128)}, u32[]{:S(2)}) copy-start(f32[16,128,128]{2,1,0:T(8,128)} %get-tuple-element.19) | copy-start | bytes 3145732
  16.8 16.2 %collective-permute-start.6 = (f32[8,128,128]{2,1,0:T(8,128)S(1)}, f32[8,128,128]{2,1,0:T(8,128)S(1)}, u32[]{:S(2)}, u32[]{:S(2)}) collective-permute-start(f32[8,128,128]{2,1,0:T(8,128)S(1)} %slice.16), channel_id=1, source_target_pairs={{0,4},{1,5},{2,6},{3,7},{16,20},{17,21},{18,22},{19,23}} | collective-permute-start | bytes 1572872 | tf_op jit(solution)/shard_map/ppermute | solution.py:85
  23.0 16.7 %collective-permute-start.9 = (f32[8,128,128]{2,1,0:T(8,128)S(1)}, f32[8,128,128]{2,1,0:T(8,128)S(1)}, u32[]{:S(2)}, u32[]{:S(2)}) collective-permute-start(f32[8,128,128]{2,1,0:T(8,128)S(1)} %slice.17), channel_id=1, source_target_pairs={{12,8},{13,9},{14,10},{15,11},{28,24},{29,25},{30,26},{31,27}} | collective-permute-start | bytes 1572872 | tf_op jit(solution)/shard_map/ppermute | solution.py:85
  33.2 7.4 %collective-permute-start.7 = (f32[8,128,128]{2,1,0:T(8,128)S(1)}, f32[8,128,128]{2,1,0:T(8,128)}, u32[]{:S(2)}, u32[]{:S(2)}) collective-permute-start(f32[8,128,128]{2,1,0:T(8,128)S(1)} %get-tuple-element.50), channel_id=1, source_target_pairs={{4,8},{5,9},{6,10},{7,11},{20,24},{21,25},{22,26},{23,27}} | collective-permute-start | bytes 1572872 | tf_op jit(solution)/shard_map/ppermute | solution.py:85
  34.7 15.3 %collective-permute-start = (f32[8,128,128]{2,1,0:T(8,128)S(1)}, f32[8,128,128]{2,1,0:T(8,128)S(1)}, u32[]{:S(2)}, u32[]{:S(2)}) collective-permute-start(f32[8,128,128]{2,1,0:T(8,128)S(1)} %get-tuple-element.51), channel_id=1, source_target_pairs={{0,4},{1,5},{2,6},{3,7},{16,20},{17,21},{18,22},{19,23}} | collective-permute-start | bytes 1572872 | tf_op jit(solution)/shard_map/ppermute | solution.py:85
  39.7 13.2 %copy-start.13 = (f32[8,128,128]{2,1,0:T(8,128)}, f32[8,128,128]{2,1,0:T(8,128)S(1)}, u32[]{:S(2)}) copy-start(f32[8,128,128]{2,1,0:T(8,128)S(1)} %collective-permute-done.9) | copy-start | bytes 1572868
  39.8 14.6 %collective-permute-start.10 = (f32[8,128,128]{2,1,0:T(8,128)S(1)}, f32[8,128,128]{2,1,0:T(8,128)S(1)}, u32[]{:S(2)}, u32[]{:S(2)}) collective-permute-start(f32[8,128,128]{2,1,0:T(8,128)S(1)} %slice_add_fusion.5), channel_id=1, source_target_pairs={{8,4},{9,5},{10,6},{11,7},{24,20},{25,21},{26,22},{27,23}} | collective-permute-start | bytes 1572872 | tf_op jit(solution)/shard_map/ppermute | solution.py:85
  52.9 34.5 %collective-permute-start.8 = (f32[8,128,128]{2,1,0:T(8,128)}, f32[8,128,128]{2,1,0:T(8,128)}, u32[]{:S(2)}, u32[]{:S(2)}) collective-permute-start(f32[8,128,128]{2,1,0:T(8,128)} %get-tuple-element.48), channel_id=1, source_target_pairs={{8,12},{9,13},{10,14},{11,15},{24,28},{25,29},{26,30},{27,31}} | collective-permute-start | bytes 1572872 | tf_op jit(solution)/shard_map/ppermute | solution.py:85
  55.6 33.9 %collective-permute-start.11 = (f32[8,128,128]{2,1,0:T(8,128)}, f32[8,128,128]{2,1,0:T(8,128)}, u32[]{:S(2)}, u32[]{:S(2)}) collective-permute-start(f32[8,128,128]{2,1,0:T(8,128)} %get-tuple-element.46), channel_id=1, source_target_pairs={{4,0},{5,1},{6,2},{7,3},{20,16},{21,17},{22,18},{23,19}} | collective-permute-start | bytes 1572872 | tf_op jit(solution)/shard_map/ppermute | solution.py:85
  56.9 32.6 %collective-permute-start.3 = (f32[8,128,128]{2,1,0:T(8,128)}, f32[8,128,128]{2,1,0:T(8,128)S(1)}, u32[]{:S(2)}, u32[]{:S(2)}) collective-permute-start(f32[8,128,128]{2,1,0:T(8,128)} %get-tuple-element.47), channel_id=1, source_target_pairs={{12,8},{13,9},{14,10},{15,11},{28,24},{29,25},{30,26},{31,27}} | collective-permute-start | bytes 1572872 | tf_op jit(solution)/shard_map/ppermute | solution.py:85
  105.7 18.0 %all-to-all-start = ((bf16[4,8,128,128]{3,2,1,0:T(8,128)(2,1)}), bf16[4,8,128,128]{3,2,1,0:T(8,128)(2,1)S(1)}, u32[]{:S(2)}, u32[]{:S(2)}) async-start(bf16[4,8,128,128]{3,2,1,0:T(8,128)(2,1)} %get-tuple-element.26), calls=%async_computation | async-start | bytes 2097152 | tf_op jit(solution)/shard_map/all_to_all | solution.py:170
  109.2 18.7 %collective-permute-start.1 = (f32[8,128,128]{2,1,0:T(8,128)}, f32[8,128,128]{2,1,0:T(8,128)}, u32[]{:S(2)}, u32[]{:S(2)}) collective-permute-start(f32[8,128,128]{2,1,0:T(8,128)} %get-tuple-element.49), channel_id=1, source_target_pairs={{4,8},{5,9},{6,10},{7,11},{20,24},{21,25},{22,26},{23,27}} | collective-permute-start | bytes 1572872 | tf_op jit(solution)/shard_map/ppermute | solution.py:85
  110.7 20.6 %collective-permute-start.4 = (f32[8,128,128]{2,1,0:T(8,128)}, f32[8,128,128]{2,1,0:T(8,128)}, u32[]{:S(2)}, u32[]{:S(2)}) collective-permute-start(f32[8,128,128]{2,1,0:T(8,128)} %get-tuple-element.45), channel_id=1, source_target_pairs={{8,4},{9,5},{10,6},{11,7},{24,20},{25,21},{26,22},{27,23}} | collective-permute-start | bytes 1572872 | tf_op jit(solution)/shard_map/ppermute | solution.py:85
  123.6 18.8 %all-to-all-start.2 = ((bf16[4,8,128,128]{3,2,1,0:T(8,128)(2,1)}), bf16[4,8,128,128]{3,2,1,0:T(8,128)(2,1)}, u32[]{:S(2)}, u32[]{:S(2)}) async-start(bf16[4,8,128,128]{3,2,1,0:T(8,128)(2,1)} %get-tuple-element.28), calls=%async_computation.2 | async-start | bytes 2097152 | tf_op jit(solution)/shard_map/all_to_all | solution.py:170
  129.8 16.2 %collective-permute-start.2 = (f32[8,128,128]{2,1,0:T(8,128)}, f32[8,128,128]{2,1,0:T(8,128)}, u32[]{:S(2)}, u32[]{:S(2)}) collective-permute-start(f32[8,128,128]{2,1,0:T(8,128)} %slice_add_fusion.2), channel_id=1, source_target_pairs={{8,12},{9,13},{10,14},{11,15},{24,28},{25,29},{26,30},{27,31}} | collective-permute-start | bytes 1572872 | tf_op jit(solution)/shard_map/ppermute | solution.py:85
  133.2 17.5 %collective-permute-start.5 = (f32[8,128,128]{2,1,0:T(8,128)}, f32[8,128,128]{2,1,0:T(8,128)}, u32[]{:S(2)}, u32[]{:S(2)}) collective-permute-start(f32[8,128,128]{2,1,0:T(8,128)} %slice_add_fusion.6), channel_id=1, source_target_pairs={{4,0},{5,1},{6,2},{7,3},{20,16},{21,17},{22,18},{23,19}} | collective-permute-start | bytes 1572872 | tf_op jit(solution)/shard_map/ppermute | solution.py:85
  142.4 24.1 %all-to-all-start.4 = ((bf16[4,8,128,128]{3,2,1,0:T(8,128)(2,1)}), bf16[4,8,128,128]{3,2,1,0:T(8,128)(2,1)S(1)}, u32[]{:S(2)}, u32[]{:S(2)}) async-start(bf16[4,8,128,128]{3,2,1,0:T(8,128)(2,1)} %get-tuple-element.30), calls=%async_computation.4 | async-start | bytes 2097152 | tf_op jit(solution)/shard_map/all_to_all | solution.py:170
  145.9 4.8 %copy-start.12 = (f32[8,128,128]{2,1,0:T(8,128)S(1)}, f32[8,128,128]{2,1,0:T(8,128)}, u32[]{:S(2)}) copy-start(f32[8,128,128]{2,1,0:T(8,128)} %copy-done.11) | copy-start | bytes 1572868
  166.5 19.0 %copy-start.3 = (bf16[4,8,128,128]{3,2,1,0:T(8,128)(2,1)}, bf16[4,8,128,128]{3,2,1,0:T(8,128)(2,1)S(1)}, u32[]{:S(2)}) copy-start(bf16[4,8,128,128]{3,2,1,0:T(8,128)(2,1)S(1)} %all-to-all-done.4) | copy-start | bytes 3145732
  166.5 18.9 %copy-start.17 = (bf16[4,8,128,128]{3,2,1,0:T(8,128)(2,1)S(1)}, bf16[4,8,128,128]{3,2,1,0:T(8,128)(2,1)}, u32[]{:S(2)}) copy-start(bf16[4,8,128,128]{3,2,1,0:T(8,128)(2,1)} %get-tuple-element.29) | copy-start | bytes 3145732
  185.5 22.2 %copy-start.2 = (bf16[16,512,128]{2,1,0:T(8,128)(2,1)S(1)}, bf16[16,512,128]{2,1,0:T(8,128)(2,1)}, u32[]{:S(2)}) copy-start(bf16[16,512,128]{2,1,0:T(8,128)(2,1)} %get-tuple-element.25) | copy-start | bytes 6291460
  203.2 18.8 %all-to-all-start.5 = ((bf16[4,8,128,128]{3,2,1,0:T(8,128)(2,1)}), bf16[4,8,128,128]{3,2,1,0:T(8,128)(2,1)}, u32[]{:S(2)}, u32[]{:S(2)}) async-start(bf16[4,8,128,128]{3,2,1,0:T(8,128)(2,1)} %get-tuple-element.31), calls=%async_computation.5 | async-start | bytes 2097152 | tf_op jit(solution)/shard_map/all_to_all | solution.py:170
  215.2 6.9 %copy-start.4 = (bf16[4,8,128,128]{3,2,1,0:T(8,128)(2,1)S(1)}, bf16[4,8,128,128]{3,2,1,0:T(8,128)(2,1)}, u32[]{:S(2)}) copy-start(bf16[4,8,128,128]{3,2,1,0:T(8,128)(2,1)} %copy-done.3) | copy-start | bytes 3145732
  (10 other events, 25.5 us)

commit v9 on v8

--- a/solution.py
+++ b/solution.py
@@ -111,20 +111,24 @@
         out_shape=[state_shape, state_shape],
     )(qh, kh, vh, dh)
 
-    all_tile = pl.BlockSpec((heads, span, head_dim), lambda c: (0, c, 0))
-    part_shape = jax.ShapeDtypeStruct((heads, tok_dev, head_dim), F32)
-    intra = pl.pallas_call(
-        functools.partial(intra_kernel, heads),
-        grid=(blocks,),
-        in_specs=[all_tile] * 4,
-        out_specs=[all_tile] * 4,
-        out_shape=[part_shape] * 4,
-        cost_estimate=pl.CostEstimate(
-            flops=12 * heads * tok_dev * span * head_dim,
-            transcendentals=0,
-            bytes_accessed=24 * heads * tok_dev * head_dim,
-        ),
-    )(qh, kh, vh, dh)
+    def intra_part(g):
+        tile = pl.BlockSpec((width, span, head_dim), lambda c: (g, c, 0))
+        out = pl.BlockSpec((width, span, head_dim), lambda c: (0, c, 0))
+        part_shape = jax.ShapeDtypeStruct((width, tok_dev, head_dim), F32)
+        return pl.pallas_call(
+            functools.partial(intra_kernel, width),
+            grid=(blocks,),
+            in_specs=[tile] * 4,
+            out_specs=[out] * 4,
+            out_shape=[part_shape] * 4,
+            cost_estimate=pl.CostEstimate(
+                flops=12 * width * tok_dev * span * head_dim,
+                transcendentals=0,
+                bytes_accessed=24 * width * tok_dev * head_dim,
+            ),
+        )(qh, kh, vh, dh)
+
+    intra = [intra_part(g) for g in range(groups)]
 
     fac = pl.BlockSpec((span, 1), lambda c: (c, 0))
     peers = lax.psum(1, ("head", "sub"))
@@ -139,6 +143,7 @@
         rest = exclusive_scan(adj_total[sel], "seq", seq_count, True) + adj_total[sel]
         gtile = pl.BlockSpec((width, span, head_dim), lambda c, g=g: (g, c, 0))
         gwhole = pl.BlockSpec((width, head_dim, head_dim), lambda c: (0, 0, 0))
+        otile_f32 = pl.BlockSpec((width, span, head_dim), lambda c: (0, c, 0))
         if split_out:
             otile = pl.BlockSpec(
                 (None, width, span, head_dim), lambda c: (c // per_peer, 0, c % per_peer, 0)
@@ -147,8 +152,8 @@
         else:
             otile = pl.BlockSpec((width, span, head_dim), lambda c: (0, c, 0))
             grad_shape = jax.ShapeDtypeStruct((width, tok_dev, head_dim), BF16)
-        args = [qh, kh, vh, dh, factor, before, rest] + list(intra)
-        specs = [gtile] * 4 + [fac, gwhole, gwhole] + [gtile] * 4
+        args = [qh, kh, vh, dh, factor, before, rest] + list(intra[g])
+        specs = [gtile] * 4 + [fac, gwhole, gwhole] + [otile_f32] * 4
         aliases = {}
         if attended is not None:
             args.append(attended)

time: 228 us -> 226 us (level)
  Pallas kernels: 61.5 us -> 64.5 us
  waiting for transfers between devices: 44.9 us -> 42.4 us
    pallas_call x1 -> x2, Pallas kernels: 29.1 us -> 32.1 us  [intra_part(): pl.pallas_call(functools.partial(intra_kernel, width), grid=(blocks,), in...]
    ppermute x12, waiting for transfers between devices: 21.3 us -> 18.8 us  [exclusive_scan(): got = lax.ppermute(carried + total, axis, perm=[pair])]
    unnamed x41 -> x43, local copies, waits for them, and re-layouts: 16.1 us -> 15.3 us
  transfers between devices with their start and end apart: 16 -> 16, of which waited for: 6 -> 5; matrix products, arithmetic and copies ran while one was open for 11% -> 11% of each run, Pallas kernels for 19% -> 20%
where the time goes in v9:
time: 226 us; the launch traced here: 224 us
  Pallas kernels  64.5 us (29%)
  waiting for transfers between devices  42.4 us (19%)
  starting transfers between devices  37 us (16%)
  blocking collectives  36.7 us (16%)
  local copies, waits for them, and re-layouts  21.5 us (10%)
  other arithmetic  21.1 us (9%)
    all_to_all x2, blocking collectives, per_device(): lax.all_to_all(x, ('head', 'sub'), split_axis=axis, concat_axis=0, tiled=...  36.7 us
    pallas_call x2, Pallas kernels, intra_part(): pl.pallas_call(functools.partial(intra_kernel, width), grid=(blocks,), in...  32.1 us
    pallas_call x2, Pallas kernels, per_device(): pl.pallas_call(functools.partial(main_kernel, width, attended is not None...  27.3 us
    all_to_all x4, waiting for transfers between devices, per_device(): lax.all_to_all(x, ('head', 'sub'), split_axis=axis, concat_axis=0, tiled=...  23.6 us
    ppermute x12, starting transfers between devices, exclusive_scan(): got = lax.ppermute(carried + total, axis, perm=[pair])  21.3 us
    ppermute x12, waiting for transfers between devices, exclusive_scan(): got = lax.ppermute(carried + total, axis, perm=[pair])  18.8 us
    all_to_all x4, starting transfers between devices, per_device(): lax.all_to_all(x, ('head', 'sub'), split_axis=axis, concat_axis=0, tiled=...  15.7 us
    unnamed x43, local copies, waits for them, and re-layouts  15.3 us
  transfers between devices with their start and end apart: 16, of which 5 were waited for; matrix products, arithmetic and copies ran while one was open for 11% of the time, Pallas kernels for 20%

profile of v9, /device:TPU:0, one launch (start us, length us, event | category | flops | bytes accessed | tf_op | source)
XLA Modules:
  0.0 224.3 jit_solution(14895376509222756383)
XLA Ops:
  0.7 3.6 %copy.41 = bf16[512,16,128]{2,0,1:T(8,128)(2,1)} copy(bf16[512,16,128]{2,1,0:T(8,128)(2,1)} %param.5) | data formatting | bytes 4194304 | tf_op args[1]
  7.2 3.3 %copy_bitcast_fusion = (bf16[16,512,128]{2,1,0:T(8,128)(2,1)}, bf16[16,512,128]{2,1,0:T(8,128)(2,1)}) fusion(bf16[512,16,128]{2,1,0:T(8,128)(2,1)S(1)} %copy-done.8, bf16[512,16,128]{2,1,0:T(8,128)(2,1)S(1)} %copy-done.9), kind=kLoop, calls=%fused_computation.5 | loop fusion | bytes 8388608 | tf_op jit(solution)/shard_map/transpose | solution.py:99
  10.5 5.1 %shard_map.75 = (f32[16,128,128]{2,1,0:T(8,128)}, f32[16,128,128]{2,1,0:T(8,128)}) custom-call(bf16[16,512,128]{2,1,0:T(8,128)(2,1)} %fusion.q_ref, bf16[16,512,128]{2,1,0:T(8,128)(2,1)} %bitcast.25, bf16[16,512,128]{2,1,0:T(8,128)(2,1)} %get-tuple-element.61.v_ref, bf16[16,512,128]{2,1,0:T(8,128)(2,1)} %get-tuple-element.60.d_ref), custom_call_target="tpu_custom_call" | custom-call | tf_op jit(solution)/shard_map/pallas_call | solution.py:106
  16.8 5.1 %collective-permute-start.6 = (f32[8,128,128]{2,1,0:T(8,128)S(1)}, f32[8,128,128]{2,1,0:T(8,128)S(1)}, u32[]{:S(2)}, u32[]{:S(2)}) collective-permute-start(f32[8,128,128]{2,1,0:T(8,128)S(1)} %slice.16), channel_id=1, source_target_pairs={{0,4},{1,5},{2,6},{3,7},{16,20},{17,21},{18,22},{19,23}} | collective-permute-start | bytes 1572872 | tf_op jit(solution)/shard_map/ppermute | solution.py:85
  23.7 9.3 %collective-permute-done.6 = f32[8,128,128]{2,1,0:T(8,128)S(1)} collective-permute-done((f32[8,128,128]{2,1,0:T(8,128)S(1)}, f32[8,128,128]{2,1,0:T(8,128)S(1)}, u32[]{:S(2)}, u32[]{:S(2)}) %collective-permute-start.6) | collective-permute-done | bytes 524320 | tf_op jit(solution)/shard_map/ppermute | solution.py:85
  33.9 5.0 %collective-permute-start = (f32[8,128,128]{2,1,0:T(8,128)S(1)}, f32[8,128,128]{2,1,0:T(8,128)S(1)}, u32[]{:S(2)}, u32[]{:S(2)}) collective-permute-start(f32[8,128,128]{2,1,0:T(8,128)S(1)} %get-tuple-element.59), channel_id=1, source_target_pairs={{0,4},{1,5},{2,6},{3,7},{16,20},{17,21},{18,22},{19,23}} | collective-permute-start | bytes 1572872 | tf_op jit(solution)/shard_map/ppermute | solution.py:85
  39.7 9.4 %collective-permute-done = f32[8,128,128]{2,1,0:T(8,128)S(1)} collective-permute-done((f32[8,128,128]{2,1,0:T(8,128)S(1)}, f32[8,128,128]{2,1,0:T(8,128)S(1)}, u32[]{:S(2)}, u32[]{:S(2)}) %collective-permute-start) | collective-permute-done | bytes 524320 | tf_op jit(solution)/shard_map/ppermute | solution.py:85
  55.0 16.0 %shard_map.77 = (f32[8,512,128]{2,1,0:T(8,128)}, f32[8,512,128]{2,1,0:T(8,128)}, f32[8,512,128]{2,1,0:T(8,128)}, f32[8,512,128]{2,1,0:T(8,128)}) custom-call(bf16[16,512,128]{2,1,0:T(8,128)(2,1)} %fusion.q_ref, bf16[16,512,128]{2,1,0:T(8,128)(2,1)} %bitcast.26, bf16[16,512,128]{2,1,0:T(8,128)(2,1)} %get-tuple-element.61.v_ref, ...), custom_call_target="tpu_custom_call" | custom-call | flops 402653184 | bytes 12582912 | tf_op jit(solution)/shard_map/pallas_call | solution.py:118
  76.4 13.7 %shard_map.78 = (bf16[16,512,128]{2,1,0:T(8,128)(2,1)}, bf16[4,8,128,128]{3,2,1,0:T(8,128)(2,1)}, bf16[4,8,128,128]{3,2,1,0:T(8,128)(2,1)}, bf16[4,8,128,128]{3,2,1,0:T(8,128)(2,1)}) custom-call(bf16[16,512,128]{2,1,0:T(8,128)(2,1)} %fusion.q_ref, bf16[16,512,128]{2,1,0:T(8,128)(2,1)} %bitcast.27, bf16[16,512,128]{2,1,0:T(8,128)(2,1)} %get-tuple-element.61.v_ref, ...), custom_call_target="tpu_custom_call" | custom-call | tf_op jit(solution)/shard_map/pallas_call | solution.py:162
  90.1 3.5 %all-to-all-start = ((bf16[4,8,128,128]{3,2,1,0:T(8,128)(2,1)}), bf16[4,8,128,128]{3,2,1,0:T(8,128)(2,1)S(1)}, u32[]{:S(2)}, u32[]{:S(2)}) async-start(bf16[4,8,128,128]{3,2,1,0:T(8,128)(2,1)} %get-tuple-element.34), calls=%async_computation | async-start | bytes 2097152 | tf_op jit(solution)/shard_map/all_to_all | solution.py:175
  96.5 11.5 %all-to-all-done = bf16[4,8,128,128]{3,2,1,0:T(8,128)(2,1)S(1)} async-done(((bf16[4,8,128,128]{3,2,1,0:T(8,128)(2,1)}), bf16[4,8,128,128]{3,2,1,0:T(8,128)(2,1)S(1)}, u32[]{:S(2)}, u32[]{:S(2)}) %all-to-all-start) | async-done | bytes 1048608 | tf_op jit(solution)/shard_map/all_to_all | solution.py:175
  108.0 4.2 %all-to-all-start.2 = ((bf16[4,8,128,128]{3,2,1,0:T(8,128)(2,1)}), bf16[4,8,128,128]{3,2,1,0:T(8,128)(2,1)}, u32[]{:S(2)}, u32[]{:S(2)}) async-start(bf16[4,8,128,128]{3,2,1,0:T(8,128)(2,1)} %get-tuple-element.36), calls=%async_computation.2 | async-start | bytes 2097152 | tf_op jit(solution)/shard_map/all_to_all | solution.py:175
  118.9 7.9 %all-to-all-done.2 = bf16[4,8,128,128]{3,2,1,0:T(8,128)(2,1)} async-done(((bf16[4,8,128,128]{3,2,1,0:T(8,128)(2,1)}), bf16[4,8,128,128]{3,2,1,0:T(8,128)(2,1)}, u32[]{:S(2)}, u32[]{:S(2)}) %all-to-all-start.2) | async-done | bytes 1048608 | tf_op jit(solution)/shard_map/all_to_all | solution.py:175
  126.8 3.5 %all-to-all-start.4 = ((bf16[4,8,128,128]{3,2,1,0:T(8,128)(2,1)}), bf16[4,8,128,128]{3,2,1,0:T(8,128)(2,1)S(1)}, u32[]{:S(2)}, u32[]{:S(2)}) async-start(bf16[4,8,128,128]{3,2,1,0:T(8,128)(2,1)} %get-tuple-element.38), calls=%async_computation.4 | async-start | bytes 2097152 | tf_op jit(solution)/shard_map/all_to_all | solution.py:175
  130.3 16.0 %shard_map.76 = (f32[8,512,128]{2,1,0:T(8,128)}, f32[8,512,128]{2,1,0:T(8,128)}, f32[8,512,128]{2,1,0:T(8,128)}, f32[8,512,128]{2,1,0:T(8,128)}) custom-call(bf16[16,512,128]{2,1,0:T(8,128)(2,1)} %fusion.q_ref, bf16[16,512,128]{2,1,0:T(8,128)(2,1)} %bitcast.28, bf16[16,512,128]{2,1,0:T(8,128)(2,1)} %get-tuple-element.61.v_ref, ...), custom_call_target="tpu_custom_call" | custom-call | flops 402653184 | bytes 12582912 | tf_op jit(solution)/shard_map/pallas_call | solution.py:118
  150.8 13.7 %shard_map.79 = (bf16[16,512,128]{2,1,0:T(8,128)(2,1)}, bf16[4,8,128,128]{3,2,1,0:T(8,128)(2,1)}, bf16[4,8,128,128]{3,2,1,0:T(8,128)(2,1)}, bf16[4,8,128,128]{3,2,1,0:T(8,128)(2,1)}) custom-call(bf16[16,512,128]{2,1,0:T(8,128)(2,1)} %fusion.q_ref, bf16[16,512,128]{2,1,0:T(8,128)(2,1)} %bitcast.29, ...), custom_call_target="tpu_custom_call", output_to_operand_aliasing={{0}: (11, {})} | custom-call | tf_op jit(solution)/shard_map/pallas_call | solution.py:162
  164.5 18.9 %all_to_all.30 = bf16[4,8,128,128]{3,2,1,0:T(8,128)(2,1)} all-to-all(bf16[4,8,128,128]{3,2,1,0:T(8,128)(2,1)} %get-tuple-element.35), channel_id=1, replica_groups=mesh['grp'=2,'seq'=4,'head'=2,'sub'=2] {'head','sub'}, dimensions={0} | all-to-all | bytes 2097152 | tf_op jit(solution)/shard_map/all_to_all | solution.py:175
  183.4 17.7 %all_to_all.31 = bf16[4,8,128,128]{3,2,1,0:T(8,128)(2,1)} all-to-all(bf16[4,8,128,128]{3,2,1,0:T(8,128)(2,1)S(1)} %copy-done.18), channel_id=1, replica_groups=mesh['grp'=2,'seq'=4,'head'=2,'sub'=2] {'head','sub'}, dimensions={0} | all-to-all | bytes 2097152 | tf_op jit(solution)/shard_map/all_to_all | solution.py:175
  201.2 4.4 %all-to-all-start.5 = ((bf16[4,8,128,128]{3,2,1,0:T(8,128)(2,1)}), bf16[4,8,128,128]{3,2,1,0:T(8,128)(2,1)}, u32[]{:S(2)}, u32[]{:S(2)}) async-start(bf16[4,8,128,128]{3,2,1,0:T(8,128)(2,1)} %get-tuple-element.39), calls=%async_computation.5 | async-start | bytes 2097152 | tf_op jit(solution)/shard_map/all_to_all | solution.py:175
  205.6 2.7 %copy.33 = bf16[512,16,128]{2,1,0:T(8,128)(2,1)} copy(bf16[512,16,128]{2,0,1:T(8,128)(2,1)S(1)} %bitcast.30) | data formatting | bytes 4194304
  208.7 2.7 %copy.34 = bf16[128,64,128]{2,1,0:T(8,128)(2,1)} copy(bf16[128,64,128]{2,0,1:T(8,128)(2,1)S(1)} %bitcast.31) | data formatting | bytes 4194304
  213.1 2.7 %copy.35 = bf16[128,64,128]{2,1,0:T(8,128)(2,1)} copy(bf16[128,64,128]{2,0,1:T(8,128)(2,1)S(1)} %bitcast.32) | data formatting | bytes 4194304
  215.8 4.2 %all-to-all-done.5 = bf16[4,8,128,128]{3,2,1,0:T(8,128)(2,1)} async-done(((bf16[4,8,128,128]{3,2,1,0:T(8,128)(2,1)}), bf16[4,8,128,128]{3,2,1,0:T(8,128)(2,1)}, u32[]{:S(2)}, u32[]{:S(2)}) %all-to-all-start.5) | async-done | bytes 1048608 | tf_op jit(solution)/shard_map/all_to_all | solution.py:175
  221.6 2.7 %copy.36 = bf16[128,64,128]{2,1,0:T(8,128)(2,1)} copy(bf16[128,64,128]{2,0,1:T(8,128)(2,1)S(1)} %bitcast.33) | data formatting | bytes 4194304
  (80 shorter events, 36.3 us)
Async XLA Ops:
  15.6 17.4 %copy-start.1 = (f32[16,128,128]{2,1,0:T(8,128)S(1)}, f32[16,128,128]{2,1,0:T(8,128)}, u32[]{:S(2)}) copy-start(f32[16,128,128]{2,1,0:T(8,128)} %get-tuple-element.22) | copy-start | bytes 3145732
  16.8 22.1 %copy-start = (f32[16,128,128]{2,1,0:T(8,128)S(1)}, f32[16,128,128]{2,1,0:T(8,128)}, u32[]{:S(2)}) copy-start(f32[16,128,128]{2,1,0:T(8,128)} %get-tuple-element.23) | copy-start | bytes 3145732
  16.8 16.2 %collective-permute-start.6 = (f32[8,128,128]{2,1,0:T(8,128)S(1)}, f32[8,128,128]{2,1,0:T(8,128)S(1)}, u32[]{:S(2)}, u32[]{:S(2)}) collective-permute-start(f32[8,128,128]{2,1,0:T(8,128)S(1)} %slice.16), channel_id=1, source_target_pairs={{0,4},{1,5},{2,6},{3,7},{16,20},{17,21},{18,22},{19,23}} | collective-permute-start | bytes 1572872 | tf_op jit(solution)/shard_map/ppermute | solution.py:85
  23.0 15.9 %collective-permute-start.9 = (f32[8,128,128]{2,1,0:T(8,128)S(1)}, f32[8,128,128]{2,1,0:T(8,128)S(1)}, u32[]{:S(2)}, u32[]{:S(2)}) collective-permute-start(f32[8,128,128]{2,1,0:T(8,128)S(1)} %slice.17), channel_id=1, source_target_pairs={{12,8},{13,9},{14,10},{15,11},{28,24},{29,25},{30,26},{31,27}} | collective-permute-start | bytes 1572872 | tf_op jit(solution)/shard_map/ppermute | solution.py:85
  33.2 6.6 %collective-permute-start.7 = (f32[8,128,128]{2,1,0:T(8,128)S(1)}, f32[8,128,128]{2,1,0:T(8,128)S(1)}, u32[]{:S(2)}, u32[]{:S(2)}) collective-permute-start(f32[8,128,128]{2,1,0:T(8,128)S(1)} %get-tuple-element.58), channel_id=1, source_target_pairs={{4,8},{5,9},{6,10},{7,11},{20,24},{21,25},{22,26},{23,27}} | collective-permute-start | bytes 1572872 | tf_op jit(solution)/shard_map/ppermute | solution.py:85
  33.9 15.3 %collective-permute-start = (f32[8,128,128]{2,1,0:T(8,128)S(1)}, f32[8,128,128]{2,1,0:T(8,128)S(1)}, u32[]{:S(2)}, u32[]{:S(2)}) collective-permute-start(f32[8,128,128]{2,1,0:T(8,128)S(1)} %get-tuple-element.59), channel_id=1, source_target_pairs={{0,4},{1,5},{2,6},{3,7},{16,20},{17,21},{18,22},{19,23}} | collective-permute-start | bytes 1572872 | tf_op jit(solution)/shard_map/ppermute | solution.py:85
  39.0 11.5 %copy-start.13 = (f32[8,128,128]{2,1,0:T(8,128)}, f32[8,128,128]{2,1,0:T(8,128)S(1)}, u32[]{:S(2)}) copy-start(f32[8,128,128]{2,1,0:T(8,128)S(1)} %collective-permute-done.9) | copy-start | bytes 1572868
  39.0 12.9 %collective-permute-start.10 = (f32[8,128,128]{2,1,0:T(8,128)S(1)}, f32[8,128,128]{2,1,0:T(8,128)S(1)}, u32[]{:S(2)}, u32[]{:S(2)}) collective-permute-start(f32[8,128,128]{2,1,0:T(8,128)S(1)} %slice_add_fusion.5), channel_id=1, source_target_pairs={{8,4},{9,5},{10,6},{11,7},{24,20},{25,21},{26,22},{27,23}} | collective-permute-start | bytes 1572872 | tf_op jit(solution)/shard_map/ppermute | solution.py:85
  39.7 13.3 %copy-start.15 = (f32[8,128,128]{2,1,0:T(8,128)}, f32[8,128,128]{2,1,0:T(8,128)S(1)}, u32[]{:S(2)}) copy-start(f32[8,128,128]{2,1,0:T(8,128)S(1)} %collective-permute-done.7) | copy-start | bytes 1572868
  50.4 21.4 %collective-permute-start.8 = (f32[8,128,128]{2,1,0:T(8,128)}, f32[8,128,128]{2,1,0:T(8,128)}, u32[]{:S(2)}, u32[]{:S(2)}) collective-permute-start(f32[8,128,128]{2,1,0:T(8,128)} %get-tuple-element.56), channel_id=1, source_target_pairs={{8,12},{9,13},{10,14},{11,15},{24,28},{25,29},{26,30},{27,31}} | collective-permute-start | bytes 1572872 | tf_op jit(solution)/shard_map/ppermute | solution.py:85
  53.0 20.9 %collective-permute-start.11 = (f32[8,128,128]{2,1,0:T(8,128)}, f32[8,128,128]{2,1,0:T(8,128)}, u32[]{:S(2)}, u32[]{:S(2)}) collective-permute-start(f32[8,128,128]{2,1,0:T(8,128)} %get-tuple-element.54), channel_id=1, source_target_pairs={{4,0},{5,1},{6,2},{7,3},{20,16},{21,17},{22,18},{23,19}} | collective-permute-start | bytes 1572872 | tf_op jit(solution)/shard_map/ppermute | solution.py:85
  54.3 19.6 %collective-permute-start.3 = (f32[8,128,128]{2,1,0:T(8,128)}, f32[8,128,128]{2,1,0:T(8,128)S(1)}, u32[]{:S(2)}, u32[]{:S(2)}) collective-permute-start(f32[8,128,128]{2,1,0:T(8,128)} %get-tuple-element.55), channel_id=1, source_target_pairs={{12,8},{13,9},{14,10},{15,11},{28,24},{29,25},{30,26},{31,27}} | collective-permute-start | bytes 1572872 | tf_op jit(solution)/shard_map/ppermute | solution.py:85
  90.1 18.0 %all-to-all-start = ((bf16[4,8,128,128]{3,2,1,0:T(8,128)(2,1)}), bf16[4,8,128,128]{3,2,1,0:T(8,128)(2,1)S(1)}, u32[]{:S(2)}, u32[]{:S(2)}) async-start(bf16[4,8,128,128]{3,2,1,0:T(8,128)(2,1)} %get-tuple-element.34), calls=%async_computation | async-start | bytes 2097152 | tf_op jit(solution)/shard_map/all_to_all | solution.py:175
  93.6 18.7 %collective-permute-start.1 = (f32[8,128,128]{2,1,0:T(8,128)}, f32[8,128,128]{2,1,0:T(8,128)}, u32[]{:S(2)}, u32[]{:S(2)}) collective-permute-start(f32[8,128,128]{2,1,0:T(8,128)} %get-tuple-element.57), channel_id=1, source_target_pairs={{4,8},{5,9},{6,10},{7,11},{20,24},{21,25},{22,26},{23,27}} | collective-permute-start | bytes 1572872 | tf_op jit(solution)/shard_map/ppermute | solution.py:85
  95.1 20.6 %collective-permute-start.4 = (f32[8,128,128]{2,1,0:T(8,128)}, f32[8,128,128]{2,1,0:T(8,128)}, u32[]{:S(2)}, u32[]{:S(2)}) collective-permute-start(f32[8,128,128]{2,1,0:T(8,128)} %get-tuple-element.53), channel_id=1, source_target_pairs={{8,4},{9,5},{10,6},{11,7},{24,20},{25,21},{26,22},{27,23}} | collective-permute-start | bytes 1572872 | tf_op jit(solution)/shard_map/ppermute | solution.py:85
  108.0 18.8 %all-to-all-start.2 = ((bf16[4,8,128,128]{3,2,1,0:T(8,128)(2,1)}), bf16[4,8,128,128]{3,2,1,0:T(8,128)(2,1)}, u32[]{:S(2)}, u32[]{:S(2)}) async-start(bf16[4,8,128,128]{3,2,1,0:T(8,128)(2,1)} %get-tuple-element.36), calls=%async_computation.2 | async-start | bytes 2097152 | tf_op jit(solution)/shard_map/all_to_all | solution.py:175
  114.2 32.2 %collective-permute-start.2 = (f32[8,128,128]{2,1,0:T(8,128)}, f32[8,128,128]{2,1,0:T(8,128)}, u32[]{:S(2)}, u32[]{:S(2)}) collective-permute-start(f32[8,128,128]{2,1,0:T(8,128)} %slice_add_fusion.2), channel_id=1, source_target_pairs={{8,12},{9,13},{10,14},{11,15},{24,28},{25,29},{26,30},{27,31}} | collective-permute-start | bytes 1572872 | tf_op jit(solution)/shard_map/ppermute | solution.py:85
  117.6 31.1 %collective-permute-start.5 = (f32[8,128,128]{2,1,0:T(8,128)}, f32[8,128,128]{2,1,0:T(8,128)}, u32[]{:S(2)}, u32[]{:S(2)}) collective-permute-start(f32[8,128,128]{2,1,0:T(8,128)} %slice_add_fusion.6), channel_id=1, source_target_pairs={{4,0},{5,1},{6,2},{7,3},{20,16},{21,17},{22,18},{23,19}} | collective-permute-start | bytes 1572872 | tf_op jit(solution)/shard_map/ppermute | solution.py:85
  126.8 37.6 %all-to-all-start.4 = ((bf16[4,8,128,128]{3,2,1,0:T(8,128)(2,1)}), bf16[4,8,128,128]{3,2,1,0:T(8,128)(2,1)S(1)}, u32[]{:S(2)}, u32[]{:S(2)}) async-start(bf16[4,8,128,128]{3,2,1,0:T(8,128)(2,1)} %get-tuple-element.38), calls=%async_computation.4 | async-start | bytes 2097152 | tf_op jit(solution)/shard_map/all_to_all | solution.py:175
  164.5 19.0 %copy-start.3 = (bf16[4,8,128,128]{3,2,1,0:T(8,128)(2,1)}, bf16[4,8,128,128]{3,2,1,0:T(8,128)(2,1)S(1)}, u32[]{:S(2)}) copy-start(bf16[4,8,128,128]{3,2,1,0:T(8,128)(2,1)S(1)} %all-to-all-done.4) | copy-start | bytes 3145732
  164.5 19.0 %copy-start.18 = (bf16[4,8,128,128]{3,2,1,0:T(8,128)(2,1)S(1)}, bf16[4,8,128,128]{3,2,1,0:T(8,128)(2,1)}, u32[]{:S(2)}) copy-start(bf16[4,8,128,128]{3,2,1,0:T(8,128)(2,1)} %get-tuple-element.37) | copy-start | bytes 3145732
  183.4 22.2 %copy-start.2 = (bf16[16,512,128]{2,1,0:T(8,128)(2,1)S(1)}, bf16[16,512,128]{2,1,0:T(8,128)(2,1)}, u32[]{:S(2)}) copy-start(bf16[16,512,128]{2,1,0:T(8,128)(2,1)} %get-tuple-element.33) | copy-start | bytes 6291460
  201.2 18.8 %all-to-all-start.5 = ((bf16[4,8,128,128]{3,2,1,0:T(8,128)(2,1)}), bf16[4,8,128,128]{3,2,1,0:T(8,128)(2,1)}, u32[]{:S(2)}, u32[]{:S(2)}) async-start(bf16[4,8,128,128]{3,2,1,0:T(8,128)(2,1)} %get-tuple-element.39), calls=%async_computation.5 | async-start | bytes 2097152 | tf_op jit(solution)/shard_map/all_to_all | solution.py:175
  213.1 6.9 %copy-start.4 = (bf16[4,8,128,128]{3,2,1,0:T(8,128)(2,1)S(1)}, bf16[4,8,128,128]{3,2,1,0:T(8,128)(2,1)}, u32[]{:S(2)}) copy-start(bf16[4,8,128,128]{3,2,1,0:T(8,128)(2,1)} %copy-done.3) | copy-start | bytes 3145732
  (11 other events, 30.8 us)

commit v10 on v7

--- a/solution.py
+++ b/solution.py
@@ -67,12 +67,14 @@
 def exclusive_scan(total, axis, count, reverse):
     carried = jnp.zeros_like(total)
     acc = jnp.zeros_like(total)
+    hops = []
     for hop in range(count - 1):
         pair = (count - 1 - hop, count - 2 - hop) if reverse else (hop, hop + 1)
         got = lax.ppermute(carried + total, axis, perm=[pair])
         acc = acc + got
         carried = got
-    return acc
+        hops.append(got)
+    return acc, hops
 
 
 def per_device(queries, key_rows, value_rows, out_adjoint, seq_count):
@@ -105,10 +107,20 @@
     per_peer = tok_out // span
     attended = None
     grads = []
+    chains = []
     for g in range(groups):
         sel = slice(g * width, (g + 1) * width)
-        before = exclusive_scan(kv_total[sel], "seq", seq_count, False)
-        rest = exclusive_scan(adj_total[sel], "seq", seq_count, True) + adj_total[sel]
+        before, before_hops = exclusive_scan(kv_total[sel], "seq", seq_count, False)
+        after, after_hops = exclusive_scan(adj_total[sel], "seq", seq_count, True)
+        chains.append([before, after + adj_total[sel], before_hops, after_hops])
+    for g in range(groups - 1):
+        if seq_count >= 3:
+            nxt = chains[g + 1]
+            chains[g][0], chains[g][1], _, _ = lax.optimization_barrier(
+                (chains[g][0], chains[g][1], nxt[2][seq_count - 3], nxt[3][seq_count - 3])
+            )
+    for g in range(groups):
+        before, rest = chains[g][0], chains[g][1]
         gtile = pl.BlockSpec((width, span, head_dim), lambda c, g=g: (g, c, 0))
         gwhole = pl.BlockSpec((width, head_dim, head_dim), lambda c: (0, 0, 0))
         if split_out:

time: 215 us -> 222 us (1.033)
  blocking collectives: 36.7 us -> 55.4 us
  waiting for transfers between devices: 54 us -> 45.5 us
    all_to_all x2 -> x3, blocking collectives: 36.7 us -> 55.4 us  [per_device(): lax.all_to_all(x, ('head', 'sub'), split_axis=axis, concat_axis=0, tiled=...]
    all_to_all x4 -> x3, waiting for transfers between devices: 23.6 us -> 13.2 us  [per_device(): lax.all_to_all(x, ('head', 'sub'), split_axis=axis, concat_axis=0, tiled=...]
    all_to_all x4 -> x3, starting transfers between devices: 15.7 us -> 11.4 us  [per_device(): lax.all_to_all(x, ('head', 'sub'), split_axis=axis, concat_axis=0, tiled=...]
    ppermute x12, starting transfers between devices: 20.6 us -> 23.1 us  [exclusive_scan(): got = lax.ppermute(carried + total, axis, perm=[pair])]
  transfers between devices with their start and end apart: 16 -> 15, of which waited for: 7 -> 6; matrix products, arithmetic and copies ran while one was open for 10% -> 10% of each run, Pallas kernels for 10% -> 9%
where the time goes in v10:
time: 222 us; the launch traced here: 221 us
  blocking collectives  55.4 us (25%)
  Pallas kernels  46.7 us (21%)
  waiting for transfers between devices  45.5 us (20%)
  starting transfers between devices  34.6 us (16%)
  local copies, waits for them, and re-layouts  21.6 us (10%)
  other arithmetic  16.2 us (7%)
    all_to_all x3, blocking collectives, per_device(): lax.all_to_all(x, ('head', 'sub'), split_axis=axis, concat_axis=0, tiled=...  55.4 us
    pallas_call x2, Pallas kernels, per_device(): pl.pallas_call(functools.partial(main_kernel, width, attended is not None...  41.5 us
    ppermute x12, waiting for transfers between devices, exclusive_scan(): got = lax.ppermute(carried + total, axis, perm=[pair])  32.3 us
    ppermute x12, starting transfers between devices, exclusive_scan(): got = lax.ppermute(carried + total, axis, perm=[pair])  23.1 us
    unnamed x33, local copies, waits for them, and re-layouts  15.3 us
    all_to_all x3, waiting for transfers between devices, per_device(): lax.all_to_all(x, ('head', 'sub'), split_axis=axis, concat_axis=0, tiled=...  13.2 us
    all_to_all x3, starting transfers between devices, per_device(): lax.all_to_all(x, ('head', 'sub'), split_axis=axis, concat_axis=0, tiled=...  11.4 us
    add x6, other arithmetic, exclusive_scan(): got = lax.ppermute(carried + total, axis, perm=[pair])  5.29 us
  transfers between devices with their start and end apart: 15, of which 6 were waited for; matrix products, arithmetic and copies ran while one was open for 10% of the time, Pallas kernels for 9%

profile of v10, /device:TPU:0, one launch (start us, length us, event | category | flops | bytes accessed | tf_op | source)
XLA Modules:
  0.0 221.0 jit_solution(13261830473487840698)
XLA Ops:
  0.7 3.6 %copy.41 = bf16[512,16,128]{2,0,1:T(8,128)(2,1)} copy(bf16[512,16,128]{2,1,0:T(8,128)(2,1)} %param.5) | data formatting | bytes 4194304 | tf_op args[1]
  7.2 3.3 %copy_bitcast_fusion = (bf16[16,512,128]{2,1,0:T(8,128)(2,1)}, bf16[16,512,128]{2,1,0:T(8,128)(2,1)}) fusion(bf16[512,16,128]{2,1,0:T(8,128)(2,1)S(1)} %copy-done.9, bf16[512,16,128]{2,1,0:T(8,128)(2,1)S(1)} %copy-done.10), kind=kLoop, calls=%fused_computation.5 | loop fusion | bytes 8388608 | tf_op jit(solution)/shard_map/transpose | solution.py:88
  10.5 5.2 %shard_map.75 = (f32[16,128,128]{2,1,0:T(8,128)}, f32[16,128,128]{2,1,0:T(8,128)}) custom-call(bf16[16,512,128]{2,1,0:T(8,128)(2,1)} %fusion.q_ref, bf16[16,512,128]{2,1,0:T(8,128)(2,1)} %bitcast.25, bf16[16,512,128]{2,1,0:T(8,128)(2,1)} %get-tuple-element.49.v_ref, bf16[16,512,128]{2,1,0:T(8,128)(2,1)} %get-tuple-element.48.d_ref), custom_call_target="tpu_custom_call" | custom-call | tf_op jit(solution)/shard_map/pallas_call | solution.py:95
  18.7 5.0 %collective-permute-start.6 = (f32[8,128,128]{2,1,0:T(8,128)S(1)}, f32[8,128,128]{2,1,0:T(8,128)S(1)}, u32[]{:S(2)}, u32[]{:S(2)}) collective-permute-start(f32[8,128,128]{2,1,0:T(8,128)S(1)} %slice.16), channel_id=1, source_target_pairs={{0,4},{1,5},{2,6},{3,7},{16,20},{17,21},{18,22},{19,23}} | collective-permute-start | bytes 1572872 | tf_op jit(solution)/shard_map/ppermute | solution.py:73
  24.5 10.3 %collective-permute-done.6 = f32[8,128,128]{2,1,0:T(8,128)S(1)} collective-permute-done((f32[8,128,128]{2,1,0:T(8,128)S(1)}, f32[8,128,128]{2,1,0:T(8,128)S(1)}, u32[]{:S(2)}, u32[]{:S(2)}) %collective-permute-start.6) | collective-permute-done | bytes 524320 | tf_op jit(solution)/shard_map/ppermute | solution.py:73
  35.6 7.7 %collective-permute-start = (f32[8,128,128]{2,1,0:T(8,128)S(1)}, f32[8,128,128]{2,1,0:T(8,128)}, u32[]{:S(2)}, u32[]{:S(2)}) collective-permute-start(f32[8,128,128]{2,1,0:T(8,128)S(1)} %get-tuple-element.47), channel_id=1, source_target_pairs={{0,4},{1,5},{2,6},{3,7},{16,20},{17,21},{18,22},{19,23}} | collective-permute-start | bytes 1572872 | tf_op jit(solution)/shard_map/ppermute | solution.py:73
  45.4 7.0 %collective-permute-done = f32[8,128,128]{2,1,0:T(8,128)} collective-permute-done((f32[8,128,128]{2,1,0:T(8,128)S(1)}, f32[8,128,128]{2,1,0:T(8,128)}, u32[]{:S(2)}, u32[]{:S(2)}) %collective-permute-start) | collective-permute-done | bytes 524320 | tf_op jit(solution)/shard_map/ppermute | solution.py:73
  55.9 5.5 %collective-permute-done.11 = f32[8,128,128]{2,1,0:T(8,128)S(1)} collective-permute-done((f32[8,128,128]{2,1,0:T(8,128)S(1)}, f32[8,128,128]{2,1,0:T(8,128)S(1)}, u32[]{:S(2)}, u32[]{:S(2)}) %collective-permute-start.11) | collective-permute-done | bytes 524320 | tf_op jit(solution)/shard_map/ppermute | solution.py:73
  65.5 20.8 %shard_map.76 = (bf16[16,512,128]{2,1,0:T(8,128)(2,1)}, bf16[4,8,128,128]{3,2,1,0:T(8,128)(2,1)}, bf16[4,8,128,128]{3,2,1,0:T(8,128)(2,1)}, bf16[4,8,128,128]{3,2,1,0:T(8,128)(2,1)}) custom-call(bf16[16,512,128]{2,1,0:T(8,128)(2,1)} %fusion.q_ref, bf16[16,512,128]{2,1,0:T(8,128)(2,1)} %bitcast.26, bf16[16,512,128]{2,1,0:T(8,128)(2,1)} %get-tuple-element.49.v_ref, ...), custom_call_target="tpu_custom_call" | custom-call | tf_op jit(solution)/shard_map/pallas_call | solution.py:141
  86.3 18.8 %all_to_all.30 = bf16[4,8,128,128]{3,2,1,0:T(8,128)(2,1)} all-to-all(bf16[4,8,128,128]{3,2,1,0:T(8,128)(2,1)} %get-tuple-element.22), channel_id=1, replica_groups=mesh['grp'=2,'seq'=4,'head'=2,'sub'=2] {'head','sub'}, dimensions={0} | all-to-all | bytes 2097152 | tf_op jit(solution)/shard_map/all_to_all | solution.py:154
  105.1 3.5 %all-to-all-start.2 = ((bf16[4,8,128,128]{3,2,1,0:T(8,128)(2,1)}), bf16[4,8,128,128]{3,2,1,0:T(8,128)(2,1)S(1)}, u32[]{:S(2)}, u32[]{:S(2)}) async-start(bf16[4,8,128,128]{3,2,1,0:T(8,128)(2,1)} %get-tuple-element.24), calls=%async_computation.2 | async-start | bytes 2097152 | tf_op jit(solution)/shard_map/all_to_all | solution.py:154
  115.2 7.9 %all-to-all-done.2 = bf16[4,8,128,128]{3,2,1,0:T(8,128)(2,1)S(1)} async-done(((bf16[4,8,128,128]{3,2,1,0:T(8,128)(2,1)}), bf16[4,8,128,128]{3,2,1,0:T(8,128)(2,1)S(1)}, u32[]{:S(2)}, u32[]{:S(2)}) %all-to-all-start.2) | async-done | bytes 1048608 | tf_op jit(solution)/shard_map/all_to_all | solution.py:154
  123.0 3.5 %all-to-all-start.4 = ((bf16[4,8,128,128]{3,2,1,0:T(8,128)(2,1)}), bf16[4,8,128,128]{3,2,1,0:T(8,128)(2,1)S(1)}, u32[]{:S(2)}, u32[]{:S(2)}) async-start(bf16[4,8,128,128]{3,2,1,0:T(8,128)(2,1)} %get-tuple-element.26), calls=%async_computation.4 | async-start | bytes 2097152 | tf_op jit(solution)/shard_map/all_to_all | solution.py:154
  126.5 2.3 %add_add_fusion.3.before_ref = f32[8,128,128]{2,1,0:T(8,128)} fusion(f32[8,128,128]{2,1,0:T(8,128)} %collective-permute-done.2, f32[8,128,128]{2,1,0:T(8,128)} %collective-permute-done, f32[8,128,128]{2,1,0:T(8,128)} %collective-permute-done.1), kind=kLoop, calls=%fused_computation.11 | loop fusion | flops 262144 | bytes 2097152 | tf_op jit(solution)/shard_map/add | solution.py:74
  128.9 9.4 %collective-permute-done.5 = f32[8,128,128]{2,1,0:T(8,128)} collective-permute-done((f32[8,128,128]{2,1,0:T(8,128)}, f32[8,128,128]{2,1,0:T(8,128)}, u32[]{:S(2)}, u32[]{:S(2)}) %collective-permute-start.5) | collective-permute-done | bytes 524320 | tf_op jit(solution)/shard_map/ppermute | solution.py:73
  140.4 20.8 %shard_map.77 = (bf16[16,512,128]{2,1,0:T(8,128)(2,1)}, bf16[4,8,128,128]{3,2,1,0:T(8,128)(2,1)}, bf16[4,8,128,128]{3,2,1,0:T(8,128)(2,1)}, bf16[4,8,128,128]{3,2,1,0:T(8,128)(2,1)}) custom-call(bf16[16,512,128]{2,1,0:T(8,128)(2,1)} %fusion.q_ref, bf16[16,512,128]{2,1,0:T(8,128)(2,1)} %bitcast.27, ...), custom_call_target="tpu_custom_call", output_to_operand_aliasing={{0}: (7, {})} | custom-call | tf_op jit(solution)/shard_map/pallas_call | solution.py:141
  161.2 18.9 %all_to_all.31 = bf16[4,8,128,128]{3,2,1,0:T(8,128)(2,1)} all-to-all(bf16[4,8,128,128]{3,2,1,0:T(8,128)(2,1)} %get-tuple-element.23), channel_id=1, replica_groups=mesh['grp'=2,'seq'=4,'head'=2,'sub'=2] {'head','sub'}, dimensions={0} | all-to-all | bytes 2097152 | tf_op jit(solution)/shard_map/all_to_all | solution.py:154
  180.1 17.7 %all_to_all.32 = bf16[4,8,128,128]{3,2,1,0:T(8,128)(2,1)} all-to-all(bf16[4,8,128,128]{3,2,1,0:T(8,128)(2,1)S(1)} %copy-done.13), channel_id=1, replica_groups=mesh['grp'=2,'seq'=4,'head'=2,'sub'=2] {'head','sub'}, dimensions={0} | all-to-all | bytes 2097152 | tf_op jit(solution)/shard_map/all_to_all | solution.py:154
  197.9 4.4 %all-to-all-start.5 = ((bf16[4,8,128,128]{3,2,1,0:T(8,128)(2,1)}), bf16[4,8,128,128]{3,2,1,0:T(8,128)(2,1)}, u32[]{:S(2)}, u32[]{:S(2)}) async-start(bf16[4,8,128,128]{3,2,1,0:T(8,128)(2,1)} %get-tuple-element.27), calls=%async_computation.5 | async-start | bytes 2097152 | tf_op jit(solution)/shard_map/all_to_all | solution.py:154
  202.3 2.7 %copy.33 = bf16[512,16,128]{2,1,0:T(8,128)(2,1)} copy(bf16[512,16,128]{2,0,1:T(8,128)(2,1)S(1)} %bitcast.31) | data formatting | bytes 4194304
  205.4 2.7 %copy.34 = bf16[128,64,128]{2,1,0:T(8,128)(2,1)} copy(bf16[128,64,128]{2,0,1:T(8,128)(2,1)S(1)} %bitcast.28) | data formatting | bytes 4194304
  208.6 2.7 %copy.35 = bf16[128,64,128]{2,1,0:T(8,128)(2,1)} copy(bf16[128,64,128]{2,0,1:T(8,128)(2,1)S(1)} %bitcast.29) | data formatting | bytes 4194304
  211.2 5.4 %all-to-all-done.5 = bf16[4,8,128,128]{3,2,1,0:T(8,128)(2,1)} async-done(((bf16[4,8,128,128]{3,2,1,0:T(8,128)(2,1)}), bf16[4,8,128,128]{3,2,1,0:T(8,128)(2,1)}, u32[]{:S(2)}, u32[]{:S(2)}) %all-to-all-start.5) | async-done | bytes 1048608 | tf_op jit(solution)/shard_map/all_to_all | solution.py:154
  218.3 2.7 %copy.36 = bf16[128,64,128]{2,1,0:T(8,128)(2,1)} copy(bf16[128,64,128]{2,0,1:T(8,128)(2,1)S(1)} %bitcast.30) | data formatting | bytes 4194304
  (67 shorter events, 28.4 us)
Async XLA Ops:
  0.6 3.6 %copy-start.8 = (bf16[512,16,128]{2,1,0:T(8,128)(2,1)S(1)}, bf16[512,16,128]{2,1,0:T(8,128)(2,1)}, u32[]{:S(2)}) copy-start(bf16[512,16,128]{2,1,0:T(8,128)(2,1)} %param.4) | copy-start | bytes 6291460
  4.3 3.0 %copy-start.10 = (bf16[512,16,128]{2,1,0:T(8,128)(2,1)S(1)}, bf16[512,16,128]{2,1,0:T(8,128)(2,1)}, u32[]{:S(2)}) copy-start(bf16[512,16,128]{2,1,0:T(8,128)(2,1)} %param.6) | copy-start | bytes 6291460
  15.7 8.0 %copy-start = (f32[16,128,128]{2,1,0:T(8,128)S(1)}, f32[16,128,128]{2,1,0:T(8,128)}, u32[]{:S(2)}) copy-start(f32[16,128,128]{2,1,0:T(8,128)} %get-tuple-element.17) | copy-start | bytes 3145732
  15.7 19.1 %copy-start.1 = (f32[16,128,128]{2,1,0:T(8,128)S(1)}, f32[16,128,128]{2,1,0:T(8,128)}, u32[]{:S(2)}) copy-start(f32[16,128,128]{2,1,0:T(8,128)} %get-tuple-element.16) | copy-start | bytes 3145732
  16.9 6.8 %collective-permute-start.9 = (f32[8,128,128]{2,1,0:T(8,128)S(1)}, f32[8,128,128]{2,1,0:T(8,128)S(1)}, u32[]{:S(2)}, u32[]{:S(2)}) collective-permute-start(f32[8,128,128]{2,1,0:T(8,128)S(1)} %slice.17), channel_id=1, source_target_pairs={{12,8},{13,9},{14,10},{15,11},{28,24},{29,25},{30,26},{31,27}} | collective-permute-start | bytes 1572872 | tf_op jit(solution)/shard_map/ppermute | solution.py:73
  18.7 16.1 %collective-permute-start.6 = (f32[8,128,128]{2,1,0:T(8,128)S(1)}, f32[8,128,128]{2,1,0:T(8,128)S(1)}, u32[]{:S(2)}, u32[]{:S(2)}) collective-permute-start(f32[8,128,128]{2,1,0:T(8,128)S(1)} %slice.16), channel_id=1, source_target_pairs={{0,4},{1,5},{2,6},{3,7},{16,20},{17,21},{18,22},{19,23}} | collective-permute-start | bytes 1572872 | tf_op jit(solution)/shard_map/ppermute | solution.py:73
  23.8 19.6 %collective-permute-start.10 = (f32[8,128,128]{2,1,0:T(8,128)S(1)}, f32[8,128,128]{2,1,0:T(8,128)S(1)}, u32[]{:S(2)}, u32[]{:S(2)}) collective-permute-start(f32[8,128,128]{2,1,0:T(8,128)S(1)} %slice_add_fusion.5), channel_id=1, source_target_pairs={{8,4},{9,5},{10,6},{11,7},{24,20},{25,21},{26,22},{27,23}} | collective-permute-start | bytes 1572872 | tf_op jit(solution)/shard_map/ppermute | solution.py:73
  34.9 10.5 %collective-permute-start.7 = (f32[8,128,128]{2,1,0:T(8,128)S(1)}, f32[8,128,128]{2,1,0:T(8,128)S(1)}, u32[]{:S(2)}, u32[]{:S(2)}) collective-permute-start(f32[8,128,128]{2,1,0:T(8,128)S(1)} %get-tuple-element.46), channel_id=1, source_target_pairs={{4,8},{5,9},{6,10},{7,11},{20,24},{21,25},{22,26},{23,27}} | collective-permute-start | bytes 1572872 | tf_op jit(solution)/shard_map/ppermute | solution.py:73
  35.6 16.9 %collective-permute-start = (f32[8,128,128]{2,1,0:T(8,128)S(1)}, f32[8,128,128]{2,1,0:T(8,128)}, u32[]{:S(2)}, u32[]{:S(2)}) collective-permute-start(f32[8,128,128]{2,1,0:T(8,128)S(1)} %get-tuple-element.47), channel_id=1, source_target_pairs={{0,4},{1,5},{2,6},{3,7},{16,20},{17,21},{18,22},{19,23}} | collective-permute-start | bytes 1572872 | tf_op jit(solution)/shard_map/ppermute | solution.py:73
  43.4 17.9 %collective-permute-start.11 = (f32[8,128,128]{2,1,0:T(8,128)S(1)}, f32[8,128,128]{2,1,0:T(8,128)S(1)}, u32[]{:S(2)}, u32[]{:S(2)}) collective-permute-start(f32[8,128,128]{2,1,0:T(8,128)S(1)} %get-tuple-element.42), channel_id=1, source_target_pairs={{4,0},{5,1},{6,2},{7,3},{20,16},{21,17},{22,18},{23,19}} | collective-permute-start | bytes 1572872 | tf_op jit(solution)/shard_map/ppermute | solution.py:73
  44.7 16.6 %collective-permute-start.3 = (f32[8,128,128]{2,1,0:T(8,128)S(1)}, f32[8,128,128]{2,1,0:T(8,128)S(1)}, u32[]{:S(2)}, u32[]{:S(2)}) collective-permute-start(f32[8,128,128]{2,1,0:T(8,128)S(1)} %get-tuple-element.43), channel_id=1, source_target_pairs={{12,8},{13,9},{14,10},{15,11},{28,24},{29,25},{30,26},{31,27}} | collective-permute-start | bytes 1572872 | tf_op jit(solution)/shard_map/ppermute | solution.py:73
  53.7 11.0 %collective-permute-start.8 = (f32[8,128,128]{2,1,0:T(8,128)S(1)}, f32[8,128,128]{2,1,0:T(8,128)S(1)}, u32[]{:S(2)}, u32[]{:S(2)}) collective-permute-start(f32[8,128,128]{2,1,0:T(8,128)S(1)} %get-tuple-element.44), channel_id=1, source_target_pairs={{8,12},{9,13},{10,14},{11,15},{24,28},{25,29},{26,30},{27,31}} | collective-permute-start | bytes 1572872 | tf_op jit(solution)/shard_map/ppermute | solution.py:73
  54.4 11.1 %collective-permute-start.1 = (f32[8,128,128]{2,1,0:T(8,128)S(1)}, f32[8,128,128]{2,1,0:T(8,128)}, u32[]{:S(2)}, u32[]{:S(2)}) collective-permute-start(f32[8,128,128]{2,1,0:T(8,128)S(1)} %get-tuple-element.45), channel_id=1, source_target_pairs={{4,8},{5,9},{6,10},{7,11},{20,24},{21,25},{22,26},{23,27}} | collective-permute-start | bytes 1572872 | tf_op jit(solution)/shard_map/ppermute | solution.py:73
  62.4 3.1 %collective-permute-start.4 = (f32[8,128,128]{2,1,0:T(8,128)S(1)}, f32[8,128,128]{2,1,0:T(8,128)}, u32[]{:S(2)}, u32[]{:S(2)}) collective-permute-start(f32[8,128,128]{2,1,0:T(8,128)S(1)} %get-tuple-element.41), channel_id=1, source_target_pairs={{8,4},{9,5},{10,6},{11,7},{24,20},{25,21},{26,22},{27,23}} | collective-permute-start | bytes 1572872 | tf_op jit(solution)/shard_map/ppermute | solution.py:73
  105.1 18.0 %all-to-all-start.2 = ((bf16[4,8,128,128]{3,2,1,0:T(8,128)(2,1)}), bf16[4,8,128,128]{3,2,1,0:T(8,128)(2,1)S(1)}, u32[]{:S(2)}, u32[]{:S(2)}) async-start(bf16[4,8,128,128]{3,2,1,0:T(8,128)(2,1)} %get-tuple-element.24), calls=%async_computation.2 | async-start | bytes 2097152 | tf_op jit(solution)/shard_map/all_to_all | solution.py:154
  110.5 16.0 %collective-permute-start.2 = (f32[8,128,128]{2,1,0:T(8,128)}, f32[8,128,128]{2,1,0:T(8,128)}, u32[]{:S(2)}, u32[]{:S(2)}) collective-permute-start(f32[8,128,128]{2,1,0:T(8,128)} %slice_add_fusion.2), channel_id=1, source_target_pairs={{8,12},{9,13},{10,14},{11,15},{24,28},{25,29},{26,30},{27,31}} | collective-permute-start | bytes 1572872 | tf_op jit(solution)/shard_map/ppermute | solution.py:73
  113.9 24.4 %collective-permute-start.5 = (f32[8,128,128]{2,1,0:T(8,128)}, f32[8,128,128]{2,1,0:T(8,128)}, u32[]{:S(2)}, u32[]{:S(2)}) collective-permute-start(f32[8,128,128]{2,1,0:T(8,128)} %slice_add_fusion.6), channel_id=1, source_target_pairs={{4,0},{5,1},{6,2},{7,3},{20,16},{21,17},{22,18},{23,19}} | collective-permute-start | bytes 1572872 | tf_op jit(solution)/shard_map/ppermute | solution.py:73
  123.0 38.2 %all-to-all-start.4 = ((bf16[4,8,128,128]{3,2,1,0:T(8,128)(2,1)}), bf16[4,8,128,128]{3,2,1,0:T(8,128)(2,1)S(1)}, u32[]{:S(2)}, u32[]{:S(2)}) async-start(bf16[4,8,128,128]{3,2,1,0:T(8,128)(2,1)} %get-tuple-element.26), calls=%async_computation.4 | async-start | bytes 2097152 | tf_op jit(solution)/shard_map/all_to_all | solution.py:154
  126.5 11.7 %copy-start.12 = (f32[8,128,128]{2,1,0:T(8,128)S(1)}, f32[8,128,128]{2,1,0:T(8,128)}, u32[]{:S(2)}) copy-start(f32[8,128,128]{2,1,0:T(8,128)} %copy-done.11) | copy-start | bytes 1572868
  161.2 18.9 %copy-start.4 = (bf16[4,8,128,128]{3,2,1,0:T(8,128)(2,1)}, bf16[4,8,128,128]{3,2,1,0:T(8,128)(2,1)S(1)}, u32[]{:S(2)}) copy-start(bf16[4,8,128,128]{3,2,1,0:T(8,128)(2,1)S(1)} %all-to-all-done.4) | copy-start | bytes 3145732
  161.2 18.9 %copy-start.13 = (bf16[4,8,128,128]{3,2,1,0:T(8,128)(2,1)S(1)}, bf16[4,8,128,128]{3,2,1,0:T(8,128)(2,1)}, u32[]{:S(2)}) copy-start(bf16[4,8,128,128]{3,2,1,0:T(8,128)(2,1)} %get-tuple-element.25) | copy-start | bytes 3145732
  180.1 22.2 %copy-start.2 = (bf16[16,512,128]{2,1,0:T(8,128)(2,1)S(1)}, bf16[16,512,128]{2,1,0:T(8,128)(2,1)}, u32[]{:S(2)}) copy-start(bf16[16,512,128]{2,1,0:T(8,128)(2,1)} %get-tuple-element.21) | copy-start | bytes 6291460
  197.9 18.8 %all-to-all-start.5 = ((bf16[4,8,128,128]{3,2,1,0:T(8,128)(2,1)}), bf16[4,8,128,128]{3,2,1,0:T(8,128)(2,1)}, u32[]{:S(2)}, u32[]{:S(2)}) async-start(bf16[4,8,128,128]{3,2,1,0:T(8,128)(2,1)} %get-tuple-element.27), calls=%async_computation.5 | async-start | bytes 2097152 | tf_op jit(solution)/shard_map/all_to_all | solution.py:154
  208.6 8.1 %copy-start.5 = (bf16[4,8,128,128]{3,2,1,0:T(8,128)(2,1)S(1)}, bf16[4,8,128,128]{3,2,1,0:T(8,128)(2,1)}, u32[]{:S(2)}) copy-start(bf16[4,8,128,128]{3,2,1,0:T(8,128)(2,1)} %copy-done.4) | copy-start | bytes 3145732
  (5 other events, 11.1 us)

commit v11 on v10

--- a/solution.py
+++ b/solution.py
@@ -149,11 +149,14 @@
             compiler_params=pltpu.CompilerParams(dimension_semantics=("arbitrary",)),
         )(*args)
         attended = outs[0]
-        axis = 0 if split_out else 1
-        grads.append([
-            lax.all_to_all(x, ("head", "sub"), split_axis=axis, concat_axis=0, tiled=True)
-            for x in outs[1:]
-        ])
+        grads.append(list(outs[1:]))
+    if groups > 1:
+        grads[0], _ = lax.optimization_barrier((grads[0], grads[-1]))
+    axis = 0 if split_out else 1
+    grads = [
+        [lax.all_to_all(x, ("head", "sub"), split_axis=axis, concat_axis=0, tiled=True) for x in gr]
+        for gr in grads
+    ]
     outs = tuple(
         jnp.transpose(
             jnp.stack([grads[g][i].reshape(peers, width, tok_out, head_dim) for g in range(groups)], 1)

time: 222 us -> 235 us (1.059)
  the two profiles are of different devices: /device:TPU:0 before, /device:TPU:24 now
where the time goes in v11:
time: 235 us; the launch traced here: 234 us
  blocking collectives  87.8 us (37%)
  Pallas kernels  46.7 us (20%)
  waiting for transfers between devices  34.9 us (15%)
  starting transfers between devices  29.7 us (13%)
  local copies, waits for them, and re-layouts  21.6 us (9%)
  other arithmetic  12.6 us (5%)
    all_to_all x5, blocking collectives, per_device(): lax.all_to_all(x, ('head', 'sub'), split_axis=axis, concat_axis=0, tiled=...  87.8 us
    pallas_call x2, Pallas kernels, per_device(): pl.pallas_call(functools.partial(main_kernel, width, attended is not None...  41.6 us
    ppermute x12, waiting for transfers between devices, exclusive_scan(): got = lax.ppermute(carried + total, axis, perm=[pair])  29.5 us
    ppermute x12, starting transfers between devices, exclusive_scan(): got = lax.ppermute(carried + total, axis, perm=[pair])  25.3 us
    unnamed x35, local copies, waits for them, and re-layouts  15.3 us
    all_to_all x1, waiting for transfers between devices, per_device(): lax.all_to_all(x, ('head', 'sub'), split_axis=axis, concat_axis=0, tiled=...  5.38 us
    pallas_call x1, Pallas kernels, per_device(): pl.pallas_call(functools.partial(totals_kernel, width), grid=(groups,), i...  5.13 us
  transfers between devices with their start and end apart: 13, of which 4 were waited for; matrix products, arithmetic and copies ran while one was open for 7% of the time, Pallas kernels for 9%

profile of v11, /device:TPU:24, one launch (start us, length us, event | category | flops | bytes accessed | tf_op | source)
XLA Modules:
  0.0 234.3 jit_solution(5441430315287216672)
XLA Ops:
  0.7 3.6 %copy.41 = bf16[512,16,128]{2,0,1:T(8,128)(2,1)} copy(bf16[512,16,128]{2,1,0:T(8,128)(2,1)} %param.5) | data formatting | bytes 4194304 | tf_op args[1]
  4.3 2.0 fusion.q_ref
  7.2 3.3 %copy_bitcast_fusion = (bf16[16,512,128]{2,1,0:T(8,128)(2,1)}, bf16[16,512,128]{2,1,0:T(8,128)(2,1)}) fusion(bf16[512,16,128]{2,1,0:T(8,128)(2,1)S(1)} %copy-done.8, bf16[512,16,128]{2,1,0:T(8,128)(2,1)S(1)} %copy-done.9), kind=kLoop, calls=%fused_computation.5 | loop fusion | bytes 8388608 | tf_op jit(solution)/shard_map/transpose | solution.py:88
  10.5 5.1 %shard_map.75 = (f32[16,128,128]{2,1,0:T(8,128)}, f32[16,128,128]{2,1,0:T(8,128)}) custom-call(bf16[16,512,128]{2,1,0:T(8,128)(2,1)} %fusion.q_ref, bf16[16,512,128]{2,1,0:T(8,128)(2,1)} %bitcast.25, bf16[16,512,128]{2,1,0:T(8,128)(2,1)} %get-tuple-element.55.v_ref, bf16[16,512,128]{2,1,0:T(8,128)(2,1)} %get-tuple-element.54.d_ref), custom_call_target="tpu_custom_call" | custom-call | tf_op jit(solution)/shard_map/pallas_call | solution.py:95
  16.9 2.4 %collective-permute-start.9 = (f32[8,128,128]{2,1,0:T(8,128)S(1)}, f32[8,128,128]{2,1,0:T(8,128)S(1)}, u32[]{:S(2)}, u32[]{:S(2)}) collective-permute-start(f32[8,128,128]{2,1,0:T(8,128)S(1)} %slice.17), channel_id=1, source_target_pairs={{12,8},{13,9},{14,10},{15,11},{28,24},{29,25},{30,26},{31,27}} | collective-permute-start | bytes 1572872 | tf_op jit(solution)/shard_map/ppermute | solution.py:73
  21.1 9.3 %collective-permute-done.9 = f32[8,128,128]{2,1,0:T(8,128)S(1)} collective-permute-done((f32[8,128,128]{2,1,0:T(8,128)S(1)}, f32[8,128,128]{2,1,0:T(8,128)S(1)}, u32[]{:S(2)}, u32[]{:S(2)}) %collective-permute-start.9) | collective-permute-done | bytes 524320 | tf_op jit(solution)/shard_map/ppermute | solution.py:73
  33.6 14.0 %collective-permute-start.3 = (f32[8,128,128]{2,1,0:T(8,128)S(1)}, f32[8,128,128]{2,1,0:T(8,128)S(1)}, u32[]{:S(2)}, u32[]{:S(2)}) collective-permute-start(f32[8,128,128]{2,1,0:T(8,128)S(1)} %get-tuple-element.49), channel_id=1, source_target_pairs={{12,8},{13,9},{14,10},{15,11},{28,24},{29,25},{30,26},{31,27}} | collective-permute-start | bytes 1572872 | tf_op jit(solution)/shard_map/ppermute | solution.py:73
  48.5 8.7 %collective-permute-done.3 = f32[8,128,128]{2,1,0:T(8,128)S(1)} collective-permute-done((f32[8,128,128]{2,1,0:T(8,128)S(1)}, f32[8,128,128]{2,1,0:T(8,128)S(1)}, u32[]{:S(2)}, u32[]{:S(2)}) %collective-permute-start.3) | collective-permute-done | bytes 524320 | tf_op jit(solution)/shard_map/ppermute | solution.py:73
  65.5 11.4 %collective-permute-done.8 = f32[8,128,128]{2,1,0:T(8,128)S(1)} collective-permute-done((f32[8,128,128]{2,1,0:T(8,128)S(1)}, f32[8,128,128]{2,1,0:T(8,128)S(1)}, u32[]{:S(2)}, u32[]{:S(2)}) %collective-permute-start.8) | collective-permute-done | bytes 524320 | tf_op jit(solution)/shard_map/ppermute | solution.py:73
  77.9 20.7 %shard_map.76 = (bf16[16,512,128]{2,1,0:T(8,128)(2,1)}, bf16[4,8,128,128]{3,2,1,0:T(8,128)(2,1)}, bf16[4,8,128,128]{3,2,1,0:T(8,128)(2,1)}, bf16[4,8,128,128]{3,2,1,0:T(8,128)(2,1)}) custom-call(bf16[16,512,128]{2,1,0:T(8,128)(2,1)} %fusion.q_ref, bf16[16,512,128]{2,1,0:T(8,128)(2,1)} %bitcast.26, bf16[16,512,128]{2,1,0:T(8,128)(2,1)} %get-tuple-element.55.v_ref, ...), custom_call_target="tpu_custom_call" | custom-call | tf_op jit(solution)/shard_map/pallas_call | solution.py:141
  98.6 2.0 add_add_fusion.3.before_ref
  100.6 1.9 add_add_fusion.2.rest_ref
  102.5 20.8 %shard_map.77 = (bf16[16,512,128]{2,1,0:T(8,128)(2,1)}, bf16[4,8,128,128]{3,2,1,0:T(8,128)(2,1)}, bf16[4,8,128,128]{3,2,1,0:T(8,128)(2,1)}, bf16[4,8,128,128]{3,2,1,0:T(8,128)(2,1)}) custom-call(bf16[16,512,128]{2,1,0:T(8,128)(2,1)} %fusion.q_ref, bf16[16,512,128]{2,1,0:T(8,128)(2,1)} %bitcast.27, ...), custom_call_target="tpu_custom_call", output_to_operand_aliasing={{0}: (7, {})} | custom-call | tf_op jit(solution)/shard_map/pallas_call | solution.py:141
  123.4 17.7 %all_to_all.30 = bf16[4,8,128,128]{3,2,1,0:T(8,128)(2,1)} all-to-all(bf16[4,8,128,128]{3,2,1,0:T(8,128)(2,1)S(1)} %copy-done.12), channel_id=1, replica_groups=mesh['grp'=2,'seq'=4,'head'=2,'sub'=2] {'head','sub'}, dimensions={0} | all-to-all | bytes 2097152 | tf_op jit(solution)/shard_map/all_to_all | solution.py:157
  141.1 17.7 %all_to_all.31 = bf16[4,8,128,128]{3,2,1,0:T(8,128)(2,1)} all-to-all(bf16[4,8,128,128]{3,2,1,0:T(8,128)(2,1)S(1)} %copy-done.11), channel_id=1, replica_groups=mesh['grp'=2,'seq'=4,'head'=2,'sub'=2] {'head','sub'}, dimensions={0} | all-to-all | bytes 2097152 | tf_op jit(solution)/shard_map/all_to_all | solution.py:157
  158.9 17.0 %all_to_all.32 = bf16[4,8,128,128]{3,2,1,0:T(8,128)(2,1)S(1)} all-to-all(bf16[4,8,128,128]{3,2,1,0:T(8,128)(2,1)S(1)} %copy-done.10), channel_id=1, replica_groups=mesh['grp'=2,'seq'=4,'head'=2,'sub'=2] {'head','sub'}, dimensions={0} | all-to-all | bytes 2097152 | tf_op jit(solution)/shard_map/all_to_all | solution.py:157
  175.9 17.6 %all_to_all.33 = bf16[4,8,128,128]{3,2,1,0:T(8,128)(2,1)} all-to-all(bf16[4,8,128,128]{3,2,1,0:T(8,128)(2,1)S(1)} %copy-done.14), channel_id=1, replica_groups=mesh['grp'=2,'seq'=4,'head'=2,'sub'=2] {'head','sub'}, dimensions={0} | all-to-all | bytes 2097152 | tf_op jit(solution)/shard_map/all_to_all | solution.py:157
  193.5 17.7 %all_to_all.34 = bf16[4,8,128,128]{3,2,1,0:T(8,128)(2,1)} all-to-all(bf16[4,8,128,128]{3,2,1,0:T(8,128)(2,1)S(1)} %copy-done.13), channel_id=1, replica_groups=mesh['grp'=2,'seq'=4,'head'=2,'sub'=2] {'head','sub'}, dimensions={0} | all-to-all | bytes 2097152 | tf_op jit(solution)/shard_map/all_to_all | solution.py:157
  211.2 4.4 %all-to-all-start.5 = ((bf16[4,8,128,128]{3,2,1,0:T(8,128)(2,1)}), bf16[4,8,128,128]{3,2,1,0:T(8,128)(2,1)}, u32[]{:S(2)}, u32[]{:S(2)}) async-start(bf16[4,8,128,128]{3,2,1,0:T(8,128)(2,1)} %get-tuple-element.30), calls=%async_computation.5 | async-start | bytes 2097152 | tf_op jit(solution)/shard_map/all_to_all | solution.py:157
  215.7 2.7 %copy.33 = bf16[512,16,128]{2,1,0:T(8,128)(2,1)} copy(bf16[512,16,128]{2,0,1:T(8,128)(2,1)S(1)} %bitcast.31) | data formatting | bytes 4194304
  218.8 2.7 %copy.34 = bf16[128,64,128]{2,1,0:T(8,128)(2,1)} copy(bf16[128,64,128]{2,0,1:T(8,128)(2,1)S(1)} %bitcast.28) | data formatting | bytes 4194304
  221.9 2.7 %copy.35 = bf16[128,64,128]{2,1,0:T(8,128)(2,1)} copy(bf16[128,64,128]{2,0,1:T(8,128)(2,1)S(1)} %bitcast.29) | data formatting | bytes 4194304
  224.6 5.4 %all-to-all-done.5 = bf16[4,8,128,128]{3,2,1,0:T(8,128)(2,1)} async-done(((bf16[4,8,128,128]{3,2,1,0:T(8,128)(2,1)}), bf16[4,8,128,128]{3,2,1,0:T(8,128)(2,1)}, u32[]{:S(2)}, u32[]{:S(2)}) %all-to-all-start.5) | async-done | bytes 1048608 | tf_op jit(solution)/shard_map/all_to_all | solution.py:157
  231.6 2.7 %copy.36 = bf16[128,64,128]{2,1,0:T(8,128)(2,1)} copy(bf16[128,64,128]{2,0,1:T(8,128)(2,1)S(1)} %bitcast.30) | data formatting | bytes 4194304
  (67 shorter events, 19.7 us)
Async XLA Ops:
  0.6 3.6 %copy-start.7 = (bf16[512,16,128]{2,1,0:T(8,128)(2,1)S(1)}, bf16[512,16,128]{2,1,0:T(8,128)(2,1)}, u32[]{:S(2)}) copy-start(bf16[512,16,128]{2,1,0:T(8,128)(2,1)} %param.4) | copy-start | bytes 6291460
  4.3 3.0 %copy-start.9 = (bf16[512,16,128]{2,1,0:T(8,128)(2,1)S(1)}, bf16[512,16,128]{2,1,0:T(8,128)(2,1)}, u32[]{:S(2)}) copy-start(bf16[512,16,128]{2,1,0:T(8,128)(2,1)} %param.6) | copy-start | bytes 6291460
  15.6 14.8 %copy-start = (f32[16,128,128]{2,1,0:T(8,128)S(1)}, f32[16,128,128]{2,1,0:T(8,128)}, u32[]{:S(2)}) copy-start(f32[16,128,128]{2,1,0:T(8,128)} %get-tuple-element.20) | copy-start | bytes 3145732
  15.6 15.6 %copy-start.1 = (f32[16,128,128]{2,1,0:T(8,128)S(1)}, f32[16,128,128]{2,1,0:T(8,128)}, u32[]{:S(2)}) copy-start(f32[16,128,128]{2,1,0:T(8,128)} %get-tuple-element.19) | copy-start | bytes 3145732
  16.9 13.5 %collective-permute-start.9 = (f32[8,128,128]{2,1,0:T(8,128)S(1)}, f32[8,128,128]{2,1,0:T(8,128)S(1)}, u32[]{:S(2)}, u32[]{:S(2)}) collective-permute-start(f32[8,128,128]{2,1,0:T(8,128)S(1)} %slice.17), channel_id=1, source_target_pairs={{12,8},{13,9},{14,10},{15,11},{28,24},{29,25},{30,26},{31,27}} | collective-permute-start | bytes 1572872 | tf_op jit(solution)/shard_map/ppermute | solution.py:73
  20.4 10.8 %collective-permute-start.6 = (f32[8,128,128]{2,1,0:T(8,128)S(1)}, f32[8,128,128]{2,1,0:T(8,128)S(1)}, u32[]{:S(2)}, u32[]{:S(2)}) collective-permute-start(f32[8,128,128]{2,1,0:T(8,128)S(1)} %slice.16), channel_id=1, source_target_pairs={{0,4},{1,5},{2,6},{3,7},{16,20},{17,21},{18,22},{19,23}} | collective-permute-start | bytes 1572872 | tf_op jit(solution)/shard_map/ppermute | solution.py:73
  30.5 2.2 collective-permute-start.10
  31.3 16.3 %collective-permute-start.7 = (f32[8,128,128]{2,1,0:T(8,128)S(1)}, f32[8,128,128]{2,1,0:T(8,128)S(1)}, u32[]{:S(2)}, u32[]{:S(2)}) collective-permute-start(f32[8,128,128]{2,1,0:T(8,128)S(1)} %get-tuple-element.52), channel_id=1, source_target_pairs={{4,8},{5,9},{6,10},{7,11},{20,24},{21,25},{22,26},{23,27}} | collective-permute-start | bytes 1572872 | tf_op jit(solution)/shard_map/ppermute | solution.py:73
  32.0 15.6 %collective-permute-start = (f32[8,128,128]{2,1,0:T(8,128)S(1)}, f32[8,128,128]{2,1,0:T(8,128)S(1)}, u32[]{:S(2)}, u32[]{:S(2)}) collective-permute-start(f32[8,128,128]{2,1,0:T(8,128)S(1)} %get-tuple-element.53), channel_id=1, source_target_pairs={{0,4},{1,5},{2,6},{3,7},{16,20},{17,21},{18,22},{19,23}} | collective-permute-start | bytes 1572872 | tf_op jit(solution)/shard_map/ppermute | solution.py:73
  32.9 15.6 %collective-permute-start.11 = (f32[8,128,128]{2,1,0:T(8,128)S(1)}, f32[8,128,128]{2,1,0:T(8,128)S(1)}, u32[]{:S(2)}, u32[]{:S(2)}) collective-permute-start(f32[8,128,128]{2,1,0:T(8,128)S(1)} %get-tuple-element.48), channel_id=1, source_target_pairs={{4,0},{5,1},{6,2},{7,3},{20,16},{21,17},{22,18},{23,19}} | collective-permute-start | bytes 1572872 | tf_op jit(solution)/shard_map/ppermute | solution.py:73
  33.6 23.7 %collective-permute-start.3 = (f32[8,128,128]{2,1,0:T(8,128)S(1)}, f32[8,128,128]{2,1,0:T(8,128)S(1)}, u32[]{:S(2)}, u32[]{:S(2)}) collective-permute-start(f32[8,128,128]{2,1,0:T(8,128)S(1)} %get-tuple-element.49), channel_id=1, source_target_pairs={{12,8},{13,9},{14,10},{15,11},{28,24},{29,25},{30,26},{31,27}} | collective-permute-start | bytes 1572872 | tf_op jit(solution)/shard_map/ppermute | solution.py:73
  47.8 13.3 %collective-permute-start.1 = (f32[8,128,128]{2,1,0:T(8,128)S(1)}, f32[8,128,128]{2,1,0:T(8,128)S(1)}, u32[]{:S(2)}, u32[]{:S(2)}) collective-permute-start(f32[8,128,128]{2,1,0:T(8,128)S(1)} %get-tuple-element.51), channel_id=1, source_target_pairs={{4,8},{5,9},{6,10},{7,11},{20,24},{21,25},{22,26},{23,27}} | collective-permute-start | bytes 1572872 | tf_op jit(solution)/shard_map/ppermute | solution.py:73
  58.3 4.9 %collective-permute-start.4 = (f32[8,128,128]{2,1,0:T(8,128)S(1)}, f32[8,128,128]{2,1,0:T(8,128)S(1)}, u32[]{:S(2)}, u32[]{:S(2)}) collective-permute-start(f32[8,128,128]{2,1,0:T(8,128)S(1)} %get-tuple-element.47), channel_id=1, source_target_pairs={{8,4},{9,5},{10,6},{11,7},{24,20},{25,21},{26,22},{27,23}} | collective-permute-start | bytes 1572872 | tf_op jit(solution)/shard_map/ppermute | solution.py:73
  59.7 17.2 %collective-permute-start.8 = (f32[8,128,128]{2,1,0:T(8,128)S(1)}, f32[8,128,128]{2,1,0:T(8,128)S(1)}, u32[]{:S(2)}, u32[]{:S(2)}) collective-permute-start(f32[8,128,128]{2,1,0:T(8,128)S(1)} %get-tuple-element.50), channel_id=1, source_target_pairs={{8,12},{9,13},{10,14},{11,15},{24,28},{25,29},{26,30},{27,31}} | collective-permute-start | bytes 1572872 | tf_op jit(solution)/shard_map/ppermute | solution.py:73
  61.9 36.7 %collective-permute-start.2 = (f32[8,128,128]{2,1,0:T(8,128)}, f32[8,128,128]{2,1,0:T(8,128)}, u32[]{:S(2)}, u32[]{:S(2)}) collective-permute-start(f32[8,128,128]{2,1,0:T(8,128)} %slice_add_fusion.2), channel_id=1, source_target_pairs={{8,12},{9,13},{10,14},{11,15},{24,28},{25,29},{26,30},{27,31}} | collective-permute-start | bytes 1572872 | tf_op jit(solution)/shard_map/ppermute | solution.py:73
  64.1 36.5 %collective-permute-start.5 = (f32[8,128,128]{2,1,0:T(8,128)}, f32[8,128,128]{2,1,0:T(8,128)}, u32[]{:S(2)}, u32[]{:S(2)}) collective-permute-start(f32[8,128,128]{2,1,0:T(8,128)} %slice_add_fusion.6), channel_id=1, source_target_pairs={{4,0},{5,1},{6,2},{7,3},{20,16},{21,17},{22,18},{23,19}} | collective-permute-start | bytes 1572872 | tf_op jit(solution)/shard_map/ppermute | solution.py:73
  102.5 20.8 %copy-start.12 = (bf16[4,8,128,128]{3,2,1,0:T(8,128)(2,1)S(1)}, bf16[4,8,128,128]{3,2,1,0:T(8,128)(2,1)}, u32[]{:S(2)}) copy-start(bf16[4,8,128,128]{3,2,1,0:T(8,128)(2,1)} %get-tuple-element.31) | copy-start | bytes 3145732
  123.4 17.8 %copy-start.11 = (bf16[4,8,128,128]{3,2,1,0:T(8,128)(2,1)S(1)}, bf16[4,8,128,128]{3,2,1,0:T(8,128)(2,1)}, u32[]{:S(2)}) copy-start(bf16[4,8,128,128]{3,2,1,0:T(8,128)(2,1)} %get-tuple-element.32) | copy-start | bytes 3145732
  123.4 35.5 %copy-start.10 = (bf16[4,8,128,128]{3,2,1,0:T(8,128)(2,1)S(1)}, bf16[4,8,128,128]{3,2,1,0:T(8,128)(2,1)}, u32[]{:S(2)}) copy-start(bf16[4,8,128,128]{3,2,1,0:T(8,128)(2,1)} %get-tuple-element.33) | copy-start | bytes 3145732
  141.1 34.7 %copy-start.14 = (bf16[4,8,128,128]{3,2,1,0:T(8,128)(2,1)S(1)}, bf16[4,8,128,128]{3,2,1,0:T(8,128)(2,1)}, u32[]{:S(2)}) copy-start(bf16[4,8,128,128]{3,2,1,0:T(8,128)(2,1)} %get-tuple-element.28) | copy-start | bytes 3145732
  158.9 34.6 %copy-start.13 = (bf16[4,8,128,128]{3,2,1,0:T(8,128)(2,1)S(1)}, bf16[4,8,128,128]{3,2,1,0:T(8,128)(2,1)}, u32[]{:S(2)}) copy-start(bf16[4,8,128,128]{3,2,1,0:T(8,128)(2,1)} %get-tuple-element.29) | copy-start | bytes 3145732
  193.5 22.2 %copy-start.2 = (bf16[16,512,128]{2,1,0:T(8,128)(2,1)S(1)}, bf16[16,512,128]{2,1,0:T(8,128)(2,1)}, u32[]{:S(2)}) copy-start(bf16[16,512,128]{2,1,0:T(8,128)(2,1)} %get-tuple-element.24) | copy-start | bytes 6291460
  211.2 18.8 %all-to-all-start.5 = ((bf16[4,8,128,128]{3,2,1,0:T(8,128)(2,1)}), bf16[4,8,128,128]{3,2,1,0:T(8,128)(2,1)}, u32[]{:S(2)}, u32[]{:S(2)}) async-start(bf16[4,8,128,128]{3,2,1,0:T(8,128)(2,1)} %get-tuple-element.30), calls=%async_computation.5 | async-start | bytes 2097152 | tf_op jit(solution)/shard_map/all_to_all | solution.py:157
  215.6 2.7 %copy-start.4 = (bf16[4,8,128,128]{3,2,1,0:T(8,128)(2,1)S(1)}, bf16[4,8,128,128]{3,2,1,0:T(8,128)(2,1)}, u32[]{:S(2)}) copy-start(bf16[4,8,128,128]{3,2,1,0:T(8,128)(2,1)} %all_to_all.30) | copy-start | bytes 3145732
  (4 other events, 10.1 us)

commit v12 on v7

--- a/solution.py
+++ b/solution.py
@@ -33,7 +33,8 @@
 def main_kernel(heads, aliased, q_ref, k_ref, v_ref, d_ref, f_ref, before_ref, rest_ref, *refs):
     if aliased:
         refs = refs[1:]
-    a_ref, qg_ref, kg_ref, vg_ref, state, suffix = refs
+    a_ref, g_ref, state, suffix = refs
+    qg_ref, kg_ref, vg_ref = g_ref.at[0], g_ref.at[1], g_ref.at[2]
 
     @pl.when(pl.program_id(0) == 0)
     def _():
@@ -113,12 +114,12 @@
         gwhole = pl.BlockSpec((width, head_dim, head_dim), lambda c: (0, 0, 0))
         if split_out:
             otile = pl.BlockSpec(
-                (None, width, span, head_dim), lambda c: (c // per_peer, 0, c % per_peer, 0)
+                (None, 3, width, span, head_dim), lambda c: (c // per_peer, 0, 0, c % per_peer, 0)
             )
-            grad_shape = jax.ShapeDtypeStruct((peers, width, tok_out, head_dim), BF16)
+            grad_shape = jax.ShapeDtypeStruct((peers, 3, width, tok_out, head_dim), BF16)
         else:
-            otile = pl.BlockSpec((width, span, head_dim), lambda c: (0, c, 0))
-            grad_shape = jax.ShapeDtypeStruct((width, tok_dev, head_dim), BF16)
+            otile = pl.BlockSpec((3, width, span, head_dim), lambda c: (0, 0, c, 0))
+            grad_shape = jax.ShapeDtypeStruct((3, width, tok_dev, head_dim), BF16)
         args = [qh, kh, vh, dh, factor, before, rest]
         specs = [gtile] * 4 + [fac, gwhole, gwhole]
         aliases = {}
@@ -130,22 +131,24 @@
             functools.partial(main_kernel, width, attended is not None),
             grid=(blocks,),
             in_specs=specs,
-            out_specs=[gtile] + [otile] * 3,
-            out_shape=[jax.ShapeDtypeStruct((heads, tok_dev, head_dim), BF16)] + [grad_shape] * 3,
+            out_specs=[gtile, otile],
+            out_shape=[jax.ShapeDtypeStruct((heads, tok_dev, head_dim), BF16), grad_shape],
             scratch_shapes=[pltpu.VMEM((width, head_dim, head_dim), F32)] * 2,
             input_output_aliases=aliases,
             compiler_params=pltpu.CompilerParams(dimension_semantics=("arbitrary",)),
         )(*args)
         attended = outs[0]
-        axis = 0 if split_out else 1
-        grads.append([
-            lax.all_to_all(x, ("head", "sub"), split_axis=axis, concat_axis=0, tiled=True)
-            for x in outs[1:]
-        ])
+        axis = 0 if split_out else 2
+        grads.append(
+            lax.all_to_all(outs[1], ("head", "sub"), split_axis=axis, concat_axis=0, tiled=True)
+        )
+    if split_out:
+        parts = [gr for gr in grads]
+    else:
+        parts = [gr.reshape(peers, 3, width, tok_out, head_dim) for gr in grads]
     outs = tuple(
         jnp.transpose(
-            jnp.stack([grads[g][i].reshape(peers, width, tok_out, head_dim) for g in range(groups)], 1)
-            .reshape(heads * peers, tok_out, head_dim),
+            jnp.stack([p[:, i] for p in parts], 1).reshape(heads * peers, tok_out, head_dim),
             (1, 0, 2),
         )
         for i in range(3)

time: 215 us -> 197 us (0.916)
  blocking collectives: 36.7 us -> 0 us
  waiting for transfers between devices: 54 us -> 86.5 us
  starting transfers between devices: 36.3 us -> 26.8 us
  other arithmetic: 17.5 us -> 8.69 us
  local copies, waits for them, and re-layouts: 21.5 us -> 27.2 us
    all_to_all x2 -> x0, blocking collectives: 36.7 us -> none  [per_device(): lax.all_to_all(x, ('head', 'sub'), split_axis=axis, concat_axis=0, tiled=...]
    ppermute x12, waiting for transfers between devices: 30.4 us -> 57.7 us  [exclusive_scan(): got = lax.ppermute(carried + total, axis, perm=[pair])]
    reshape x0 -> x3, local copies, waits for them, and re-layouts: none -> 8.01 us  [per_device(): jnp.stack([p[:, i] for p in parts], 1)]
    all_to_all x4 -> x2, starting transfers between devices: 15.7 us -> 8.54 us  [per_device(): lax.all_to_all(outs[1], ('head', 'sub'), split_axis=axis, concat_axis=0,...]
    unnamed x33 -> x18, local copies, waits for them, and re-layouts: 15.3 us -> 9.86 us
    all_to_all x4 -> x2, waiting for transfers between devices: 23.6 us -> 28.8 us  [per_device(): lax.all_to_all(outs[1], ('head', 'sub'), split_axis=axis, concat_axis=0,...]
    slice x0 -> x2, local copies, waits for them, and re-layouts: none -> 3.85 us  [per_device(): p[:, i]]
    add x6, other arithmetic: 5.06 us -> 1.33 us  [exclusive_scan(): got = lax.ppermute(carried + total, axis, perm=[pair])]
  transfers between devices with their start and end apart: 16 -> 14, of which waited for: 7 -> 5; matrix products, arithmetic and copies ran while one was open for 10% -> 7% of each run, Pallas kernels for 10% -> 11%
where the time goes in v12:
time: 197 us
  waiting for transfers between devices  86.5 us (44%)
  Pallas kernels  46.5 us (24%)
  local copies, waits for them, and re-layouts  27.2 us (14%)
  starting transfers between devices  26.8 us (14%)
  other arithmetic  8.69 us (4%)
    ppermute x12, waiting for transfers between devices, exclusive_scan(): got = lax.ppermute(carried + total, axis, perm=[pair])  57.7 us
    pallas_call x2, Pallas kernels, per_device(): pl.pallas_call(functools.partial(main_kernel, width, attended is not None...  41.4 us
    all_to_all x2, waiting for transfers between devices, per_device(): lax.all_to_all(outs[1], ('head', 'sub'), split_axis=axis, concat_axis=0,...  28.8 us
    ppermute x12, starting transfers between devices, exclusive_scan(): got = lax.ppermute(carried + total, axis, perm=[pair])  18.3 us
    unnamed x18, local copies, waits for them, and re-layouts  9.86 us
    all_to_all x2, starting transfers between devices, per_device(): lax.all_to_all(outs[1], ('head', 'sub'), split_axis=axis, concat_axis=0,...  8.54 us
    reshape x3, local copies, waits for them, and re-layouts, per_device(): jnp.stack([p[:, i] for p in parts], 1)  8.01 us
    pallas_call x1, Pallas kernels, per_device(): pl.pallas_call(functools.partial(totals_kernel, width), grid=(groups,), i...  5.13 us
  transfers between devices with their start and end apart: 14, of which 5 were waited for; matrix products, arithmetic and copies ran while one was open for 7% of the time, Pallas kernels for 11%

profile of v12, /device:TPU:0, one launch (start us, length us, event | category | flops | bytes accessed | tf_op | source)
XLA Modules:
  0.0 196.7 jit_solution(5790139830565751816)
XLA Ops:
  0.7 3.6 %copy.36 = bf16[512,16,128]{2,0,1:T(8,128)(2,1)} copy(bf16[512,16,128]{2,1,0:T(8,128)(2,1)} %param.5) | data formatting | bytes 4194304 | tf_op args[1]
  4.3 2.0 %fusion.q_ref = bf16[16,512,128]{2,1,0:T(8,128)(2,1)} fusion(bf16[512,16,128]{2,1,0:T(8,128)(2,1)S(1)} %copy-done.5, f32[512]{0:T(512)S(1)} %multiply_rsqrt_fusion.1), kind=kLoop, calls=%fused_computation.1 | loop fusion | flops 3145728 | bytes 4196352 | tf_op jit(solution)/shard_map/transpose | solution.py:87
  7.2 3.3 %copy_bitcast_fusion.3 = (bf16[16,512,128]{2,1,0:T(8,128)(2,1)}, bf16[16,512,128]{2,1,0:T(8,128)(2,1)}) fusion(bf16[512,16,128]{2,1,0:T(8,128)(2,1)S(1)} %copy-done.6, bf16[512,16,128]{2,1,0:T(8,128)(2,1)S(1)} %copy-done.7), kind=kLoop, calls=%fused_computation.8 | loop fusion | bytes 8388608 | tf_op jit(solution)/shard_map/transpose | solution.py:87
  10.5 5.1 %shard_map.75 = (f32[16,128,128]{2,1,0:T(8,128)}, f32[16,128,128]{2,1,0:T(8,128)}) custom-call(bf16[16,512,128]{2,1,0:T(8,128)(2,1)} %fusion.q_ref, bf16[16,512,128]{2,1,0:T(8,128)(2,1)} %bitcast.22, bf16[16,512,128]{2,1,0:T(8,128)(2,1)} %get-tuple-element.39.v_ref, bf16[16,512,128]{2,1,0:T(8,128)(2,1)} %get-tuple-element.38.d_ref), custom_call_target="tpu_custom_call" | custom-call | tf_op jit(solution)/shard_map/pallas_call | solution.py:94
  15.6 1.2 slice.34
  16.8 5.1 %collective-permute-start.6 = (f32[8,128,128]{2,1,0:T(8,128)S(1)}, f32[8,128,128]{2,1,0:T(8,128)S(1)}, u32[]{:S(2)}, u32[]{:S(2)}) collective-permute-start(f32[8,128,128]{2,1,0:T(8,128)S(1)} %slice.34), channel_id=1, source_target_pairs={{0,4},{1,5},{2,6},{3,7},{16,20},{17,21},{18,22},{19,23}} | collective-permute-start | bytes 1572872 | tf_op jit(solution)/shard_map/ppermute | solution.py:73
  23.7 9.3 %collective-permute-done.6 = f32[8,128,128]{2,1,0:T(8,128)S(1)} collective-permute-done((f32[8,128,128]{2,1,0:T(8,128)S(1)}, f32[8,128,128]{2,1,0:T(8,128)S(1)}, u32[]{:S(2)}, u32[]{:S(2)}) %collective-permute-start.6) | collective-permute-done | bytes 524320 | tf_op jit(solution)/shard_map/ppermute | solution.py:73
  33.9 5.0 %collective-permute-start = (f32[8,128,128]{2,1,0:T(8,128)S(1)}, f32[8,128,128]{2,1,0:T(8,128)S(1)}, u32[]{:S(2)}, u32[]{:S(2)}) collective-permute-start(f32[8,128,128]{2,1,0:T(8,128)S(1)} %get-tuple-element.37), channel_id=1, source_target_pairs={{0,4},{1,5},{2,6},{3,7},{16,20},{17,21},{18,22},{19,23}} | collective-permute-start | bytes 1572872 | tf_op jit(solution)/shard_map/ppermute | solution.py:73
  39.7 9.4 %collective-permute-done = f32[8,128,128]{2,1,0:T(8,128)S(1)} collective-permute-done((f32[8,128,128]{2,1,0:T(8,128)S(1)}, f32[8,128,128]{2,1,0:T(8,128)S(1)}, u32[]{:S(2)}, u32[]{:S(2)}) %collective-permute-start) | collective-permute-done | bytes 524320 | tf_op jit(solution)/shard_map/ppermute | solution.py:73
  50.9 1.3 collective-permute-start.11
  54.6 10.2 %collective-permute-done.11 = f32[8,128,128]{2,1,0:T(8,128)S(1)} collective-permute-done((f32[8,128,128]{2,1,0:T(8,128)S(1)}, f32[8,128,128]{2,1,0:T(8,128)S(1)}, u32[]{:S(2)}, u32[]{:S(2)}) %collective-permute-start.11) | collective-permute-done | bytes 524320 | tf_op jit(solution)/shard_map/ppermute | solution.py:73
  64.8 1.2 add_add_fusion
  66.0 20.7 %shard_map.76 = (bf16[16,512,128]{2,1,0:T(8,128)(2,1)}, bf16[4,3,8,128,128]{4,3,2,1,0:T(8,128)(2,1)}) custom-call(bf16[16,512,128]{2,1,0:T(8,128)(2,1)} %fusion.q_ref, bf16[16,512,128]{2,1,0:T(8,128)(2,1)} %bitcast.23, bf16[16,512,128]{2,1,0:T(8,128)(2,1)} %get-tuple-element.39.v_ref, bf16[16,512,128]{2,1,0:T(8,128)(2,1)} %get-tuple-element.38.d_ref, ...), custom_call_target="tpu_custom_call" | custom-call | tf_op jit(solution)/shard_map/pallas_call | solution.py:130
  86.8 4.6 %all-to-all-start = ((bf16[4,3,8,128,128]{4,3,2,1,0:T(8,128)(2,1)}), bf16[4,3,8,128,128]{4,3,2,1,0:T(8,128)(2,1)}, u32[]{:S(2)}, u32[]{:S(2)}) async-start(bf16[4,3,8,128,128]{4,3,2,1,0:T(8,128)(2,1)} %get-tuple-element.14), calls=%async_computation | async-start | bytes 6291456 | tf_op jit(solution)/shard_map/all_to_all | solution.py:143
  93.7 1.3 collective-permute-start.5
  95.9 28.7 %collective-permute-done.5 = f32[8,128,128]{2,1,0:T(8,128)S(1)} collective-permute-done((f32[8,128,128]{2,1,0:T(8,128)S(1)}, f32[8,128,128]{2,1,0:T(8,128)S(1)}, u32[]{:S(2)}, u32[]{:S(2)}) %collective-permute-start.5) | collective-permute-done | bytes 524320 | tf_op jit(solution)/shard_map/ppermute | solution.py:73
  125.5 20.7 %shard_map.77 = (bf16[16,512,128]{2,1,0:T(8,128)(2,1)}, bf16[4,3,8,128,128]{4,3,2,1,0:T(8,128)(2,1)}) custom-call(bf16[16,512,128]{2,1,0:T(8,128)(2,1)} %fusion.q_ref, bf16[16,512,128]{2,1,0:T(8,128)(2,1)} %bitcast.24, bf16[16,512,128]{2,1,0:T(8,128)(2,1)} %get-tuple-element.39.v_ref, ...), custom_call_target="tpu_custom_call", output_to_operand_aliasing={{0}: (7, {})} | custom-call | tf_op jit(solution)/shard_map/pallas_call | solution.py:130
  146.2 3.9 %all-to-all-start.1 = ((bf16[4,3,8,128,128]{4,3,2,1,0:T(8,128)(2,1)}), bf16[4,3,8,128,128]{4,3,2,1,0:T(8,128)(2,1)S(1)}, u32[]{:S(2)}, u32[]{:S(2)}) async-start(bf16[4,3,8,128,128]{4,3,2,1,0:T(8,128)(2,1)} %get-tuple-element.15), calls=%async_computation.1 | async-start | bytes 6291456 | tf_op jit(solution)/shard_map/all_to_all | solution.py:143
  150.1 4.3 %copy.25 = bf16[512,16,128]{2,1,0:T(8,128)(2,1)} copy(bf16[512,16,128]{2,0,1:T(8,128)(2,1)} %bitcast.28) | data formatting | bytes 4194304
  154.4 3.6 %fusion.1 = (bf16[4,1,8,128,128]{4,3,2,1,0:T(8,128)(2,1)}, bf16[4,1,8,128,128]{4,3,2,1,0:T(8,128)(2,1)}, bf16[4,1,8,128,128]{4,3,2,1,0:T(8,128)(2,1)}) fusion(bf16[4,3,8,128,128]{4,3,2,1,0:T(8,128)(2,1)} %all-to-all-done), kind=kLoop, calls=%fused_computation.25 | loop fusion | bytes 6291456 | tf_op jit(solution)/shard_map/slice | solution.py:151
  158.0 28.8 %all-to-all-done.1 = bf16[4,3,8,128,128]{4,3,2,1,0:T(8,128)(2,1)S(1)} async-done(((bf16[4,3,8,128,128]{4,3,2,1,0:T(8,128)(2,1)}), bf16[4,3,8,128,128]{4,3,2,1,0:T(8,128)(2,1)S(1)}, u32[]{:S(2)}, u32[]{:S(2)}) %all-to-all-start.1) | async-done | bytes 3145760 | tf_op jit(solution)/shard_map/all_to_all | solution.py:143
  188.3 2.7 %copy.33 = bf16[64,128,128]{2,0,1:T(8,128)(2,1)} copy(bf16[64,128,128]{2,1,0:T(8,128)(2,1)S(1)} %bitcast.25) | data formatting | bytes 4194304 | tf_op jit(solution)/shard_map/reshape | solution.py:151
  191.1 2.7 %copy.34 = bf16[64,128,128]{2,0,1:T(8,128)(2,1)} copy(bf16[64,128,128]{2,1,0:T(8,128)(2,1)S(1)} %bitcast.26) | data formatting | bytes 4194304 | tf_op jit(solution)/shard_map/reshape | solution.py:151
  194.0 2.7 %copy.35 = bf16[64,128,128]{2,0,1:T(8,128)(2,1)} copy(bf16[64,128,128]{2,1,0:T(8,128)(2,1)S(1)} %bitcast.27) | data formatting | bytes 4194304 | tf_op jit(solution)/shard_map/reshape | solution.py:151
  (49 shorter events, 14.3 us)
Async XLA Ops:
  0.6 3.6 %copy-start.5 = (bf16[512,16,128]{2,1,0:T(8,128)(2,1)S(1)}, bf16[512,16,128]{2,1,0:T(8,128)(2,1)}, u32[]{:S(2)}) copy-start(bf16[512,16,128]{2,1,0:T(8,128)(2,1)} %param.4) | copy-start | bytes 6291460
  4.3 2.0 %copy-start.6 = (bf16[512,16,128]{2,1,0:T(8,128)(2,1)S(1)}, bf16[512,16,128]{2,1,0:T(8,128)(2,1)}, u32[]{:S(2)}) copy-start(bf16[512,16,128]{2,1,0:T(8,128)(2,1)} %param.7) | copy-start | bytes 6291460
  4.3 3.0 %copy-start.7 = (bf16[512,16,128]{2,1,0:T(8,128)(2,1)S(1)}, bf16[512,16,128]{2,1,0:T(8,128)(2,1)}, u32[]{:S(2)}) copy-start(bf16[512,16,128]{2,1,0:T(8,128)(2,1)} %param.6) | copy-start | bytes 6291460
  15.6 17.4 %copy-start.1 = (f32[16,128,128]{2,1,0:T(8,128)S(1)}, f32[16,128,128]{2,1,0:T(8,128)}, u32[]{:S(2)}) copy-start(f32[16,128,128]{2,1,0:T(8,128)} %get-tuple-element.10) | copy-start | bytes 3145732
  16.8 22.1 %copy-start = (f32[16,128,128]{2,1,0:T(8,128)S(1)}, f32[16,128,128]{2,1,0:T(8,128)}, u32[]{:S(2)}) copy-start(f32[16,128,128]{2,1,0:T(8,128)} %get-tuple-element.11) | copy-start | bytes 3145732
  16.8 16.2 %collective-permute-start.6 = (f32[8,128,128]{2,1,0:T(8,128)S(1)}, f32[8,128,128]{2,1,0:T(8,128)S(1)}, u32[]{:S(2)}, u32[]{:S(2)}) collective-permute-start(f32[8,128,128]{2,1,0:T(8,128)S(1)} %slice.34), channel_id=1, source_target_pairs={{0,4},{1,5},{2,6},{3,7},{16,20},{17,21},{18,22},{19,23}} | collective-permute-start | bytes 1572872 | tf_op jit(solution)/shard_map/ppermute | solution.py:73
  23.0 15.9 %collective-permute-start.9 = (f32[8,128,128]{2,1,0:T(8,128)S(1)}, f32[8,128,128]{2,1,0:T(8,128)S(1)}, u32[]{:S(2)}, u32[]{:S(2)}) collective-permute-start(f32[8,128,128]{2,1,0:T(8,128)S(1)} %slice.35), channel_id=1, source_target_pairs={{12,8},{13,9},{14,10},{15,11},{28,24},{29,25},{30,26},{31,27}} | collective-permute-start | bytes 1572872 | tf_op jit(solution)/shard_map/ppermute | solution.py:73
  33.2 6.6 %collective-permute-start.7 = (f32[8,128,128]{2,1,0:T(8,128)S(1)}, f32[8,128,128]{2,1,0:T(8,128)S(1)}, u32[]{:S(2)}, u32[]{:S(2)}) collective-permute-start(f32[8,128,128]{2,1,0:T(8,128)S(1)} %get-tuple-element.36), channel_id=1, source_target_pairs={{4,8},{5,9},{6,10},{7,11},{20,24},{21,25},{22,26},{23,27}} | collective-permute-start | bytes 1572872 | tf_op jit(solution)/shard_map/ppermute | solution.py:73
  33.9 15.3 %collective-permute-start = (f32[8,128,128]{2,1,0:T(8,128)S(1)}, f32[8,128,128]{2,1,0:T(8,128)S(1)}, u32[]{:S(2)}, u32[]{:S(2)}) collective-permute-start(f32[8,128,128]{2,1,0:T(8,128)S(1)} %get-tuple-element.37), channel_id=1, source_target_pairs={{0,4},{1,5},{2,6},{3,7},{16,20},{17,21},{18,22},{19,23}} | collective-permute-start | bytes 1572872 | tf_op jit(solution)/shard_map/ppermute | solution.py:73
  39.0 11.8 %collective-permute-start.10 = (f32[8,128,128]{2,1,0:T(8,128)S(1)}, f32[8,128,128]{2,1,0:T(8,128)S(1)}, u32[]{:S(2)}, u32[]{:S(2)}) collective-permute-start(f32[8,128,128]{2,1,0:T(8,128)S(1)} %slice_add_fusion.5), channel_id=1, source_target_pairs={{8,4},{9,5},{10,6},{11,7},{24,20},{25,21},{26,22},{27,23}} | collective-permute-start | bytes 1572872 | tf_op jit(solution)/shard_map/ppermute | solution.py:73
  50.1 3.6 %collective-permute-start.8 = (f32[8,128,128]{2,1,0:T(8,128)S(1)}, f32[8,128,128]{2,1,0:T(8,128)S(1)}, u32[]{:S(2)}, u32[]{:S(2)}) collective-permute-start(f32[8,128,128]{2,1,0:T(8,128)S(1)} %get-tuple-element.34), channel_id=1, source_target_pairs={{8,12},{9,13},{10,14},{11,15},{24,28},{25,29},{26,30},{27,31}} | collective-permute-start | bytes 1572872 | tf_op jit(solution)/shard_map/ppermute | solution.py:73
  50.9 13.9 %collective-permute-start.11 = (f32[8,128,128]{2,1,0:T(8,128)S(1)}, f32[8,128,128]{2,1,0:T(8,128)S(1)}, u32[]{:S(2)}, u32[]{:S(2)}) collective-permute-start(f32[8,128,128]{2,1,0:T(8,128)S(1)} %get-tuple-element.32), channel_id=1, source_target_pairs={{4,0},{5,1},{6,2},{7,3},{20,16},{21,17},{22,18},{23,19}} | collective-permute-start | bytes 1572872 | tf_op jit(solution)/shard_map/ppermute | solution.py:73
  52.2 12.6 %collective-permute-start.3 = (f32[8,128,128]{2,1,0:T(8,128)S(1)}, f32[8,128,128]{2,1,0:T(8,128)S(1)}, u32[]{:S(2)}, u32[]{:S(2)}) collective-permute-start(f32[8,128,128]{2,1,0:T(8,128)S(1)} %get-tuple-element.33), channel_id=1, source_target_pairs={{12,8},{13,9},{14,10},{15,11},{28,24},{29,25},{30,26},{31,27}} | collective-permute-start | bytes 1572872 | tf_op jit(solution)/shard_map/ppermute | solution.py:73
  86.8 59.5 %all-to-all-start = ((bf16[4,3,8,128,128]{4,3,2,1,0:T(8,128)(2,1)}), bf16[4,3,8,128,128]{4,3,2,1,0:T(8,128)(2,1)}, u32[]{:S(2)}, u32[]{:S(2)}) async-start(bf16[4,3,8,128,128]{4,3,2,1,0:T(8,128)(2,1)} %get-tuple-element.14), calls=%async_computation | async-start | bytes 6291456 | tf_op jit(solution)/shard_map/all_to_all | solution.py:143
  91.4 1.4 collective-permute-start.1
  92.1 1.5 collective-permute-start.4
  92.9 2.1 %collective-permute-start.2 = (f32[8,128,128]{2,1,0:T(8,128)S(1)}, f32[8,128,128]{2,1,0:T(8,128)S(1)}, u32[]{:S(2)}, u32[]{:S(2)}) collective-permute-start(f32[8,128,128]{2,1,0:T(8,128)S(1)} %slice_add_fusion.2), channel_id=1, source_target_pairs={{8,12},{9,13},{10,14},{11,15},{24,28},{25,29},{26,30},{27,31}} | collective-permute-start | bytes 1572872 | tf_op jit(solution)/shard_map/ppermute | solution.py:73
  93.7 30.9 %collective-permute-start.5 = (f32[8,128,128]{2,1,0:T(8,128)S(1)}, f32[8,128,128]{2,1,0:T(8,128)S(1)}, u32[]{:S(2)}, u32[]{:S(2)}) collective-permute-start(f32[8,128,128]{2,1,0:T(8,128)S(1)} %slice_add_fusion.6), channel_id=1, source_target_pairs={{4,0},{5,1},{6,2},{7,3},{20,16},{21,17},{22,18},{23,19}} | collective-permute-start | bytes 1572872 | tf_op jit(solution)/shard_map/ppermute | solution.py:73
  146.2 40.6 %all-to-all-start.1 = ((bf16[4,3,8,128,128]{4,3,2,1,0:T(8,128)(2,1)}), bf16[4,3,8,128,128]{4,3,2,1,0:T(8,128)(2,1)S(1)}, u32[]{:S(2)}, u32[]{:S(2)}) async-start(bf16[4,3,8,128,128]{4,3,2,1,0:T(8,128)(2,1)} %get-tuple-element.15), calls=%async_computation.1 | async-start | bytes 6291456 | tf_op jit(solution)/shard_map/all_to_all | solution.py:143
  186.8 1.2 copy-start.4
  188.3 2.7 %copy-start.3 = (bf16[4,1,8,128,128]{4,3,2,1,0:T(8,128)(2,1)S(1)}, bf16[4,1,8,128,128]{4,3,2,1,0:T(8,128)(2,1)}, u32[]{:S(2)}) copy-start(bf16[4,1,8,128,128]{4,3,2,1,0:T(8,128)(2,1)} %get-tuple-element.25) | copy-start | bytes 3145732
  191.1 2.7 %copy-start.2 = (bf16[4,1,8,128,128]{4,3,2,1,0:T(8,128)(2,1)S(1)}, bf16[4,1,8,128,128]{4,3,2,1,0:T(8,128)(2,1)}, u32[]{:S(2)}) copy-start(bf16[4,1,8,128,128]{4,3,2,1,0:T(8,128)(2,1)} %get-tuple-element.26) | copy-start | bytes 3145732

commit v13 on v12

--- a/solution.py
+++ b/solution.py
@@ -68,12 +68,14 @@
 def exclusive_scan(total, axis, count, reverse):
     carried = jnp.zeros_like(total)
     acc = jnp.zeros_like(total)
+    hops = []
     for hop in range(count - 1):
         pair = (count - 1 - hop, count - 2 - hop) if reverse else (hop, hop + 1)
         got = lax.ppermute(carried + total, axis, perm=[pair])
         acc = acc + got
         carried = got
-    return acc
+        hops.append(got)
+    return acc, hops
 
 
 def per_device(queries, key_rows, value_rows, out_adjoint, seq_count):
@@ -106,10 +108,20 @@
     per_peer = tok_out // span
     attended = None
     grads = []
+    chains = []
     for g in range(groups):
         sel = slice(g * width, (g + 1) * width)
-        before = exclusive_scan(kv_total[sel], "seq", seq_count, False)
-        rest = exclusive_scan(adj_total[sel], "seq", seq_count, True) + adj_total[sel]
+        before, before_hops = exclusive_scan(kv_total[sel], "seq", seq_count, False)
+        after, after_hops = exclusive_scan(adj_total[sel], "seq", seq_count, True)
+        chains.append([before, after + adj_total[sel], before_hops, after_hops])
+    for g in range(groups - 1):
+        if seq_count >= 3:
+            nxt = chains[g + 1]
+            chains[g][0], chains[g][1], _, _ = lax.optimization_barrier(
+                (chains[g][0], chains[g][1], nxt[2][seq_count - 3], nxt[3][seq_count - 3])
+            )
+    for g in range(groups):
+        before, rest = chains[g][0], chains[g][1]
         gtile = pl.BlockSpec((width, span, head_dim), lambda c, g=g: (g, c, 0))
         gwhole = pl.BlockSpec((width, head_dim, head_dim), lambda c: (0, 0, 0))
         if split_out:

time: 197 us -> 189 us (0.959)
  waiting for transfers between devices: 86.5 us -> 76.8 us
    ppermute x12, waiting for transfers between devices: 57.7 us -> 47.9 us  [exclusive_scan(): got = lax.ppermute(carried + total, axis, perm=[pair])]
    unnamed x18 -> x26, local copies, waits for them, and re-layouts: 9.86 us -> 9.87 us
  transfers between devices with their start and end apart: 14 -> 14, of which waited for: 5 -> 5; matrix products, arithmetic and copies ran while one was open for 7% -> 8% of each run, Pallas kernels for 11% -> 11%
where the time goes in v13:
time: 189 us; the launch traced here: 188 us
  waiting for transfers between devices  76.8 us (41%)
  Pallas kernels  46.5 us (25%)
  starting transfers between devices  28.6 us (15%)
  local copies, waits for them, and re-layouts  27.3 us (14%)
  other arithmetic  7.74 us (4%)
    ppermute x12, waiting for transfers between devices, exclusive_scan(): got = lax.ppermute(carried + total, axis, perm=[pair])  47.9 us
    pallas_call x2, Pallas kernels, per_device(): pl.pallas_call(functools.partial(main_kernel, width, attended is not None...  41.4 us
    all_to_all x2, waiting for transfers between devices, per_device(): lax.all_to_all(outs[1], ('head', 'sub'), split_axis=axis, concat_axis=0,...  28.8 us
    ppermute x12, starting transfers between devices, exclusive_scan(): got = lax.ppermute(carried + total, axis, perm=[pair])  20.1 us
    unnamed x26, local copies, waits for them, and re-layouts  9.87 us
    all_to_all x2, starting transfers between devices, per_device(): lax.all_to_all(outs[1], ('head', 'sub'), split_axis=axis, concat_axis=0,...  8.53 us
    reshape x3, local copies, waits for them, and re-layouts, per_device(): jnp.stack([p[:, i] for p in parts], 1)  8.01 us
    pallas_call x1, Pallas kernels, per_device(): pl.pallas_call(functools.partial(totals_kernel, width), grid=(groups,), i...  5.13 us
  transfers between devices with their start and end apart: 14, of which 5 were waited for; matrix products, arithmetic and copies ran while one was open for 8% of the time, Pallas kernels for 11%

profile of v13, /device:TPU:0, one launch (start us, length us, event | category | flops | bytes accessed | tf_op | source)
XLA Modules:
  0.0 187.9 jit_solution(8504724194826796604)
XLA Ops:
  0.7 3.6 %copy.36 = bf16[512,16,128]{2,0,1:T(8,128)(2,1)} copy(bf16[512,16,128]{2,1,0:T(8,128)(2,1)} %param.5) | data formatting | bytes 4194304 | tf_op args[1]
  4.3 2.0 %fusion.q_ref = bf16[16,512,128]{2,1,0:T(8,128)(2,1)} fusion(bf16[512,16,128]{2,1,0:T(8,128)(2,1)S(1)} %copy-done.5, f32[512]{0:T(512)S(1)} %multiply_rsqrt_fusion.1), kind=kLoop, calls=%fused_computation.1 | loop fusion | flops 3145728 | bytes 4196352 | tf_op jit(solution)/shard_map/transpose | solution.py:89
  7.2 3.3 %copy_bitcast_fusion.3 = (bf16[16,512,128]{2,1,0:T(8,128)(2,1)}, bf16[16,512,128]{2,1,0:T(8,128)(2,1)}) fusion(bf16[512,16,128]{2,1,0:T(8,128)(2,1)S(1)} %copy-done.6, bf16[512,16,128]{2,1,0:T(8,128)(2,1)S(1)} %copy-done.7), kind=kLoop, calls=%fused_computation.8 | loop fusion | bytes 8388608 | tf_op jit(solution)/shard_map/transpose | solution.py:89
  10.5 5.1 %shard_map.75 = (f32[16,128,128]{2,1,0:T(8,128)}, f32[16,128,128]{2,1,0:T(8,128)}) custom-call(bf16[16,512,128]{2,1,0:T(8,128)(2,1)} %fusion.q_ref, bf16[16,512,128]{2,1,0:T(8,128)(2,1)} %bitcast.22, bf16[16,512,128]{2,1,0:T(8,128)(2,1)} %get-tuple-element.43.v_ref, bf16[16,512,128]{2,1,0:T(8,128)(2,1)} %get-tuple-element.42.d_ref), custom_call_target="tpu_custom_call" | custom-call | tf_op jit(solution)/shard_map/pallas_call | solution.py:96
  15.6 1.2 slice.35
  18.6 5.0 %collective-permute-start.6 = (f32[8,128,128]{2,1,0:T(8,128)S(1)}, f32[8,128,128]{2,1,0:T(8,128)S(1)}, u32[]{:S(2)}, u32[]{:S(2)}) collective-permute-start(f32[8,128,128]{2,1,0:T(8,128)S(1)} %slice.34), channel_id=1, source_target_pairs={{0,4},{1,5},{2,6},{3,7},{16,20},{17,21},{18,22},{19,23}} | collective-permute-start | bytes 1572872 | tf_op jit(solution)/shard_map/ppermute | solution.py:74
  24.4 10.3 %collective-permute-done.6 = f32[8,128,128]{2,1,0:T(8,128)S(1)} collective-permute-done((f32[8,128,128]{2,1,0:T(8,128)S(1)}, f32[8,128,128]{2,1,0:T(8,128)S(1)}, u32[]{:S(2)}, u32[]{:S(2)}) %collective-permute-start.6) | collective-permute-done | bytes 524320 | tf_op jit(solution)/shard_map/ppermute | solution.py:74
  35.6 6.9 %collective-permute-start = (f32[8,128,128]{2,1,0:T(8,128)S(1)}, f32[8,128,128]{2,1,0:T(8,128)S(1)}, u32[]{:S(2)}, u32[]{:S(2)}) collective-permute-start(f32[8,128,128]{2,1,0:T(8,128)S(1)} %get-tuple-element.41), channel_id=1, source_target_pairs={{0,4},{1,5},{2,6},{3,7},{16,20},{17,21},{18,22},{19,23}} | collective-permute-start | bytes 1572872 | tf_op jit(solution)/shard_map/ppermute | solution.py:74
  42.6 1.3 collective-permute-start.11
  44.6 7.8 %collective-permute-done = f32[8,128,128]{2,1,0:T(8,128)S(1)} collective-permute-done((f32[8,128,128]{2,1,0:T(8,128)S(1)}, f32[8,128,128]{2,1,0:T(8,128)S(1)}, u32[]{:S(2)}, u32[]{:S(2)}) %collective-permute-start) | collective-permute-done | bytes 524320 | tf_op jit(solution)/shard_map/ppermute | solution.py:74
  54.0 7.2 %collective-permute-done.11 = f32[8,128,128]{2,1,0:T(8,128)S(1)} collective-permute-done((f32[8,128,128]{2,1,0:T(8,128)S(1)}, f32[8,128,128]{2,1,0:T(8,128)S(1)}, u32[]{:S(2)}, u32[]{:S(2)}) %collective-permute-start.11) | collective-permute-done | bytes 524320 | tf_op jit(solution)/shard_map/ppermute | solution.py:74
  61.2 1.1 add_add_fusion
  64.7 20.7 %shard_map.76 = (bf16[16,512,128]{2,1,0:T(8,128)(2,1)}, bf16[4,3,8,128,128]{4,3,2,1,0:T(8,128)(2,1)}) custom-call(bf16[16,512,128]{2,1,0:T(8,128)(2,1)} %fusion.q_ref, bf16[16,512,128]{2,1,0:T(8,128)(2,1)} %bitcast.23, bf16[16,512,128]{2,1,0:T(8,128)(2,1)} %get-tuple-element.43.v_ref, bf16[16,512,128]{2,1,0:T(8,128)(2,1)} %get-tuple-element.42.d_ref, ...), custom_call_target="tpu_custom_call" | custom-call | tf_op jit(solution)/shard_map/pallas_call | solution.py:142
  85.4 4.6 %all-to-all-start = ((bf16[4,3,8,128,128]{4,3,2,1,0:T(8,128)(2,1)}), bf16[4,3,8,128,128]{4,3,2,1,0:T(8,128)(2,1)}, u32[]{:S(2)}, u32[]{:S(2)}) async-start(bf16[4,3,8,128,128]{4,3,2,1,0:T(8,128)(2,1)} %get-tuple-element.18), calls=%async_computation | async-start | bytes 6291456 | tf_op jit(solution)/shard_map/all_to_all | solution.py:155
  91.1 1.3 collective-permute-start.5
  93.3 22.5 %collective-permute-done.5 = f32[8,128,128]{2,1,0:T(8,128)S(1)} collective-permute-done((f32[8,128,128]{2,1,0:T(8,128)S(1)}, f32[8,128,128]{2,1,0:T(8,128)S(1)}, u32[]{:S(2)}, u32[]{:S(2)}) %collective-permute-start.5) | collective-permute-done | bytes 524320 | tf_op jit(solution)/shard_map/ppermute | solution.py:74
  116.7 20.7 %shard_map.77 = (bf16[16,512,128]{2,1,0:T(8,128)(2,1)}, bf16[4,3,8,128,128]{4,3,2,1,0:T(8,128)(2,1)}) custom-call(bf16[16,512,128]{2,1,0:T(8,128)(2,1)} %fusion.q_ref, bf16[16,512,128]{2,1,0:T(8,128)(2,1)} %bitcast.24, bf16[16,512,128]{2,1,0:T(8,128)(2,1)} %get-tuple-element.43.v_ref, ...), custom_call_target="tpu_custom_call", output_to_operand_aliasing={{0}: (7, {})} | custom-call | tf_op jit(solution)/shard_map/pallas_call | solution.py:142
  137.4 3.9 %all-to-all-start.1 = ((bf16[4,3,8,128,128]{4,3,2,1,0:T(8,128)(2,1)}), bf16[4,3,8,128,128]{4,3,2,1,0:T(8,128)(2,1)S(1)}, u32[]{:S(2)}, u32[]{:S(2)}) async-start(bf16[4,3,8,128,128]{4,3,2,1,0:T(8,128)(2,1)} %get-tuple-element.19), calls=%async_computation.1 | async-start | bytes 6291456 | tf_op jit(solution)/shard_map/all_to_all | solution.py:155
  141.3 4.3 %copy.25 = bf16[512,16,128]{2,1,0:T(8,128)(2,1)} copy(bf16[512,16,128]{2,0,1:T(8,128)(2,1)} %bitcast.28) | data formatting | bytes 4194304
  145.6 3.6 %fusion.1 = (bf16[4,1,8,128,128]{4,3,2,1,0:T(8,128)(2,1)}, bf16[4,1,8,128,128]{4,3,2,1,0:T(8,128)(2,1)}, bf16[4,1,8,128,128]{4,3,2,1,0:T(8,128)(2,1)}) fusion(bf16[4,3,8,128,128]{4,3,2,1,0:T(8,128)(2,1)} %all-to-all-done), kind=kLoop, calls=%fused_computation.25 | loop fusion | bytes 6291456 | tf_op jit(solution)/shard_map/slice | solution.py:163
  149.2 28.8 %all-to-all-done.1 = bf16[4,3,8,128,128]{4,3,2,1,0:T(8,128)(2,1)S(1)} async-done(((bf16[4,3,8,128,128]{4,3,2,1,0:T(8,128)(2,1)}), bf16[4,3,8,128,128]{4,3,2,1,0:T(8,128)(2,1)S(1)}, u32[]{:S(2)}, u32[]{:S(2)}) %all-to-all-start.1) | async-done | bytes 3145760 | tf_op jit(solution)/shard_map/all_to_all | solution.py:155
  179.5 2.7 %copy.33 = bf16[64,128,128]{2,0,1:T(8,128)(2,1)} copy(bf16[64,128,128]{2,1,0:T(8,128)(2,1)S(1)} %bitcast.25) | data formatting | bytes 4194304 | tf_op jit(solution)/shard_map/reshape | solution.py:163
  182.3 2.7 %copy.34 = bf16[64,128,128]{2,0,1:T(8,128)(2,1)} copy(bf16[64,128,128]{2,1,0:T(8,128)(2,1)S(1)} %bitcast.26) | data formatting | bytes 4194304 | tf_op jit(solution)/shard_map/reshape | solution.py:163
  185.2 2.7 %copy.35 = bf16[64,128,128]{2,0,1:T(8,128)(2,1)} copy(bf16[64,128,128]{2,1,0:T(8,128)(2,1)S(1)} %bitcast.27) | data formatting | bytes 4194304 | tf_op jit(solution)/shard_map/reshape | solution.py:163
  (57 shorter events, 13.7 us)
Async XLA Ops:
  0.6 3.6 %copy-start.5 = (bf16[512,16,128]{2,1,0:T(8,128)(2,1)S(1)}, bf16[512,16,128]{2,1,0:T(8,128)(2,1)}, u32[]{:S(2)}) copy-start(bf16[512,16,128]{2,1,0:T(8,128)(2,1)} %param.4) | copy-start | bytes 6291460
  4.3 2.0 %copy-start.6 = (bf16[512,16,128]{2,1,0:T(8,128)(2,1)S(1)}, bf16[512,16,128]{2,1,0:T(8,128)(2,1)}, u32[]{:S(2)}) copy-start(bf16[512,16,128]{2,1,0:T(8,128)(2,1)} %param.7) | copy-start | bytes 6291460
  4.3 3.0 %copy-start.7 = (bf16[512,16,128]{2,1,0:T(8,128)(2,1)S(1)}, bf16[512,16,128]{2,1,0:T(8,128)(2,1)}, u32[]{:S(2)}) copy-start(bf16[512,16,128]{2,1,0:T(8,128)(2,1)} %param.6) | copy-start | bytes 6291460
  15.6 8.0 %copy-start = (f32[16,128,128]{2,1,0:T(8,128)S(1)}, f32[16,128,128]{2,1,0:T(8,128)}, u32[]{:S(2)}) copy-start(f32[16,128,128]{2,1,0:T(8,128)} %get-tuple-element.13) | copy-start | bytes 3145732
  15.6 19.1 %copy-start.1 = (f32[16,128,128]{2,1,0:T(8,128)S(1)}, f32[16,128,128]{2,1,0:T(8,128)}, u32[]{:S(2)}) copy-start(f32[16,128,128]{2,1,0:T(8,128)} %get-tuple-element.12) | copy-start | bytes 3145732
  16.9 6.8 %collective-permute-start.9 = (f32[8,128,128]{2,1,0:T(8,128)S(1)}, f32[8,128,128]{2,1,0:T(8,128)S(1)}, u32[]{:S(2)}, u32[]{:S(2)}) collective-permute-start(f32[8,128,128]{2,1,0:T(8,128)S(1)} %slice.35), channel_id=1, source_target_pairs={{12,8},{13,9},{14,10},{15,11},{28,24},{29,25},{30,26},{31,27}} | collective-permute-start | bytes 1572872 | tf_op jit(solution)/shard_map/ppermute | solution.py:74
  18.6 16.1 %collective-permute-start.6 = (f32[8,128,128]{2,1,0:T(8,128)S(1)}, f32[8,128,128]{2,1,0:T(8,128)S(1)}, u32[]{:S(2)}, u32[]{:S(2)}) collective-permute-start(f32[8,128,128]{2,1,0:T(8,128)S(1)} %slice.34), channel_id=1, source_target_pairs={{0,4},{1,5},{2,6},{3,7},{16,20},{17,21},{18,22},{19,23}} | collective-permute-start | bytes 1572872 | tf_op jit(solution)/shard_map/ppermute | solution.py:74
  23.7 18.8 %collective-permute-start.10 = (f32[8,128,128]{2,1,0:T(8,128)S(1)}, f32[8,128,128]{2,1,0:T(8,128)S(1)}, u32[]{:S(2)}, u32[]{:S(2)}) collective-permute-start(f32[8,128,128]{2,1,0:T(8,128)S(1)} %slice_add_fusion.5), channel_id=1, source_target_pairs={{8,4},{9,5},{10,6},{11,7},{24,20},{25,21},{26,22},{27,23}} | collective-permute-start | bytes 1572872 | tf_op jit(solution)/shard_map/ppermute | solution.py:74
  34.9 9.7 %collective-permute-start.7 = (f32[8,128,128]{2,1,0:T(8,128)S(1)}, f32[8,128,128]{2,1,0:T(8,128)S(1)}, u32[]{:S(2)}, u32[]{:S(2)}) collective-permute-start(f32[8,128,128]{2,1,0:T(8,128)S(1)} %get-tuple-element.40), channel_id=1, source_target_pairs={{4,8},{5,9},{6,10},{7,11},{20,24},{21,25},{22,26},{23,27}} | collective-permute-start | bytes 1572872 | tf_op jit(solution)/shard_map/ppermute | solution.py:74
  35.6 16.9 %collective-permute-start = (f32[8,128,128]{2,1,0:T(8,128)S(1)}, f32[8,128,128]{2,1,0:T(8,128)S(1)}, u32[]{:S(2)}, u32[]{:S(2)}) collective-permute-start(f32[8,128,128]{2,1,0:T(8,128)S(1)} %get-tuple-element.41), channel_id=1, source_target_pairs={{0,4},{1,5},{2,6},{3,7},{16,20},{17,21},{18,22},{19,23}} | collective-permute-start | bytes 1572872 | tf_op jit(solution)/shard_map/ppermute | solution.py:74
  42.6 18.6 %collective-permute-start.11 = (f32[8,128,128]{2,1,0:T(8,128)S(1)}, f32[8,128,128]{2,1,0:T(8,128)S(1)}, u32[]{:S(2)}, u32[]{:S(2)}) collective-permute-start(f32[8,128,128]{2,1,0:T(8,128)S(1)} %get-tuple-element.36), channel_id=1, source_target_pairs={{4,0},{5,1},{6,2},{7,3},{20,16},{21,17},{22,18},{23,19}} | collective-permute-start | bytes 1572872 | tf_op jit(solution)/shard_map/ppermute | solution.py:74
  43.9 17.3 %collective-permute-start.3 = (f32[8,128,128]{2,1,0:T(8,128)S(1)}, f32[8,128,128]{2,1,0:T(8,128)S(1)}, u32[]{:S(2)}, u32[]{:S(2)}) collective-permute-start(f32[8,128,128]{2,1,0:T(8,128)S(1)} %get-tuple-element.37), channel_id=1, source_target_pairs={{12,8},{13,9},{14,10},{15,11},{28,24},{29,25},{30,26},{31,27}} | collective-permute-start | bytes 1572872 | tf_op jit(solution)/shard_map/ppermute | solution.py:74
  52.6 11.2 %collective-permute-start.8 = (f32[8,128,128]{2,1,0:T(8,128)S(1)}, f32[8,128,128]{2,1,0:T(8,128)S(1)}, u32[]{:S(2)}, u32[]{:S(2)}) collective-permute-start(f32[8,128,128]{2,1,0:T(8,128)S(1)} %get-tuple-element.38), channel_id=1, source_target_pairs={{8,12},{9,13},{10,14},{11,15},{24,28},{25,29},{26,30},{27,31}} | collective-permute-start | bytes 1572872 | tf_op jit(solution)/shard_map/ppermute | solution.py:74
  53.3 11.4 %collective-permute-start.1 = (f32[8,128,128]{2,1,0:T(8,128)S(1)}, f32[8,128,128]{2,1,0:T(8,128)S(1)}, u32[]{:S(2)}, u32[]{:S(2)}) collective-permute-start(f32[8,128,128]{2,1,0:T(8,128)S(1)} %get-tuple-element.39), channel_id=1, source_target_pairs={{4,8},{5,9},{6,10},{7,11},{20,24},{21,25},{22,26},{23,27}} | collective-permute-start | bytes 1572872 | tf_op jit(solution)/shard_map/ppermute | solution.py:74
  62.3 2.4 %collective-permute-start.4 = (f32[8,128,128]{2,1,0:T(8,128)S(1)}, f32[8,128,128]{2,1,0:T(8,128)S(1)}, u32[]{:S(2)}, u32[]{:S(2)}) collective-permute-start(f32[8,128,128]{2,1,0:T(8,128)S(1)} %get-tuple-element.35), channel_id=1, source_target_pairs={{8,4},{9,5},{10,6},{11,7},{24,20},{25,21},{26,22},{27,23}} | collective-permute-start | bytes 1572872 | tf_op jit(solution)/shard_map/ppermute | solution.py:74
  85.4 52.0 %all-to-all-start = ((bf16[4,3,8,128,128]{4,3,2,1,0:T(8,128)(2,1)}), bf16[4,3,8,128,128]{4,3,2,1,0:T(8,128)(2,1)}, u32[]{:S(2)}, u32[]{:S(2)}) async-start(bf16[4,3,8,128,128]{4,3,2,1,0:T(8,128)(2,1)} %get-tuple-element.18), calls=%async_computation | async-start | bytes 6291456 | tf_op jit(solution)/shard_map/all_to_all | solution.py:155
  90.1 2.3 %copy-start.9 = (f32[8,128,128]{2,1,0:T(8,128)S(1)}, f32[8,128,128]{2,1,0:T(8,128)}, u32[]{:S(2)}) copy-start(f32[8,128,128]{2,1,0:T(8,128)} %copy-done.8) | copy-start | bytes 1572868
  90.2 25.6 %copy-start.11 = (f32[8,128,128]{2,1,0:T(8,128)S(1)}, f32[8,128,128]{2,1,0:T(8,128)}, u32[]{:S(2)}) copy-start(f32[8,128,128]{2,1,0:T(8,128)} %copy-done.10) | copy-start | bytes 1572868
  90.2 2.2 %collective-permute-start.2 = (f32[8,128,128]{2,1,0:T(8,128)S(1)}, f32[8,128,128]{2,1,0:T(8,128)S(1)}, u32[]{:S(2)}, u32[]{:S(2)}) collective-permute-start(f32[8,128,128]{2,1,0:T(8,128)S(1)} %slice_add_fusion.2), channel_id=1, source_target_pairs={{8,12},{9,13},{10,14},{11,15},{24,28},{25,29},{26,30},{27,31}} | collective-permute-start | bytes 1572872 | tf_op jit(solution)/shard_map/ppermute | solution.py:74
  91.1 24.7 %collective-permute-start.5 = (f32[8,128,128]{2,1,0:T(8,128)S(1)}, f32[8,128,128]{2,1,0:T(8,128)S(1)}, u32[]{:S(2)}, u32[]{:S(2)}) collective-permute-start(f32[8,128,128]{2,1,0:T(8,128)S(1)} %slice_add_fusion.6), channel_id=1, source_target_pairs={{4,0},{5,1},{6,2},{7,3},{20,16},{21,17},{22,18},{23,19}} | collective-permute-start | bytes 1572872 | tf_op jit(solution)/shard_map/ppermute | solution.py:74
  137.4 40.6 %all-to-all-start.1 = ((bf16[4,3,8,128,128]{4,3,2,1,0:T(8,128)(2,1)}), bf16[4,3,8,128,128]{4,3,2,1,0:T(8,128)(2,1)S(1)}, u32[]{:S(2)}, u32[]{:S(2)}) async-start(bf16[4,3,8,128,128]{4,3,2,1,0:T(8,128)(2,1)} %get-tuple-element.19), calls=%async_computation.1 | async-start | bytes 6291456 | tf_op jit(solution)/shard_map/all_to_all | solution.py:155
  178.0 1.2 copy-start.4
  179.4 2.7 %copy-start.3 = (bf16[4,1,8,128,128]{4,3,2,1,0:T(8,128)(2,1)S(1)}, bf16[4,1,8,128,128]{4,3,2,1,0:T(8,128)(2,1)}, u32[]{:S(2)}) copy-start(bf16[4,1,8,128,128]{4,3,2,1,0:T(8,128)(2,1)} %get-tuple-element.29) | copy-start | bytes 3145732
  182.3 2.7 %copy-start.2 = (bf16[4,1,8,128,128]{4,3,2,1,0:T(8,128)(2,1)S(1)}, bf16[4,1,8,128,128]{4,3,2,1,0:T(8,128)(2,1)}, u32[]{:S(2)}) copy-start(bf16[4,1,8,128,128]{4,3,2,1,0:T(8,128)(2,1)} %get-tuple-element.30) | copy-start | bytes 3145732
  (2 other events, 1.9 us)

commit v14 on v13

--- a/solution.py
+++ b/solution.py
@@ -115,10 +115,10 @@
         after, after_hops = exclusive_scan(adj_total[sel], "seq", seq_count, True)
         chains.append([before, after + adj_total[sel], before_hops, after_hops])
     for g in range(groups - 1):
-        if seq_count >= 3:
+        if seq_count >= 2:
             nxt = chains[g + 1]
             chains[g][0], chains[g][1], _, _ = lax.optimization_barrier(
-                (chains[g][0], chains[g][1], nxt[2][seq_count - 3], nxt[3][seq_count - 3])
+                (chains[g][0], chains[g][1], nxt[2][seq_count - 2], nxt[3][seq_count - 2])
             )
     for g in range(groups):
         before, rest = chains[g][0], chains[g][1]

time: 189 us -> 221 us (1.17)
  blocking collectives: 0 us -> 42.3 us
  starting transfers between devices: 28.6 us -> 23.8 us
  waiting for transfers between devices: 76.8 us -> 74 us
    all_to_all x0 -> x1, blocking collectives: none -> 42.3 us  [per_device(): lax.all_to_all(outs[1], ('head', 'sub'), split_axis=axis, concat_axis=0,...]
    all_to_all x2 -> x1, starting transfers between devices: 8.53 us -> 3.88 us  [per_device(): lax.all_to_all(outs[1], ('head', 'sub'), split_axis=axis, concat_axis=0,...]
    ppermute x12, waiting for transfers between devices: 47.9 us -> 43.5 us  [exclusive_scan(): got = lax.ppermute(carried + total, axis, perm=[pair])]
    all_to_all x2 -> x1, waiting for transfers between devices: 28.8 us -> 30.5 us  [per_device(): lax.all_to_all(outs[1], ('head', 'sub'), split_axis=axis, concat_axis=0,...]
    unnamed x26 -> x20, local copies, waits for them, and re-layouts: 9.87 us -> 10 us
  transfers between devices with their start and end apart: 14 -> 13, of which waited for: 5 -> 5; matrix products, arithmetic and copies ran while one was open for 8% -> 5% of each run, Pallas kernels for 11% -> 0%
where the time goes in v14:
time: 221 us
  waiting for transfers between devices  74 us (33%)
  Pallas kernels  46.5 us (21%)
  blocking collectives  42.3 us (19%)
  local copies, waits for them, and re-layouts  25.6 us (12%)
  starting transfers between devices  23.8 us (11%)
  other arithmetic  7.66 us (3%)
    ppermute x12, waiting for transfers between devices, exclusive_scan(): got = lax.ppermute(carried + total, axis, perm=[pair])  43.5 us
    all_to_all x1, blocking collectives, per_device(): lax.all_to_all(outs[1], ('head', 'sub'), split_axis=axis, concat_axis=0,...  42.3 us
    pallas_call x2, Pallas kernels, per_device(): pl.pallas_call(functools.partial(main_kernel, width, attended is not None...  41.4 us
    all_to_all x1, waiting for transfers between devices, per_device(): lax.all_to_all(outs[1], ('head', 'sub'), split_axis=axis, concat_axis=0,...  30.5 us
    ppermute x12, starting transfers between devices, exclusive_scan(): got = lax.ppermute(carried + total, axis, perm=[pair])  19.9 us
    unnamed x20, local copies, waits for them, and re-layouts  10 us
    reshape x3, local copies, waits for them, and re-layouts, per_device(): jnp.stack([p[:, i] for p in parts], 1)  8.01 us
    pallas_call x1, Pallas kernels, per_device(): pl.pallas_call(functools.partial(totals_kernel, width), grid=(groups,), i...  5.15 us
  transfers between devices with their start and end apart: 13, of which 5 were waited for; matrix products, arithmetic and copies ran while one was open for 5% of the time, Pallas kernels for 0%

profile of v14, /device:TPU:0, one launch (start us, length us, event | category | flops | bytes accessed | tf_op | source)
XLA Modules:
  0.0 220.8 jit_solution(13935487539634298596)
XLA Ops:
  0.7 3.6 %copy.36 = bf16[512,16,128]{2,0,1:T(8,128)(2,1)} copy(bf16[512,16,128]{2,1,0:T(8,128)(2,1)} %param.5) | data formatting | bytes 4194304 | tf_op args[1]
  4.3 2.0 fusion.q_ref
  7.2 3.3 %copy_bitcast_fusion.3 = (bf16[16,512,128]{2,1,0:T(8,128)(2,1)}, bf16[16,512,128]{2,1,0:T(8,128)(2,1)}) fusion(bf16[512,16,128]{2,1,0:T(8,128)(2,1)S(1)} %copy-done.7, bf16[512,16,128]{2,1,0:T(8,128)(2,1)S(1)} %copy-done.8), kind=kLoop, calls=%fused_computation.8 | loop fusion | bytes 8388608 | tf_op jit(solution)/shard_map/transpose | solution.py:89
  10.5 5.1 %shard_map.75 = (f32[16,128,128]{2,1,0:T(8,128)}, f32[16,128,128]{2,1,0:T(8,128)}) custom-call(bf16[16,512,128]{2,1,0:T(8,128)(2,1)} %fusion.q_ref, bf16[16,512,128]{2,1,0:T(8,128)(2,1)} %bitcast.22, bf16[16,512,128]{2,1,0:T(8,128)(2,1)} %get-tuple-element.43.v_ref, bf16[16,512,128]{2,1,0:T(8,128)(2,1)} %get-tuple-element.42.d_ref), custom_call_target="tpu_custom_call" | custom-call | tf_op jit(solution)/shard_map/pallas_call | solution.py:96
  15.7 1.2 slice.35
  17.6 1.1 slice.34
  18.7 5.0 %collective-permute-start.6 = (f32[8,128,128]{2,1,0:T(8,128)S(1)}, f32[8,128,128]{2,1,0:T(8,128)S(1)}, u32[]{:S(2)}, u32[]{:S(2)}) collective-permute-start(f32[8,128,128]{2,1,0:T(8,128)S(1)} %slice.34), channel_id=1, source_target_pairs={{0,4},{1,5},{2,6},{3,7},{16,20},{17,21},{18,22},{19,23}} | collective-permute-start | bytes 1572872 | tf_op jit(solution)/shard_map/ppermute | solution.py:74
  24.4 10.3 %collective-permute-done.6 = f32[8,128,128]{2,1,0:T(8,128)S(1)} collective-permute-done((f32[8,128,128]{2,1,0:T(8,128)S(1)}, f32[8,128,128]{2,1,0:T(8,128)S(1)}, u32[]{:S(2)}, u32[]{:S(2)}) %collective-permute-start.6) | collective-permute-done | bytes 524320 | tf_op jit(solution)/shard_map/ppermute | solution.py:74
  35.6 6.9 %collective-permute-start = (f32[8,128,128]{2,1,0:T(8,128)S(1)}, f32[8,128,128]{2,1,0:T(8,128)S(1)}, u32[]{:S(2)}, u32[]{:S(2)}) collective-permute-start(f32[8,128,128]{2,1,0:T(8,128)S(1)} %get-tuple-element.41), channel_id=1, source_target_pairs={{0,4},{1,5},{2,6},{3,7},{16,20},{17,21},{18,22},{19,23}} | collective-permute-start | bytes 1572872 | tf_op jit(solution)/shard_map/ppermute | solution.py:74
  42.6 1.3 collective-permute-start.11
  44.6 7.8 %collective-permute-done = f32[8,128,128]{2,1,0:T(8,128)S(1)} collective-permute-done((f32[8,128,128]{2,1,0:T(8,128)S(1)}, f32[8,128,128]{2,1,0:T(8,128)S(1)}, u32[]{:S(2)}, u32[]{:S(2)}) %collective-permute-start) | collective-permute-done | bytes 524320 | tf_op jit(solution)/shard_map/ppermute | solution.py:74
  53.3 8.0 %collective-permute-done.11 = f32[8,128,128]{2,1,0:T(8,128)S(1)} collective-permute-done((f32[8,128,128]{2,1,0:T(8,128)S(1)}, f32[8,128,128]{2,1,0:T(8,128)S(1)}, u32[]{:S(2)}, u32[]{:S(2)}) %collective-permute-start.11) | collective-permute-done | bytes 524320 | tf_op jit(solution)/shard_map/ppermute | solution.py:74
  65.3 1.3 collective-permute-start.5
  68.4 17.3 %collective-permute-done.5 = f32[8,128,128]{2,1,0:T(8,128)S(1)} collective-permute-done((f32[8,128,128]{2,1,0:T(8,128)S(1)}, f32[8,128,128]{2,1,0:T(8,128)S(1)}, u32[]{:S(2)}, u32[]{:S(2)}) %collective-permute-start.5) | collective-permute-done | bytes 524320 | tf_op jit(solution)/shard_map/ppermute | solution.py:74
  85.8 20.7 %shard_map.76 = (bf16[16,512,128]{2,1,0:T(8,128)(2,1)}, bf16[4,3,8,128,128]{4,3,2,1,0:T(8,128)(2,1)}) custom-call(bf16[16,512,128]{2,1,0:T(8,128)(2,1)} %fusion.q_ref, bf16[16,512,128]{2,1,0:T(8,128)(2,1)} %bitcast.23, bf16[16,512,128]{2,1,0:T(8,128)(2,1)} %get-tuple-element.43.v_ref, bf16[16,512,128]{2,1,0:T(8,128)(2,1)} %get-tuple-element.42.d_ref, ...), custom_call_target="tpu_custom_call" | custom-call | tf_op jit(solution)/shard_map/pallas_call | solution.py:142
  107.4 20.7 %shard_map.77 = (bf16[16,512,128]{2,1,0:T(8,128)(2,1)}, bf16[4,3,8,128,128]{4,3,2,1,0:T(8,128)(2,1)}) custom-call(bf16[16,512,128]{2,1,0:T(8,128)(2,1)} %fusion.q_ref, bf16[16,512,128]{2,1,0:T(8,128)(2,1)} %bitcast.24, bf16[16,512,128]{2,1,0:T(8,128)(2,1)} %get-tuple-element.43.v_ref, ...), custom_call_target="tpu_custom_call", output_to_operand_aliasing={{0}: (7, {})} | custom-call | tf_op jit(solution)/shard_map/pallas_call | solution.py:142
  128.0 42.3 %all_to_all.10 = bf16[4,3,8,128,128]{4,3,2,1,0:T(8,128)(2,1)} all-to-all(bf16[4,3,8,128,128]{4,3,2,1,0:T(8,128)(2,1)} %get-tuple-element.19), channel_id=1, replica_groups=mesh['grp'=2,'seq'=4,'head'=2,'sub'=2] {'head','sub'}, dimensions={0} | all-to-all | bytes 6291456 | tf_op jit(solution)/shard_map/all_to_all | solution.py:155
  170.3 3.9 %all-to-all-start = ((bf16[4,3,8,128,128]{4,3,2,1,0:T(8,128)(2,1)}), bf16[4,3,8,128,128]{4,3,2,1,0:T(8,128)(2,1)S(1)}, u32[]{:S(2)}, u32[]{:S(2)}) async-start(bf16[4,3,8,128,128]{4,3,2,1,0:T(8,128)(2,1)} %get-tuple-element.18), calls=%async_computation | async-start | bytes 6291456 | tf_op jit(solution)/shard_map/all_to_all | solution.py:155
  174.2 4.4 %copy.25 = bf16[512,16,128]{2,1,0:T(8,128)(2,1)} copy(bf16[512,16,128]{2,0,1:T(8,128)(2,1)} %bitcast.28) | data formatting | bytes 4194304
  178.6 1.8 fusion.2
  180.4 30.5 %all-to-all-done = bf16[4,3,8,128,128]{4,3,2,1,0:T(8,128)(2,1)S(1)} async-done(((bf16[4,3,8,128,128]{4,3,2,1,0:T(8,128)(2,1)}), bf16[4,3,8,128,128]{4,3,2,1,0:T(8,128)(2,1)S(1)}, u32[]{:S(2)}, u32[]{:S(2)}) %all-to-all-start) | async-done | bytes 3145760 | tf_op jit(solution)/shard_map/all_to_all | solution.py:155
  212.3 2.7 %copy.33 = bf16[64,128,128]{2,0,1:T(8,128)(2,1)} copy(bf16[64,128,128]{2,1,0:T(8,128)(2,1)S(1)} %bitcast.25) | data formatting | bytes 4194304 | tf_op jit(solution)/shard_map/reshape | solution.py:163
  215.2 2.7 %copy.34 = bf16[64,128,128]{2,0,1:T(8,128)(2,1)} copy(bf16[64,128,128]{2,1,0:T(8,128)(2,1)S(1)} %bitcast.26) | data formatting | bytes 4194304 | tf_op jit(solution)/shard_map/reshape | solution.py:163
  218.1 2.7 %copy.35 = bf16[64,128,128]{2,0,1:T(8,128)(2,1)} copy(bf16[64,128,128]{2,1,0:T(8,128)(2,1)S(1)} %bitcast.27) | data formatting | bytes 4194304 | tf_op jit(solution)/shard_map/reshape | solution.py:163
  (50 shorter events, 13.4 us)
Async XLA Ops:
  0.6 3.6 %copy-start.6 = (bf16[512,16,128]{2,1,0:T(8,128)(2,1)S(1)}, bf16[512,16,128]{2,1,0:T(8,128)(2,1)}, u32[]{:S(2)}) copy-start(bf16[512,16,128]{2,1,0:T(8,128)(2,1)} %param.4) | copy-start | bytes 6291460
  4.3 2.0 copy-start.7
  4.3 3.0 %copy-start.8 = (bf16[512,16,128]{2,1,0:T(8,128)(2,1)S(1)}, bf16[512,16,128]{2,1,0:T(8,128)(2,1)}, u32[]{:S(2)}) copy-start(bf16[512,16,128]{2,1,0:T(8,128)(2,1)} %param.6) | copy-start | bytes 6291460
  15.7 8.0 %copy-start = (f32[16,128,128]{2,1,0:T(8,128)S(1)}, f32[16,128,128]{2,1,0:T(8,128)}, u32[]{:S(2)}) copy-start(f32[16,128,128]{2,1,0:T(8,128)} %get-tuple-element.13) | copy-start | bytes 3145732
  15.7 19.1 %copy-start.2 = (f32[16,128,128]{2,1,0:T(8,128)S(1)}, f32[16,128,128]{2,1,0:T(8,128)}, u32[]{:S(2)}) copy-start(f32[16,128,128]{2,1,0:T(8,128)} %get-tuple-element.12) | copy-start | bytes 3145732
  16.9 6.8 %collective-permute-start.9 = (f32[8,128,128]{2,1,0:T(8,128)S(1)}, f32[8,128,128]{2,1,0:T(8,128)S(1)}, u32[]{:S(2)}, u32[]{:S(2)}) collective-permute-start(f32[8,128,128]{2,1,0:T(8,128)S(1)} %slice.35), channel_id=1, source_target_pairs={{12,8},{13,9},{14,10},{15,11},{28,24},{29,25},{30,26},{31,27}} | collective-permute-start | bytes 1572872 | tf_op jit(solution)/shard_map/ppermute | solution.py:74
  18.7 16.1 %collective-permute-start.6 = (f32[8,128,128]{2,1,0:T(8,128)S(1)}, f32[8,128,128]{2,1,0:T(8,128)S(1)}, u32[]{:S(2)}, u32[]{:S(2)}) collective-permute-start(f32[8,128,128]{2,1,0:T(8,128)S(1)} %slice.34), channel_id=1, source_target_pairs={{0,4},{1,5},{2,6},{3,7},{16,20},{17,21},{18,22},{19,23}} | collective-permute-start | bytes 1572872 | tf_op jit(solution)/shard_map/ppermute | solution.py:74
  23.7 18.7 %collective-permute-start.10 = (f32[8,128,128]{2,1,0:T(8,128)S(1)}, f32[8,128,128]{2,1,0:T(8,128)S(1)}, u32[]{:S(2)}, u32[]{:S(2)}) collective-permute-start(f32[8,128,128]{2,1,0:T(8,128)S(1)} %slice_add_fusion.5), channel_id=1, source_target_pairs={{8,4},{9,5},{10,6},{11,7},{24,20},{25,21},{26,22},{27,23}} | collective-permute-start | bytes 1572872 | tf_op jit(solution)/shard_map/ppermute | solution.py:74
  34.9 9.7 %collective-permute-start.7 = (f32[8,128,128]{2,1,0:T(8,128)S(1)}, f32[8,128,128]{2,1,0:T(8,128)S(1)}, u32[]{:S(2)}, u32[]{:S(2)}) collective-permute-start(f32[8,128,128]{2,1,0:T(8,128)S(1)} %get-tuple-element.40), channel_id=1, source_target_pairs={{4,8},{5,9},{6,10},{7,11},{20,24},{21,25},{22,26},{23,27}} | collective-permute-start | bytes 1572872 | tf_op jit(solution)/shard_map/ppermute | solution.py:74
  35.6 16.9 %collective-permute-start = (f32[8,128,128]{2,1,0:T(8,128)S(1)}, f32[8,128,128]{2,1,0:T(8,128)S(1)}, u32[]{:S(2)}, u32[]{:S(2)}) collective-permute-start(f32[8,128,128]{2,1,0:T(8,128)S(1)} %get-tuple-element.41), channel_id=1, source_target_pairs={{0,4},{1,5},{2,6},{3,7},{16,20},{17,21},{18,22},{19,23}} | collective-permute-start | bytes 1572872 | tf_op jit(solution)/shard_map/ppermute | solution.py:74
  42.6 18.6 %collective-permute-start.11 = (f32[8,128,128]{2,1,0:T(8,128)S(1)}, f32[8,128,128]{2,1,0:T(8,128)S(1)}, u32[]{:S(2)}, u32[]{:S(2)}) collective-permute-start(f32[8,128,128]{2,1,0:T(8,128)S(1)} %get-tuple-element.36), channel_id=1, source_target_pairs={{4,0},{5,1},{6,2},{7,3},{20,16},{21,17},{22,18},{23,19}} | collective-permute-start | bytes 1572872 | tf_op jit(solution)/shard_map/ppermute | solution.py:74
  43.9 17.3 %collective-permute-start.3 = (f32[8,128,128]{2,1,0:T(8,128)S(1)}, f32[8,128,128]{2,1,0:T(8,128)S(1)}, u32[]{:S(2)}, u32[]{:S(2)}) collective-permute-start(f32[8,128,128]{2,1,0:T(8,128)S(1)} %get-tuple-element.37), channel_id=1, source_target_pairs={{12,8},{13,9},{14,10},{15,11},{28,24},{29,25},{30,26},{31,27}} | collective-permute-start | bytes 1572872 | tf_op jit(solution)/shard_map/ppermute | solution.py:74
  52.6 11.9 %collective-permute-start.1 = (f32[8,128,128]{2,1,0:T(8,128)S(1)}, f32[8,128,128]{2,1,0:T(8,128)S(1)}, u32[]{:S(2)}, u32[]{:S(2)}) collective-permute-start(f32[8,128,128]{2,1,0:T(8,128)S(1)} %get-tuple-element.39), channel_id=1, source_target_pairs={{4,8},{5,9},{6,10},{7,11},{20,24},{21,25},{22,26},{23,27}} | collective-permute-start | bytes 1572872 | tf_op jit(solution)/shard_map/ppermute | solution.py:74
  62.3 3.0 %collective-permute-start.4 = (f32[8,128,128]{2,1,0:T(8,128)S(1)}, f32[8,128,128]{2,1,0:T(8,128)S(1)}, u32[]{:S(2)}, u32[]{:S(2)}) collective-permute-start(f32[8,128,128]{2,1,0:T(8,128)S(1)} %get-tuple-element.35), channel_id=1, source_target_pairs={{8,4},{9,5},{10,6},{11,7},{24,20},{25,21},{26,22},{27,23}} | collective-permute-start | bytes 1572872 | tf_op jit(solution)/shard_map/ppermute | solution.py:74
  63.7 2.8 %collective-permute-start.8 = (f32[8,128,128]{2,1,0:T(8,128)S(1)}, f32[8,128,128]{2,1,0:T(8,128)S(1)}, u32[]{:S(2)}, u32[]{:S(2)}) collective-permute-start(f32[8,128,128]{2,1,0:T(8,128)S(1)} %get-tuple-element.38), channel_id=1, source_target_pairs={{8,12},{9,13},{10,14},{11,15},{24,28},{25,29},{26,30},{27,31}} | collective-permute-start | bytes 1572872 | tf_op jit(solution)/shard_map/ppermute | solution.py:74
  64.5 3.0 %collective-permute-start.2 = (f32[8,128,128]{2,1,0:T(8,128)S(1)}, f32[8,128,128]{2,1,0:T(8,128)S(1)}, u32[]{:S(2)}, u32[]{:S(2)}) collective-permute-start(f32[8,128,128]{2,1,0:T(8,128)S(1)} %slice_add_fusion.2), channel_id=1, source_target_pairs={{8,12},{9,13},{10,14},{11,15},{24,28},{25,29},{26,30},{27,31}} | collective-permute-start | bytes 1572872 | tf_op jit(solution)/shard_map/ppermute | solution.py:74
  65.3 20.5 %collective-permute-start.5 = (f32[8,128,128]{2,1,0:T(8,128)S(1)}, f32[8,128,128]{2,1,0:T(8,128)S(1)}, u32[]{:S(2)}, u32[]{:S(2)}) collective-permute-start(f32[8,128,128]{2,1,0:T(8,128)S(1)} %slice_add_fusion.6), channel_id=1, source_target_pairs={{4,0},{5,1},{6,2},{7,3},{20,16},{21,17},{22,18},{23,19}} | collective-permute-start | bytes 1572872 | tf_op jit(solution)/shard_map/ppermute | solution.py:74
  170.3 40.6 %all-to-all-start = ((bf16[4,3,8,128,128]{4,3,2,1,0:T(8,128)(2,1)}), bf16[4,3,8,128,128]{4,3,2,1,0:T(8,128)(2,1)S(1)}, u32[]{:S(2)}, u32[]{:S(2)}) async-start(bf16[4,3,8,128,128]{4,3,2,1,0:T(8,128)(2,1)} %get-tuple-element.18), calls=%async_computation | async-start | bytes 6291456 | tf_op jit(solution)/shard_map/all_to_all | solution.py:155
  174.2 4.4 %copy-start.1 = (bf16[4,3,8,128,128]{4,3,2,1,0:T(8,128)(2,1)S(1)}, bf16[4,3,8,128,128]{4,3,2,1,0:T(8,128)(2,1)}, u32[]{:S(2)}) copy-start(bf16[4,3,8,128,128]{4,3,2,1,0:T(8,128)(2,1)} %all_to_all.10) | copy-start | bytes 9437188
  210.9 1.2 copy-start.5
  212.3 2.7 %copy-start.4 = (bf16[4,1,8,128,128]{4,3,2,1,0:T(8,128)(2,1)S(1)}, bf16[4,1,8,128,128]{4,3,2,1,0:T(8,128)(2,1)}, u32[]{:S(2)}) copy-start(bf16[4,1,8,128,128]{4,3,2,1,0:T(8,128)(2,1)} %get-tuple-element.32) | copy-start | bytes 3145732
  215.2 2.7 %copy-start.3 = (bf16[4,1,8,128,128]{4,3,2,1,0:T(8,128)(2,1)S(1)}, bf16[4,1,8,128,128]{4,3,2,1,0:T(8,128)(2,1)}, u32[]{:S(2)}) copy-start(bf16[4,1,8,128,128]{4,3,2,1,0:T(8,128)(2,1)} %get-tuple-element.33) | copy-start | bytes 3145732

commit v15 on v13

--- a/solution.py
+++ b/solution.py
@@ -88,7 +88,7 @@
     scaled = (queries.astype(F32) * factor[:, :, None]).astype(BF16)
     qh, kh, vh, dh = (jnp.transpose(x, (1, 0, 2)) for x in (scaled, key_rows, value_rows, out_adjoint))
 
-    width = 8 if heads % 8 == 0 and heads > 8 else heads
+    width = 4 if heads % 4 == 0 and heads > 4 else heads
     groups = heads // width
     state_shape = jax.ShapeDtypeStruct((heads, head_dim, head_dim), F32)
     rows = pl.BlockSpec((width, tok_dev, head_dim), lambda g: (g, 0, 0))

time: 189 us -> 225 us (1.19)
  blocking collectives: 0 us -> 24.5 us
  waiting for transfers between devices: 76.8 us -> 54.2 us
  starting transfers between devices: 28.6 us -> 45.6 us
  other arithmetic: 7.74 us -> 16.5 us
  Pallas kernels: 46.5 us -> 54 us
    all_to_all x0 -> x1, blocking collectives: none -> 24.5 us  [per_device(): lax.all_to_all(outs[1], ('head', 'sub'), split_axis=axis, concat_axis=0,...]
    all_to_all x2 -> x3, waiting for transfers between devices: 28.8 us -> 12.7 us  [per_device(): lax.all_to_all(outs[1], ('head', 'sub'), split_axis=axis, concat_axis=0,...]
    ppermute x12 -> x24, starting transfers between devices: 20.1 us -> 32.9 us  [exclusive_scan(): got = lax.ppermute(carried + total, axis, perm=[pair])]
    pallas_call x2 -> x4, Pallas kernels: 41.4 us -> 48.1 us  [per_device(): pl.pallas_call(functools.partial(main_kernel, width, attended is not None...]
    ppermute x12 -> x24, waiting for transfers between devices: 47.9 us -> 41.5 us  [exclusive_scan(): got = lax.ppermute(carried + total, axis, perm=[pair])]
    all_to_all x2 -> x3, starting transfers between devices: 8.53 us -> 12.7 us  [per_device(): lax.all_to_all(outs[1], ('head', 'sub'), split_axis=axis, concat_axis=0,...]
    add x2 -> x4, other arithmetic: 1.8 us -> 5.94 us  [exclusive_scan(): acc = acc + got]
    add x6, other arithmetic: 0.56 us -> 4.21 us  [exclusive_scan(): got = lax.ppermute(carried + total, axis, perm=[pair])]
  transfers between devices with their start and end apart: 14 -> 27, of which waited for: 5 -> 8; matrix products, arithmetic and copies ran while one was open for 8% -> 9% of each run, Pallas kernels for 11% -> 21%
where the time goes in v15:
time: 225 us; the launch traced here: 224 us
  waiting for transfers between devices  54.2 us (24%)
  Pallas kernels  54 us (24%)
  starting transfers between devices  45.6 us (20%)
  local copies, waits for them, and re-layouts  28.1 us (12%)
  blocking collectives  24.5 us (11%)
  other arithmetic  16.5 us (7%)
    pallas_call x4, Pallas kernels, per_device(): pl.pallas_call(functools.partial(main_kernel, width, attended is not None...  48.1 us
    ppermute x24, waiting for transfers between devices, exclusive_scan(): got = lax.ppermute(carried + total, axis, perm=[pair])  41.5 us
    ppermute x24, starting transfers between devices, exclusive_scan(): got = lax.ppermute(carried + total, axis, perm=[pair])  32.9 us
    all_to_all x1, blocking collectives, per_device(): lax.all_to_all(outs[1], ('head', 'sub'), split_axis=axis, concat_axis=0,...  24.5 us
    all_to_all x3, starting transfers between devices, per_device(): lax.all_to_all(outs[1], ('head', 'sub'), split_axis=axis, concat_axis=0,...  12.7 us
    all_to_all x3, waiting for transfers between devices, per_device(): lax.all_to_all(outs[1], ('head', 'sub'), split_axis=axis, concat_axis=0,...  12.7 us
    unnamed x54, local copies, waits for them, and re-layouts  9.54 us
    reshape x3, local copies, waits for them, and re-layouts, per_device(): jnp.stack([p[:, i] for p in parts], 1)  8.01 us
  transfers between devices with their start and end apart: 27, of which 8 were waited for; matrix products, arithmetic and copies ran while one was open for 9% of the time, Pallas kernels for 21%

profile of v15, /device:TPU:0, one launch (start us, length us, event | category | flops | bytes accessed | tf_op | source)
XLA Modules:
  0.0 224.0 jit_solution(69070316911704466)
XLA Ops:
  0.7 3.6 %copy.29 = bf16[512,16,128]{2,0,1:T(8,128)(2,1)} copy(bf16[512,16,128]{2,1,0:T(8,128)(2,1)} %param.5) | data formatting | bytes 4194304 | tf_op args[1]
  7.2 3.3 %copy_bitcast_fusion.3 = (bf16[16,512,128]{2,1,0:T(8,128)(2,1)}, bf16[16,512,128]{2,1,0:T(8,128)(2,1)}) fusion(bf16[512,16,128]{2,1,0:T(8,128)(2,1)S(1)} %copy-done.7, bf16[512,16,128]{2,1,0:T(8,128)(2,1)S(1)} %copy-done.8), kind=kLoop, calls=%fused_computation.8 | loop fusion | bytes 8388608 | tf_op jit(solution)/shard_map/transpose | solution.py:89
  10.5 5.9 %shard_map.75 = (f32[16,128,128]{2,1,0:T(8,128)}, f32[16,128,128]{2,1,0:T(8,128)}) custom-call(bf16[16,512,128]{2,1,0:T(8,128)(2,1)} %fusion.q_ref, bf16[16,512,128]{2,1,0:T(8,128)(2,1)} %bitcast.22, bf16[16,512,128]{2,1,0:T(8,128)(2,1)} %get-tuple-element.77.v_ref, bf16[16,512,128]{2,1,0:T(8,128)(2,1)} %get-tuple-element.76.d_ref), custom_call_target="tpu_custom_call" | custom-call | tf_op jit(solution)/shard_map/pallas_call | solution.py:96
  19.2 4.9 %collective-permute-start.18 = (f32[4,128,128]{2,1,0:T(8,128)S(1)}, f32[4,128,128]{2,1,0:T(8,128)S(1)}, u32[]{:S(2)}, u32[]{:S(2)}) collective-permute-start(f32[4,128,128]{2,1,0:T(8,128)S(1)} %slice.70), channel_id=1, source_target_pairs={{0,4},{1,5},{2,6},{3,7},{16,20},{17,21},{18,22},{19,23}} | collective-permute-start | bytes 786440 | tf_op jit(solution)/shard_map/ppermute | solution.py:74
  25.8 3.9 %collective-permute-done.18 = f32[4,128,128]{2,1,0:T(8,128)S(1)} collective-permute-done((f32[4,128,128]{2,1,0:T(8,128)S(1)}, f32[4,128,128]{2,1,0:T(8,128)S(1)}, u32[]{:S(2)}, u32[]{:S(2)}) %collective-permute-start.18) | collective-permute-done | bytes 262176 | tf_op jit(solution)/shard_map/ppermute | solution.py:74
  30.4 7.9 %collective-permute-start.12 = (f32[4,128,128]{2,1,0:T(8,128)S(1)}, f32[4,128,128]{2,1,0:T(8,128)S(1)}, u32[]{:S(2)}, u32[]{:S(2)}) collective-permute-start(f32[4,128,128]{2,1,0:T(8,128)S(1)} %get-tuple-element.65), channel_id=1, source_target_pairs={{0,4},{1,5},{2,6},{3,7},{16,20},{17,21},{18,22},{19,23}} | collective-permute-start | bytes 786440 | tf_op jit(solution)/shard_map/ppermute | solution.py:74
  45.7 4.9 %collective-permute-done.6 = f32[4,128,128]{2,1,0:T(8,128)S(1)} collective-permute-done((f32[4,128,128]{2,1,0:T(8,128)S(1)}, f32[4,128,128]{2,1,0:T(8,128)S(1)}, u32[]{:S(2)}, u32[]{:S(2)}) %collective-permute-start.6) | collective-permute-done | bytes 262176 | tf_op jit(solution)/shard_map/ppermute | solution.py:74
  51.3 2.6 %collective-permute-done = f32[4,128,128]{2,1,0:T(8,128)S(1)} collective-permute-done((f32[4,128,128]{2,1,0:T(8,128)S(1)}, f32[4,128,128]{2,1,0:T(8,128)S(1)}, u32[]{:S(2)}, u32[]{:S(2)}) %collective-permute-start) | collective-permute-done | bytes 262176 | tf_op jit(solution)/shard_map/ppermute | solution.py:74
  62.2 12.1 %shard_map.76 = (bf16[16,512,128]{2,1,0:T(8,128)(2,1)}, bf16[4,3,4,128,128]{4,3,2,1,0:T(8,128)(2,1)}) custom-call(bf16[16,512,128]{2,1,0:T(8,128)(2,1)} %fusion.q_ref, bf16[16,512,128]{2,1,0:T(8,128)(2,1)} %bitcast.23, bf16[16,512,128]{2,1,0:T(8,128)(2,1)} %get-tuple-element.77.v_ref, bf16[16,512,128]{2,1,0:T(8,128)(2,1)} %get-tuple-element.76.d_ref, ...), custom_call_target="tpu_custom_call" | custom-call | tf_op jit(solution)/shard_map/pallas_call | solution.py:142
  74.3 4.4 %all-to-all-start = ((bf16[4,3,4,128,128]{4,3,2,1,0:T(8,128)(2,1)}), bf16[4,3,4,128,128]{4,3,2,1,0:T(8,128)(2,1)}, u32[]{:S(2)}, u32[]{:S(2)}) async-start(bf16[4,3,4,128,128]{4,3,2,1,0:T(8,128)(2,1)} %get-tuple-element.32), calls=%async_computation | async-start | bytes 3145728 | tf_op jit(solution)/shard_map/all_to_all | solution.py:155
  85.9 14.7 %collective-permute-done.17 = f32[4,128,128]{2,1,0:T(8,128)S(1)} collective-permute-done((f32[4,128,128]{2,1,0:T(8,128)S(1)}, f32[4,128,128]{2,1,0:T(8,128)S(1)}, u32[]{:S(2)}, u32[]{:S(2)}) %collective-permute-start.17) | collective-permute-done | bytes 262176 | tf_op jit(solution)/shard_map/ppermute | solution.py:74
  101.5 12.0 %shard_map.77 = (bf16[16,512,128]{2,1,0:T(8,128)(2,1)}, bf16[4,3,4,128,128]{4,3,2,1,0:T(8,128)(2,1)}) custom-call(bf16[16,512,128]{2,1,0:T(8,128)(2,1)} %fusion.q_ref, bf16[16,512,128]{2,1,0:T(8,128)(2,1)} %bitcast.24, bf16[16,512,128]{2,1,0:T(8,128)(2,1)} %get-tuple-element.77.v_ref, ...), custom_call_target="tpu_custom_call", output_to_operand_aliasing={{0}: (7, {})} | custom-call | tf_op jit(solution)/shard_map/pallas_call | solution.py:142
  113.6 3.7 %all-to-all-start.1 = ((bf16[4,3,4,128,128]{4,3,2,1,0:T(8,128)(2,1)}), bf16[4,3,4,128,128]{4,3,2,1,0:T(8,128)(2,1)S(1)}, u32[]{:S(2)}, u32[]{:S(2)}) async-start(bf16[4,3,4,128,128]{4,3,2,1,0:T(8,128)(2,1)} %get-tuple-element.33), calls=%async_computation.1 | async-start | bytes 3145728 | tf_op jit(solution)/shard_map/all_to_all | solution.py:155
  124.9 8.0 %collective-permute-done.5 = f32[4,128,128]{2,1,0:T(8,128)S(1)} collective-permute-done((f32[4,128,128]{2,1,0:T(8,128)}, f32[4,128,128]{2,1,0:T(8,128)S(1)}, u32[]{:S(2)}, u32[]{:S(2)}) %collective-permute-start.5) | collective-permute-done | bytes 262176 | tf_op jit(solution)/shard_map/ppermute | solution.py:74
  132.9 5.4 %collective-permute-done.11 = f32[4,128,128]{2,1,0:T(8,128)S(1)} collective-permute-done((f32[4,128,128]{2,1,0:T(8,128)}, f32[4,128,128]{2,1,0:T(8,128)S(1)}, u32[]{:S(2)}, u32[]{:S(2)}) %collective-permute-start.11) | collective-permute-done | bytes 262176 | tf_op jit(solution)/shard_map/ppermute | solution.py:74
  139.2 12.0 %shard_map.78 = (bf16[16,512,128]{2,1,0:T(8,128)(2,1)}, bf16[4,3,4,128,128]{4,3,2,1,0:T(8,128)(2,1)}) custom-call(bf16[16,512,128]{2,1,0:T(8,128)(2,1)} %fusion.q_ref, bf16[16,512,128]{2,1,0:T(8,128)(2,1)} %bitcast.25, bf16[16,512,128]{2,1,0:T(8,128)(2,1)} %get-tuple-element.77.v_ref, ...), custom_call_target="tpu_custom_call", output_to_operand_aliasing={{0}: (7, {})} | custom-call | tf_op jit(solution)/shard_map/pallas_call | solution.py:142
  151.2 12.0 %shard_map.79 = (bf16[16,512,128]{2,1,0:T(8,128)(2,1)}, bf16[4,3,4,128,128]{4,3,2,1,0:T(8,128)(2,1)}) custom-call(bf16[16,512,128]{2,1,0:T(8,128)(2,1)} %fusion.q_ref, bf16[16,512,128]{2,1,0:T(8,128)(2,1)} %bitcast.26, bf16[16,512,128]{2,1,0:T(8,128)(2,1)} %get-tuple-element.77.v_ref, ...), custom_call_target="tpu_custom_call", output_to_operand_aliasing={{0}: (7, {})} | custom-call | tf_op jit(solution)/shard_map/pallas_call | solution.py:142
  164.4 24.5 %all_to_all.20 = bf16[4,3,4,128,128]{4,3,2,1,0:T(8,128)(2,1)} all-to-all(bf16[4,3,4,128,128]{4,3,2,1,0:T(8,128)(2,1)} %get-tuple-element.35), channel_id=1, replica_groups=mesh['grp'=2,'seq'=4,'head'=2,'sub'=2] {'head','sub'}, dimensions={0} | all-to-all | bytes 3145728 | tf_op jit(solution)/shard_map/all_to_all | solution.py:155
  188.9 4.7 %all-to-all-start.2 = ((bf16[4,3,4,128,128]{4,3,2,1,0:T(8,128)(2,1)}), bf16[4,3,4,128,128]{4,3,2,1,0:T(8,128)(2,1)}, u32[]{:S(2)}, u32[]{:S(2)}) async-start(bf16[4,3,4,128,128]{4,3,2,1,0:T(8,128)(2,1)} %get-tuple-element.34), calls=%async_computation.2 | async-start | bytes 3145728 | tf_op jit(solution)/shard_map/all_to_all | solution.py:155
  193.6 2.7 %copy.18 = bf16[512,16,128]{2,1,0:T(8,128)(2,1)} copy(bf16[512,16,128]{2,0,1:T(8,128)(2,1)S(1)} %bitcast.27) | data formatting | bytes 4194304
  200.8 12.7 %all-to-all-done.2 = bf16[4,3,4,128,128]{4,3,2,1,0:T(8,128)(2,1)} async-done(((bf16[4,3,4,128,128]{4,3,2,1,0:T(8,128)(2,1)}), bf16[4,3,4,128,128]{4,3,2,1,0:T(8,128)(2,1)}, u32[]{:S(2)}, u32[]{:S(2)}) %all-to-all-start.2) | async-done | bytes 1572896 | tf_op jit(solution)/shard_map/all_to_all | solution.py:155
  215.5 2.7 %copy.26 = bf16[64,128,128]{2,0,1:T(8,128)(2,1)} copy(bf16[64,128,128]{2,1,0:T(8,128)(2,1)S(1)} %bitcast.28) | data formatting | bytes 4194304 | tf_op jit(solution)/shard_map/reshape | solution.py:163
  218.4 2.7 %copy.27 = bf16[64,128,128]{2,0,1:T(8,128)(2,1)} copy(bf16[64,128,128]{2,1,0:T(8,128)(2,1)S(1)} %bitcast.29) | data formatting | bytes 4194304 | tf_op jit(solution)/shard_map/reshape | solution.py:163
  221.3 2.7 %copy.28 = bf16[64,128,128]{2,0,1:T(8,128)(2,1)} copy(bf16[64,128,128]{2,1,0:T(8,128)(2,1)S(1)} %bitcast.30) | data formatting | bytes 4194304 | tf_op jit(solution)/shard_map/reshape | solution.py:163
  (119 shorter events, 49.1 us)
Async XLA Ops:
  17.5 6.6 %collective-permute-start.21 = (f32[4,128,128]{2,1,0:T(8,128)S(1)}, f32[4,128,128]{2,1,0:T(8,128)S(1)}, u32[]{:S(2)}, u32[]{:S(2)}) collective-permute-start(f32[4,128,128]{2,1,0:T(8,128)S(1)} %slice.71), channel_id=1, source_target_pairs={{12,8},{13,9},{14,10},{15,11},{28,24},{29,25},{30,26},{31,27}} | collective-permute-start | bytes 786440 | tf_op jit(solution)/shard_map/ppermute | solution.py:74
  19.2 10.5 %collective-permute-start.18 = (f32[4,128,128]{2,1,0:T(8,128)S(1)}, f32[4,128,128]{2,1,0:T(8,128)S(1)}, u32[]{:S(2)}, u32[]{:S(2)}) collective-permute-start(f32[4,128,128]{2,1,0:T(8,128)S(1)} %slice.70), channel_id=1, source_target_pairs={{0,4},{1,5},{2,6},{3,7},{16,20},{17,21},{18,22},{19,23}} | collective-permute-start | bytes 786440 | tf_op jit(solution)/shard_map/ppermute | solution.py:74
  25.1 15.8 %collective-permute-start.22 = (f32[4,128,128]{2,1,0:T(8,128)S(1)}, f32[4,128,128]{2,1,0:T(8,128)S(1)}, u32[]{:S(2)}, u32[]{:S(2)}) collective-permute-start(f32[4,128,128]{2,1,0:T(8,128)S(1)} %slice_add_fusion.9), channel_id=1, source_target_pairs={{8,4},{9,5},{10,6},{11,7},{24,20},{25,21},{26,22},{27,23}} | collective-permute-start | bytes 786440 | tf_op jit(solution)/shard_map/ppermute | solution.py:74
  29.8 12.6 %collective-permute-start.19 = (f32[4,128,128]{2,1,0:T(8,128)S(1)}, f32[4,128,128]{2,1,0:T(8,128)S(1)}, u32[]{:S(2)}, u32[]{:S(2)}) collective-permute-start(f32[4,128,128]{2,1,0:T(8,128)S(1)} %get-tuple-element.64), channel_id=1, source_target_pairs={{4,8},{5,9},{6,10},{7,11},{20,24},{21,25},{22,26},{23,27}} | collective-permute-start | bytes 786440 | tf_op jit(solution)/shard_map/ppermute | solution.py:74
  30.4 14.6 %collective-permute-start.12 = (f32[4,128,128]{2,1,0:T(8,128)S(1)}, f32[4,128,128]{2,1,0:T(8,128)S(1)}, u32[]{:S(2)}, u32[]{:S(2)}) collective-permute-start(f32[4,128,128]{2,1,0:T(8,128)S(1)} %get-tuple-element.65), channel_id=1, source_target_pairs={{0,4},{1,5},{2,6},{3,7},{16,20},{17,21},{18,22},{19,23}} | collective-permute-start | bytes 786440 | tf_op jit(solution)/shard_map/ppermute | solution.py:74
  38.3 12.3 %collective-permute-start.6 = (f32[4,128,128]{2,1,0:T(8,128)S(1)}, f32[4,128,128]{2,1,0:T(8,128)S(1)}, u32[]{:S(2)}, u32[]{:S(2)}) collective-permute-start(f32[4,128,128]{2,1,0:T(8,128)S(1)} %get-tuple-element.66), channel_id=1, source_target_pairs={{0,4},{1,5},{2,6},{3,7},{16,20},{17,21},{18,22},{19,23}} | collective-permute-start | bytes 786440 | tf_op jit(solution)/shard_map/ppermute | solution.py:74
  39.6 14.3 %collective-permute-start = (f32[4,128,128]{2,1,0:T(8,128)S(1)}, f32[4,128,128]{2,1,0:T(8,128)S(1)}, u32[]{:S(2)}, u32[]{:S(2)}) collective-permute-start(f32[4,128,128]{2,1,0:T(8,128)S(1)} %get-tuple-element.67), channel_id=1, source_target_pairs={{0,4},{1,5},{2,6},{3,7},{16,20},{17,21},{18,22},{19,23}} | collective-permute-start | bytes 786440 | tf_op jit(solution)/shard_map/ppermute | solution.py:74
  41.1 14.5 %collective-permute-start.23 = (f32[4,128,128]{2,1,0:T(8,128)S(1)}, f32[4,128,128]{2,1,0:T(8,128)S(1)}, u32[]{:S(2)}, u32[]{:S(2)}) collective-permute-start(f32[4,128,128]{2,1,0:T(8,128)S(1)} %get-tuple-element.56), channel_id=1, source_target_pairs={{4,0},{5,1},{6,2},{7,3},{20,16},{21,17},{22,18},{23,19}} | collective-permute-start | bytes 786440 | tf_op jit(solution)/shard_map/ppermute | solution.py:74
  42.4 14.6 %collective-permute-start.15 = (f32[4,128,128]{2,1,0:T(8,128)S(1)}, f32[4,128,128]{2,1,0:T(8,128)S(1)}, u32[]{:S(2)}, u32[]{:S(2)}) collective-permute-start(f32[4,128,128]{2,1,0:T(8,128)S(1)} %get-tuple-element.57), channel_id=1, source_target_pairs={{12,8},{13,9},{14,10},{15,11},{28,24},{29,25},{30,26},{31,27}} | collective-permute-start | bytes 786440 | tf_op jit(solution)/shard_map/ppermute | solution.py:74
  45.1 11.9 %collective-permute-start.9 = (f32[4,128,128]{2,1,0:T(8,128)S(1)}, f32[4,128,128]{2,1,0:T(8,128)S(1)}, u32[]{:S(2)}, u32[]{:S(2)}) collective-permute-start(f32[4,128,128]{2,1,0:T(8,128)S(1)} %get-tuple-element.58), channel_id=1, source_target_pairs={{12,8},{13,9},{14,10},{15,11},{28,24},{29,25},{30,26},{31,27}} | collective-permute-start | bytes 786440 | tf_op jit(solution)/shard_map/ppermute | solution.py:74
  50.7 6.3 %collective-permute-start.3 = (f32[4,128,128]{2,1,0:T(8,128)S(1)}, f32[4,128,128]{2,1,0:T(8,128)S(1)}, u32[]{:S(2)}, u32[]{:S(2)}) collective-permute-start(f32[4,128,128]{2,1,0:T(8,128)S(1)} %get-tuple-element.59), channel_id=1, source_target_pairs={{12,8},{13,9},{14,10},{15,11},{28,24},{29,25},{30,26},{31,27}} | collective-permute-start | bytes 786440 | tf_op jit(solution)/shard_map/ppermute | solution.py:74
  54.9 6.5 %collective-permute-start.20 = (f32[4,128,128]{2,1,0:T(8,128)S(1)}, f32[4,128,128]{2,1,0:T(8,128)S(1)}, u32[]{:S(2)}, u32[]{:S(2)}) collective-permute-start(f32[4,128,128]{2,1,0:T(8,128)S(1)} %get-tuple-element.60), channel_id=1, source_target_pairs={{8,12},{9,13},{10,14},{11,15},{24,28},{25,29},{26,30},{27,31}} | collective-permute-start | bytes 786440 | tf_op jit(solution)/shard_map/ppermute | solution.py:74
  55.6 6.6 %collective-permute-start.13 = (f32[4,128,128]{2,1,0:T(8,128)S(1)}, f32[4,128,128]{2,1,0:T(8,128)}, u32[]{:S(2)}, u32[]{:S(2)}) collective-permute-start(f32[4,128,128]{2,1,0:T(8,128)S(1)} %get-tuple-element.63), channel_id=1, source_target_pairs={{4,8},{5,9},{6,10},{7,11},{20,24},{21,25},{22,26},{23,27}} | collective-permute-start | bytes 786440 | tf_op jit(solution)/shard_map/ppermute | solution.py:74
  58.0 4.2 %collective-permute-start.16 = (f32[4,128,128]{2,1,0:T(8,128)S(1)}, f32[4,128,128]{2,1,0:T(8,128)S(1)}, u32[]{:S(2)}, u32[]{:S(2)}) collective-permute-start(f32[4,128,128]{2,1,0:T(8,128)S(1)} %get-tuple-element.55), channel_id=1, source_target_pairs={{8,4},{9,5},{10,6},{11,7},{24,20},{25,21},{26,22},{27,23}} | collective-permute-start | bytes 786440 | tf_op jit(solution)/shard_map/ppermute | solution.py:74
  59.4 19.3 %collective-permute-start.1 = (f32[4,128,128]{2,1,0:T(8,128)}, f32[4,128,128]{2,1,0:T(8,128)}, u32[]{:S(2)}, u32[]{:S(2)}) collective-permute-start(f32[4,128,128]{2,1,0:T(8,128)} %get-tuple-element.61), channel_id=1, source_target_pairs={{4,8},{5,9},{6,10},{7,11},{20,24},{21,25},{22,26},{23,27}} | collective-permute-start | bytes 786440 | tf_op jit(solution)/shard_map/ppermute | solution.py:74
  60.8 17.9 %collective-permute-start.7 = (f32[4,128,128]{2,1,0:T(8,128)}, f32[4,128,128]{2,1,0:T(8,128)S(1)}, u32[]{:S(2)}, u32[]{:S(2)}) collective-permute-start(f32[4,128,128]{2,1,0:T(8,128)} %get-tuple-element.62), channel_id=1, source_target_pairs={{4,8},{5,9},{6,10},{7,11},{20,24},{21,25},{22,26},{23,27}} | collective-permute-start | bytes 786440 | tf_op jit(solution)/shard_map/ppermute | solution.py:74
  74.3 39.3 %all-to-all-start = ((bf16[4,3,4,128,128]{4,3,2,1,0:T(8,128)(2,1)}), bf16[4,3,4,128,128]{4,3,2,1,0:T(8,128)(2,1)}, u32[]{:S(2)}, u32[]{:S(2)}) async-start(bf16[4,3,4,128,128]{4,3,2,1,0:T(8,128)(2,1)} %get-tuple-element.32), calls=%async_computation | async-start | bytes 3145728 | tf_op jit(solution)/shard_map/all_to_all | solution.py:155
  81.4 4.4 %collective-permute-start.4 = (f32[4,128,128]{2,1,0:T(8,128)S(1)}, f32[4,128,128]{2,1,0:T(8,128)S(1)}, u32[]{:S(2)}, u32[]{:S(2)}) collective-permute-start(f32[4,128,128]{2,1,0:T(8,128)S(1)} %copy-done.25), channel_id=1, source_target_pairs={{8,4},{9,5},{10,6},{11,7},{24,20},{25,21},{26,22},{27,23}} | collective-permute-start | bytes 786440 | tf_op jit(solution)/shard_map/ppermute | solution.py:74
  82.9 17.8 %collective-permute-start.17 = (f32[4,128,128]{2,1,0:T(8,128)S(1)}, f32[4,128,128]{2,1,0:T(8,128)S(1)}, u32[]{:S(2)}, u32[]{:S(2)}) collective-permute-start(f32[4,128,128]{2,1,0:T(8,128)S(1)} %slice_add_fusion.10), channel_id=1, source_target_pairs={{4,0},{5,1},{6,2},{7,3},{20,16},{21,17},{22,18},{23,19}} | collective-permute-start | bytes 786440 | tf_op jit(solution)/shard_map/ppermute | solution.py:74
  113.6 49.7 %all-to-all-start.1 = ((bf16[4,3,4,128,128]{4,3,2,1,0:T(8,128)(2,1)}), bf16[4,3,4,128,128]{4,3,2,1,0:T(8,128)(2,1)S(1)}, u32[]{:S(2)}, u32[]{:S(2)}) async-start(bf16[4,3,4,128,128]{4,3,2,1,0:T(8,128)(2,1)} %get-tuple-element.33), calls=%async_computation.1 | async-start | bytes 3145728 | tf_op jit(solution)/shard_map/all_to_all | solution.py:155
  118.1 5.1 %collective-permute-start.8 = (f32[4,128,128]{2,1,0:T(8,128)}, f32[4,128,128]{2,1,0:T(8,128)S(1)}, u32[]{:S(2)}, u32[]{:S(2)}) collective-permute-start(f32[4,128,128]{2,1,0:T(8,128)} %get-tuple-element.73), channel_id=1, source_target_pairs={{8,12},{9,13},{10,14},{11,15},{24,28},{25,29},{26,30},{27,31}} | collective-permute-start | bytes 786440 | tf_op jit(solution)/shard_map/ppermute | solution.py:74
  118.8 14.1 %collective-permute-start.5 = (f32[4,128,128]{2,1,0:T(8,128)}, f32[4,128,128]{2,1,0:T(8,128)S(1)}, u32[]{:S(2)}, u32[]{:S(2)}) collective-permute-start(f32[4,128,128]{2,1,0:T(8,128)} %get-tuple-element.69), channel_id=1, source_target_pairs={{4,0},{5,1},{6,2},{7,3},{20,16},{21,17},{22,18},{23,19}} | collective-permute-start | bytes 786440 | tf_op jit(solution)/shard_map/ppermute | solution.py:74
  120.1 18.2 %collective-permute-start.11 = (f32[4,128,128]{2,1,0:T(8,128)}, f32[4,128,128]{2,1,0:T(8,128)S(1)}, u32[]{:S(2)}, u32[]{:S(2)}) collective-permute-start(f32[4,128,128]{2,1,0:T(8,128)} %get-tuple-element.70), channel_id=1, source_target_pairs={{4,0},{5,1},{6,2},{7,3},{20,16},{21,17},{22,18},{23,19}} | collective-permute-start | bytes 786440 | tf_op jit(solution)/shard_map/ppermute | solution.py:74
  188.9 24.7 %all-to-all-start.2 = ((bf16[4,3,4,128,128]{4,3,2,1,0:T(8,128)(2,1)}), bf16[4,3,4,128,128]{4,3,2,1,0:T(8,128)(2,1)}, u32[]{:S(2)}, u32[]{:S(2)}) async-start(bf16[4,3,4,128,128]{4,3,2,1,0:T(8,128)(2,1)} %get-tuple-element.34), calls=%async_computation.2 | async-start | bytes 3145728 | tf_op jit(solution)/shard_map/all_to_all | solution.py:155
  (29 other events, 236.4 us)

commit v16 on v13

--- a/solution.py
+++ b/solution.py
@@ -150,9 +150,12 @@
             compiler_params=pltpu.CompilerParams(dimension_semantics=("arbitrary",)),
         )(*args)
         attended = outs[0]
+        sent = outs[1]
+        if g + 1 < groups:
+            sent, _, _ = lax.optimization_barrier((sent, chains[g + 1][0], chains[g + 1][1]))
         axis = 0 if split_out else 2
         grads.append(
-            lax.all_to_all(outs[1], ("head", "sub"), split_axis=axis, concat_axis=0, tiled=True)
+            lax.all_to_all(sent, ("head", "sub"), split_axis=axis, concat_axis=0, tiled=True)
         )
     if split_out:
         parts = [gr for gr in grads]

time: 189 us -> 196 us (1.037)
  the two profiles are of different devices: /device:TPU:0 before, /device:TPU:28 now
where the time goes in v16:
time: 196 us
  waiting for transfers between devices  76.5 us (39%)
  Pallas kernels  46.5 us (24%)
  starting transfers between devices  33.8 us (17%)
  local copies, waits for them, and re-layouts  26.4 us (13%)
  other arithmetic  11.4 us (6%)
    all_to_all x2, waiting for transfers between devices, per_device(): lax.all_to_all(sent, ('head', 'sub'), split_axis=axis, concat_axis=0, til...  47 us
    pallas_call x2, Pallas kernels, per_device(): pl.pallas_call(functools.partial(main_kernel, width, attended is not None...  41.4 us
    ppermute x12, waiting for transfers between devices, exclusive_scan(): got = lax.ppermute(carried + total, axis, perm=[pair])  29.5 us
    ppermute x12, starting transfers between devices, exclusive_scan(): got = lax.ppermute(carried + total, axis, perm=[pair])  25.3 us
    unnamed x18, local copies, waits for them, and re-layouts  8.86 us
    all_to_all x2, starting transfers between devices, per_device(): lax.all_to_all(sent, ('head', 'sub'), split_axis=axis, concat_axis=0, til...  8.55 us
    reshape x3, local copies, waits for them, and re-layouts, per_device(): jnp.stack([p[:, i] for p in parts], 1)  8.01 us
    pallas_call x1, Pallas kernels, per_device(): pl.pallas_call(functools.partial(totals_kernel, width), grid=(groups,), i...  5.13 us
  transfers between devices with their start and end apart: 14, of which 5 were waited for; matrix products, arithmetic and copies ran while one was open for 7% of the time, Pallas kernels for 21%

profile of v16, /device:TPU:28, one launch (start us, length us, event | category | flops | bytes accessed | tf_op | source)
XLA Modules:
  0.0 195.6 jit_solution(2773769797049488117)
XLA Ops:
  0.7 3.6 %copy.36 = bf16[512,16,128]{2,0,1:T(8,128)(2,1)} copy(bf16[512,16,128]{2,1,0:T(8,128)(2,1)} %param.5) | data formatting | bytes 4194304 | tf_op args[1]
  4.3 2.0 %fusion.q_ref = bf16[16,512,128]{2,1,0:T(8,128)(2,1)} fusion(bf16[512,16,128]{2,1,0:T(8,128)(2,1)S(1)} %copy-done.5, f32[512]{0:T(512)S(1)} %multiply_rsqrt_fusion.1), kind=kLoop, calls=%fused_computation.1 | loop fusion | flops 3145728 | bytes 4196352 | tf_op jit(solution)/shard_map/transpose | solution.py:89
  7.2 3.3 %copy_bitcast_fusion.3 = (bf16[16,512,128]{2,1,0:T(8,128)(2,1)}, bf16[16,512,128]{2,1,0:T(8,128)(2,1)}) fusion(bf16[512,16,128]{2,1,0:T(8,128)(2,1)S(1)} %copy-done.6, bf16[512,16,128]{2,1,0:T(8,128)(2,1)S(1)} %copy-done.7), kind=kLoop, calls=%fused_computation.8 | loop fusion | bytes 8388608 | tf_op jit(solution)/shard_map/transpose | solution.py:89
  10.5 5.1 %shard_map.75 = (f32[16,128,128]{2,1,0:T(8,128)}, f32[16,128,128]{2,1,0:T(8,128)}) custom-call(bf16[16,512,128]{2,1,0:T(8,128)(2,1)} %fusion.q_ref, bf16[16,512,128]{2,1,0:T(8,128)(2,1)} %bitcast.22, bf16[16,512,128]{2,1,0:T(8,128)(2,1)} %get-tuple-element.45.v_ref, bf16[16,512,128]{2,1,0:T(8,128)(2,1)} %get-tuple-element.44.d_ref), custom_call_target="tpu_custom_call" | custom-call | tf_op jit(solution)/shard_map/pallas_call | solution.py:96
  16.9 2.4 %collective-permute-start.9 = (f32[8,128,128]{2,1,0:T(8,128)S(1)}, f32[8,128,128]{2,1,0:T(8,128)S(1)}, u32[]{:S(2)}, u32[]{:S(2)}) collective-permute-start(f32[8,128,128]{2,1,0:T(8,128)S(1)} %slice.35), channel_id=1, source_target_pairs={{12,8},{13,9},{14,10},{15,11},{28,24},{29,25},{30,26},{31,27}} | collective-permute-start | bytes 1572872 | tf_op jit(solution)/shard_map/ppermute | solution.py:74
  21.1 9.3 %collective-permute-done.9 = f32[8,128,128]{2,1,0:T(8,128)S(1)} collective-permute-done((f32[8,128,128]{2,1,0:T(8,128)S(1)}, f32[8,128,128]{2,1,0:T(8,128)S(1)}, u32[]{:S(2)}, u32[]{:S(2)}) %collective-permute-start.9) | collective-permute-done | bytes 524320 | tf_op jit(solution)/shard_map/ppermute | solution.py:74
  33.5 14.0 %collective-permute-start.3 = (f32[8,128,128]{2,1,0:T(8,128)S(1)}, f32[8,128,128]{2,1,0:T(8,128)S(1)}, u32[]{:S(2)}, u32[]{:S(2)}) collective-permute-start(f32[8,128,128]{2,1,0:T(8,128)S(1)} %get-tuple-element.39), channel_id=1, source_target_pairs={{12,8},{13,9},{14,10},{15,11},{28,24},{29,25},{30,26},{31,27}} | collective-permute-start | bytes 1572872 | tf_op jit(solution)/shard_map/ppermute | solution.py:74
  48.5 8.7 %collective-permute-done.3 = f32[8,128,128]{2,1,0:T(8,128)S(1)} collective-permute-done((f32[8,128,128]{2,1,0:T(8,128)S(1)}, f32[8,128,128]{2,1,0:T(8,128)S(1)}, u32[]{:S(2)}, u32[]{:S(2)}) %collective-permute-start.3) | collective-permute-done | bytes 524320 | tf_op jit(solution)/shard_map/ppermute | solution.py:74
  64.1 1.5 collective-permute-start.5
  65.5 11.4 %collective-permute-done.8 = f32[8,128,128]{2,1,0:T(8,128)S(1)} collective-permute-done((f32[8,128,128]{2,1,0:T(8,128)S(1)}, f32[8,128,128]{2,1,0:T(8,128)S(1)}, u32[]{:S(2)}, u32[]{:S(2)}) %collective-permute-start.8) | collective-permute-done | bytes 524320 | tf_op jit(solution)/shard_map/ppermute | solution.py:74
  77.8 20.7 %shard_map.76 = (bf16[16,512,128]{2,1,0:T(8,128)(2,1)}, bf16[4,3,8,128,128]{4,3,2,1,0:T(8,128)(2,1)}) custom-call(bf16[16,512,128]{2,1,0:T(8,128)(2,1)} %fusion.q_ref, bf16[16,512,128]{2,1,0:T(8,128)(2,1)} %bitcast.23, bf16[16,512,128]{2,1,0:T(8,128)(2,1)} %get-tuple-element.45.v_ref, bf16[16,512,128]{2,1,0:T(8,128)(2,1)} %get-tuple-element.44.d_ref, ...), custom_call_target="tpu_custom_call" | custom-call | tf_op jit(solution)/shard_map/pallas_call | solution.py:142
  98.5 2.0 %add_add_fusion.3.before_ref = f32[8,128,128]{2,1,0:T(8,128)} fusion(f32[8,128,128]{2,1,0:T(8,128)} %collective-permute-done.2, f32[8,128,128]{2,1,0:T(8,128)S(1)} %collective-permute-done, f32[8,128,128]{2,1,0:T(8,128)S(1)} %collective-permute-done.1), kind=kLoop, calls=%fused_computation.14 | loop fusion | flops 262144 | bytes 2097152 | tf_op jit(solution)/shard_map/add | solution.py:75
  100.5 1.9 add_add_fusion.2.rest_ref
  102.4 3.7 %all-to-all-start = ((bf16[4,3,8,128,128]{4,3,2,1,0:T(8,128)(2,1)}), bf16[4,3,8,128,128]{4,3,2,1,0:T(8,128)(2,1)S(1)}, u32[]{:S(2)}, u32[]{:S(2)}) async-start(bf16[4,3,8,128,128]{4,3,2,1,0:T(8,128)(2,1)} %get-tuple-element.20), calls=%async_computation | async-start | bytes 6291456 | tf_op jit(solution)/shard_map/all_to_all | solution.py:158
  106.1 20.7 %shard_map.77 = (bf16[16,512,128]{2,1,0:T(8,128)(2,1)}, bf16[4,3,8,128,128]{4,3,2,1,0:T(8,128)(2,1)}) custom-call(bf16[16,512,128]{2,1,0:T(8,128)(2,1)} %fusion.q_ref, bf16[16,512,128]{2,1,0:T(8,128)(2,1)} %bitcast.24, bf16[16,512,128]{2,1,0:T(8,128)(2,1)} %get-tuple-element.45.v_ref, ...), custom_call_target="tpu_custom_call", output_to_operand_aliasing={{0}: (7, {})} | custom-call | tf_op jit(solution)/shard_map/pallas_call | solution.py:142
  126.8 16.2 %all-to-all-done = bf16[4,3,8,128,128]{4,3,2,1,0:T(8,128)(2,1)S(1)} async-done(((bf16[4,3,8,128,128]{4,3,2,1,0:T(8,128)(2,1)}), bf16[4,3,8,128,128]{4,3,2,1,0:T(8,128)(2,1)S(1)}, u32[]{:S(2)}, u32[]{:S(2)}) %all-to-all-start) | async-done | bytes 3145760 | tf_op jit(solution)/shard_map/all_to_all | solution.py:158
  143.0 4.8 %all-to-all-start.1 = ((bf16[4,3,8,128,128]{4,3,2,1,0:T(8,128)(2,1)}), bf16[4,3,8,128,128]{4,3,2,1,0:T(8,128)(2,1)}, u32[]{:S(2)}, u32[]{:S(2)}) async-start(bf16[4,3,8,128,128]{4,3,2,1,0:T(8,128)(2,1)} %get-tuple-element.21), calls=%async_computation.1 | async-start | bytes 6291456 | tf_op jit(solution)/shard_map/all_to_all | solution.py:158
  147.9 4.3 %copy.25 = bf16[512,16,128]{2,1,0:T(8,128)(2,1)} copy(bf16[512,16,128]{2,0,1:T(8,128)(2,1)} %bitcast.28) | data formatting | bytes 4194304
  152.1 1.7 fusion.1
  153.9 30.8 %all-to-all-done.1 = bf16[4,3,8,128,128]{4,3,2,1,0:T(8,128)(2,1)} async-done(((bf16[4,3,8,128,128]{4,3,2,1,0:T(8,128)(2,1)}), bf16[4,3,8,128,128]{4,3,2,1,0:T(8,128)(2,1)}, u32[]{:S(2)}, u32[]{:S(2)}) %all-to-all-start.1) | async-done | bytes 3145760 | tf_op jit(solution)/shard_map/all_to_all | solution.py:158
  184.7 2.2 %fusion.2 = (bf16[4,1,8,128,128]{4,3,2,1,0:T(8,128)(2,1)S(1)}, bf16[4,1,8,128,128]{4,3,2,1,0:T(8,128)(2,1)S(1)}, bf16[4,1,8,128,128]{4,3,2,1,0:T(8,128)(2,1)S(1)}) fusion(bf16[4,3,8,128,128]{4,3,2,1,0:T(8,128)(2,1)} %all-to-all-done.1), kind=kLoop, calls=%fused_computation.26 | loop fusion | bytes 6291456 | tf_op jit(solution)/shard_map/slice | solution.py:166
  187.1 2.7 %copy.33 = bf16[64,128,128]{2,0,1:T(8,128)(2,1)} copy(bf16[64,128,128]{2,1,0:T(8,128)(2,1)S(1)} %bitcast.25) | data formatting | bytes 4194304 | tf_op jit(solution)/shard_map/reshape | solution.py:166
  190.0 2.7 %copy.34 = bf16[64,128,128]{2,0,1:T(8,128)(2,1)} copy(bf16[64,128,128]{2,1,0:T(8,128)(2,1)S(1)} %bitcast.26) | data formatting | bytes 4194304 | tf_op jit(solution)/shard_map/reshape | solution.py:166
  192.9 2.7 %copy.35 = bf16[64,128,128]{2,0,1:T(8,128)(2,1)} copy(bf16[64,128,128]{2,1,0:T(8,128)(2,1)S(1)} %bitcast.27) | data formatting | bytes 4194304 | tf_op jit(solution)/shard_map/reshape | solution.py:166
  (49 shorter events, 16.2 us)
Async XLA Ops:
  0.6 3.6 %copy-start.5 = (bf16[512,16,128]{2,1,0:T(8,128)(2,1)S(1)}, bf16[512,16,128]{2,1,0:T(8,128)(2,1)}, u32[]{:S(2)}) copy-start(bf16[512,16,128]{2,1,0:T(8,128)(2,1)} %param.4) | copy-start | bytes 6291460
  4.3 2.0 %copy-start.6 = (bf16[512,16,128]{2,1,0:T(8,128)(2,1)S(1)}, bf16[512,16,128]{2,1,0:T(8,128)(2,1)}, u32[]{:S(2)}) copy-start(bf16[512,16,128]{2,1,0:T(8,128)(2,1)} %param.7) | copy-start | bytes 6291460
  4.3 3.0 %copy-start.7 = (bf16[512,16,128]{2,1,0:T(8,128)(2,1)S(1)}, bf16[512,16,128]{2,1,0:T(8,128)(2,1)}, u32[]{:S(2)}) copy-start(bf16[512,16,128]{2,1,0:T(8,128)(2,1)} %param.6) | copy-start | bytes 6291460
  15.6 14.8 %copy-start = (f32[16,128,128]{2,1,0:T(8,128)S(1)}, f32[16,128,128]{2,1,0:T(8,128)}, u32[]{:S(2)}) copy-start(f32[16,128,128]{2,1,0:T(8,128)} %get-tuple-element.14) | copy-start | bytes 3145732
  15.6 15.5 %copy-start.1 = (f32[16,128,128]{2,1,0:T(8,128)S(1)}, f32[16,128,128]{2,1,0:T(8,128)}, u32[]{:S(2)}) copy-start(f32[16,128,128]{2,1,0:T(8,128)} %get-tuple-element.13) | copy-start | bytes 3145732
  16.9 13.5 %collective-permute-start.9 = (f32[8,128,128]{2,1,0:T(8,128)S(1)}, f32[8,128,128]{2,1,0:T(8,128)S(1)}, u32[]{:S(2)}, u32[]{:S(2)}) collective-permute-start(f32[8,128,128]{2,1,0:T(8,128)S(1)} %slice.35), channel_id=1, source_target_pairs={{12,8},{13,9},{14,10},{15,11},{28,24},{29,25},{30,26},{31,27}} | collective-permute-start | bytes 1572872 | tf_op jit(solution)/shard_map/ppermute | solution.py:74
  20.3 10.8 %collective-permute-start.6 = (f32[8,128,128]{2,1,0:T(8,128)S(1)}, f32[8,128,128]{2,1,0:T(8,128)S(1)}, u32[]{:S(2)}, u32[]{:S(2)}) collective-permute-start(f32[8,128,128]{2,1,0:T(8,128)S(1)} %slice.34), channel_id=1, source_target_pairs={{0,4},{1,5},{2,6},{3,7},{16,20},{17,21},{18,22},{19,23}} | collective-permute-start | bytes 1572872 | tf_op jit(solution)/shard_map/ppermute | solution.py:74
  30.5 2.2 %collective-permute-start.10 = (f32[8,128,128]{2,1,0:T(8,128)S(1)}, f32[8,128,128]{2,1,0:T(8,128)S(1)}, u32[]{:S(2)}, u32[]{:S(2)}) collective-permute-start(f32[8,128,128]{2,1,0:T(8,128)S(1)} %slice_add_fusion.5), channel_id=1, source_target_pairs={{8,4},{9,5},{10,6},{11,7},{24,20},{25,21},{26,22},{27,23}} | collective-permute-start | bytes 1572872 | tf_op jit(solution)/shard_map/ppermute | solution.py:74
  31.3 16.3 %collective-permute-start.7 = (f32[8,128,128]{2,1,0:T(8,128)S(1)}, f32[8,128,128]{2,1,0:T(8,128)S(1)}, u32[]{:S(2)}, u32[]{:S(2)}) collective-permute-start(f32[8,128,128]{2,1,0:T(8,128)S(1)} %get-tuple-element.42), channel_id=1, source_target_pairs={{4,8},{5,9},{6,10},{7,11},{20,24},{21,25},{22,26},{23,27}} | collective-permute-start | bytes 1572872 | tf_op jit(solution)/shard_map/ppermute | solution.py:74
  32.0 15.6 %collective-permute-start = (f32[8,128,128]{2,1,0:T(8,128)S(1)}, f32[8,128,128]{2,1,0:T(8,128)S(1)}, u32[]{:S(2)}, u32[]{:S(2)}) collective-permute-start(f32[8,128,128]{2,1,0:T(8,128)S(1)} %get-tuple-element.43), channel_id=1, source_target_pairs={{0,4},{1,5},{2,6},{3,7},{16,20},{17,21},{18,22},{19,23}} | collective-permute-start | bytes 1572872 | tf_op jit(solution)/shard_map/ppermute | solution.py:74
  32.8 15.6 %collective-permute-start.11 = (f32[8,128,128]{2,1,0:T(8,128)S(1)}, f32[8,128,128]{2,1,0:T(8,128)S(1)}, u32[]{:S(2)}, u32[]{:S(2)}) collective-permute-start(f32[8,128,128]{2,1,0:T(8,128)S(1)} %get-tuple-element.38), channel_id=1, source_target_pairs={{4,0},{5,1},{6,2},{7,3},{20,16},{21,17},{22,18},{23,19}} | collective-permute-start | bytes 1572872 | tf_op jit(solution)/shard_map/ppermute | solution.py:74
  33.5 23.7 %collective-permute-start.3 = (f32[8,128,128]{2,1,0:T(8,128)S(1)}, f32[8,128,128]{2,1,0:T(8,128)S(1)}, u32[]{:S(2)}, u32[]{:S(2)}) collective-permute-start(f32[8,128,128]{2,1,0:T(8,128)S(1)} %get-tuple-element.39), channel_id=1, source_target_pairs={{12,8},{13,9},{14,10},{15,11},{28,24},{29,25},{30,26},{31,27}} | collective-permute-start | bytes 1572872 | tf_op jit(solution)/shard_map/ppermute | solution.py:74
  47.8 13.2 %collective-permute-start.1 = (f32[8,128,128]{2,1,0:T(8,128)S(1)}, f32[8,128,128]{2,1,0:T(8,128)S(1)}, u32[]{:S(2)}, u32[]{:S(2)}) collective-permute-start(f32[8,128,128]{2,1,0:T(8,128)S(1)} %get-tuple-element.41), channel_id=1, source_target_pairs={{4,8},{5,9},{6,10},{7,11},{20,24},{21,25},{22,26},{23,27}} | collective-permute-start | bytes 1572872 | tf_op jit(solution)/shard_map/ppermute | solution.py:74
  58.2 5.0 %collective-permute-start.4 = (f32[8,128,128]{2,1,0:T(8,128)S(1)}, f32[8,128,128]{2,1,0:T(8,128)S(1)}, u32[]{:S(2)}, u32[]{:S(2)}) collective-permute-start(f32[8,128,128]{2,1,0:T(8,128)S(1)} %get-tuple-element.37), channel_id=1, source_target_pairs={{8,4},{9,5},{10,6},{11,7},{24,20},{25,21},{26,22},{27,23}} | collective-permute-start | bytes 1572872 | tf_op jit(solution)/shard_map/ppermute | solution.py:74
  59.7 17.2 %collective-permute-start.8 = (f32[8,128,128]{2,1,0:T(8,128)S(1)}, f32[8,128,128]{2,1,0:T(8,128)S(1)}, u32[]{:S(2)}, u32[]{:S(2)}) collective-permute-start(f32[8,128,128]{2,1,0:T(8,128)S(1)} %get-tuple-element.40), channel_id=1, source_target_pairs={{8,12},{9,13},{10,14},{11,15},{24,28},{25,29},{26,30},{27,31}} | collective-permute-start | bytes 1572872 | tf_op jit(solution)/shard_map/ppermute | solution.py:74
  61.9 36.6 %collective-permute-start.2 = (f32[8,128,128]{2,1,0:T(8,128)}, f32[8,128,128]{2,1,0:T(8,128)}, u32[]{:S(2)}, u32[]{:S(2)}) collective-permute-start(f32[8,128,128]{2,1,0:T(8,128)} %slice_add_fusion.2), channel_id=1, source_target_pairs={{8,12},{9,13},{10,14},{11,15},{24,28},{25,29},{26,30},{27,31}} | collective-permute-start | bytes 1572872 | tf_op jit(solution)/shard_map/ppermute | solution.py:74
  64.1 36.4 %collective-permute-start.5 = (f32[8,128,128]{2,1,0:T(8,128)}, f32[8,128,128]{2,1,0:T(8,128)}, u32[]{:S(2)}, u32[]{:S(2)}) collective-permute-start(f32[8,128,128]{2,1,0:T(8,128)} %slice_add_fusion.6), channel_id=1, source_target_pairs={{4,0},{5,1},{6,2},{7,3},{20,16},{21,17},{22,18},{23,19}} | collective-permute-start | bytes 1572872 | tf_op jit(solution)/shard_map/ppermute | solution.py:74
  102.4 40.6 %all-to-all-start = ((bf16[4,3,8,128,128]{4,3,2,1,0:T(8,128)(2,1)}), bf16[4,3,8,128,128]{4,3,2,1,0:T(8,128)(2,1)S(1)}, u32[]{:S(2)}, u32[]{:S(2)}) async-start(bf16[4,3,8,128,128]{4,3,2,1,0:T(8,128)(2,1)} %get-tuple-element.20), calls=%async_computation | async-start | bytes 6291456 | tf_op jit(solution)/shard_map/all_to_all | solution.py:158
  143.0 41.7 %all-to-all-start.1 = ((bf16[4,3,8,128,128]{4,3,2,1,0:T(8,128)(2,1)}), bf16[4,3,8,128,128]{4,3,2,1,0:T(8,128)(2,1)}, u32[]{:S(2)}, u32[]{:S(2)}) async-start(bf16[4,3,8,128,128]{4,3,2,1,0:T(8,128)(2,1)} %get-tuple-element.21), calls=%async_computation.1 | async-start | bytes 6291456 | tf_op jit(solution)/shard_map/all_to_all | solution.py:158
  153.8 33.1 %copy-start.4 = (bf16[4,1,8,128,128]{4,3,2,1,0:T(8,128)(2,1)S(1)}, bf16[4,1,8,128,128]{4,3,2,1,0:T(8,128)(2,1)}, u32[]{:S(2)}) copy-start(bf16[4,1,8,128,128]{4,3,2,1,0:T(8,128)(2,1)} %get-tuple-element.30) | copy-start | bytes 3145732
  187.1 2.7 %copy-start.3 = (bf16[4,1,8,128,128]{4,3,2,1,0:T(8,128)(2,1)S(1)}, bf16[4,1,8,128,128]{4,3,2,1,0:T(8,128)(2,1)}, u32[]{:S(2)}) copy-start(bf16[4,1,8,128,128]{4,3,2,1,0:T(8,128)(2,1)} %get-tuple-element.31) | copy-start | bytes 3145732
  190.0 2.7 %copy-start.2 = (bf16[4,1,8,128,128]{4,3,2,1,0:T(8,128)(2,1)S(1)}, bf16[4,1,8,128,128]{4,3,2,1,0:T(8,128)(2,1)}, u32[]{:S(2)}) copy-start(bf16[4,1,8,128,128]{4,3,2,1,0:T(8,128)(2,1)} %get-tuple-element.32) | copy-start | bytes 3145732

commit v17 on v15

--- a/solution.py
+++ b/solution.py
@@ -88,14 +88,17 @@
     scaled = (queries.astype(F32) * factor[:, :, None]).astype(BF16)
     qh, kh, vh, dh = (jnp.transpose(x, (1, 0, 2)) for x in (scaled, key_rows, value_rows, out_adjoint))
 
-    width = 4 if heads % 4 == 0 and heads > 4 else heads
-    groups = heads // width
+    small = heads // 4 if heads % 4 == 0 and heads >= 8 else heads
+    starts = [heads - small, 0] if small < heads else [0]
+    widths = [small, heads - small] if small < heads else [heads]
+    groups = len(widths)
+    width = heads // 2 if heads % 16 == 0 else heads
     state_shape = jax.ShapeDtypeStruct((heads, head_dim, head_dim), F32)
     rows = pl.BlockSpec((width, tok_dev, head_dim), lambda g: (g, 0, 0))
     group_state = pl.BlockSpec((width, head_dim, head_dim), lambda g: (g, 0, 0))
     kv_total, adj_total = pl.pallas_call(
         functools.partial(totals_kernel, width),
-        grid=(groups,),
+        grid=(heads // width,),
         in_specs=[rows] * 4,
         out_specs=[group_state, group_state],
         out_shape=[state_shape, state_shape],
@@ -110,7 +113,7 @@
     grads = []
     chains = []
     for g in range(groups):
-        sel = slice(g * width, (g + 1) * width)
+        sel = slice(starts[g], starts[g] + widths[g])
         before, before_hops = exclusive_scan(kv_total[sel], "seq", seq_count, False)
         after, after_hops = exclusive_scan(adj_total[sel], "seq", seq_count, True)
         chains.append([before, after + adj_total[sel], before_hops, after_hops])
@@ -122,7 +125,9 @@
             )
     for g in range(groups):
         before, rest = chains[g][0], chains[g][1]
-        gtile = pl.BlockSpec((width, span, head_dim), lambda c, g=g: (g, c, 0))
+        width = widths[g]
+        first = starts[g] // width
+        gtile = pl.BlockSpec((width, span, head_dim), lambda c, first=first: (first, c, 0))
         gwhole = pl.BlockSpec((width, head_dim, head_dim), lambda c: (0, 0, 0))
         if split_out:
             otile = pl.BlockSpec(
@@ -158,9 +163,10 @@
         parts = [gr for gr in grads]
     else:
         parts = [gr.reshape(peers, 3, width, tok_out, head_dim) for gr in grads]
+    order = sorted(range(groups), key=lambda g: starts[g])
     outs = tuple(
         jnp.transpose(
-            jnp.stack([p[:, i] for p in parts], 1).reshape(heads * peers, tok_out, head_dim),
+            jnp.concatenate([parts[g][:, i] for g in order], 1).reshape(heads * peers, tok_out, head_dim),
             (1, 0, 2),
         )
         for i in range(3)

time: 225 us -> 215 us (0.956)
  waiting for transfers between devices: 54.2 us -> 104 us
  blocking collectives: 24.5 us -> 0 us
  starting transfers between devices: 45.6 us -> 25.1 us
  Pallas kernels: 54 us -> 46.5 us
  other arithmetic: 16.5 us -> 11.9 us
  local copies, waits for them, and re-layouts: 28.1 us -> 25.5 us
    all_to_all x3 -> x2, waiting for transfers between devices: 12.7 us -> 50.9 us  [per_device(): lax.all_to_all(outs[1], ('head', 'sub'), split_axis=axis, concat_axis=0,...]
    all_to_all x1 -> x0, blocking collectives: 24.5 us -> none  [per_device(): lax.all_to_all(outs[1], ('head', 'sub'), split_axis=axis, concat_axis=0,...]
    ppermute x24 -> x12, starting transfers between devices: 32.9 us -> 16.3 us  [exclusive_scan(): got = lax.ppermute(carried + total, axis, perm=[pair])]
    ppermute x24 -> x12, waiting for transfers between devices: 41.5 us -> 53.6 us  [exclusive_scan(): got = lax.ppermute(carried + total, axis, perm=[pair])]
    pallas_call x4 -> x2, Pallas kernels: 48.1 us -> 41.4 us  [per_device(): pl.pallas_call(functools.partial(main_kernel, width, attended is not None...]
    slice x4 -> x0, local copies, waits for them, and re-layouts: 5.17 us -> none  [per_device(): p[:, i]]
    all_to_all x3 -> x2, starting transfers between devices: 12.7 us -> 8.84 us  [per_device(): lax.all_to_all(outs[1], ('head', 'sub'), split_axis=axis, concat_axis=0,...]
    squeeze x0 -> x2, local copies, waits for them, and re-layouts: none -> 3.41 us  [per_device(): parts[g][:, i]]
  transfers between devices with their start and end apart: 27 -> 14, of which waited for: 8 -> 4; matrix products, arithmetic and copies ran while one was open for 9% -> 6% of each run, Pallas kernels for 21% -> 19%
where the time goes in v17:
time: 215 us
  waiting for transfers between devices  104 us (48%)
  Pallas kernels  46.5 us (22%)
  local copies, waits for them, and re-layouts  25.5 us (12%)
  starting transfers between devices  25.1 us (12%)
  other arithmetic  11.9 us (6%)
    ppermute x12, waiting for transfers between devices, exclusive_scan(): got = lax.ppermute(carried + total, axis, perm=[pair])  53.6 us
    all_to_all x2, waiting for transfers between devices, per_device(): lax.all_to_all(outs[1], ('head', 'sub'), split_axis=axis, concat_axis=0,...  50.9 us
    pallas_call x2, Pallas kernels, per_device(): pl.pallas_call(functools.partial(main_kernel, width, attended is not None...  41.4 us
    ppermute x12, starting transfers between devices, exclusive_scan(): got = lax.ppermute(carried + total, axis, perm=[pair])  16.3 us
    all_to_all x2, starting transfers between devices, per_device(): lax.all_to_all(outs[1], ('head', 'sub'), split_axis=axis, concat_axis=0,...  8.84 us
    unnamed x26, local copies, waits for them, and re-layouts  8.49 us
    reshape x3, local copies, waits for them, and re-layouts, per_device(): jnp.concatenate([parts[g][:, i] for g in order], 1)  8.01 us
    pallas_call x1, Pallas kernels, per_device(): pl.pallas_call(functools.partial(totals_kernel, width), grid=(heads // wi...  5.14 us
  transfers between devices with their start and end apart: 14, of which 4 were waited for; matrix products, arithmetic and copies ran while one was open for 6% of the time, Pallas kernels for 19%

profile of v17, /device:TPU:0, one launch (start us, length us, event | category | flops | bytes accessed | tf_op | source)
XLA Modules:
  0.0 214.5 jit_solution(5415926645721019558)
XLA Ops:
  0.7 3.6 %copy.54 = bf16[512,16,128]{2,0,1:T(8,128)(2,1)} copy(bf16[512,16,128]{2,1,0:T(8,128)(2,1)} %param.5) | data formatting | bytes 4194304 | tf_op args[1]
  4.3 2.0 fusion.q_ref
  7.2 3.3 %copy_bitcast_fusion.3 = (bf16[16,512,128]{2,1,0:T(8,128)(2,1)}, bf16[16,512,128]{2,1,0:T(8,128)(2,1)}) fusion(bf16[512,16,128]{2,1,0:T(8,128)(2,1)S(1)} %copy-done.10, bf16[512,16,128]{2,1,0:T(8,128)(2,1)S(1)} %copy-done.11), kind=kLoop, calls=%fused_computation.8 | loop fusion | bytes 8388608 | tf_op jit(solution)/shard_map/transpose | solution.py:89
  10.5 5.1 %shard_map.75 = (f32[16,128,128]{2,1,0:T(8,128)}, f32[16,128,128]{2,1,0:T(8,128)}) custom-call(bf16[16,512,128]{2,1,0:T(8,128)(2,1)} %fusion.q_ref, bf16[16,512,128]{2,1,0:T(8,128)(2,1)} %bitcast.40, bf16[16,512,128]{2,1,0:T(8,128)(2,1)} %get-tuple-element.39.v_ref, bf16[16,512,128]{2,1,0:T(8,128)(2,1)} %get-tuple-element.38.d_ref), custom_call_target="tpu_custom_call" | custom-call | tf_op jit(solution)/shard_map/pallas_call | solution.py:99
  15.6 1.3 slice.32
  17.0 5.0 %collective-permute-start = (f32[12,128,128]{2,1,0:T(8,128)S(1)}, f32[12,128,128]{2,1,0:T(8,128)S(1)}, u32[]{:S(2)}, u32[]{:S(2)}) collective-permute-start(f32[12,128,128]{2,1,0:T(8,128)S(1)} %slice.32), channel_id=1, source_target_pairs={{0,4},{1,5},{2,6},{3,7},{16,20},{17,21},{18,22},{19,23}} | collective-permute-start | bytes 2359304 | tf_op jit(solution)/shard_map/ppermute | solution.py:74
  27.2 17.1 %collective-permute-done.6 = f32[4,128,128]{2,1,0:T(8,128)S(1)} collective-permute-done((f32[4,128,128]{2,1,0:T(8,128)S(1)}, f32[4,128,128]{2,1,0:T(8,128)S(1)}, u32[]{:S(2)}, u32[]{:S(2)}) %collective-permute-start.6) | collective-permute-done | bytes 262176 | tf_op jit(solution)/shard_map/ppermute | solution.py:74
  48.1 1.6 collective-permute-start.4
  49.6 6.7 %collective-permute-done.11 = f32[4,128,128]{2,1,0:T(8,128)S(1)} collective-permute-done((f32[4,128,128]{2,1,0:T(8,128)S(1)}, f32[4,128,128]{2,1,0:T(8,128)S(1)}, u32[]{:S(2)}, u32[]{:S(2)}) %collective-permute-start.11) | collective-permute-done | bytes 262176 | tf_op jit(solution)/shard_map/ppermute | solution.py:74
  58.3 1.6 collective-permute-start.2
  60.6 12.0 %shard_map.76 = (bf16[16,512,128]{2,1,0:T(8,128)(2,1)}, bf16[4,3,4,128,128]{4,3,2,1,0:T(8,128)(2,1)}) custom-call(bf16[16,512,128]{2,1,0:T(8,128)(2,1)} %fusion.q_ref, bf16[16,512,128]{2,1,0:T(8,128)(2,1)} %bitcast.41, bf16[16,512,128]{2,1,0:T(8,128)(2,1)} %get-tuple-element.39.v_ref, bf16[16,512,128]{2,1,0:T(8,128)(2,1)} %get-tuple-element.38.d_ref, ...), custom_call_target="tpu_custom_call" | custom-call | tf_op jit(solution)/shard_map/pallas_call | solution.py:147
  72.6 3.6 %all-to-all-start.1 = ((bf16[4,3,4,128,128]{4,3,2,1,0:T(8,128)(2,1)}), bf16[4,3,4,128,128]{4,3,2,1,0:T(8,128)(2,1)S(1)}, u32[]{:S(2)}, u32[]{:S(2)}) async-start(bf16[4,3,4,128,128]{4,3,2,1,0:T(8,128)(2,1)} %get-tuple-element.19), calls=%async_computation.1 | async-start | bytes 3145728 | tf_op jit(solution)/shard_map/all_to_all | solution.py:160
  77.5 1.4 collective-permute-start.5
  79.0 2.1 %add_add_fusion.1.before_ref = f32[12,128,128]{2,1,0:T(8,128)} fusion(f32[12,128,128]{2,1,0:T(8,128)} %collective-permute-done.2, f32[12,128,128]{2,1,0:T(8,128)S(1)} %collective-permute-done, f32[12,128,128]{2,1,0:T(8,128)S(1)} %copy-done.6), kind=kLoop, calls=%fused_computation.15 | loop fusion | flops 393216 | bytes 3145728 | tf_op jit(solution)/shard_map/add | solution.py:75
  81.1 29.7 %collective-permute-done.5 = f32[12,128,128]{2,1,0:T(8,128)S(1)} collective-permute-done((f32[12,128,128]{2,1,0:T(8,128)S(1)}, f32[12,128,128]{2,1,0:T(8,128)S(1)}, u32[]{:S(2)}, u32[]{:S(2)}) %collective-permute-start.5) | collective-permute-done | bytes 786464 | tf_op jit(solution)/shard_map/ppermute | solution.py:74
  110.9 2.3 %add_add_fusion.rest_ref = f32[12,128,128]{2,1,0:T(8,128)} fusion(f32[12,128,128]{2,1,0:T(8,128)S(1)} %collective-permute-done.5, f32[12,128,128]{2,1,0:T(8,128)S(1)} %copy-done.8, f32[12,128,128]{2,1,0:T(8,128)} %collective-permute-done.4, f32[16,128,128]{2,1,0:T(8,128)S(1)} %copy-done), kind=kLoop, calls=%fused_computation.14 | loop fusion | flops 589824 | bytes 3932160 | tf_op jit(solution)/shard_map/add | solution.py:119
  113.1 29.4 %shard_map.77 = (bf16[16,512,128]{2,1,0:T(8,128)(2,1)}, bf16[4,3,12,128,128]{4,3,2,1,0:T(8,128)(2,1)}) custom-call(bf16[16,512,128]{2,1,0:T(8,128)(2,1)} %fusion.q_ref, bf16[16,512,128]{2,1,0:T(8,128)(2,1)} %bitcast.42, bf16[16,512,128]{2,1,0:T(8,128)(2,1)} %get-tuple-element.39.v_ref, ...), custom_call_target="tpu_custom_call", output_to_operand_aliasing={{0}: (7, {})} | custom-call | tf_op jit(solution)/shard_map/pallas_call | solution.py:147
  143.7 5.3 %all-to-all-start = ((bf16[4,3,12,128,128]{4,3,2,1,0:T(8,128)(2,1)}), bf16[4,3,12,128,128]{4,3,2,1,0:T(8,128)(2,1)}, u32[]{:S(2)}, u32[]{:S(2)}) async-start(bf16[4,3,12,128,128]{4,3,2,1,0:T(8,128)(2,1)} %get-tuple-element.18), calls=%async_computation | async-start | bytes 9437184 | tf_op jit(solution)/shard_map/all_to_all | solution.py:160
  149.0 2.7 %copy.40 = bf16[512,16,128]{2,1,0:T(8,128)(2,1)} copy(bf16[512,16,128]{2,0,1:T(8,128)(2,1)S(1)} %bitcast.46) | data formatting | bytes 4194304
  151.8 50.9 %all-to-all-done = bf16[4,3,12,128,128]{4,3,2,1,0:T(8,128)(2,1)} async-done(((bf16[4,3,12,128,128]{4,3,2,1,0:T(8,128)(2,1)}), bf16[4,3,12,128,128]{4,3,2,1,0:T(8,128)(2,1)}, u32[]{:S(2)}, u32[]{:S(2)}) %all-to-all-start) | async-done | bytes 4718624 | tf_op jit(solution)/shard_map/all_to_all | solution.py:160
  202.6 3.3 %slice_bitcast_fusion = (bf16[4,12,128,128]{3,2,1,0:T(8,128)(2,1)S(1)}, bf16[4,12,128,128]{3,2,1,0:T(8,128)(2,1)S(1)}, bf16[4,12,128,128]{3,2,1,0:T(8,128)(2,1)S(1)}) fusion(bf16[4,3,12,128,128]{4,3,2,1,0:T(8,128)(2,1)} %all-to-all-done), kind=kLoop, calls=%fused_computation.11 | loop fusion | bytes 9437184 | tf_op jit(solution)/shard_map/squeeze | solution.py:169
  206.1 2.7 %copy.51 = bf16[64,128,128]{2,0,1:T(8,128)(2,1)} copy(bf16[64,128,128]{2,1,0:T(8,128)(2,1)S(1)} %bitcast.43) | data formatting | bytes 4194304 | tf_op jit(solution)/shard_map/reshape | solution.py:169
  209.0 2.7 %copy.52 = bf16[64,128,128]{2,0,1:T(8,128)(2,1)} copy(bf16[64,128,128]{2,1,0:T(8,128)(2,1)S(1)} %bitcast.44) | data formatting | bytes 4194304 | tf_op jit(solution)/shard_map/reshape | solution.py:169
  211.8 2.7 %copy.53 = bf16[64,128,128]{2,0,1:T(8,128)(2,1)} copy(bf16[64,128,128]{2,1,0:T(8,128)(2,1)S(1)} %bitcast.45) | data formatting | bytes 4194304 | tf_op jit(solution)/shard_map/reshape | solution.py:169
  (61 shorter events, 15.6 us)
Async XLA Ops:
  0.6 3.6 %copy-start.9 = (bf16[512,16,128]{2,1,0:T(8,128)(2,1)S(1)}, bf16[512,16,128]{2,1,0:T(8,128)(2,1)}, u32[]{:S(2)}) copy-start(bf16[512,16,128]{2,1,0:T(8,128)(2,1)} %param.4) | copy-start | bytes 6291460
  4.3 2.0 copy-start.10
  4.3 3.0 %copy-start.11 = (bf16[512,16,128]{2,1,0:T(8,128)(2,1)S(1)}, bf16[512,16,128]{2,1,0:T(8,128)(2,1)}, u32[]{:S(2)}) copy-start(bf16[512,16,128]{2,1,0:T(8,128)(2,1)} %param.6) | copy-start | bytes 6291460
  15.6 8.0 %copy-start.1 = (f32[16,128,128]{2,1,0:T(8,128)S(1)}, f32[16,128,128]{2,1,0:T(8,128)}, u32[]{:S(2)}) copy-start(f32[16,128,128]{2,1,0:T(8,128)} %get-tuple-element.12) | copy-start | bytes 3145732
  15.6 9.3 %copy-start = (f32[16,128,128]{2,1,0:T(8,128)S(1)}, f32[16,128,128]{2,1,0:T(8,128)}, u32[]{:S(2)}) copy-start(f32[16,128,128]{2,1,0:T(8,128)} %get-tuple-element.13) | copy-start | bytes 3145732
  17.0 28.1 %collective-permute-start = (f32[12,128,128]{2,1,0:T(8,128)S(1)}, f32[12,128,128]{2,1,0:T(8,128)S(1)}, u32[]{:S(2)}, u32[]{:S(2)}) collective-permute-start(f32[12,128,128]{2,1,0:T(8,128)S(1)} %slice.32), channel_id=1, source_target_pairs={{0,4},{1,5},{2,6},{3,7},{16,20},{17,21},{18,22},{19,23}} | collective-permute-start | bytes 2359304 | tf_op jit(solution)/shard_map/ppermute | solution.py:74
  22.9 3.6 %collective-permute-start.9 = (f32[4,128,128]{2,1,0:T(8,128)S(1)}, f32[4,128,128]{2,1,0:T(8,128)S(1)}, u32[]{:S(2)}, u32[]{:S(2)}) collective-permute-start(f32[4,128,128]{2,1,0:T(8,128)S(1)} %slice.35), channel_id=1, source_target_pairs={{12,8},{13,9},{14,10},{15,11},{28,24},{29,25},{30,26},{31,27}} | collective-permute-start | bytes 786440 | tf_op jit(solution)/shard_map/ppermute | solution.py:74
  23.7 20.7 %collective-permute-start.6 = (f32[4,128,128]{2,1,0:T(8,128)S(1)}, f32[4,128,128]{2,1,0:T(8,128)S(1)}, u32[]{:S(2)}, u32[]{:S(2)}) collective-permute-start(f32[4,128,128]{2,1,0:T(8,128)S(1)} %slice.34), channel_id=1, source_target_pairs={{0,4},{1,5},{2,6},{3,7},{16,20},{17,21},{18,22},{19,23}} | collective-permute-start | bytes 786440 | tf_op jit(solution)/shard_map/ppermute | solution.py:74
  25.0 22.9 %collective-permute-start.3 = (f32[12,128,128]{2,1,0:T(8,128)S(1)}, f32[12,128,128]{2,1,0:T(8,128)S(1)}, u32[]{:S(2)}, u32[]{:S(2)}) collective-permute-start(f32[12,128,128]{2,1,0:T(8,128)S(1)} %slice.33), channel_id=1, source_target_pairs={{12,8},{13,9},{14,10},{15,11},{28,24},{29,25},{30,26},{31,27}} | collective-permute-start | bytes 2359304 | tf_op jit(solution)/shard_map/ppermute | solution.py:74
  26.6 19.3 %collective-permute-start.10 = (f32[4,128,128]{2,1,0:T(8,128)S(1)}, f32[4,128,128]{2,1,0:T(8,128)S(1)}, u32[]{:S(2)}, u32[]{:S(2)}) collective-permute-start(f32[4,128,128]{2,1,0:T(8,128)S(1)} %slice_add_fusion.3), channel_id=1, source_target_pairs={{8,4},{9,5},{10,6},{11,7},{24,20},{25,21},{26,22},{27,23}} | collective-permute-start | bytes 786440 | tf_op jit(solution)/shard_map/ppermute | solution.py:74
  44.4 2.9 %collective-permute-start.7 = (f32[4,128,128]{2,1,0:T(8,128)S(1)}, f32[4,128,128]{2,1,0:T(8,128)S(1)}, u32[]{:S(2)}, u32[]{:S(2)}) collective-permute-start(f32[4,128,128]{2,1,0:T(8,128)S(1)} %slice_add_fusion.1), channel_id=1, source_target_pairs={{4,8},{5,9},{6,10},{7,11},{20,24},{21,25},{22,26},{23,27}} | collective-permute-start | bytes 786440 | tf_op jit(solution)/shard_map/ppermute | solution.py:74
  45.1 12.0 %collective-permute-start.1 = (f32[12,128,128]{2,1,0:T(8,128)S(1)}, f32[12,128,128]{2,1,0:T(8,128)S(1)}, u32[]{:S(2)}, u32[]{:S(2)}) collective-permute-start(f32[12,128,128]{2,1,0:T(8,128)S(1)} %slice_add_fusion.5), channel_id=1, source_target_pairs={{4,8},{5,9},{6,10},{7,11},{20,24},{21,25},{22,26},{23,27}} | collective-permute-start | bytes 2359304 | tf_op jit(solution)/shard_map/ppermute | solution.py:74
  45.9 10.4 %collective-permute-start.11 = (f32[4,128,128]{2,1,0:T(8,128)S(1)}, f32[4,128,128]{2,1,0:T(8,128)S(1)}, u32[]{:S(2)}, u32[]{:S(2)}) collective-permute-start(f32[4,128,128]{2,1,0:T(8,128)S(1)} %slice_add_fusion.2), channel_id=1, source_target_pairs={{4,0},{5,1},{6,2},{7,3},{20,16},{21,17},{22,18},{23,19}} | collective-permute-start | bytes 786440 | tf_op jit(solution)/shard_map/ppermute | solution.py:74
  47.3 12.6 %collective-permute-start.8 = (f32[4,128,128]{2,1,0:T(8,128)S(1)}, f32[4,128,128]{2,1,0:T(8,128)S(1)}, u32[]{:S(2)}, u32[]{:S(2)}) collective-permute-start(f32[4,128,128]{2,1,0:T(8,128)S(1)} %slice_add_fusion), channel_id=1, source_target_pairs={{8,12},{9,13},{10,14},{11,15},{24,28},{25,29},{26,30},{27,31}} | collective-permute-start | bytes 786440 | tf_op jit(solution)/shard_map/ppermute | solution.py:74
  48.0 10.3 %copy-start.7 = (f32[12,128,128]{2,1,0:T(8,128)}, f32[12,128,128]{2,1,0:T(8,128)S(1)}, u32[]{:S(2)}) copy-start(f32[12,128,128]{2,1,0:T(8,128)S(1)} %collective-permute-done.3) | copy-start | bytes 2359300
  48.1 12.6 %collective-permute-start.4 = (f32[12,128,128]{2,1,0:T(8,128)S(1)}, f32[12,128,128]{2,1,0:T(8,128)}, u32[]{:S(2)}, u32[]{:S(2)}) collective-permute-start(f32[12,128,128]{2,1,0:T(8,128)S(1)} %slice_add_fusion.7), channel_id=1, source_target_pairs={{8,4},{9,5},{10,6},{11,7},{24,20},{25,21},{26,22},{27,23}} | collective-permute-start | bytes 2359304 | tf_op jit(solution)/shard_map/ppermute | solution.py:74
  58.3 20.7 %collective-permute-start.2 = (f32[12,128,128]{2,1,0:T(8,128)}, f32[12,128,128]{2,1,0:T(8,128)}, u32[]{:S(2)}, u32[]{:S(2)}) collective-permute-start(f32[12,128,128]{2,1,0:T(8,128)} %slice_add_fusion.4), channel_id=1, source_target_pairs={{8,12},{9,13},{10,14},{11,15},{24,28},{25,29},{26,30},{27,31}} | collective-permute-start | bytes 2359304 | tf_op jit(solution)/shard_map/ppermute | solution.py:74
  72.6 69.9 %all-to-all-start.1 = ((bf16[4,3,4,128,128]{4,3,2,1,0:T(8,128)(2,1)}), bf16[4,3,4,128,128]{4,3,2,1,0:T(8,128)(2,1)S(1)}, u32[]{:S(2)}, u32[]{:S(2)}) async-start(bf16[4,3,4,128,128]{4,3,2,1,0:T(8,128)(2,1)} %get-tuple-element.19), calls=%async_computation.1 | async-start | bytes 3145728 | tf_op jit(solution)/shard_map/all_to_all | solution.py:160
  76.2 2.8 %copy-start.6 = (f32[12,128,128]{2,1,0:T(8,128)S(1)}, f32[12,128,128]{2,1,0:T(8,128)}, u32[]{:S(2)}) copy-start(f32[12,128,128]{2,1,0:T(8,128)} %copy-done.5) | copy-start | bytes 2359300
  77.5 33.4 %copy-start.8 = (f32[12,128,128]{2,1,0:T(8,128)S(1)}, f32[12,128,128]{2,1,0:T(8,128)}, u32[]{:S(2)}) copy-start(f32[12,128,128]{2,1,0:T(8,128)} %copy-done.7) | copy-start | bytes 2359300
  77.5 33.3 %collective-permute-start.5 = (f32[12,128,128]{2,1,0:T(8,128)S(1)}, f32[12,128,128]{2,1,0:T(8,128)S(1)}, u32[]{:S(2)}, u32[]{:S(2)}) collective-permute-start(f32[12,128,128]{2,1,0:T(8,128)S(1)} %slice_add_fusion.6), channel_id=1, source_target_pairs={{4,0},{5,1},{6,2},{7,3},{20,16},{21,17},{22,18},{23,19}} | collective-permute-start | bytes 2359304 | tf_op jit(solution)/shard_map/ppermute | solution.py:74
  143.7 5.3 %copy-start.2 = (bf16[16,512,128]{2,1,0:T(8,128)(2,1)S(1)}, bf16[16,512,128]{2,1,0:T(8,128)(2,1)}, u32[]{:S(2)}) copy-start(bf16[16,512,128]{2,1,0:T(8,128)(2,1)} %get-tuple-element.17) | copy-start | bytes 6291460
  143.7 59.0 %all-to-all-start = ((bf16[4,3,12,128,128]{4,3,2,1,0:T(8,128)(2,1)}), bf16[4,3,12,128,128]{4,3,2,1,0:T(8,128)(2,1)}, u32[]{:S(2)}, u32[]{:S(2)}) async-start(bf16[4,3,12,128,128]{4,3,2,1,0:T(8,128)(2,1)} %get-tuple-element.18), calls=%async_computation | async-start | bytes 9437184 | tf_op jit(solution)/shard_map/all_to_all | solution.py:160
  149.0 2.7 %copy-start.4 = (bf16[4,3,4,128,128]{4,3,2,1,0:T(8,128)(2,1)S(1)}, bf16[4,3,4,128,128]{4,3,2,1,0:T(8,128)(2,1)}, u32[]{:S(2)}) copy-start(bf16[4,3,4,128,128]{4,3,2,1,0:T(8,128)(2,1)} %copy-done.3) | copy-start | bytes 4718596
  (2 other events, 2.3 us)

commit v18 on v13

--- a/solution.py
+++ b/solution.py
@@ -148,6 +148,11 @@
             scratch_shapes=[pltpu.VMEM((width, head_dim, head_dim), F32)] * 2,
             input_output_aliases=aliases,
             compiler_params=pltpu.CompilerParams(dimension_semantics=("arbitrary",)),
+            cost_estimate=pl.CostEstimate(
+                flops=360 * width * tok_dev * span * head_dim * head_dim // span,
+                transcendentals=0,
+                bytes_accessed=16 * width * tok_dev * head_dim,
+            ),
         )(*args)
         attended = outs[0]
         axis = 0 if split_out else 2

time: 189 us -> 189 us (level)
  the two profiles are of different devices: /device:TPU:0 before, /device:TPU:8 now
where the time goes in v18:
time: 189 us; the launch traced here: 188 us
  waiting for transfers between devices  77.2 us (41%)
  Pallas kernels  46.5 us (25%)
  local copies, waits for them, and re-layouts  27.3 us (14%)
  starting transfers between devices  25.1 us (13%)
  other arithmetic  11.5 us (6%)
    pallas_call x2, Pallas kernels, per_device(): pl.pallas_call(functools.partial(main_kernel, width, attended is not None...  41.4 us
    all_to_all x2, waiting for transfers between devices, per_device(): lax.all_to_all(outs[1], ('head', 'sub'), split_axis=axis, concat_axis=0,...  41.2 us
    ppermute x12, waiting for transfers between devices, exclusive_scan(): got = lax.ppermute(carried + total, axis, perm=[pair])  36 us
    ppermute x12, starting transfers between devices, exclusive_scan(): got = lax.ppermute(carried + total, axis, perm=[pair])  16.5 us
    unnamed x18, local copies, waits for them, and re-layouts  9.86 us
    all_to_all x2, starting transfers between devices, per_device(): lax.all_to_all(outs[1], ('head', 'sub'), split_axis=axis, concat_axis=0,...  8.53 us
    reshape x3, local copies, waits for them, and re-layouts, per_device(): jnp.stack([p[:, i] for p in parts], 1)  8.01 us
    pallas_call x1, Pallas kernels, per_device(): pl.pallas_call(functools.partial(totals_kernel, width), grid=(groups,), i...  5.13 us
  transfers between devices with their start and end apart: 14, of which 8 were waited for; matrix products, arithmetic and copies ran while one was open for 9% of the time, Pallas kernels for 22%

profile of v18, /device:TPU:8, one launch (start us, length us, event | category | flops | bytes accessed | tf_op | source)
XLA Modules:
  0.0 188.4 jit_solution(16823542827938967734)
XLA Ops:
  0.7 3.6 %copy.36 = bf16[512,16,128]{2,0,1:T(8,128)(2,1)} copy(bf16[512,16,128]{2,1,0:T(8,128)(2,1)} %param.5) | data formatting | bytes 4194304 | tf_op args[1]
  4.3 2.0 %fusion.q_ref = bf16[16,512,128]{2,1,0:T(8,128)(2,1)} fusion(bf16[512,16,128]{2,1,0:T(8,128)(2,1)S(1)} %copy-done.5, f32[512]{0:T(512)S(1)} %multiply_rsqrt_fusion.1), kind=kLoop, calls=%fused_computation.1 | loop fusion | flops 3145728 | bytes 4196352 | tf_op jit(solution)/shard_map/transpose | solution.py:89
  7.2 3.3 %copy_bitcast_fusion.3 = (bf16[16,512,128]{2,1,0:T(8,128)(2,1)}, bf16[16,512,128]{2,1,0:T(8,128)(2,1)}) fusion(bf16[512,16,128]{2,1,0:T(8,128)(2,1)S(1)} %copy-done.6, bf16[512,16,128]{2,1,0:T(8,128)(2,1)S(1)} %copy-done.7), kind=kLoop, calls=%fused_computation.8 | loop fusion | bytes 8388608 | tf_op jit(solution)/shard_map/transpose | solution.py:89
  10.5 5.1 %shard_map.75 = (f32[16,128,128]{2,1,0:T(8,128)}, f32[16,128,128]{2,1,0:T(8,128)}) custom-call(bf16[16,512,128]{2,1,0:T(8,128)(2,1)} %fusion.q_ref, bf16[16,512,128]{2,1,0:T(8,128)(2,1)} %bitcast.25, bf16[16,512,128]{2,1,0:T(8,128)(2,1)} %get-tuple-element.43.v_ref, bf16[16,512,128]{2,1,0:T(8,128)(2,1)} %get-tuple-element.42.d_ref), custom_call_target="tpu_custom_call" | custom-call | tf_op jit(solution)/shard_map/pallas_call | solution.py:96
  21.3 12.9 %collective-permute-done.6 = f32[8,128,128]{2,1,0:T(8,128)S(1)} collective-permute-done((f32[8,128,128]{2,1,0:T(8,128)S(1)}, f32[8,128,128]{2,1,0:T(8,128)S(1)}, u32[]{:S(2)}, u32[]{:S(2)}) %collective-permute-start.6) | collective-permute-done | bytes 524320 | tf_op jit(solution)/shard_map/ppermute | solution.py:74
  34.3 3.1 %collective-permute-start.7 = (f32[8,128,128]{2,1,0:T(8,128)S(1)}, f32[8,128,128]{2,1,0:T(8,128)S(1)}, u32[]{:S(2)}, u32[]{:S(2)}) collective-permute-start(f32[8,128,128]{2,1,0:T(8,128)S(1)} %get-tuple-element.40), channel_id=1, source_target_pairs={{4,8},{5,9},{6,10},{7,11},{20,24},{21,25},{22,26},{23,27}} | collective-permute-start | bytes 1572872 | tf_op jit(solution)/shard_map/ppermute | solution.py:74
  38.8 7.6 %collective-permute-done.10 = f32[8,128,128]{2,1,0:T(8,128)S(1)} collective-permute-done((f32[8,128,128]{2,1,0:T(8,128)S(1)}, f32[8,128,128]{2,1,0:T(8,128)S(1)}, u32[]{:S(2)}, u32[]{:S(2)}) %collective-permute-start.10) | collective-permute-done | bytes 524320 | tf_op jit(solution)/shard_map/ppermute | solution.py:74
  48.6 3.3 %collective-permute-done = f32[8,128,128]{2,1,0:T(8,128)S(1)} collective-permute-done((f32[8,128,128]{2,1,0:T(8,128)S(1)}, f32[8,128,128]{2,1,0:T(8,128)S(1)}, u32[]{:S(2)}, u32[]{:S(2)}) %collective-permute-start) | collective-permute-done | bytes 524320 | tf_op jit(solution)/shard_map/ppermute | solution.py:74
  54.8 2.9 %collective-permute-done.11 = f32[8,128,128]{2,1,0:T(8,128)S(1)} collective-permute-done((f32[8,128,128]{2,1,0:T(8,128)S(1)}, f32[8,128,128]{2,1,0:T(8,128)S(1)}, u32[]{:S(2)}, u32[]{:S(2)}) %collective-permute-start.11) | collective-permute-done | bytes 524320 | tf_op jit(solution)/shard_map/ppermute | solution.py:74
  60.1 2.6 %collective-permute-done.1 = f32[8,128,128]{2,1,0:T(8,128)S(1)} collective-permute-done((f32[8,128,128]{2,1,0:T(8,128)S(1)}, f32[8,128,128]{2,1,0:T(8,128)S(1)}, u32[]{:S(2)}, u32[]{:S(2)}) %collective-permute-start.1) | collective-permute-done | bytes 524320 | tf_op jit(solution)/shard_map/ppermute | solution.py:74
  66.0 6.7 %collective-permute-done.4 = f32[8,128,128]{2,1,0:T(8,128)S(1)} collective-permute-done((f32[8,128,128]{2,1,0:T(8,128)S(1)}, f32[8,128,128]{2,1,0:T(8,128)S(1)}, u32[]{:S(2)}, u32[]{:S(2)}) %collective-permute-start.4) | collective-permute-done | bytes 524320 | tf_op jit(solution)/shard_map/ppermute | solution.py:74
  73.5 2.1 %collective-permute-start.5 = (f32[8,128,128]{2,1,0:T(8,128)}, f32[8,128,128]{2,1,0:T(8,128)}, u32[]{:S(2)}, u32[]{:S(2)}) collective-permute-start(f32[8,128,128]{2,1,0:T(8,128)} %slice_add_fusion.6), channel_id=1, source_target_pairs={{4,0},{5,1},{6,2},{7,3},{20,16},{21,17},{22,18},{23,19}} | collective-permute-start | bytes 1572872 | tf_op jit(solution)/shard_map/ppermute | solution.py:74
  75.6 20.7 %shard_map.76 = (bf16[16,512,128]{2,1,0:T(8,128)(2,1)}, bf16[4,3,8,128,128]{4,3,2,1,0:T(8,128)(2,1)}) custom-call(bf16[16,512,128]{2,1,0:T(8,128)(2,1)} %fusion.q_ref, bf16[16,512,128]{2,1,0:T(8,128)(2,1)} %bitcast.26, bf16[16,512,128]{2,1,0:T(8,128)(2,1)} %get-tuple-element.43.v_ref, bf16[16,512,128]{2,1,0:T(8,128)(2,1)} %get-tuple-element.42.d_ref, ...), custom_call_target="tpu_custom_call" | custom-call | flops 24159191040 | bytes 8388608 | tf_op jit(solution)/shard_map/pallas_call | solution.py:142
  96.3 4.6 %all-to-all-start = ((bf16[4,3,8,128,128]{4,3,2,1,0:T(8,128)(2,1)}), bf16[4,3,8,128,128]{4,3,2,1,0:T(8,128)(2,1)}, u32[]{:S(2)}, u32[]{:S(2)}) async-start(bf16[4,3,8,128,128]{4,3,2,1,0:T(8,128)(2,1)} %get-tuple-element.18), calls=%async_computation | async-start | bytes 6291456 | tf_op jit(solution)/shard_map/all_to_all | solution.py:160
  102.9 2.0 %add_add_fusion.2.rest_ref = f32[8,128,128]{2,1,0:T(8,128)} fusion(f32[8,128,128]{2,1,0:T(8,128)} %collective-permute-done.5, f32[8,128,128]{2,1,0:T(8,128)S(1)} %collective-permute-done.3, f32[8,128,128]{2,1,0:T(8,128)S(1)} %collective-permute-done.4, f32[16,128,128]{2,1,0:T(8,128)S(1)} %copy-done), kind=kLoop, calls=%fused_computation.13 | loop fusion | flops 393216 | bytes 2621440 | tf_op jit(solution)/shard_map/add | solution.py:116
  104.9 20.7 %shard_map.77 = (bf16[16,512,128]{2,1,0:T(8,128)(2,1)}, bf16[4,3,8,128,128]{4,3,2,1,0:T(8,128)(2,1)}) custom-call(bf16[16,512,128]{2,1,0:T(8,128)(2,1)} %fusion.q_ref, bf16[16,512,128]{2,1,0:T(8,128)(2,1)} %bitcast.27, bf16[16,512,128]{2,1,0:T(8,128)(2,1)} %get-tuple-element.43.v_ref, ...), custom_call_target="tpu_custom_call", output_to_operand_aliasing={{0}: (7, {})} | custom-call | flops 24159191040 | bytes 8388608 | tf_op jit(solution)/shard_map/pallas_call | solution.py:142
  125.5 12.4 %all-to-all-done = bf16[4,3,8,128,128]{4,3,2,1,0:T(8,128)(2,1)} async-done(((bf16[4,3,8,128,128]{4,3,2,1,0:T(8,128)(2,1)}), bf16[4,3,8,128,128]{4,3,2,1,0:T(8,128)(2,1)}, u32[]{:S(2)}, u32[]{:S(2)}) %all-to-all-start) | async-done | bytes 3145760 | tf_op jit(solution)/shard_map/all_to_all | solution.py:160
  137.9 3.9 %all-to-all-start.1 = ((bf16[4,3,8,128,128]{4,3,2,1,0:T(8,128)(2,1)}), bf16[4,3,8,128,128]{4,3,2,1,0:T(8,128)(2,1)S(1)}, u32[]{:S(2)}, u32[]{:S(2)}) async-start(bf16[4,3,8,128,128]{4,3,2,1,0:T(8,128)(2,1)} %get-tuple-element.19), calls=%async_computation.1 | async-start | bytes 6291456 | tf_op jit(solution)/shard_map/all_to_all | solution.py:160
  141.8 4.3 %copy.25 = bf16[512,16,128]{2,1,0:T(8,128)(2,1)} copy(bf16[512,16,128]{2,0,1:T(8,128)(2,1)} %bitcast.28) | data formatting | bytes 4194304
  146.1 3.6 %fusion.1 = (bf16[4,1,8,128,128]{4,3,2,1,0:T(8,128)(2,1)}, bf16[4,1,8,128,128]{4,3,2,1,0:T(8,128)(2,1)}, bf16[4,1,8,128,128]{4,3,2,1,0:T(8,128)(2,1)}) fusion(bf16[4,3,8,128,128]{4,3,2,1,0:T(8,128)(2,1)} %all-to-all-done), kind=kLoop, calls=%fused_computation.25 | loop fusion | bytes 6291456 | tf_op jit(solution)/shard_map/slice | solution.py:168
  149.7 28.8 %all-to-all-done.1 = bf16[4,3,8,128,128]{4,3,2,1,0:T(8,128)(2,1)S(1)} async-done(((bf16[4,3,8,128,128]{4,3,2,1,0:T(8,128)(2,1)}), bf16[4,3,8,128,128]{4,3,2,1,0:T(8,128)(2,1)S(1)}, u32[]{:S(2)}, u32[]{:S(2)}) %all-to-all-start.1) | async-done | bytes 3145760 | tf_op jit(solution)/shard_map/all_to_all | solution.py:160
  180.0 2.7 %copy.33 = bf16[64,128,128]{2,0,1:T(8,128)(2,1)} copy(bf16[64,128,128]{2,1,0:T(8,128)(2,1)S(1)} %bitcast.22) | data formatting | bytes 4194304 | tf_op jit(solution)/shard_map/reshape | solution.py:168
  182.9 2.7 %copy.34 = bf16[64,128,128]{2,0,1:T(8,128)(2,1)} copy(bf16[64,128,128]{2,1,0:T(8,128)(2,1)S(1)} %bitcast.23) | data formatting | bytes 4194304 | tf_op jit(solution)/shard_map/reshape | solution.py:168
  185.7 2.7 %copy.35 = bf16[64,128,128]{2,0,1:T(8,128)(2,1)} copy(bf16[64,128,128]{2,1,0:T(8,128)(2,1)S(1)} %bitcast.24) | data formatting | bytes 4194304 | tf_op jit(solution)/shard_map/reshape | solution.py:168
  (49 shorter events, 23.4 us)
Async XLA Ops:
  0.6 3.6 %copy-start.5 = (bf16[512,16,128]{2,1,0:T(8,128)(2,1)S(1)}, bf16[512,16,128]{2,1,0:T(8,128)(2,1)}, u32[]{:S(2)}) copy-start(bf16[512,16,128]{2,1,0:T(8,128)(2,1)} %param.4) | copy-start | bytes 6291460
  4.3 2.0 %copy-start.6 = (bf16[512,16,128]{2,1,0:T(8,128)(2,1)S(1)}, bf16[512,16,128]{2,1,0:T(8,128)(2,1)}, u32[]{:S(2)}) copy-start(bf16[512,16,128]{2,1,0:T(8,128)(2,1)} %param.7) | copy-start | bytes 6291460
  4.3 3.0 %copy-start.7 = (bf16[512,16,128]{2,1,0:T(8,128)(2,1)S(1)}, bf16[512,16,128]{2,1,0:T(8,128)(2,1)}, u32[]{:S(2)}) copy-start(bf16[512,16,128]{2,1,0:T(8,128)(2,1)} %param.6) | copy-start | bytes 6291460
  15.6 4.3 %copy-start = (f32[16,128,128]{2,1,0:T(8,128)S(1)}, f32[16,128,128]{2,1,0:T(8,128)}, u32[]{:S(2)}) copy-start(f32[16,128,128]{2,1,0:T(8,128)} %get-tuple-element.13) | copy-start | bytes 3145732
  15.6 18.6 %copy-start.1 = (f32[16,128,128]{2,1,0:T(8,128)S(1)}, f32[16,128,128]{2,1,0:T(8,128)}, u32[]{:S(2)}) copy-start(f32[16,128,128]{2,1,0:T(8,128)} %get-tuple-element.12) | copy-start | bytes 3145732
  16.9 3.1 %collective-permute-start.9 = (f32[8,128,128]{2,1,0:T(8,128)S(1)}, f32[8,128,128]{2,1,0:T(8,128)S(1)}, u32[]{:S(2)}, u32[]{:S(2)}) collective-permute-start(f32[8,128,128]{2,1,0:T(8,128)S(1)} %slice.35), channel_id=1, source_target_pairs={{12,8},{13,9},{14,10},{15,11},{28,24},{29,25},{30,26},{31,27}} | collective-permute-start | bytes 1572872 | tf_op jit(solution)/shard_map/ppermute | solution.py:74
  18.7 15.6 %collective-permute-start.6 = (f32[8,128,128]{2,1,0:T(8,128)S(1)}, f32[8,128,128]{2,1,0:T(8,128)S(1)}, u32[]{:S(2)}, u32[]{:S(2)}) collective-permute-start(f32[8,128,128]{2,1,0:T(8,128)S(1)} %slice.34), channel_id=1, source_target_pairs={{0,4},{1,5},{2,6},{3,7},{16,20},{17,21},{18,22},{19,23}} | collective-permute-start | bytes 1572872 | tf_op jit(solution)/shard_map/ppermute | solution.py:74
  20.0 26.4 %collective-permute-start.10 = (f32[8,128,128]{2,1,0:T(8,128)S(1)}, f32[8,128,128]{2,1,0:T(8,128)S(1)}, u32[]{:S(2)}, u32[]{:S(2)}) collective-permute-start(f32[8,128,128]{2,1,0:T(8,128)S(1)} %slice_add_fusion.5), channel_id=1, source_target_pairs={{8,4},{9,5},{10,6},{11,7},{24,20},{25,21},{26,22},{27,23}} | collective-permute-start | bytes 1572872 | tf_op jit(solution)/shard_map/ppermute | solution.py:74
  34.3 14.2 %collective-permute-start.7 = (f32[8,128,128]{2,1,0:T(8,128)S(1)}, f32[8,128,128]{2,1,0:T(8,128)S(1)}, u32[]{:S(2)}, u32[]{:S(2)}) collective-permute-start(f32[8,128,128]{2,1,0:T(8,128)S(1)} %get-tuple-element.40), channel_id=1, source_target_pairs={{4,8},{5,9},{6,10},{7,11},{20,24},{21,25},{22,26},{23,27}} | collective-permute-start | bytes 1572872 | tf_op jit(solution)/shard_map/ppermute | solution.py:74
  37.5 14.4 %collective-permute-start = (f32[8,128,128]{2,1,0:T(8,128)S(1)}, f32[8,128,128]{2,1,0:T(8,128)S(1)}, u32[]{:S(2)}, u32[]{:S(2)}) collective-permute-start(f32[8,128,128]{2,1,0:T(8,128)S(1)} %get-tuple-element.41), channel_id=1, source_target_pairs={{0,4},{1,5},{2,6},{3,7},{16,20},{17,21},{18,22},{19,23}} | collective-permute-start | bytes 1572872 | tf_op jit(solution)/shard_map/ppermute | solution.py:74
  46.5 11.2 %collective-permute-start.11 = (f32[8,128,128]{2,1,0:T(8,128)S(1)}, f32[8,128,128]{2,1,0:T(8,128)S(1)}, u32[]{:S(2)}, u32[]{:S(2)}) collective-permute-start(f32[8,128,128]{2,1,0:T(8,128)S(1)} %get-tuple-element.36), channel_id=1, source_target_pairs={{4,0},{5,1},{6,2},{7,3},{20,16},{21,17},{22,18},{23,19}} | collective-permute-start | bytes 1572872 | tf_op jit(solution)/shard_map/ppermute | solution.py:74
  47.8 9.9 %collective-permute-start.3 = (f32[8,128,128]{2,1,0:T(8,128)S(1)}, f32[8,128,128]{2,1,0:T(8,128)S(1)}, u32[]{:S(2)}, u32[]{:S(2)}) collective-permute-start(f32[8,128,128]{2,1,0:T(8,128)S(1)} %get-tuple-element.37), channel_id=1, source_target_pairs={{12,8},{13,9},{14,10},{15,11},{28,24},{29,25},{30,26},{31,27}} | collective-permute-start | bytes 1572872 | tf_op jit(solution)/shard_map/ppermute | solution.py:74
  52.0 10.7 %collective-permute-start.1 = (f32[8,128,128]{2,1,0:T(8,128)S(1)}, f32[8,128,128]{2,1,0:T(8,128)S(1)}, u32[]{:S(2)}, u32[]{:S(2)}) collective-permute-start(f32[8,128,128]{2,1,0:T(8,128)S(1)} %get-tuple-element.39), channel_id=1, source_target_pairs={{4,8},{5,9},{6,10},{7,11},{20,24},{21,25},{22,26},{23,27}} | collective-permute-start | bytes 1572872 | tf_op jit(solution)/shard_map/ppermute | solution.py:74
  54.2 10.9 %collective-permute-start.8 = (f32[8,128,128]{2,1,0:T(8,128)S(1)}, f32[8,128,128]{2,1,0:T(8,128)S(1)}, u32[]{:S(2)}, u32[]{:S(2)}) collective-permute-start(f32[8,128,128]{2,1,0:T(8,128)S(1)} %get-tuple-element.38), channel_id=1, source_target_pairs={{8,12},{9,13},{10,14},{11,15},{24,28},{25,29},{26,30},{27,31}} | collective-permute-start | bytes 1572872 | tf_op jit(solution)/shard_map/ppermute | solution.py:74
  58.8 13.8 %collective-permute-start.4 = (f32[8,128,128]{2,1,0:T(8,128)S(1)}, f32[8,128,128]{2,1,0:T(8,128)S(1)}, u32[]{:S(2)}, u32[]{:S(2)}) collective-permute-start(f32[8,128,128]{2,1,0:T(8,128)S(1)} %get-tuple-element.35), channel_id=1, source_target_pairs={{8,4},{9,5},{10,6},{11,7},{24,20},{25,21},{26,22},{27,23}} | collective-permute-start | bytes 1572872 | tf_op jit(solution)/shard_map/ppermute | solution.py:74
  63.6 37.3 %collective-permute-start.2 = (f32[8,128,128]{2,1,0:T(8,128)}, f32[8,128,128]{2,1,0:T(8,128)}, u32[]{:S(2)}, u32[]{:S(2)}) collective-permute-start(f32[8,128,128]{2,1,0:T(8,128)} %slice_add_fusion.2), channel_id=1, source_target_pairs={{8,12},{9,13},{10,14},{11,15},{24,28},{25,29},{26,30},{27,31}} | collective-permute-start | bytes 1572872 | tf_op jit(solution)/shard_map/ppermute | solution.py:74
  73.5 29.4 %collective-permute-start.5 = (f32[8,128,128]{2,1,0:T(8,128)}, f32[8,128,128]{2,1,0:T(8,128)}, u32[]{:S(2)}, u32[]{:S(2)}) collective-permute-start(f32[8,128,128]{2,1,0:T(8,128)} %slice_add_fusion.6), channel_id=1, source_target_pairs={{4,0},{5,1},{6,2},{7,3},{20,16},{21,17},{22,18},{23,19}} | collective-permute-start | bytes 1572872 | tf_op jit(solution)/shard_map/ppermute | solution.py:74
  96.3 41.6 %all-to-all-start = ((bf16[4,3,8,128,128]{4,3,2,1,0:T(8,128)(2,1)}), bf16[4,3,8,128,128]{4,3,2,1,0:T(8,128)(2,1)}, u32[]{:S(2)}, u32[]{:S(2)}) async-start(bf16[4,3,8,128,128]{4,3,2,1,0:T(8,128)(2,1)} %get-tuple-element.18), calls=%async_computation | async-start | bytes 6291456 | tf_op jit(solution)/shard_map/all_to_all | solution.py:160
  137.9 40.6 %all-to-all-start.1 = ((bf16[4,3,8,128,128]{4,3,2,1,0:T(8,128)(2,1)}), bf16[4,3,8,128,128]{4,3,2,1,0:T(8,128)(2,1)S(1)}, u32[]{:S(2)}, u32[]{:S(2)}) async-start(bf16[4,3,8,128,128]{4,3,2,1,0:T(8,128)(2,1)} %get-tuple-element.19), calls=%async_computation.1 | async-start | bytes 6291456 | tf_op jit(solution)/shard_map/all_to_all | solution.py:160
  178.6 1.2 copy-start.4
  180.0 2.7 %copy-start.3 = (bf16[4,1,8,128,128]{4,3,2,1,0:T(8,128)(2,1)S(1)}, bf16[4,1,8,128,128]{4,3,2,1,0:T(8,128)(2,1)}, u32[]{:S(2)}) copy-start(bf16[4,1,8,128,128]{4,3,2,1,0:T(8,128)(2,1)} %get-tuple-element.29) | copy-start | bytes 3145732
  182.9 2.7 %copy-start.2 = (bf16[4,1,8,128,128]{4,3,2,1,0:T(8,128)(2,1)S(1)}, bf16[4,1,8,128,128]{4,3,2,1,0:T(8,128)(2,1)}, u32[]{:S(2)}) copy-start(bf16[4,1,8,128,128]{4,3,2,1,0:T(8,128)(2,1)} %get-tuple-element.30) | copy-start | bytes 3145732

commit v19 on v17

--- a/solution.py
+++ b/solution.py
@@ -153,6 +153,11 @@
             scratch_shapes=[pltpu.VMEM((width, head_dim, head_dim), F32)] * 2,
             input_output_aliases=aliases,
             compiler_params=pltpu.CompilerParams(dimension_semantics=("arbitrary",)),
+            cost_estimate=pl.CostEstimate(
+                flops=360 * width * tok_dev * span * head_dim * head_dim // span,
+                transcendentals=0,
+                bytes_accessed=16 * width * tok_dev * head_dim,
+            ),
         )(*args)
         attended = outs[0]
         axis = 0 if split_out else 2

time: 215 us -> 191 us (0.89)
  waiting for transfers between devices: 104 us -> 79.3 us
    ppermute x12, waiting for transfers between devices: 53.6 us -> 30 us  [exclusive_scan(): got = lax.ppermute(carried + total, axis, perm=[pair])]
    unnamed x26 -> x20, local copies, waits for them, and re-layouts: 8.49 us -> 8.86 us
  transfers between devices with their start and end apart: 14 -> 14, of which waited for: 4 -> 4; matrix products, arithmetic and copies ran while one was open for 6% -> 9% of each run, Pallas kernels for 19% -> 22%
where the time goes in v19:
time: 191 us; the launch traced here: 190 us
  waiting for transfers between devices  79.3 us (42%)
  Pallas kernels  46.5 us (24%)
  local copies, waits for them, and re-layouts  26.9 us (14%)
  starting transfers between devices  24 us (13%)
  other arithmetic  12.2 us (6%)
    all_to_all x2, waiting for transfers between devices, per_device(): lax.all_to_all(outs[1], ('head', 'sub'), split_axis=axis, concat_axis=0,...  49.2 us
    pallas_call x2, Pallas kernels, per_device(): pl.pallas_call(functools.partial(main_kernel, width, attended is not None...  41.4 us
    ppermute x12, waiting for transfers between devices, exclusive_scan(): got = lax.ppermute(carried + total, axis, perm=[pair])  30 us
    ppermute x12, starting transfers between devices, exclusive_scan(): got = lax.ppermute(carried + total, axis, perm=[pair])  15.3 us
    unnamed x20, local copies, waits for them, and re-layouts  8.86 us
    all_to_all x2, starting transfers between devices, per_device(): lax.all_to_all(outs[1], ('head', 'sub'), split_axis=axis, concat_axis=0,...  8.73 us
    reshape x3, local copies, waits for them, and re-layouts, per_device(): jnp.concatenate([parts[g][:, i] for g in order], 1)  8.01 us
    pallas_call x1, Pallas kernels, per_device(): pl.pallas_call(functools.partial(totals_kernel, width), grid=(heads // wi...  5.13 us
  transfers between devices with their start and end apart: 14, of which 4 were waited for; matrix products, arithmetic and copies ran while one was open for 9% of the time, Pallas kernels for 22%

profile of v19, /device:TPU:0, one launch (start us, length us, event | category | flops | bytes accessed | tf_op | source)
XLA Modules:
  0.0 189.8 jit_solution(3255119162070879235)
XLA Ops:
  0.7 3.6 %copy.54 = bf16[512,16,128]{2,0,1:T(8,128)(2,1)} copy(bf16[512,16,128]{2,1,0:T(8,128)(2,1)} %param.5) | data formatting | bytes 4194304 | tf_op args[1]
  4.3 2.0 %fusion.q_ref = bf16[16,512,128]{2,1,0:T(8,128)(2,1)} fusion(bf16[512,16,128]{2,1,0:T(8,128)(2,1)S(1)} %copy-done.6, f32[512]{0:T(512)S(1)} %multiply_rsqrt_fusion.1), kind=kLoop, calls=%fused_computation.1 | loop fusion | flops 3145728 | bytes 4196352 | tf_op jit(solution)/shard_map/transpose | solution.py:89
  7.2 3.3 %copy_bitcast_fusion.3 = (bf16[16,512,128]{2,1,0:T(8,128)(2,1)}, bf16[16,512,128]{2,1,0:T(8,128)(2,1)}) fusion(bf16[512,16,128]{2,1,0:T(8,128)(2,1)S(1)} %copy-done.7, bf16[512,16,128]{2,1,0:T(8,128)(2,1)S(1)} %copy-done.8), kind=kLoop, calls=%fused_computation.8 | loop fusion | bytes 8388608 | tf_op jit(solution)/shard_map/transpose | solution.py:89
  10.5 5.1 %shard_map.75 = (f32[16,128,128]{2,1,0:T(8,128)}, f32[16,128,128]{2,1,0:T(8,128)}) custom-call(bf16[16,512,128]{2,1,0:T(8,128)(2,1)} %fusion.q_ref, bf16[16,512,128]{2,1,0:T(8,128)(2,1)} %bitcast.43, bf16[16,512,128]{2,1,0:T(8,128)(2,1)} %get-tuple-element.39.v_ref, bf16[16,512,128]{2,1,0:T(8,128)(2,1)} %get-tuple-element.38.d_ref), custom_call_target="tpu_custom_call" | custom-call | tf_op jit(solution)/shard_map/pallas_call | solution.py:99
  18.4 4.9 %collective-permute-start.6 = (f32[4,128,128]{2,1,0:T(8,128)S(1)}, f32[4,128,128]{2,1,0:T(8,128)S(1)}, u32[]{:S(2)}, u32[]{:S(2)}) collective-permute-start(f32[4,128,128]{2,1,0:T(8,128)S(1)} %slice.34), channel_id=1, source_target_pairs={{0,4},{1,5},{2,6},{3,7},{16,20},{17,21},{18,22},{19,23}} | collective-permute-start | bytes 786440 | tf_op jit(solution)/shard_map/ppermute | solution.py:74
  25.4 1.3 collective-permute-start
  27.4 2.6 %collective-permute-done.6 = f32[4,128,128]{2,1,0:T(8,128)S(1)} collective-permute-done((f32[4,128,128]{2,1,0:T(8,128)S(1)}, f32[4,128,128]{2,1,0:T(8,128)S(1)}, u32[]{:S(2)}, u32[]{:S(2)}) %collective-permute-start.6) | collective-permute-done | bytes 262176 | tf_op jit(solution)/shard_map/ppermute | solution.py:74
  31.6 1.3 collective-permute-start.11
  34.4 11.3 %collective-permute-done = f32[12,128,128]{2,1,0:T(8,128)S(1)} collective-permute-done((f32[12,128,128]{2,1,0:T(8,128)S(1)}, f32[12,128,128]{2,1,0:T(8,128)S(1)}, u32[]{:S(2)}, u32[]{:S(2)}) %collective-permute-start) | collective-permute-done | bytes 786464 | tf_op jit(solution)/shard_map/ppermute | solution.py:74
  49.2 1.3 collective-permute-start.5
  51.6 1.6 collective-permute-start.2
  53.2 12.0 %shard_map.76 = (bf16[16,512,128]{2,1,0:T(8,128)(2,1)}, bf16[4,3,4,128,128]{4,3,2,1,0:T(8,128)(2,1)}) custom-call(bf16[16,512,128]{2,1,0:T(8,128)(2,1)} %fusion.q_ref, bf16[16,512,128]{2,1,0:T(8,128)(2,1)} %bitcast.44, bf16[16,512,128]{2,1,0:T(8,128)(2,1)} %get-tuple-element.39.v_ref, bf16[16,512,128]{2,1,0:T(8,128)(2,1)} %get-tuple-element.38.d_ref, ...), custom_call_target="tpu_custom_call" | custom-call | flops 12079595520 | bytes 4194304 | tf_op jit(solution)/shard_map/pallas_call | solution.py:147
  65.2 3.6 %all-to-all-start.1 = ((bf16[4,3,4,128,128]{4,3,2,1,0:T(8,128)(2,1)}), bf16[4,3,4,128,128]{4,3,2,1,0:T(8,128)(2,1)S(1)}, u32[]{:S(2)}, u32[]{:S(2)}) async-start(bf16[4,3,4,128,128]{4,3,2,1,0:T(8,128)(2,1)} %get-tuple-element.19), calls=%async_computation.1 | async-start | bytes 3145728 | tf_op jit(solution)/shard_map/all_to_all | solution.py:165
  68.8 16.1 %collective-permute-done.5 = f32[12,128,128]{2,1,0:T(8,128)} collective-permute-done((f32[12,128,128]{2,1,0:T(8,128)}, f32[12,128,128]{2,1,0:T(8,128)}, u32[]{:S(2)}, u32[]{:S(2)}) %collective-permute-start.5) | collective-permute-done | bytes 786464 | tf_op jit(solution)/shard_map/ppermute | solution.py:74
  84.9 2.7 %add_add_fusion.rest_ref = f32[12,128,128]{2,1,0:T(8,128)} fusion(f32[12,128,128]{2,1,0:T(8,128)} %collective-permute-done.5, f32[12,128,128]{2,1,0:T(8,128)} %copy-done.4, f32[12,128,128]{2,1,0:T(8,128)} %copy-done.5, f32[16,128,128]{2,1,0:T(8,128)S(1)} %copy-done), kind=kLoop, calls=%fused_computation.14 | loop fusion | flops 589824 | bytes 3932160 | tf_op jit(solution)/shard_map/add | solution.py:119
  87.5 2.2 %add_add_fusion.1.before_ref = f32[12,128,128]{2,1,0:T(8,128)} fusion(f32[12,128,128]{2,1,0:T(8,128)} %collective-permute-done.2, f32[12,128,128]{2,1,0:T(8,128)S(1)} %collective-permute-done, f32[12,128,128]{2,1,0:T(8,128)S(1)} %copy-done.3), kind=kLoop, calls=%fused_computation.15 | loop fusion | flops 393216 | bytes 3145728 | tf_op jit(solution)/shard_map/add | solution.py:75
  89.7 29.4 %shard_map.77 = (bf16[16,512,128]{2,1,0:T(8,128)(2,1)}, bf16[4,3,12,128,128]{4,3,2,1,0:T(8,128)(2,1)}) custom-call(bf16[16,512,128]{2,1,0:T(8,128)(2,1)} %fusion.q_ref, bf16[16,512,128]{2,1,0:T(8,128)(2,1)} %bitcast.45, bf16[16,512,128]{2,1,0:T(8,128)(2,1)} %get-tuple-element.39.v_ref, ...), custom_call_target="tpu_custom_call", output_to_operand_aliasing={{0}: (7, {})} | custom-call | flops 36238786560 | bytes 12582912 | tf_op jit(solution)/shard_map/pallas_call | solution.py:147
  119.1 5.2 %all-to-all-start = ((bf16[4,3,12,128,128]{4,3,2,1,0:T(8,128)(2,1)}), bf16[4,3,12,128,128]{4,3,2,1,0:T(8,128)(2,1)}, u32[]{:S(2)}, u32[]{:S(2)}) async-start(bf16[4,3,12,128,128]{4,3,2,1,0:T(8,128)(2,1)} %get-tuple-element.18), calls=%async_computation | async-start | bytes 9437184 | tf_op jit(solution)/shard_map/all_to_all | solution.py:165
  124.3 4.3 %copy.40 = bf16[512,16,128]{2,1,0:T(8,128)(2,1)} copy(bf16[512,16,128]{2,0,1:T(8,128)(2,1)} %bitcast.46) | data formatting | bytes 4194304
  128.7 49.2 %all-to-all-done = bf16[4,3,12,128,128]{4,3,2,1,0:T(8,128)(2,1)} async-done(((bf16[4,3,12,128,128]{4,3,2,1,0:T(8,128)(2,1)}), bf16[4,3,12,128,128]{4,3,2,1,0:T(8,128)(2,1)}, u32[]{:S(2)}, u32[]{:S(2)}) %all-to-all-start) | async-done | bytes 4718624 | tf_op jit(solution)/shard_map/all_to_all | solution.py:165
  177.9 3.3 %slice_bitcast_fusion = (bf16[4,12,128,128]{3,2,1,0:T(8,128)(2,1)S(1)}, bf16[4,12,128,128]{3,2,1,0:T(8,128)(2,1)S(1)}, bf16[4,12,128,128]{3,2,1,0:T(8,128)(2,1)S(1)}) fusion(bf16[4,3,12,128,128]{4,3,2,1,0:T(8,128)(2,1)} %all-to-all-done), kind=kLoop, calls=%fused_computation.11 | loop fusion | bytes 9437184 | tf_op jit(solution)/shard_map/squeeze | solution.py:174
  181.4 2.7 %copy.51 = bf16[64,128,128]{2,0,1:T(8,128)(2,1)} copy(bf16[64,128,128]{2,1,0:T(8,128)(2,1)S(1)} %bitcast.40) | data formatting | bytes 4194304 | tf_op jit(solution)/shard_map/reshape | solution.py:174
  184.3 2.7 %copy.52 = bf16[64,128,128]{2,0,1:T(8,128)(2,1)} copy(bf16[64,128,128]{2,1,0:T(8,128)(2,1)S(1)} %bitcast.41) | data formatting | bytes 4194304 | tf_op jit(solution)/shard_map/reshape | solution.py:174
  187.2 2.7 %copy.53 = bf16[64,128,128]{2,0,1:T(8,128)(2,1)} copy(bf16[64,128,128]{2,1,0:T(8,128)(2,1)S(1)} %bitcast.42) | data formatting | bytes 4194304 | tf_op jit(solution)/shard_map/reshape | solution.py:174
  (55 shorter events, 14.7 us)
Async XLA Ops:
  0.6 3.6 %copy-start.6 = (bf16[512,16,128]{2,1,0:T(8,128)(2,1)S(1)}, bf16[512,16,128]{2,1,0:T(8,128)(2,1)}, u32[]{:S(2)}) copy-start(bf16[512,16,128]{2,1,0:T(8,128)(2,1)} %param.4) | copy-start | bytes 6291460
  4.3 2.0 %copy-start.7 = (bf16[512,16,128]{2,1,0:T(8,128)(2,1)S(1)}, bf16[512,16,128]{2,1,0:T(8,128)(2,1)}, u32[]{:S(2)}) copy-start(bf16[512,16,128]{2,1,0:T(8,128)(2,1)} %param.7) | copy-start | bytes 6291460
  4.3 3.0 %copy-start.8 = (bf16[512,16,128]{2,1,0:T(8,128)(2,1)S(1)}, bf16[512,16,128]{2,1,0:T(8,128)(2,1)}, u32[]{:S(2)}) copy-start(bf16[512,16,128]{2,1,0:T(8,128)(2,1)} %param.6) | copy-start | bytes 6291460
  15.6 9.6 %copy-start.1 = (f32[16,128,128]{2,1,0:T(8,128)S(1)}, f32[16,128,128]{2,1,0:T(8,128)}, u32[]{:S(2)}) copy-start(f32[16,128,128]{2,1,0:T(8,128)} %get-tuple-element.12) | copy-start | bytes 3145732
  15.6 11.1 %copy-start = (f32[16,128,128]{2,1,0:T(8,128)S(1)}, f32[16,128,128]{2,1,0:T(8,128)}, u32[]{:S(2)}) copy-start(f32[16,128,128]{2,1,0:T(8,128)} %get-tuple-element.13) | copy-start | bytes 3145732
  16.8 9.9 %collective-permute-start.9 = (f32[4,128,128]{2,1,0:T(8,128)S(1)}, f32[4,128,128]{2,1,0:T(8,128)S(1)}, u32[]{:S(2)}, u32[]{:S(2)}) collective-permute-start(f32[4,128,128]{2,1,0:T(8,128)S(1)} %slice.35), channel_id=1, source_target_pairs={{12,8},{13,9},{14,10},{15,11},{28,24},{29,25},{30,26},{31,27}} | collective-permute-start | bytes 786440 | tf_op jit(solution)/shard_map/ppermute | solution.py:74
  18.4 11.6 %collective-permute-start.6 = (f32[4,128,128]{2,1,0:T(8,128)S(1)}, f32[4,128,128]{2,1,0:T(8,128)S(1)}, u32[]{:S(2)}, u32[]{:S(2)}) collective-permute-start(f32[4,128,128]{2,1,0:T(8,128)S(1)} %slice.34), channel_id=1, source_target_pairs={{0,4},{1,5},{2,6},{3,7},{16,20},{17,21},{18,22},{19,23}} | collective-permute-start | bytes 786440 | tf_op jit(solution)/shard_map/ppermute | solution.py:74
  24.6 9.1 %collective-permute-start.3 = (f32[12,128,128]{2,1,0:T(8,128)S(1)}, f32[12,128,128]{2,1,0:T(8,128)S(1)}, u32[]{:S(2)}, u32[]{:S(2)}) collective-permute-start(f32[12,128,128]{2,1,0:T(8,128)S(1)} %slice.33), channel_id=1, source_target_pairs={{12,8},{13,9},{14,10},{15,11},{28,24},{29,25},{30,26},{31,27}} | collective-permute-start | bytes 2359304 | tf_op jit(solution)/shard_map/ppermute | solution.py:74
  25.4 20.4 %collective-permute-start = (f32[12,128,128]{2,1,0:T(8,128)S(1)}, f32[12,128,128]{2,1,0:T(8,128)S(1)}, u32[]{:S(2)}, u32[]{:S(2)}) collective-permute-start(f32[12,128,128]{2,1,0:T(8,128)S(1)} %slice.32), channel_id=1, source_target_pairs={{0,4},{1,5},{2,6},{3,7},{16,20},{17,21},{18,22},{19,23}} | collective-permute-start | bytes 2359304 | tf_op jit(solution)/shard_map/ppermute | solution.py:74
  26.8 4.8 %collective-permute-start.10 = (f32[4,128,128]{2,1,0:T(8,128)S(1)}, f32[4,128,128]{2,1,0:T(8,128)S(1)}, u32[]{:S(2)}, u32[]{:S(2)}) collective-permute-start(f32[4,128,128]{2,1,0:T(8,128)S(1)} %slice_add_fusion.3), channel_id=1, source_target_pairs={{8,4},{9,5},{10,6},{11,7},{24,20},{25,21},{26,22},{27,23}} | collective-permute-start | bytes 786440 | tf_op jit(solution)/shard_map/ppermute | solution.py:74
  30.1 2.8 %collective-permute-start.7 = (f32[4,128,128]{2,1,0:T(8,128)S(1)}, f32[4,128,128]{2,1,0:T(8,128)S(1)}, u32[]{:S(2)}, u32[]{:S(2)}) collective-permute-start(f32[4,128,128]{2,1,0:T(8,128)S(1)} %slice_add_fusion.1), channel_id=1, source_target_pairs={{4,8},{5,9},{6,10},{7,11},{20,24},{21,25},{22,26},{23,27}} | collective-permute-start | bytes 786440 | tf_op jit(solution)/shard_map/ppermute | solution.py:74
  31.6 15.8 %collective-permute-start.11 = (f32[4,128,128]{2,1,0:T(8,128)S(1)}, f32[4,128,128]{2,1,0:T(8,128)S(1)}, u32[]{:S(2)}, u32[]{:S(2)}) collective-permute-start(f32[4,128,128]{2,1,0:T(8,128)S(1)} %slice_add_fusion.2), channel_id=1, source_target_pairs={{4,0},{5,1},{6,2},{7,3},{20,16},{21,17},{22,18},{23,19}} | collective-permute-start | bytes 786440 | tf_op jit(solution)/shard_map/ppermute | solution.py:74
  32.9 13.6 %collective-permute-start.8 = (f32[4,128,128]{2,1,0:T(8,128)S(1)}, f32[4,128,128]{2,1,0:T(8,128)S(1)}, u32[]{:S(2)}, u32[]{:S(2)}) collective-permute-start(f32[4,128,128]{2,1,0:T(8,128)S(1)} %slice_add_fusion), channel_id=1, source_target_pairs={{8,12},{9,13},{10,14},{11,15},{24,28},{25,29},{26,30},{27,31}} | collective-permute-start | bytes 786440 | tf_op jit(solution)/shard_map/ppermute | solution.py:74
  33.6 12.2 %copy-start.4 = (f32[12,128,128]{2,1,0:T(8,128)}, f32[12,128,128]{2,1,0:T(8,128)S(1)}, u32[]{:S(2)}) copy-start(f32[12,128,128]{2,1,0:T(8,128)S(1)} %collective-permute-done.3) | copy-start | bytes 2359300
  33.7 14.4 %collective-permute-start.4 = (f32[12,128,128]{2,1,0:T(8,128)S(1)}, f32[12,128,128]{2,1,0:T(8,128)S(1)}, u32[]{:S(2)}, u32[]{:S(2)}) collective-permute-start(f32[12,128,128]{2,1,0:T(8,128)S(1)} %slice_add_fusion.7), channel_id=1, source_target_pairs={{8,4},{9,5},{10,6},{11,7},{24,20},{25,21},{26,22},{27,23}} | collective-permute-start | bytes 2359304 | tf_op jit(solution)/shard_map/ppermute | solution.py:74
  45.9 4.6 %collective-permute-start.1 = (f32[12,128,128]{2,1,0:T(8,128)S(1)}, f32[12,128,128]{2,1,0:T(8,128)S(1)}, u32[]{:S(2)}, u32[]{:S(2)}) collective-permute-start(f32[12,128,128]{2,1,0:T(8,128)S(1)} %slice_add_fusion.5), channel_id=1, source_target_pairs={{4,8},{5,9},{6,10},{7,11},{20,24},{21,25},{22,26},{23,27}} | collective-permute-start | bytes 2359304 | tf_op jit(solution)/shard_map/ppermute | solution.py:74
  48.1 3.5 %copy-start.5 = (f32[12,128,128]{2,1,0:T(8,128)}, f32[12,128,128]{2,1,0:T(8,128)S(1)}, u32[]{:S(2)}) copy-start(f32[12,128,128]{2,1,0:T(8,128)S(1)} %collective-permute-done.4) | copy-start | bytes 2359300
  49.2 35.7 %collective-permute-start.5 = (f32[12,128,128]{2,1,0:T(8,128)}, f32[12,128,128]{2,1,0:T(8,128)}, u32[]{:S(2)}, u32[]{:S(2)}) collective-permute-start(f32[12,128,128]{2,1,0:T(8,128)} %slice_add_fusion.6), channel_id=1, source_target_pairs={{4,0},{5,1},{6,2},{7,3},{20,16},{21,17},{22,18},{23,19}} | collective-permute-start | bytes 2359304 | tf_op jit(solution)/shard_map/ppermute | solution.py:74
  50.5 14.7 %copy-start.2 = (f32[12,128,128]{2,1,0:T(8,128)}, f32[12,128,128]{2,1,0:T(8,128)S(1)}, u32[]{:S(2)}) copy-start(f32[12,128,128]{2,1,0:T(8,128)S(1)} %collective-permute-done.1) | copy-start | bytes 2359300
  51.6 35.9 %collective-permute-start.2 = (f32[12,128,128]{2,1,0:T(8,128)}, f32[12,128,128]{2,1,0:T(8,128)}, u32[]{:S(2)}, u32[]{:S(2)}) collective-permute-start(f32[12,128,128]{2,1,0:T(8,128)} %slice_add_fusion.4), channel_id=1, source_target_pairs={{8,12},{9,13},{10,14},{11,15},{24,28},{25,29},{26,30},{27,31}} | collective-permute-start | bytes 2359304 | tf_op jit(solution)/shard_map/ppermute | solution.py:74
  65.2 53.9 %all-to-all-start.1 = ((bf16[4,3,4,128,128]{4,3,2,1,0:T(8,128)(2,1)}), bf16[4,3,4,128,128]{4,3,2,1,0:T(8,128)(2,1)S(1)}, u32[]{:S(2)}, u32[]{:S(2)}) async-start(bf16[4,3,4,128,128]{4,3,2,1,0:T(8,128)(2,1)} %get-tuple-element.19), calls=%async_computation.1 | async-start | bytes 3145728 | tf_op jit(solution)/shard_map/all_to_all | solution.py:165
  68.8 18.8 %copy-start.3 = (f32[12,128,128]{2,1,0:T(8,128)S(1)}, f32[12,128,128]{2,1,0:T(8,128)}, u32[]{:S(2)}) copy-start(f32[12,128,128]{2,1,0:T(8,128)} %copy-done.2) | copy-start | bytes 2359300
  119.1 58.8 %all-to-all-start = ((bf16[4,3,12,128,128]{4,3,2,1,0:T(8,128)(2,1)}), bf16[4,3,12,128,128]{4,3,2,1,0:T(8,128)(2,1)}, u32[]{:S(2)}, u32[]{:S(2)}) async-start(bf16[4,3,12,128,128]{4,3,2,1,0:T(8,128)(2,1)} %get-tuple-element.18), calls=%async_computation | async-start | bytes 9437184 | tf_op jit(solution)/shard_map/all_to_all | solution.py:165
